TPU v7x, 32 devices: a whole 2x2x4 slice. The times are simulated.
32 devices in a mesh: blk: 8 (over z, y), uly: 4 (over x, core).
Axes of the slice: x: 2, y: 2, z: 4, core: 2. Of those that a mesh axis runs over, the one named last changes fastest.
Arguments:
- tokens: bfloat16 [8, 16, 8, 1024], P('blk', None, 'uly'), may hold values from -12 to 12, as said below
- conv_weight: float32 [27, 1024], replicated, may hold values from -1.2 to 1.2
- conv_bias: float32 [1024], replicated, may hold values from -3 to 3
- qkv_weight: bfloat16 [3072, 1024], P('uly'), may hold values from -0.25 to 0.25
- out_weight: bfloat16 [1024, 1024], P('uly'), may hold values from -1.5 to 1.5
Outputs:
- attended_out: bfloat16 [8, 16, 8, 1024], P('blk', None, 'uly')
Inputs may be any that keep to these rules, and one draw needn't show every extreme that they name: `tokens`: patch embeddings of the subvolume.
All inputs are finite; a program needn't handle non-finite values.
Results may differ from a plain program's by a relative error of at most 0.012.
The roundings to bfloat16 on the way count: a program that leaves them out, or rounds other values in their place, can miss the bound.
Values may be sent and summed in bfloat16 or wider, within the bound.
No kernel may reach another device: no remote copies, remote signals or barrier semaphores. Data moves between devices by JAX's collectives and lax.ppermute only.
A program may use at most 64 MiB of HBM per device.

v0:
```python
import math

import jax
import jax.numpy as jnp
from jax import lax
from jax.sharding import PartitionSpec as P

HS = 64


def padded_2(shard, sides, width):
    for axis, dim in sides:
        size, length = (lax.axis_size(axis), shard.shape[dim])
        up = [(i, (i + 1) % size) for i in range(size - 1)]
        down = [(j, i) for i, j in up]
        last = lax.slice_in_dim(shard, length - width, length, axis=dim)
        initial = lax.slice_in_dim(shard, 0, width, axis=dim)
        before = lax.ppermute(last, axis, up)
        after = lax.ppermute(initial, axis, down)
        shard = jnp.concatenate([before, shard, after], axis=dim)
    return shard


def times_transposed(left, right):
    return lax.dot_general(
        left, right, (((1,), (1,)), ((), ())), preferred_element_type=jnp.float32
    )


def on_device(tokens, conv_weight, conv_bias, qkv_weight, out_weight):
    z_count, x_count, y_count, features = tokens.shape
    padded = padded_2(tokens, (("blk", 0), ("uly", 2)), 1)
    padded = jnp.pad(padded, ((0, 0), (1, 1), (0, 0), (0, 0)))
    summed = tokens.astype(jnp.float32) + conv_bias
    for step_z in range(3):
        for step_x in range(3):
            for step_y in range(3):
                summed = (
                    summed
                    + conv_weight[9 * step_z + 3 * step_x + step_y]
                    * padded[
                        step_z : step_z + z_count,
                        step_x : step_x + x_count,
                        step_y : step_y + y_count,
                    ]
                )
    token_rows = summed.astype(jnp.bfloat16).reshape(-1, features)
    local_tok = token_rows.shape[0]
    groups = lax.axis_size("uly")
    heads_here = qkv_weight.shape[0] // (3 * HS)
    slab_tok = groups * local_tok
    projected = times_transposed(
        token_rows, lax.all_gather(qkv_weight, "uly", axis=0, tiled=True)
    ).astype(jnp.bfloat16)
    grouped = projected.reshape(local_tok, groups, heads_here * 3 * HS)
    slab_data = lax.all_to_all(grouped, "uly", split_axis=1, concat_axis=0, tiled=True).reshape(
        slab_tok, heads_here * 3 * HS
    )
    split_heads = slab_data.reshape(slab_tok, heads_here, 3, HS)
    queries = split_heads[:, :, 0]
    key_rows = split_heads[:, :, 1]
    val_rows = split_heads[:, :, 2]
    score_scale = 1.0 / math.sqrt(HS)

    def key_block(carry_state, key_value):
        running_max, running_sum, weighted = carry_state
        key_part, value_part = key_value
        scores = (
            jnp.einsum("qhd,khd->hqk", queries, key_part, preferred_element_type=jnp.float32)
            * score_scale
        )
        new_max = jnp.maximum(running_max, jnp.max(scores, axis=2))
        shrink = jnp.exp(running_max - new_max)
        weights = jnp.exp(scores - new_max[:, :, None])
        running_sum = running_sum * shrink + jnp.sum(weights, axis=2)
        weighted = weighted * shrink[:, :, None] + jnp.einsum(
            "hqk,khd->hqd",
            weights.astype(jnp.bfloat16),
            value_part,
            preferred_element_type=jnp.float32,
        )
        return ((new_max, running_sum, weighted), None)

    start_state = (
        jnp.full((heads_here, slab_tok), -1e30, jnp.float32),
        jnp.zeros((heads_here, slab_tok), jnp.float32),
        jnp.zeros((heads_here, slab_tok, HS), jnp.float32),
    )
    key_piece = lax.all_gather(key_rows, "blk", axis=0, tiled=True)
    value_piece = lax.all_gather(val_rows, "blk", axis=0, tiled=True)
    key_count = key_piece.shape[0]
    block_len = 1024
    key_blocks = key_piece.reshape(key_count // block_len, block_len, heads_here, HS)
    value_blocks = value_piece.reshape(key_count // block_len, block_len, heads_here, HS)
    folded, unused = lax.scan(key_block, start_state, (key_blocks, value_blocks))
    running_max, running_sum, weighted = folded
    attended = (weighted / running_sum[:, :, None]).astype(jnp.bfloat16)
    head_rows = attended.transpose(1, 0, 2).reshape(slab_tok, heads_here * HS)
    split_rows = head_rows.reshape(groups, local_tok, 1, heads_here * HS)
    token_heads = lax.all_to_all(
        split_rows, "uly", split_axis=0, concat_axis=2, tiled=True
    ).reshape(local_tok, groups * heads_here * HS)
    result = jnp.dot(
        token_heads,
        lax.all_gather(out_weight, "uly", axis=0, tiled=True),
        preferred_element_type=jnp.float32,
    )
    return result.astype(jnp.bfloat16).reshape(z_count, x_count, y_count, features)


def solution(mesh):
    in_specs = (P("blk", None, "uly", None), P(), P(), P("uly", None), P("uly", None))
    out_specs = P("blk", None, "uly", None)
    return jax.shard_map(
        on_device, mesh=mesh, in_specs=in_specs, out_specs=out_specs, check_vma=False
    )
```

profile of v0, /device:TPU:0, one launch (start us, length us, event | category | flops | bytes accessed | tf_op | source)
XLA Modules:
  0.0 148.9 jit_solution(1447349733474581471)
XLA Ops:
  6.5 0.0 copy-start
  6.5 0.0 copy-start.1
  6.5 0.0 copy-start.2
  6.5 0.0 all-gather.5.cloned.1.call-start
  6.5 0.7 all-gather.5.cloned.1.call-update
  7.3 0.0 all-gather.7.cloned.1.call-start
  7.3 4.9 %collective-permute-start = (bf16[1,16,2,1024]{3,2,1,0:T(2,128)(2,1)}, bf16[1,16,2,1024]{3,2,1,0:T(2,128)(2,1)S(1)}, u32[]{:S(2)}, u32[]{:S(2)}) collective-permute-start(bf16[1,16,2,1024]{3,2,1,0:T(2,128)(2,1)} %param.5), channel_id=1, source_target_pairs={{0,4},{4,8},{8,12},{12,16},{16,20},{20,24},{24,28},{1,5},{5,9},{9,... | collective-permute-start | bytes 196616 | tf_op jit(solution)/shard_map/ppermute | solution.py:18
  12.2 1.3 collective-permute-start.1
  13.5 0.0 all-gather.7.cloned.1.call-update
  13.5 0.0 copy-done.1
  13.5 0.1 fusion.28
  13.6 0.8 collective-permute-done
  14.4 0.0 copy-done
  14.5 0.1 constant_dynamic-update-slice_fusion.1
  14.5 4.0 %collective-permute-done.1 = bf16[1,16,2,1024]{3,2,1,0:T(2,128)(2,1)S(1)} collective-permute-done((bf16[1,16,2,1024]{3,2,1,0:T(2,128)(2,1)}, bf16[1,16,2,1024]{3,2,1,0:T(2,128)(2,1)S(1)}, u32[]{:S(2)}, u32[]{:S(2)}) %collective-permute-start.1) | collective-permute-done | bytes 65568 | tf_op jit(solution)/shard_map/ppermute | solution.py:19
  18.6 0.1 constant_dynamic-update-slice_fusion
  18.6 0.3 fusion.27
  18.9 1.3 collective-permute-start.2
  20.2 1.3 collective-permute-start.3
  21.5 0.0 collective-permute-done.2
  21.6 3.7 %collective-permute-done.3 = bf16[3,16,1,1024]{3,2,1,0:T(2,128)(2,1)S(1)} collective-permute-done((bf16[3,16,1,1024]{3,2,1,0:T(2,128)(2,1)S(1)}, bf16[3,16,1,1024]{3,2,1,0:T(2,128)(2,1)S(1)}, u32[]{:S(2)}, u32[]{:S(2)}) %collective-permute-start.3) | collective-permute-done | bytes 98336 | tf_op jit(solution)/shard_map/ppermute | solution.py:19
  25.3 0.7 select_maximum_fusion
  25.9 0.0 copy-done.2
  25.9 2.5 %add_convert_fusion = bf16[1,16,2,1024]{3,2,1,0:T(2,128)(2,1)S(1)} fusion(bf16[1,16,2,1024]{3,2,1,0:T(2,128)(2,1)S(1)} %collective-permute-done.1, bf16[1,16,2,1024]{3,2,1,0:T(2,128)(2,1)S(1)} %copy-done, bf16[1,16,2,1024]{3,2,1,0:T(2,128)(2,1)S(1)} %collective-permute-done, bf16[3,18,4,1024]{3,2,1,0:T(4,128)(2,1)S(1)} %select_maximum_fusion, ...), kind=kLoop, calls=%fused_computation.35 | loop fusion | flops 3309568 | bytes 1949696 | tf_op jit(solution)/shard_map/convert_element_type | solution.py:47
  28.4 31.7 %all-gather.5.cloned.1.call-done = bf16[3072,1024]{1,0:T(8,128)(2,1)} async-done(((bf16[768,1024]{1,0:T(8,128)(2,1)}), bf16[3072,1024]{1,0:T(8,128)(2,1)}) %all-gather.5.cloned.1.call-update) | async-done | bytes 6291472 | tf_op jit(solution)/shard_map/all_gather | solution.py:53
  60.1 4.7 %convolution_convert_fusion = bf16[32,3072]{1,0:T(8,128)(2,1)S(1)} fusion(bf16[32,1024]{1,0:T(8,128)(2,1)S(1)} %reshape.117, bf16[3072,1024]{1,0:T(8,128)(2,1)} %all-gather.5.cloned.1.call-done), kind=kOutput, calls=%fused_computation | convolution fusion | flops 201424896 | bytes 6553600 | tf_op jit(solution)/shard_map/dot_general | solution.py:25
  64.9 9.2 %all_to_all.30 = bf16[32,4,768]{2,0,1:T(8,128)(2,1)S(1)} all-to-all(bf16[32,4,768]{2,0,1:T(8,128)(2,1)S(1)} %bitcast.78), channel_id=1, replica_groups=mesh['blk'=8,'uly'=4] {'uly'}, dimensions={1} | all-to-all | bytes 393216 | tf_op jit(solution)/shard_map/all_to_all | solution.py:56
  74.1 0.3 reshape_reshape.6
  74.5 0.6 fusion.26
  75.0 0.1 copy.20
  75.2 0.1 copy.19
  75.3 0.1 copy.21
  75.4 27.6 %all-gather = bf16[1024,4,1,64]{0,3,1,2:T(8,128)(2,1)S(1)} all-gather(bf16[128,4,1,64]{0,3,1,2:T(8,128)(2,1)S(1)} %copy.20), channel_id=2, replica_groups=mesh['blk'=8,'uly'=4] {'blk'}, dimensions={0}, use_global_device_ids=true | all-gather | bytes 589824 | tf_op jit(solution)/shard_map/all_gather | solution.py:89
  103.1 0.6 multiply_reduce_fusion
  103.6 0.5 fusion
  104.2 27.7 %all-gather.1 = bf16[1024,4,1,64]{0,3,1,2:T(8,128)(2,1)S(1)} all-gather(bf16[128,4,1,64]{0,3,1,2:T(8,128)(2,1)S(1)} %copy.21), channel_id=3, replica_groups=mesh['blk'=8,'uly'=4] {'blk'}, dimensions={0}, use_global_device_ids=true | all-gather | bytes 589824 | tf_op jit(solution)/shard_map/all_gather | solution.py:90
  131.9 0.6 fusion.4
  132.5 0.1 copy.16
  132.6 0.1 reshape_reshape.7
  132.8 6.5 %all_to_all.31 = bf16[4,32,1,256]{3,1,2,0:T(8,128)(2,1)S(1)} all-to-all(bf16[4,32,1,256]{3,1,2,0:T(8,128)(2,1)S(1)} %bitcast.81), channel_id=1, replica_groups=mesh['blk'=8,'uly'=4] {'uly'}, dimensions={0} | all-to-all | bytes 131072 | tf_op jit(solution)/shard_map/all_to_all | solution.py:100
  139.3 0.1 copy.18
  139.4 0.0 all-gather.7.cloned.1.call-done
  139.4 2.1 %convolution_convert_fusion.1 = bf16[32,1024]{1,0:T(8,128)(2,1)S(1)} fusion(bf16[32,1024]{1,0:T(8,128)(2,1)S(1)} %bitcast.80, bf16[1024,1024]{1,0:T(8,128)(2,1)} %all-gather.7.cloned.1.call-done), kind=kOutput, calls=%fused_computation.11 | convolution fusion | flops 67141632 | bytes 2228224 | tf_op jit(solution)/shard_map/dot_general | solution.py:103
  141.4 0.7 reshape.120
  (7 shorter events, 0.2 us)
Async XLA Ops:
  6.5 7.9 %copy-start = (bf16[1,16,2,1024]{3,2,1,0:T(2,128)(2,1)S(1)}, bf16[1,16,2,1024]{3,2,1,0:T(2,128)(2,1)}, u32[]{:S(2)}) copy-start(bf16[1,16,2,1024]{3,2,1,0:T(2,128)(2,1)} %param.5) | copy-start | bytes 196612
  6.5 7.0 %copy-start.1 = (f32[27,1024]{1,0:T(8,128)S(1)}, f32[27,1024]{1,0:T(8,128)}, u32[]{:S(2)}) copy-start(f32[27,1024]{1,0:T(8,128)} %param.6) | copy-start | bytes 331780
  6.5 19.4 %copy-start.2 = (f32[1024]{0:T(1024)S(1)}, f32[1024]{0:T(1024)}, u32[]{:S(2)}) copy-start(f32[1024]{0:T(1024)} %param.7) | copy-start | bytes 12292
  6.5 53.6 %all-gather.5.cloned.1.call-start = ((), (), s32[]{:S(2)}) async-start(), calls=%async_computation.2 | async-start | bytes 7864320 | tf_op jit(solution)/shard_map/all_gather | solution.py:53
  7.3 132.1 %all-gather.7.cloned.1.call-start = ((), (), s32[]{:S(2)}) async-start(), calls=%async_computation.3 | async-start | bytes 2621440 | tf_op jit(solution)/shard_map/all_gather | solution.py:105
  7.3 7.1 %collective-permute-start = (bf16[1,16,2,1024]{3,2,1,0:T(2,128)(2,1)}, bf16[1,16,2,1024]{3,2,1,0:T(2,128)(2,1)S(1)}, u32[]{:S(2)}, u32[]{:S(2)}) collective-permute-start(bf16[1,16,2,1024]{3,2,1,0:T(2,128)(2,1)} %param.5), channel_id=1, source_target_pairs={{0,4},{4,8},{8,12},{12,16},{16,20},{20,24},{24,28},{1,5},{5,9},{9,... | collective-permute-start | bytes 196616 | tf_op jit(solution)/shard_map/ppermute | solution.py:18
  12.2 6.4 %collective-permute-start.1 = (bf16[1,16,2,1024]{3,2,1,0:T(2,128)(2,1)}, bf16[1,16,2,1024]{3,2,1,0:T(2,128)(2,1)S(1)}, u32[]{:S(2)}, u32[]{:S(2)}) collective-permute-start(bf16[1,16,2,1024]{3,2,1,0:T(2,128)(2,1)} %param.5), channel_id=1, source_target_pairs={{4,0},{8,4},{12,8},{16,12},{20,16},{24,20},{28,24},{5,1},{9,5},{13... | collective-permute-start | bytes 196616 | tf_op jit(solution)/shard_map/ppermute | solution.py:19
  18.9 2.6 %collective-permute-start.2 = (bf16[3,16,1,1024]{3,2,1,0:T(2,128)(2,1)S(1)}, bf16[3,16,1,1024]{3,2,1,0:T(2,128)(2,1)S(1)}, u32[]{:S(2)}, u32[]{:S(2)}) collective-permute-start(bf16[3,16,1,1024]{3,2,1,0:T(2,128)(2,1)S(1)} %get-tuple-element.20), channel_id=1, source_target_pairs={{0,1},{1,2},{2,3},{4,5},{5,6},{6,7},{8,9},{9,10},{10,11},{12,13},{... | collective-permute-start | bytes 294920 | tf_op jit(solution)/shard_map/ppermute | solution.py:18
  20.2 5.1 %collective-permute-start.3 = (bf16[3,16,1,1024]{3,2,1,0:T(2,128)(2,1)S(1)}, bf16[3,16,1,1024]{3,2,1,0:T(2,128)(2,1)S(1)}, u32[]{:S(2)}, u32[]{:S(2)}) collective-permute-start(bf16[3,16,1,1024]{3,2,1,0:T(2,128)(2,1)S(1)} %get-tuple-element.28), channel_id=1, source_target_pairs={{1,0},{2,1},{3,2},{5,4},{6,5},{7,6},{9,8},{10,9},{11,10},{13,12},{... | collective-permute-start | bytes 294920 | tf_op jit(solution)/shard_map/ppermute | solution.py:19
Sparse Core Ops, SparseCore 0:
  8.9 51.1 all-gather.4
  61.7 23.6 all-gather.6
where the time goes:
time: 149 us
  blocking collectives  71.1 us (48%)
  waiting for transfers between devices  41 us (28%)
  between operations  13.6 us (9%)
  starting transfers between devices  8.8 us (6%)
  matrix products  7.93 us (5%)
  other arithmetic  3.67 us (2%)
  local copies, waits for them, and re-layouts  2.91 us (2%)
    all_gather x1, waiting for transfers between devices, on_device(): lax.all_gather(qkv_weight, 'uly', axis=0, tiled=True)  31.7 us
    all_gather x1, blocking collectives, on_device(): value_piece = lax.all_gather(val_rows, 'blk', axis=0, tiled=True)  27.7 us
    all_gather x1, blocking collectives, on_device(): key_piece = lax.all_gather(key_rows, 'blk', axis=0, tiled=True)  27.6 us
    all_to_all x1, blocking collectives, on_device(): lax.all_to_all(grouped, 'uly', split_axis=1, concat_axis=0, tiled=True)  9.21 us
    ppermute x2, waiting for transfers between devices, padded_2(): after = lax.ppermute(initial, axis, down)  7.75 us
    all_to_all x1, blocking collectives, on_device(): lax.all_to_all(split_rows, 'uly', split_axis=0, concat_axis=2, tiled=True)  6.49 us
    ppermute x2, starting transfers between devices, padded_2(): before = lax.ppermute(last, axis, up)  6.18 us
    dot_general x1, matrix products, times_transposed(): lax.dot_general(left, right, (((1,), (1,)), ((), ())), preferred_element_...  4.72 us
  transfers between devices with their start and end apart: 6, of which 4 were waited for; matrix products, arithmetic and copies ran while one was open for 8% of the time, Pallas kernels for 0%

commit v1 on v0

--- a/solution.py
+++ b/solution.py
@@ -46,17 +46,11 @@
                 )
     token_rows = summed.astype(jnp.bfloat16).reshape(-1, features)
     local_tok = token_rows.shape[0]
-    groups = lax.axis_size("uly")
     heads_here = qkv_weight.shape[0] // (3 * HS)
-    slab_tok = groups * local_tok
-    projected = times_transposed(
-        token_rows, lax.all_gather(qkv_weight, "uly", axis=0, tiled=True)
-    ).astype(jnp.bfloat16)
-    grouped = projected.reshape(local_tok, groups, heads_here * 3 * HS)
-    slab_data = lax.all_to_all(grouped, "uly", split_axis=1, concat_axis=0, tiled=True).reshape(
-        slab_tok, heads_here * 3 * HS
-    )
-    split_heads = slab_data.reshape(slab_tok, heads_here, 3, HS)
+    slab_rows = lax.all_gather(token_rows, "uly", axis=0, tiled=True)
+    slab_tok = slab_rows.shape[0]
+    projected = times_transposed(slab_rows, qkv_weight).astype(jnp.bfloat16)
+    split_heads = projected.reshape(slab_tok, heads_here, 3, HS)
     queries = split_heads[:, :, 0]
     key_rows = split_heads[:, :, 1]
     val_rows = split_heads[:, :, 2]
@@ -89,22 +83,15 @@
     key_piece = lax.all_gather(key_rows, "blk", axis=0, tiled=True)
     value_piece = lax.all_gather(val_rows, "blk", axis=0, tiled=True)
     key_count = key_piece.shape[0]
-    block_len = 1024
+    block_len = min(1024, key_count)
     key_blocks = key_piece.reshape(key_count // block_len, block_len, heads_here, HS)
     value_blocks = value_piece.reshape(key_count // block_len, block_len, heads_here, HS)
     folded, unused = lax.scan(key_block, start_state, (key_blocks, value_blocks))
     running_max, running_sum, weighted = folded
     attended = (weighted / running_sum[:, :, None]).astype(jnp.bfloat16)
     head_rows = attended.transpose(1, 0, 2).reshape(slab_tok, heads_here * HS)
-    split_rows = head_rows.reshape(groups, local_tok, 1, heads_here * HS)
-    token_heads = lax.all_to_all(
-        split_rows, "uly", split_axis=0, concat_axis=2, tiled=True
-    ).reshape(local_tok, groups * heads_here * HS)
-    result = jnp.dot(
-        token_heads,
-        lax.all_gather(out_weight, "uly", axis=0, tiled=True),
-        preferred_element_type=jnp.float32,
-    )
+    partial = jnp.dot(head_rows, out_weight, preferred_element_type=jnp.float32)
+    result = lax.psum_scatter(partial, "uly", scatter_dimension=0, tiled=True)
     return result.astype(jnp.bfloat16).reshape(z_count, x_count, y_count, features)
 
 

time: 149 us -> 124 us (0.83)
  waiting for transfers between devices: 41 us -> 24.3 us
  blocking collectives: 71.1 us -> 64.4 us
  matrix products: 7.93 us -> 2.88 us
  local copies, waits for them, and re-layouts: 2.91 us -> 4.73 us
    all_gather x2 -> x0, waiting for transfers between devices: 31.7 us -> none  [the longest x1 31.7 us: on_device(): lax.all_gather(qkv_weight, 'uly', axis=0, tiled=True)]
    reduce_scatter x0 -> x1, waiting for transfers between devices: none -> 19 us  [on_device(): result = lax.psum_scatter(partial, 'uly', scatter_dimension=0, tiled=True)]
    all_to_all x2 -> x0, blocking collectives: 15.7 us -> none  [the longest x1 9.21 us: on_device(): lax.all_to_all(grouped, 'uly', split_axis=1, concat_axis=0, tiled=True)]
    all_gather x0 -> x1, blocking collectives: none -> 8.62 us  [on_device(): slab_rows = lax.all_gather(token_rows, 'uly', axis=0, tiled=True)]
    dot_general x1, matrix products: 4.72 us -> 0.65 us  [times_transposed(): lax.dot_general(left, right, (((1,), (1,)), ((), ())), preferred_element_...]
    slice x2, local copies, waits for them, and re-layouts: 0.08 us -> 2.58 us  [on_device(): conv_weight[9 * step_z + 3 * step_x + step_y]]
    ppermute x2, waiting for transfers between devices: 7.75 us -> 5.26 us  [padded_2(): after = lax.ppermute(initial, axis, down)]
  transfers between devices with their start and end apart: 6 -> 5, of which waited for: 4 -> 3; matrix products, arithmetic and copies ran while one was open for 8% -> 3% of each run, Pallas kernels for 0% -> 0%
where the time goes in v1:
time: 124 us; the launch traced here: 123 us
  blocking collectives  64.4 us (52%)
  waiting for transfers between devices  24.3 us (20%)
  between operations  13.5 us (11%)
  starting transfers between devices  8.9 us (7%)
  local copies, waits for them, and re-layouts  4.73 us (4%)
  other arithmetic  4.58 us (4%)
  matrix products  2.88 us (2%)
    all_gather x1, blocking collectives, on_device(): key_piece = lax.all_gather(key_rows, 'blk', axis=0, tiled=True)  28 us
    all_gather x1, blocking collectives, on_device(): value_piece = lax.all_gather(val_rows, 'blk', axis=0, tiled=True)  27.7 us
    reduce_scatter x1, waiting for transfers between devices, on_device(): result = lax.psum_scatter(partial, 'uly', scatter_dimension=0, tiled=True)  19 us
    all_gather x1, blocking collectives, on_device(): slab_rows = lax.all_gather(token_rows, 'uly', axis=0, tiled=True)  8.62 us
    ppermute x2, starting transfers between devices, padded_2(): before = lax.ppermute(last, axis, up)  6.31 us
    ppermute x2, waiting for transfers between devices, padded_2(): after = lax.ppermute(initial, axis, down)  5.26 us
    ppermute x2, starting transfers between devices, padded_2(): after = lax.ppermute(initial, axis, down)  2.58 us
    slice x2, local copies, waits for them, and re-layouts, on_device(): conv_weight[9 * step_z + 3 * step_x + step_y]  2.58 us
  transfers between devices with their start and end apart: 5, of which 3 were waited for; matrix products, arithmetic and copies ran while one was open for 3% of the time, Pallas kernels for 0%

profile of v1, /device:TPU:0, one launch (start us, length us, event | category | flops | bytes accessed | tf_op | source)
XLA Modules:
  0.0 123.3 jit_solution(7568137373259578012)
XLA Ops:
  6.5 0.0 copy-start
  6.5 0.0 copy-start.2
  6.5 0.0 copy-start.3
  6.5 0.0 reduce-scatter.2.cloned.1.call-start
  6.5 5.0 %collective-permute-start = (bf16[1,16,2,1024]{3,2,1,0:T(2,128)(2,1)}, bf16[1,16,2,1024]{3,2,1,0:T(2,128)(2,1)S(1)}, u32[]{:S(2)}, u32[]{:S(2)}) collective-permute-start(bf16[1,16,2,1024]{3,2,1,0:T(2,128)(2,1)} %param.5), channel_id=1, source_target_pairs={{0,4},{4,8},{8,12},{12,16},{16,20},{20,24},{24,28},{1,5},{5,9},{9,... | collective-permute-start | bytes 196616 | tf_op jit(solution)/shard_map/ppermute | solution.py:18
  11.6 1.3 %collective-permute-start.1 = (bf16[1,16,2,1024]{3,2,1,0:T(2,128)(2,1)}, bf16[1,16,2,1024]{3,2,1,0:T(2,128)(2,1)S(1)}, u32[]{:S(2)}, u32[]{:S(2)}) collective-permute-start(bf16[1,16,2,1024]{3,2,1,0:T(2,128)(2,1)} %param.5), channel_id=1, source_target_pairs={{4,0},{8,4},{12,8},{16,12},{20,16},{24,20},{28,24},{5,1},{9,5},{13... | collective-permute-start | bytes 196616 | tf_op jit(solution)/shard_map/ppermute | solution.py:19
  12.9 1.4 %fusion.26 = (f32[1,1024]{1,0:T(1,128)S(1)}, f32[1,1024]{1,0:T(1,128)S(1)}, f32[1,1024]{1,0:T(1,128)S(1)}, f32[1,1024]{1,0:T(1,128)S(1)}, f32[1,1024]{1,0:T(1,12...) fusion(f32[27,1024]{1,0:T(8,128)} %param.6), kind=kLoop, calls=%fused_computation.47 | loop fusion | bytes 155648 | tf_op jit(solution)/shard_map/slice | solution.py:40
  14.3 0.0 collective-permute-done
  14.3 0.9 constant_dynamic-update-slice_fusion.1
  15.2 2.7 %collective-permute-done.1 = bf16[1,16,2,1024]{3,2,1,0:T(2,128)(2,1)S(1)} collective-permute-done((bf16[1,16,2,1024]{3,2,1,0:T(2,128)(2,1)}, bf16[1,16,2,1024]{3,2,1,0:T(2,128)(2,1)S(1)}, u32[]{:S(2)}, u32[]{:S(2)}) %collective-permute-start.1) | collective-permute-done | bytes 65568 | tf_op jit(solution)/shard_map/ppermute | solution.py:19
  17.9 0.1 constant_dynamic-update-slice_fusion
  18.0 0.3 fusion.25
  18.3 1.3 %collective-permute-start.2 = (bf16[3,16,1,1024]{3,2,1,0:T(2,128)(2,1)S(1)}, bf16[3,16,1,1024]{3,2,1,0:T(2,128)(2,1)S(1)}, u32[]{:S(2)}, u32[]{:S(2)}) collective-permute-start(bf16[3,16,1,1024]{3,2,1,0:T(2,128)(2,1)S(1)} %get-tuple-element.19), channel_id=1, source_target_pairs={{0,1},{1,2},{2,3},{4,5},{5,6},{6,7},{8,9},{9,10},{10,11},{12,13},{... | collective-permute-start | bytes 294920 | tf_op jit(solution)/shard_map/ppermute | solution.py:18
  19.6 1.3 %collective-permute-start.3 = (bf16[3,16,1,1024]{3,2,1,0:T(2,128)(2,1)S(1)}, bf16[3,16,1,1024]{3,2,1,0:T(2,128)(2,1)S(1)}, u32[]{:S(2)}, u32[]{:S(2)}) collective-permute-start(bf16[3,16,1,1024]{3,2,1,0:T(2,128)(2,1)S(1)} %get-tuple-element.20), channel_id=1, source_target_pairs={{1,0},{2,1},{3,2},{5,4},{6,5},{7,6},{9,8},{10,9},{11,10},{13,12},{... | collective-permute-start | bytes 294920 | tf_op jit(solution)/shard_map/ppermute | solution.py:19
  20.9 1.2 fusion.27
  22.1 0.0 collective-permute-done.2
  22.1 2.6 %collective-permute-done.3 = bf16[3,16,1,1024]{3,2,1,0:T(2,128)(2,1)S(1)} collective-permute-done((bf16[3,16,1,1024]{3,2,1,0:T(2,128)(2,1)S(1)}, bf16[3,16,1,1024]{3,2,1,0:T(2,128)(2,1)S(1)}, u32[]{:S(2)}, u32[]{:S(2)}) %collective-permute-start.3) | collective-permute-done | bytes 98336 | tf_op jit(solution)/shard_map/ppermute | solution.py:19
  24.6 0.7 select_maximum_fusion
  25.3 0.0 copy-done.2
  25.3 0.0 copy-done.3
  25.3 2.5 %add_convert_fusion = bf16[1,16,2,1024]{3,2,1,0:T(2,128)(2,1)S(1)} fusion(bf16[1,16,2,1024]{3,2,1,0:T(2,128)(2,1)S(1)} %collective-permute-done.1, bf16[1,16,2,1024]{3,2,1,0:T(2,128)(2,1)S(1)} %copy-done.2, bf16[1,16,2,1024]{3,2,1,0:T(2,128)(2,1)S(1)} %collective-permute-done, bf16[3,18,4,1024]{3,2,1,0:T(4,128)(2,1)S(1)} %select_maximum_fusion, ...), kind=kLoop, calls=%fused_computation.33 | loop fusion | flops 3309568 | bytes 1949696 | tf_op jit(solution)/shard_map/convert_element_type | solution.py:47
  27.8 8.6 %all_gather.9 = bf16[128,1024]{1,0:T(8,128)(2,1)S(1)} all-gather(bf16[32,1024]{1,0:T(8,128)(2,1)S(1)} %reshape.115), channel_id=1, replica_groups=mesh['blk'=8,'uly'=4] {'uly'}, dimensions={0}, use_global_device_ids=true | all-gather | bytes 327680 | tf_op jit(solution)/shard_map/all_gather | solution.py:50
  36.5 0.0 copy-done
  36.5 0.7 convolution_convert_fusion
  37.1 0.2 copy.9
  37.3 28.0 %all-gather = bf16[1024,4,1,64]{0,3,1,2:T(8,128)(2,1)S(1)} all-gather(bf16[128,4,1,64]{0,3,1,2:T(8,128)(2,1)S(1)} %get-tuple-element.18), channel_id=2, replica_groups=mesh['blk'=8,'uly'=4] {'blk'}, dimensions={0}, use_global_device_ids=true | all-gather | bytes 589824 | tf_op jit(solution)/shard_map/all_gather | solution.py:83
  65.3 0.6 multiply_reduce_fusion
  65.9 0.5 fusion
  66.4 0.0 copy-start.1
  66.5 27.7 %all-gather.1 = bf16[1024,4,1,64]{0,3,1,2:T(8,128)(2,1)S(1)} all-gather(bf16[128,4,1,64]{0,3,1,2:T(8,128)(2,1)S(1)} %get-tuple-element.17), channel_id=3, replica_groups=mesh['blk'=8,'uly'=4] {'blk'}, dimensions={0}, use_global_device_ids=true | all-gather | bytes 589824 | tf_op jit(solution)/shard_map/all_gather | solution.py:84
  94.2 0.6 fusion.4
  94.8 0.0 copy-done.1
  94.8 1.1 fusion.28
  95.9 0.0 reduce-scatter.2.cloned.1.call-update
  95.9 19.0 %reduce-scatter.2.cloned.1.call-done = f32[32,1024]{1,0:T(8,128)} async-done(((f32[128,1024]{1,0:T(8,128)}), f32[32,1024]{1,0:T(8,128)}) %reduce-scatter.2.cloned.1.call-update) | async-done | bytes 131088 | tf_op jit(solution)/shard_map/reduce_scatter | solution.py:94
  114.9 0.9 convert_element_type.132
  115.8 0.7 reshape.118
  (5 shorter events, 0.1 us)
Async XLA Ops:
  6.5 29.9 %copy-start = (bf16[768,1024]{1,0:T(8,128)(2,1)S(1)}, bf16[768,1024]{1,0:T(8,128)(2,1)}, u32[]{:S(2)}) copy-start(bf16[768,1024]{1,0:T(8,128)(2,1)} %param.8) | copy-start | bytes 4718596
  6.5 18.8 %copy-start.2 = (bf16[1,16,2,1024]{3,2,1,0:T(2,128)(2,1)S(1)}, bf16[1,16,2,1024]{3,2,1,0:T(2,128)(2,1)}, u32[]{:S(2)}) copy-start(bf16[1,16,2,1024]{3,2,1,0:T(2,128)(2,1)} %param.5) | copy-start | bytes 196612
  6.5 18.8 %copy-start.3 = (f32[1024]{0:T(1024)S(1)}, f32[1024]{0:T(1024)}, u32[]{:S(2)}) copy-start(f32[1024]{0:T(1024)} %param.7) | copy-start | bytes 12292
  6.5 108.4 %reduce-scatter.2.cloned.1.call-start = ((), (), s32[]{:S(2)}) async-start(), calls=%async_computation.1 | async-start | bytes 655360 | tf_op jit(solution)/shard_map/reduce_scatter | solution.py:94
  6.5 7.7 %collective-permute-start = (bf16[1,16,2,1024]{3,2,1,0:T(2,128)(2,1)}, bf16[1,16,2,1024]{3,2,1,0:T(2,128)(2,1)S(1)}, u32[]{:S(2)}, u32[]{:S(2)}) collective-permute-start(bf16[1,16,2,1024]{3,2,1,0:T(2,128)(2,1)} %param.5), channel_id=1, source_target_pairs={{0,4},{4,8},{8,12},{12,16},{16,20},{20,24},{24,28},{1,5},{5,9},{9,... | collective-permute-start | bytes 196616 | tf_op jit(solution)/shard_map/ppermute | solution.py:18
  11.6 6.4 %collective-permute-start.1 = (bf16[1,16,2,1024]{3,2,1,0:T(2,128)(2,1)}, bf16[1,16,2,1024]{3,2,1,0:T(2,128)(2,1)S(1)}, u32[]{:S(2)}, u32[]{:S(2)}) collective-permute-start(bf16[1,16,2,1024]{3,2,1,0:T(2,128)(2,1)} %param.5), channel_id=1, source_target_pairs={{4,0},{8,4},{12,8},{16,12},{20,16},{24,20},{28,24},{5,1},{9,5},{13... | collective-permute-start | bytes 196616 | tf_op jit(solution)/shard_map/ppermute | solution.py:19
  18.3 3.8 %collective-permute-start.2 = (bf16[3,16,1,1024]{3,2,1,0:T(2,128)(2,1)S(1)}, bf16[3,16,1,1024]{3,2,1,0:T(2,128)(2,1)S(1)}, u32[]{:S(2)}, u32[]{:S(2)}) collective-permute-start(bf16[3,16,1,1024]{3,2,1,0:T(2,128)(2,1)S(1)} %get-tuple-element.19), channel_id=1, source_target_pairs={{0,1},{1,2},{2,3},{4,5},{5,6},{6,7},{8,9},{9,10},{10,11},{12,13},{... | collective-permute-start | bytes 294920 | tf_op jit(solution)/shard_map/ppermute | solution.py:18
  19.6 5.1 %collective-permute-start.3 = (bf16[3,16,1,1024]{3,2,1,0:T(2,128)(2,1)S(1)}, bf16[3,16,1,1024]{3,2,1,0:T(2,128)(2,1)S(1)}, u32[]{:S(2)}, u32[]{:S(2)}) collective-permute-start(bf16[3,16,1,1024]{3,2,1,0:T(2,128)(2,1)S(1)} %get-tuple-element.20), channel_id=1, source_target_pairs={{1,0},{2,1},{3,2},{5,4},{6,5},{7,6},{9,8},{10,9},{11,10},{13,12},{... | collective-permute-start | bytes 294920 | tf_op jit(solution)/shard_map/ppermute | solution.py:19
  66.4 28.4 %copy-start.1 = (bf16[256,1024]{1,0:T(8,128)(2,1)S(1)}, bf16[256,1024]{1,0:T(8,128)(2,1)}, u32[]{:S(2)}) copy-start(bf16[256,1024]{1,0:T(8,128)(2,1)} %param.9) | copy-start | bytes 1572868
Sparse Core Ops, SparseCore 0:
  96.0 18.8 reduce-scatter.1

commit v2 on v1

--- a/solution.py
+++ b/solution.py
@@ -19,6 +19,27 @@
         after = lax.ppermute(initial, axis, down)
         shard = jnp.concatenate([before, shard, after], axis=dim)
     return shard
+
+
+def gathered(piece, axis):
+    size = lax.axis_size(axis)
+    parts = [piece]
+    for shift in range(1, size):
+        pairs = [(i, (i + shift) % size) for i in range(size)]
+        parts.append(lax.ppermute(piece, axis, pairs))
+    return jnp.concatenate(parts, axis=0)
+
+
+def scattered_sum(whole, axis):
+    size = lax.axis_size(axis)
+    rank = lax.axis_index(axis)
+    blocks = whole.reshape(size, whole.shape[0] // size, *whole.shape[1:])
+    total = lax.dynamic_index_in_dim(blocks, rank, 0, keepdims=False)
+    for shift in range(1, size):
+        pairs = [(i, (i + shift) % size) for i in range(size)]
+        outgoing = lax.dynamic_index_in_dim(blocks, (rank + shift) % size, 0, keepdims=False)
+        total = total + lax.ppermute(outgoing, axis, pairs)
+    return total
 
 
 def times_transposed(left, right):
@@ -52,8 +73,9 @@
     projected = times_transposed(slab_rows, qkv_weight).astype(jnp.bfloat16)
     split_heads = projected.reshape(slab_tok, heads_here, 3, HS)
     queries = split_heads[:, :, 0]
-    key_rows = split_heads[:, :, 1]
-    val_rows = split_heads[:, :, 2]
+    key_value = gathered(split_heads[:, :, 1:], "blk")
+    key_piece = key_value[:, :, 0]
+    value_piece = key_value[:, :, 1]
     score_scale = 1.0 / math.sqrt(HS)
 
     def key_block(carry_state, key_value):
@@ -80,8 +102,6 @@
         jnp.zeros((heads_here, slab_tok), jnp.float32),
         jnp.zeros((heads_here, slab_tok, HS), jnp.float32),
     )
-    key_piece = lax.all_gather(key_rows, "blk", axis=0, tiled=True)
-    value_piece = lax.all_gather(val_rows, "blk", axis=0, tiled=True)
     key_count = key_piece.shape[0]
     block_len = min(1024, key_count)
     key_blocks = key_piece.reshape(key_count // block_len, block_len, heads_here, HS)
@@ -91,7 +111,7 @@
     attended = (weighted / running_sum[:, :, None]).astype(jnp.bfloat16)
     head_rows = attended.transpose(1, 0, 2).reshape(slab_tok, heads_here * HS)
     partial = jnp.dot(head_rows, out_weight, preferred_element_type=jnp.float32)
-    result = lax.psum_scatter(partial, "uly", scatter_dimension=0, tiled=True)
+    result = scattered_sum(partial, "uly")
     return result.astype(jnp.bfloat16).reshape(z_count, x_count, y_count, features)
 
 

time: 124 us -> 71.2 us (0.57)
  the two profiles are of different devices: /device:TPU:0 before, /device:TPU:15 now
where the time goes in v2:
time: 71.2 us; the launch traced here: 70.7 us
  waiting for transfers between devices  28.3 us (40%)
  starting transfers between devices  19.9 us (28%)
  blocking collectives  9.6 us (13%)
  local copies, waits for them, and re-layouts  5.75 us (8%)
  other arithmetic  3.69 us (5%)
  matrix products  3.16 us (4%)
    ppermute x7, waiting for transfers between devices, gathered(): parts.append(lax.ppermute(piece, axis, pairs))  20.2 us
    all_gather x1, blocking collectives, on_device(): slab_rows = lax.all_gather(token_rows, 'uly', axis=0, tiled=True)  9.6 us
    ppermute x2, starting transfers between devices, padded_2(): after = lax.ppermute(initial, axis, down)  6.79 us
    ppermute x7, starting transfers between devices, gathered(): parts.append(lax.ppermute(piece, axis, pairs))  6.67 us
    ppermute x3, waiting for transfers between devices, scattered_sum(): total = total + lax.ppermute(outgoing, axis, pairs)  6.56 us
    ppermute x2, starting transfers between devices, padded_2(): before = lax.ppermute(last, axis, up)  4.57 us
    slice x2, local copies, waits for them, and re-layouts, on_device(): conv_weight[9 * step_z + 3 * step_x + step_y]  2.58 us
    convert_element_type x1, other arithmetic, on_device(): token_rows = summed.astype(jnp.bfloat16).reshape(-1, features)  2.46 us
  transfers between devices with their start and end apart: 14, of which 9 were waited for; matrix products, arithmetic and copies ran while one was open for 5% of the time, Pallas kernels for 0%

profile of v2, /device:TPU:15, one launch (start us, length us, event | category | flops | bytes accessed | tf_op | source)
XLA Modules:
  0.0 70.7 jit_solution(18221268678943710223)
XLA Ops:
  0.0 0.0 copy-start
  0.0 0.0 copy-start.3
  0.0 0.0 copy-start.4
  0.0 3.3 %collective-permute-start = (bf16[1,16,2,1024]{3,2,1,0:T(2,128)(2,1)}, bf16[1,16,2,1024]{3,2,1,0:T(2,128)(2,1)S(1)}, u32[]{:S(2)}, u32[]{:S(2)}) collective-permute-start(bf16[1,16,2,1024]{3,2,1,0:T(2,128)(2,1)} %param.5), channel_id=1, source_target_pairs={{0,4},{4,8},{8,12},{12,16},{16,20},{20,24},{24,28},{1,5},{5,9},{9,... | collective-permute-start | bytes 196616 | tf_op jit(solution)/shard_map/ppermute | solution.py:18
  3.3 2.1 %collective-permute-start.1 = (bf16[1,16,2,1024]{3,2,1,0:T(2,128)(2,1)}, bf16[1,16,2,1024]{3,2,1,0:T(2,128)(2,1)S(1)}, u32[]{:S(2)}, u32[]{:S(2)}) collective-permute-start(bf16[1,16,2,1024]{3,2,1,0:T(2,128)(2,1)} %param.5), channel_id=1, source_target_pairs={{4,0},{8,4},{12,8},{16,12},{20,16},{24,20},{28,24},{5,1},{9,5},{13... | collective-permute-start | bytes 196616 | tf_op jit(solution)/shard_map/ppermute | solution.py:19
  5.4 1.4 %fusion.30 = (f32[1,1024]{1,0:T(1,128)S(1)}, f32[1,1024]{1,0:T(1,128)S(1)}, f32[1,1024]{1,0:T(1,128)S(1)}, f32[1,1024]{1,0:T(1,128)S(1)}, f32[1,1024]{1,0:T(1,12...) fusion(f32[27,1024]{1,0:T(8,128)} %param.6), kind=kLoop, calls=%fused_computation.63 | loop fusion | bytes 155648 | tf_op jit(solution)/shard_map/slice | solution.py:61
  6.8 0.0 collective-permute-done
  6.9 0.9 %constant_dynamic-update-slice_fusion.1 = bf16[3,16,2,1024]{3,2,1,0:T(2,128)(2,1)S(1)} fusion(bf16[3,16,2,1024]{3,2,1,0:T(2,128)(2,1)S(1)} %constant_dynamic-update-slice_fusion.2, bf16[1,16,2,1024]{3,2,1,0:T(2,128)(2,1)} %param.5), kind=kLoop, calls=%fused_computation.47 | loop fusion | bytes 131072
  7.8 1.6 %collective-permute-done.1 = bf16[1,16,2,1024]{3,2,1,0:T(2,128)(2,1)S(1)} collective-permute-done((bf16[1,16,2,1024]{3,2,1,0:T(2,128)(2,1)}, bf16[1,16,2,1024]{3,2,1,0:T(2,128)(2,1)S(1)}, u32[]{:S(2)}, u32[]{:S(2)}) %collective-permute-start.1) | collective-permute-done | bytes 65568 | tf_op jit(solution)/shard_map/ppermute | solution.py:19
  9.4 0.1 constant_dynamic-update-slice_fusion
  9.5 0.3 fusion.28
  9.8 1.3 %collective-permute-start.2 = (bf16[3,16,1,1024]{3,2,1,0:T(2,128)(2,1)S(1)}, bf16[3,16,1,1024]{3,2,1,0:T(2,128)(2,1)S(1)}, u32[]{:S(2)}, u32[]{:S(2)}) collective-permute-start(bf16[3,16,1,1024]{3,2,1,0:T(2,128)(2,1)S(1)} %get-tuple-element.20), channel_id=1, source_target_pairs={{0,1},{1,2},{2,3},{4,5},{5,6},{6,7},{8,9},{9,10},{10,11},{12,13},{... | collective-permute-start | bytes 294920 | tf_op jit(solution)/shard_map/ppermute | solution.py:18
  11.1 4.6 %collective-permute-start.3 = (bf16[3,16,1,1024]{3,2,1,0:T(2,128)(2,1)S(1)}, bf16[3,16,1,1024]{3,2,1,0:T(2,128)(2,1)S(1)}, u32[]{:S(2)}, u32[]{:S(2)}) collective-permute-start(bf16[3,16,1,1024]{3,2,1,0:T(2,128)(2,1)S(1)} %get-tuple-element.28), channel_id=1, source_target_pairs={{1,0},{2,1},{3,2},{5,4},{6,5},{7,6},{9,8},{10,9},{11,10},{13,12},{... | collective-permute-start | bytes 294920 | tf_op jit(solution)/shard_map/ppermute | solution.py:19
  15.7 1.2 %fusion.31 = (f32[1,1024]{1,0:T(1,128)S(1)}, f32[1,1024]{1,0:T(1,128)S(1)}, f32[1,1024]{1,0:T(1,128)S(1)}, f32[1,1024]{1,0:T(1,128)S(1)}, f32[1,1024]{1,0:T(1,12...) fusion(f32[27,1024]{1,0:T(8,128)} %param.6), kind=kLoop, calls=%fused_computation.64 | loop fusion | bytes 65536 | tf_op jit(solution)/shard_map/slice | solution.py:61
  16.9 0.0 collective-permute-done.2
  16.9 0.0 collective-permute-done.3
  16.9 0.7 select_maximum_fusion
  17.6 0.0 copy-done.3
  17.6 0.0 copy-done.4
  17.6 2.5 %add_convert_fusion = bf16[1,16,2,1024]{3,2,1,0:T(2,128)(2,1)S(1)} fusion(bf16[1,16,2,1024]{3,2,1,0:T(2,128)(2,1)S(1)} %collective-permute-done.1, bf16[1,16,2,1024]{3,2,1,0:T(2,128)(2,1)S(1)} %copy-done.3, bf16[1,16,2,1024]{3,2,1,0:T(2,128)(2,1)S(1)} %collective-permute-done, bf16[3,18,4,1024]{3,2,1,0:T(4,128)(2,1)S(1)} %select_maximum_fusion, ...), kind=kLoop, calls=%fused_computation.42 | loop fusion | flops 3309568 | bytes 1949696 | tf_op jit(solution)/shard_map/convert_element_type | solution.py:68
  20.1 9.6 %all_gather.3 = bf16[128,1024]{1,0:T(8,128)(2,1)S(1)} all-gather(bf16[32,1024]{1,0:T(8,128)(2,1)S(1)} %reshape.112), channel_id=1, replica_groups=mesh['blk'=8,'uly'=4] {'uly'}, dimensions={0}, use_global_device_ids=true | all-gather | bytes 327680 | tf_op jit(solution)/shard_map/all_gather | solution.py:71
  29.7 0.0 copy-done
  29.7 0.7 convolution_convert_fusion
  30.4 0.2 copy.9
  30.6 0.4 collective-permute-start.4
  31.0 1.3 %collective-permute-start.5 = (bf16[128,4,2,64]{0,3,1,2:T(8,128)(2,1)S(1)}, bf16[128,4,2,64]{0,3,1,2:T(8,128)(2,1)S(1)}, u32[]{:S(2)}, u32[]{:S(2)}) collective-permute-start(bf16[128,4,2,64]{0,3,1,2:T(8,128)(2,1)S(1)} %get-tuple-element.30), channel_id=1, source_target_pairs={{0,8},{4,12},{8,16},{12,20},{16,24},{20,28},{24,0},{28,4},{1,9},{5... | collective-permute-start | bytes 393224 | tf_op jit(solution)/shard_map/ppermute | solution.py:29
  32.3 1.8 %collective-permute-start.6 = (bf16[128,4,2,64]{0,3,1,2:T(8,128)(2,1)S(1)}, bf16[128,4,2,64]{0,3,1,2:T(8,128)(2,1)S(1)}, u32[]{:S(2)}, u32[]{:S(2)}) collective-permute-start(bf16[128,4,2,64]{0,3,1,2:T(8,128)(2,1)S(1)} %get-tuple-element.30), channel_id=1, source_target_pairs={{0,12},{4,16},{8,20},{12,24},{16,28},{20,0},{24,4},{28,8},{1,13},{... | collective-permute-start | bytes 393224 | tf_op jit(solution)/shard_map/ppermute | solution.py:29
  34.1 1.4 %collective-permute-start.7 = (bf16[128,4,2,64]{0,3,1,2:T(8,128)(2,1)S(1)}, bf16[128,4,2,64]{0,3,1,2:T(8,128)(2,1)S(1)}, u32[]{:S(2)}, u32[]{:S(2)}) collective-permute-start(bf16[128,4,2,64]{0,3,1,2:T(8,128)(2,1)S(1)} %get-tuple-element.30), channel_id=1, source_target_pairs={{0,16},{4,20},{8,24},{12,28},{16,0},{20,4},{24,8},{28,12},{1,17},{... | collective-permute-start | bytes 393224 | tf_op jit(solution)/shard_map/ppermute | solution.py:29
  35.5 0.1 collective-permute-start.8
  35.6 0.0 collective-permute-done.4
  35.6 1.1 %collective-permute-start.9 = (bf16[128,4,2,64]{0,3,1,2:T(8,128)(2,1)S(1)}, bf16[128,4,2,64]{0,3,1,2:T(8,128)(2,1)S(1)}, u32[]{:S(2)}, u32[]{:S(2)}) collective-permute-start(bf16[128,4,2,64]{0,3,1,2:T(8,128)(2,1)S(1)} %get-tuple-element.30), channel_id=1, source_target_pairs={{0,24},{4,28},{8,0},{12,4},{16,8},{20,12},{24,16},{28,20},{1,25},{... | collective-permute-start | bytes 393224 | tf_op jit(solution)/shard_map/ppermute | solution.py:29
  36.8 0.7 collective-permute-done.5
  37.4 0.5 collective-permute-start.10
  38.0 12.6 %collective-permute-done.6 = bf16[128,4,2,64]{0,3,1,2:T(8,128)(2,1)S(1)} collective-permute-done((bf16[128,4,2,64]{0,3,1,2:T(8,128)(2,1)S(1)}, bf16[128,4,2,64]{0,3,1,2:T(8,128)(2,1)S(1)}, u32[]{:S(2)}, u32[]{:S(2)}) %collective-permute-start.6) | collective-permute-done | bytes 131104 | tf_op jit(solution)/shard_map/ppermute | solution.py:29
  50.6 2.8 %collective-permute-done.7 = bf16[128,4,2,64]{0,3,1,2:T(8,128)(2,1)S(1)} collective-permute-done((bf16[128,4,2,64]{0,3,1,2:T(8,128)(2,1)S(1)}, bf16[128,4,2,64]{0,3,1,2:T(8,128)(2,1)S(1)}, u32[]{:S(2)}, u32[]{:S(2)}) %collective-permute-start.7) | collective-permute-done | bytes 131104 | tf_op jit(solution)/shard_map/ppermute | solution.py:29
  53.4 0.0 collective-permute-done.8
  53.5 2.1 %collective-permute-done.9 = bf16[128,4,2,64]{0,3,1,2:T(8,128)(2,1)S(1)} collective-permute-done((bf16[128,4,2,64]{0,3,1,2:T(8,128)(2,1)S(1)}, bf16[128,4,2,64]{0,3,1,2:T(8,128)(2,1)S(1)}, u32[]{:S(2)}, u32[]{:S(2)}) %collective-permute-start.9) | collective-permute-done | bytes 131104 | tf_op jit(solution)/shard_map/ppermute | solution.py:29
  55.6 2.1 %collective-permute-done.10 = bf16[128,4,2,64]{0,3,1,2:T(8,128)(2,1)S(1)} collective-permute-done((bf16[128,4,2,64]{0,3,1,2:T(8,128)(2,1)S(1)}, bf16[128,4,2,64]{0,3,1,2:T(8,128)(2,1)S(1)}, u32[]{:S(2)}, u32[]{:S(2)}) %collective-permute-start.10) | collective-permute-done | bytes 131104 | tf_op jit(solution)/shard_map/ppermute | solution.py:29
  57.7 0.0 copy-start.2
  57.8 0.6 multiply_reduce_fusion
  58.3 0.4 copy-done.2
  58.7 0.5 fusion
  59.2 0.0 copy-start.1
  59.3 1.7 %fusion.4 = bf16[128,4,64]{0,2,1:T(8,128)(2,1)S(1)} fusion(f32[4,128,1024]{2,1,0:T(8,128)S(1)} %get-tuple-element.63, f32[4,128]{1,0:T(4,128)S(1)} %get-tuple-element.61, bf16[1024,4,2,64]{0,3,1,2:T(8,128)(2,1)} %copy-done.2, f32[128,4]{0,1:T(4,128)S(1)} %bitcast_add_fusion.1, f32[128,4]{0,1:T(4,128)S(1)} %get-tuple-element.60), kind=kOutput, calls=%fused_computation.10 | convolution fusion | flops 68780032 | bytes 2693120 | tf_op jit(solution)/shard_map/while/body/eval_jaxpr/hqk,khd->hqd/dot_general | solution.py:92
  61.0 0.1 copy.12
  61.1 0.1 dot_general.22
  61.3 0.0 copy-done.1
  61.3 0.2 fusion.10
  61.6 0.7 collective-permute-start.11
  62.2 1.2 %collective-permute-start.12 = (f32[32,1024]{1,0:T(8,128)S(1)}, f32[32,1024]{1,0:T(8,128)S(1)}, u32[]{:S(2)}, u32[]{:S(2)}) collective-permute-start(f32[32,1024]{1,0:T(8,128)S(1)} %get-tuple-element.19), channel_id=1, source_target_pairs={{0,2},{1,3},{2,0},{3,1},{4,6},{5,7},{6,4},{7,5},{8,10},{9,11},{10,... | collective-permute-start | bytes 393224 | tf_op jit(solution)/shard_map/ppermute | solution.py:41
  63.5 0.0 collective-permute-start.13
  63.5 1.5 %collective-permute-done.11 = f32[32,1024]{1,0:T(8,128)S(1)} collective-permute-done((f32[32,1024]{1,0:T(8,128)S(1)}, f32[32,1024]{1,0:T(8,128)S(1)}, u32[]{:S(2)}, u32[]{:S(2)}) %collective-permute-start.11) | collective-permute-done | bytes 131104 | tf_op jit(solution)/shard_map/ppermute | solution.py:41
  65.0 4.5 %collective-permute-done.12 = f32[32,1024]{1,0:T(8,128)S(1)} collective-permute-done((f32[32,1024]{1,0:T(8,128)S(1)}, f32[32,1024]{1,0:T(8,128)S(1)}, u32[]{:S(2)}, u32[]{:S(2)}) %collective-permute-start.12) | collective-permute-done | bytes 131104 | tf_op jit(solution)/shard_map/ppermute | solution.py:41
  69.4 0.6 collective-permute-done.13
  70.1 0.7 reshape.114
  (14 shorter events, 0.5 us)
Async XLA Ops:
  0.0 29.7 %copy-start = (bf16[768,1024]{1,0:T(8,128)(2,1)S(1)}, bf16[768,1024]{1,0:T(8,128)(2,1)}, u32[]{:S(2)}) copy-start(bf16[768,1024]{1,0:T(8,128)(2,1)} %param.8) | copy-start | bytes 4718596
  0.0 17.6 %copy-start.3 = (bf16[1,16,2,1024]{3,2,1,0:T(2,128)(2,1)S(1)}, bf16[1,16,2,1024]{3,2,1,0:T(2,128)(2,1)}, u32[]{:S(2)}) copy-start(bf16[1,16,2,1024]{3,2,1,0:T(2,128)(2,1)} %param.5) | copy-start | bytes 196612
  0.0 17.6 %copy-start.4 = (f32[1024]{0:T(1024)S(1)}, f32[1024]{0:T(1024)}, u32[]{:S(2)}) copy-start(f32[1024]{0:T(1024)} %param.7) | copy-start | bytes 12292
  0.0 6.8 %collective-permute-start = (bf16[1,16,2,1024]{3,2,1,0:T(2,128)(2,1)}, bf16[1,16,2,1024]{3,2,1,0:T(2,128)(2,1)S(1)}, u32[]{:S(2)}, u32[]{:S(2)}) collective-permute-start(bf16[1,16,2,1024]{3,2,1,0:T(2,128)(2,1)} %param.5), channel_id=1, source_target_pairs={{0,4},{4,8},{8,12},{12,16},{16,20},{20,24},{24,28},{1,5},{5,9},{9,... | collective-permute-start | bytes 196616 | tf_op jit(solution)/shard_map/ppermute | solution.py:18
  3.3 6.1 %collective-permute-start.1 = (bf16[1,16,2,1024]{3,2,1,0:T(2,128)(2,1)}, bf16[1,16,2,1024]{3,2,1,0:T(2,128)(2,1)S(1)}, u32[]{:S(2)}, u32[]{:S(2)}) collective-permute-start(bf16[1,16,2,1024]{3,2,1,0:T(2,128)(2,1)} %param.5), channel_id=1, source_target_pairs={{4,0},{8,4},{12,8},{16,12},{20,16},{24,20},{28,24},{5,1},{9,5},{13... | collective-permute-start | bytes 196616 | tf_op jit(solution)/shard_map/ppermute | solution.py:19
  9.8 7.1 %collective-permute-start.2 = (bf16[3,16,1,1024]{3,2,1,0:T(2,128)(2,1)S(1)}, bf16[3,16,1,1024]{3,2,1,0:T(2,128)(2,1)S(1)}, u32[]{:S(2)}, u32[]{:S(2)}) collective-permute-start(bf16[3,16,1,1024]{3,2,1,0:T(2,128)(2,1)S(1)} %get-tuple-element.20), channel_id=1, source_target_pairs={{0,1},{1,2},{2,3},{4,5},{5,6},{6,7},{8,9},{9,10},{10,11},{12,13},{... | collective-permute-start | bytes 294920 | tf_op jit(solution)/shard_map/ppermute | solution.py:18
  11.1 5.9 %collective-permute-start.3 = (bf16[3,16,1,1024]{3,2,1,0:T(2,128)(2,1)S(1)}, bf16[3,16,1,1024]{3,2,1,0:T(2,128)(2,1)S(1)}, u32[]{:S(2)}, u32[]{:S(2)}) collective-permute-start(bf16[3,16,1,1024]{3,2,1,0:T(2,128)(2,1)S(1)} %get-tuple-element.28), channel_id=1, source_target_pairs={{1,0},{2,1},{3,2},{5,4},{6,5},{7,6},{9,8},{10,9},{11,10},{13,12},{... | collective-permute-start | bytes 294920 | tf_op jit(solution)/shard_map/ppermute | solution.py:19
  30.6 5.0 %collective-permute-start.4 = (bf16[128,4,2,64]{0,3,1,2:T(8,128)(2,1)S(1)}, bf16[128,4,2,64]{0,3,1,2:T(8,128)(2,1)S(1)}, u32[]{:S(2)}, u32[]{:S(2)}) collective-permute-start(bf16[128,4,2,64]{0,3,1,2:T(8,128)(2,1)S(1)} %get-tuple-element.30), channel_id=1, source_target_pairs={{0,4},{4,8},{8,12},{12,16},{16,20},{20,24},{24,28},{28,0},{1,5},{5... | collective-permute-start | bytes 393224 | tf_op jit(solution)/shard_map/ppermute | solution.py:29
  31.0 6.5 %collective-permute-start.5 = (bf16[128,4,2,64]{0,3,1,2:T(8,128)(2,1)S(1)}, bf16[128,4,2,64]{0,3,1,2:T(8,128)(2,1)S(1)}, u32[]{:S(2)}, u32[]{:S(2)}) collective-permute-start(bf16[128,4,2,64]{0,3,1,2:T(8,128)(2,1)S(1)} %get-tuple-element.30), channel_id=1, source_target_pairs={{0,8},{4,12},{8,16},{12,20},{16,24},{20,28},{24,0},{28,4},{1,9},{5... | collective-permute-start | bytes 393224 | tf_op jit(solution)/shard_map/ppermute | solution.py:29
  32.3 18.3 %collective-permute-start.6 = (bf16[128,4,2,64]{0,3,1,2:T(8,128)(2,1)S(1)}, bf16[128,4,2,64]{0,3,1,2:T(8,128)(2,1)S(1)}, u32[]{:S(2)}, u32[]{:S(2)}) collective-permute-start(bf16[128,4,2,64]{0,3,1,2:T(8,128)(2,1)S(1)} %get-tuple-element.30), channel_id=1, source_target_pairs={{0,12},{4,16},{8,20},{12,24},{16,28},{20,0},{24,4},{28,8},{1,13},{... | collective-permute-start | bytes 393224 | tf_op jit(solution)/shard_map/ppermute | solution.py:29
  34.1 19.3 %collective-permute-start.7 = (bf16[128,4,2,64]{0,3,1,2:T(8,128)(2,1)S(1)}, bf16[128,4,2,64]{0,3,1,2:T(8,128)(2,1)S(1)}, u32[]{:S(2)}, u32[]{:S(2)}) collective-permute-start(bf16[128,4,2,64]{0,3,1,2:T(8,128)(2,1)S(1)} %get-tuple-element.30), channel_id=1, source_target_pairs={{0,16},{4,20},{8,24},{12,28},{16,0},{20,4},{24,8},{28,12},{1,17},{... | collective-permute-start | bytes 393224 | tf_op jit(solution)/shard_map/ppermute | solution.py:29
  35.5 17.9 %collective-permute-start.8 = (bf16[128,4,2,64]{0,3,1,2:T(8,128)(2,1)S(1)}, bf16[128,4,2,64]{0,3,1,2:T(8,128)(2,1)S(1)}, u32[]{:S(2)}, u32[]{:S(2)}) collective-permute-start(bf16[128,4,2,64]{0,3,1,2:T(8,128)(2,1)S(1)} %get-tuple-element.30), channel_id=1, source_target_pairs={{0,20},{4,24},{8,28},{12,0},{16,4},{20,8},{24,12},{28,16},{1,21},{... | collective-permute-start | bytes 393224 | tf_op jit(solution)/shard_map/ppermute | solution.py:29
  35.6 20.0 %collective-permute-start.9 = (bf16[128,4,2,64]{0,3,1,2:T(8,128)(2,1)S(1)}, bf16[128,4,2,64]{0,3,1,2:T(8,128)(2,1)S(1)}, u32[]{:S(2)}, u32[]{:S(2)}) collective-permute-start(bf16[128,4,2,64]{0,3,1,2:T(8,128)(2,1)S(1)} %get-tuple-element.30), channel_id=1, source_target_pairs={{0,24},{4,28},{8,0},{12,4},{16,8},{20,12},{24,16},{28,20},{1,25},{... | collective-permute-start | bytes 393224 | tf_op jit(solution)/shard_map/ppermute | solution.py:29
  37.4 20.3 %collective-permute-start.10 = (bf16[128,4,2,64]{0,3,1,2:T(8,128)(2,1)S(1)}, bf16[128,4,2,64]{0,3,1,2:T(8,128)(2,1)S(1)}, u32[]{:S(2)}, u32[]{:S(2)}) collective-permute-start(bf16[128,4,2,64]{0,3,1,2:T(8,128)(2,1)S(1)} %get-tuple-element.30), channel_id=1, source_target_pairs={{0,28},{4,0},{8,4},{12,8},{16,12},{20,16},{24,20},{28,24},{1,29},{... | collective-permute-start | bytes 393224 | tf_op jit(solution)/shard_map/ppermute | solution.py:29
  57.7 1.0 %copy-start.2 = (bf16[1024,4,2,64]{0,3,1,2:T(8,128)(2,1)}, bf16[1024,4,2,64]{0,3,1,2:T(8,128)(2,1)S(1)}, u32[]{:S(2)}) copy-start(bf16[1024,4,2,64]{0,3,1,2:T(8,128)(2,1)S(1)} %constant_dynamic-update-slice_fusion.3) | copy-start | bytes 3145732
  59.2 2.0 %copy-start.1 = (bf16[256,1024]{1,0:T(8,128)(2,1)S(1)}, bf16[256,1024]{1,0:T(8,128)(2,1)}, u32[]{:S(2)}) copy-start(bf16[256,1024]{1,0:T(8,128)(2,1)} %param.9) | copy-start | bytes 1572868
  61.6 3.4 %collective-permute-start.11 = (f32[32,1024]{1,0:T(8,128)S(1)}, f32[32,1024]{1,0:T(8,128)S(1)}, u32[]{:S(2)}, u32[]{:S(2)}) collective-permute-start(f32[32,1024]{1,0:T(8,128)S(1)} %get-tuple-element.17), channel_id=1, source_target_pairs={{0,1},{1,2},{2,3},{3,0},{4,5},{5,6},{6,7},{7,4},{8,9},{9,10},{10,1... | collective-permute-start | bytes 393224 | tf_op jit(solution)/shard_map/ppermute | solution.py:41
  62.2 7.2 %collective-permute-start.12 = (f32[32,1024]{1,0:T(8,128)S(1)}, f32[32,1024]{1,0:T(8,128)S(1)}, u32[]{:S(2)}, u32[]{:S(2)}) collective-permute-start(f32[32,1024]{1,0:T(8,128)S(1)} %get-tuple-element.19), channel_id=1, source_target_pairs={{0,2},{1,3},{2,0},{3,1},{4,6},{5,7},{6,4},{7,5},{8,10},{9,11},{10,... | collective-permute-start | bytes 393224 | tf_op jit(solution)/shard_map/ppermute | solution.py:41
  63.5 6.6 %collective-permute-start.13 = (f32[32,1024]{1,0:T(8,128)S(1)}, f32[32,1024]{1,0:T(8,128)S(1)}, u32[]{:S(2)}, u32[]{:S(2)}) collective-permute-start(f32[32,1024]{1,0:T(8,128)S(1)} %get-tuple-element.18), channel_id=1, source_target_pairs={{0,3},{1,0},{2,1},{3,2},{4,7},{5,4},{6,5},{7,6},{8,11},{9,8},{10,9... | collective-permute-start | bytes 393224 | tf_op jit(solution)/shard_map/ppermute | solution.py:41

commit v3 on v2

--- a/solution.py
+++ b/solution.py
@@ -50,9 +50,15 @@
 
 def on_device(tokens, conv_weight, conv_bias, qkv_weight, out_weight):
     z_count, x_count, y_count, features = tokens.shape
-    padded = padded_2(tokens, (("blk", 0), ("uly", 2)), 1)
-    padded = jnp.pad(padded, ((0, 0), (1, 1), (0, 0), (0, 0)))
-    summed = tokens.astype(jnp.float32) + conv_bias
+    groups = lax.axis_size("uly")
+    with_halo = padded_2(tokens, (("blk", 0),), 1)
+    slab_in = lax.all_gather(with_halo, "uly", axis=0, tiled=False)
+    slab_in = slab_in.transpose(1, 2, 0, 3, 4).reshape(
+        z_count + 2, x_count, groups * y_count, features
+    )
+    slab_y = groups * y_count
+    padded = jnp.pad(slab_in, ((0, 0), (1, 1), (1, 1), (0, 0)))
+    summed = slab_in[1 : 1 + z_count].astype(jnp.float32) + conv_bias
     for step_z in range(3):
         for step_x in range(3):
             for step_y in range(3):
@@ -62,13 +68,17 @@
                     * padded[
                         step_z : step_z + z_count,
                         step_x : step_x + x_count,
-                        step_y : step_y + y_count,
+                        step_y : step_y + slab_y,
                     ]
                 )
-    token_rows = summed.astype(jnp.bfloat16).reshape(-1, features)
-    local_tok = token_rows.shape[0]
+    positioned = summed.astype(jnp.bfloat16)
+    local_tok = z_count * x_count * y_count
     heads_here = qkv_weight.shape[0] // (3 * HS)
-    slab_rows = lax.all_gather(token_rows, "uly", axis=0, tiled=True)
+    slab_rows = (
+        positioned.reshape(z_count, x_count, groups, y_count, features)
+        .transpose(2, 0, 1, 3, 4)
+        .reshape(groups * local_tok, features)
+    )
     slab_tok = slab_rows.shape[0]
     projected = times_transposed(slab_rows, qkv_weight).astype(jnp.bfloat16)
     split_heads = projected.reshape(slab_tok, heads_here, 3, HS)

time: 71.2 us -> 64.6 us (0.907)
  the two profiles are of different devices: /device:TPU:15 before, /device:TPU:13 now
where the time goes in v3:
time: 64.6 us; the launch traced here: 64.1 us
  waiting for transfers between devices  27.2 us (42%)
  starting transfers between devices  14.1 us (22%)
  blocking collectives  10.5 us (16%)
  local copies, waits for them, and re-layouts  5.89 us (9%)
  matrix products  3.16 us (5%)
  other arithmetic  2.91 us (5%)
    ppermute x7, waiting for transfers between devices, gathered(): parts.append(lax.ppermute(piece, axis, pairs))  20.2 us
    all_gather x1, blocking collectives, on_device(): slab_in = lax.all_gather(with_halo, 'uly', axis=0, tiled=False)  10.5 us
    ppermute x7, starting transfers between devices, gathered(): parts.append(lax.ppermute(piece, axis, pairs))  6.66 us
    ppermute x3, waiting for transfers between devices, scattered_sum(): total = total + lax.ppermute(outgoing, axis, pairs)  5.9 us
    ppermute x1, starting transfers between devices, padded_2(): before = lax.ppermute(last, axis, up)  3.15 us
    slice x2, local copies, waits for them, and re-layouts, on_device(): conv_weight[9 * step_z + 3 * step_x + step_y]  2.58 us
    convert_element_type x1, other arithmetic, on_device(): positioned = summed.astype(jnp.bfloat16)  2.34 us
    ppermute x3, starting transfers between devices, scattered_sum(): total = total + lax.ppermute(outgoing, axis, pairs)  2.19 us
  transfers between devices with their start and end apart: 12, of which 8 were waited for; matrix products, arithmetic and copies ran while one was open for 4% of the time, Pallas kernels for 0%

profile of v3, /device:TPU:13, one launch (start us, length us, event | category | flops | bytes accessed | tf_op | source)
XLA Modules:
  0.0 64.1 jit_solution(3876097426278551939)
XLA Ops:
  0.0 0.0 copy-start
  0.0 1.0 %copy.23 = bf16[1,16,2,1024]{3,1,2,0:T(8,128)(2,1)S(1)} copy(bf16[1,16,2,1024]{3,2,1,0:T(2,128)(2,1)} %param.5) | data formatting | bytes 131072 | tf_op args[0]
  1.0 3.1 %collective-permute-start = (bf16[1,16,2,1024]{3,1,2,0:T(8,128)(2,1)S(1)}, bf16[1,16,2,1024]{3,1,2,0:T(8,128)(2,1)S(1)}, u32[]{:S(2)}, u32[]{:S(2)}) collective-permute-start(bf16[1,16,2,1024]{3,1,2,0:T(8,128)(2,1)S(1)} %copy.23), channel_id=1, source_target_pairs={{0,4},{4,8},{8,12},{12,16},{16,20},{20,24},{24,28},{1,5},{5,9},{9,... | collective-permute-start | bytes 196616 | tf_op jit(solution)/shard_map/ppermute | solution.py:18
  4.1 2.1 %collective-permute-start.1 = (bf16[1,16,2,1024]{3,1,2,0:T(8,128)(2,1)S(1)}, bf16[1,16,2,1024]{3,1,2,0:T(8,128)(2,1)S(1)}, u32[]{:S(2)}, u32[]{:S(2)}) collective-permute-start(bf16[1,16,2,1024]{3,1,2,0:T(8,128)(2,1)S(1)} %copy.23), channel_id=1, source_target_pairs={{4,0},{8,4},{12,8},{16,12},{20,16},{24,20},{28,24},{5,1},{9,5},{13... | collective-permute-start | bytes 196616 | tf_op jit(solution)/shard_map/ppermute | solution.py:19
  6.3 1.4 %fusion.42 = (f32[1,1024]{1,0:T(1,128)S(1)}, f32[1,1024]{1,0:T(1,128)S(1)}, f32[1,1024]{1,0:T(1,128)S(1)}, f32[1,1024]{1,0:T(1,128)S(1)}, f32[1,1024]{1,0:T(1,12...) fusion(f32[27,1024]{1,0:T(8,128)} %param.6), kind=kLoop, calls=%fused_computation.94 | loop fusion | bytes 155648 | tf_op jit(solution)/shard_map/slice | solution.py:67
  7.7 1.2 %fusion.43 = (f32[1,1024]{1,0:T(1,128)S(1)}, f32[1,1024]{1,0:T(1,128)S(1)}, f32[1,1024]{1,0:T(1,128)S(1)}, f32[1,1024]{1,0:T(1,128)S(1)}, f32[1,1024]{1,0:T(1,12...) fusion(f32[27,1024]{1,0:T(8,128)} %param.6), kind=kLoop, calls=%fused_computation.95 | loop fusion | bytes 65536 | tf_op jit(solution)/shard_map/slice | solution.py:67
  8.9 0.0 collective-permute-done
  8.9 1.2 %collective-permute-done.1 = bf16[1,16,2,1024]{3,1,2,0:T(8,128)(2,1)S(1)} collective-permute-done((bf16[1,16,2,1024]{3,1,2,0:T(8,128)(2,1)S(1)}, bf16[1,16,2,1024]{3,1,2,0:T(8,128)(2,1)S(1)}, u32[]{:S(2)}, u32[]{:S(2)}) %collective-permute-start.1) | collective-permute-done | bytes 65568 | tf_op jit(solution)/shard_map/ppermute | solution.py:19
  10.1 0.0 copy-start.3
  10.1 10.5 %all-gather = bf16[12,16,2,1024]{3,1,2,0:T(8,128)(2,1)S(1)} all-gather(bf16[3,16,2,1024]{3,1,2,0:T(8,128)(2,1)S(1)} %pad_maximum_fusion), channel_id=2, replica_groups=mesh['blk'=8,'uly'=4] {'uly'}, dimensions={0}, use_global_device_ids=true | all-gather | bytes 983040 | tf_op jit(solution)/shard_map/all_gather | solution.py:55
  20.6 0.1 fusion.40
  20.7 0.1 copy.26
  20.7 0.0 copy-done.3
  20.8 2.3 %add_convert_fusion = bf16[1,16,8,1024]{3,1,2,0:T(8,128)(2,1)S(1)} fusion(bf16[1,16,8,1024]{3,1,2,0:T(8,128)(2,1)S(1)} %bitcast.99, bf16[1,16,8,1024]{3,1,2,0:T(8,128)(2,1)S(1)} %bitcast.100, bf16[1,16,8,1024]{3,1,2,0:T(8,128)(2,1)S(1)} %bitcast.98, bf16[3,16,8,1024]{3,1,2,0:T(8,128)(2,1)S(1)} %bitcast.95, f32[1024]{0:T(1024)S(1)} %bitcast.128, ...), kind=kLoop, calls=%fused_computation.69 | loop fusion | flops 10878976 | bytes 1949696 | tf_op jit(solution)/shard_map/convert_element_type | solution.py:74
  23.1 0.3 copy.37
  23.4 0.1 reshape.176
  23.5 0.0 copy-done
  23.5 0.7 %convolution_convert_fusion = bf16[128,768]{1,0:T(8,128)(2,1)S(1)} fusion(bf16[128,1024]{1,0:T(8,128)(2,1)S(1)} %reshape.176, bf16[768,1024]{1,0:T(8,128)(2,1)S(1)} %copy-done), kind=kOutput, calls=%fused_computation.28 | convolution fusion | flops 201424896 | bytes 2031616 | tf_op jit(solution)/shard_map/dot_general | solution.py:46
  24.2 0.2 copy.28
  24.4 0.4 collective-permute-start.2
  24.8 1.3 %collective-permute-start.3 = (bf16[128,4,2,64]{0,3,1,2:T(8,128)(2,1)S(1)}, bf16[128,4,2,64]{0,3,1,2:T(8,128)(2,1)S(1)}, u32[]{:S(2)}, u32[]{:S(2)}) collective-permute-start(bf16[128,4,2,64]{0,3,1,2:T(8,128)(2,1)S(1)} %get-tuple-element.32), channel_id=1, source_target_pairs={{0,8},{4,12},{8,16},{12,20},{16,24},{20,28},{24,0},{28,4},{1,9},{5... | collective-permute-start | bytes 393224 | tf_op jit(solution)/shard_map/ppermute | solution.py:29
  26.1 1.8 %collective-permute-start.4 = (bf16[128,4,2,64]{0,3,1,2:T(8,128)(2,1)S(1)}, bf16[128,4,2,64]{0,3,1,2:T(8,128)(2,1)S(1)}, u32[]{:S(2)}, u32[]{:S(2)}) collective-permute-start(bf16[128,4,2,64]{0,3,1,2:T(8,128)(2,1)S(1)} %get-tuple-element.32), channel_id=1, source_target_pairs={{0,12},{4,16},{8,20},{12,24},{16,28},{20,0},{24,4},{28,8},{1,13},{... | collective-permute-start | bytes 393224 | tf_op jit(solution)/shard_map/ppermute | solution.py:29
  27.9 1.4 %collective-permute-start.5 = (bf16[128,4,2,64]{0,3,1,2:T(8,128)(2,1)S(1)}, bf16[128,4,2,64]{0,3,1,2:T(8,128)(2,1)S(1)}, u32[]{:S(2)}, u32[]{:S(2)}) collective-permute-start(bf16[128,4,2,64]{0,3,1,2:T(8,128)(2,1)S(1)} %get-tuple-element.32), channel_id=1, source_target_pairs={{0,16},{4,20},{8,24},{12,28},{16,0},{20,4},{24,8},{28,12},{1,17},{... | collective-permute-start | bytes 393224 | tf_op jit(solution)/shard_map/ppermute | solution.py:29
  29.3 0.1 collective-permute-start.6
  29.4 0.0 collective-permute-done.2
  29.4 1.1 %collective-permute-start.7 = (bf16[128,4,2,64]{0,3,1,2:T(8,128)(2,1)S(1)}, bf16[128,4,2,64]{0,3,1,2:T(8,128)(2,1)S(1)}, u32[]{:S(2)}, u32[]{:S(2)}) collective-permute-start(bf16[128,4,2,64]{0,3,1,2:T(8,128)(2,1)S(1)} %get-tuple-element.32), channel_id=1, source_target_pairs={{0,24},{4,28},{8,0},{12,4},{16,8},{20,12},{24,16},{28,20},{1,25},{... | collective-permute-start | bytes 393224 | tf_op jit(solution)/shard_map/ppermute | solution.py:29
  30.6 0.7 %collective-permute-done.3 = bf16[128,4,2,64]{0,3,1,2:T(8,128)(2,1)S(1)} collective-permute-done((bf16[128,4,2,64]{0,3,1,2:T(8,128)(2,1)S(1)}, bf16[128,4,2,64]{0,3,1,2:T(8,128)(2,1)S(1)}, u32[]{:S(2)}, u32[]{:S(2)}) %collective-permute-start.3) | collective-permute-done | bytes 131104 | tf_op jit(solution)/shard_map/ppermute | solution.py:29
  31.2 0.5 collective-permute-start.8
  31.8 12.6 %collective-permute-done.4 = bf16[128,4,2,64]{0,3,1,2:T(8,128)(2,1)S(1)} collective-permute-done((bf16[128,4,2,64]{0,3,1,2:T(8,128)(2,1)S(1)}, bf16[128,4,2,64]{0,3,1,2:T(8,128)(2,1)S(1)}, u32[]{:S(2)}, u32[]{:S(2)}) %collective-permute-start.4) | collective-permute-done | bytes 131104 | tf_op jit(solution)/shard_map/ppermute | solution.py:29
  44.4 2.8 %collective-permute-done.5 = bf16[128,4,2,64]{0,3,1,2:T(8,128)(2,1)S(1)} collective-permute-done((bf16[128,4,2,64]{0,3,1,2:T(8,128)(2,1)S(1)}, bf16[128,4,2,64]{0,3,1,2:T(8,128)(2,1)S(1)}, u32[]{:S(2)}, u32[]{:S(2)}) %collective-permute-start.5) | collective-permute-done | bytes 131104 | tf_op jit(solution)/shard_map/ppermute | solution.py:29
  47.2 0.0 collective-permute-done.6
  47.3 2.1 %collective-permute-done.7 = bf16[128,4,2,64]{0,3,1,2:T(8,128)(2,1)S(1)} collective-permute-done((bf16[128,4,2,64]{0,3,1,2:T(8,128)(2,1)S(1)}, bf16[128,4,2,64]{0,3,1,2:T(8,128)(2,1)S(1)}, u32[]{:S(2)}, u32[]{:S(2)}) %collective-permute-start.7) | collective-permute-done | bytes 131104 | tf_op jit(solution)/shard_map/ppermute | solution.py:29
  49.4 2.1 %collective-permute-done.8 = bf16[128,4,2,64]{0,3,1,2:T(8,128)(2,1)S(1)} collective-permute-done((bf16[128,4,2,64]{0,3,1,2:T(8,128)(2,1)S(1)}, bf16[128,4,2,64]{0,3,1,2:T(8,128)(2,1)S(1)}, u32[]{:S(2)}, u32[]{:S(2)}) %collective-permute-start.8) | collective-permute-done | bytes 131104 | tf_op jit(solution)/shard_map/ppermute | solution.py:29
  51.5 0.0 copy-start.2
  51.5 0.6 multiply_reduce_fusion
  52.1 0.4 copy-done.2
  52.5 0.5 fusion
  53.0 0.0 copy-start.1
  53.0 1.7 %fusion.4 = bf16[128,4,64]{0,2,1:T(8,128)(2,1)S(1)} fusion(f32[4,128,1024]{2,1,0:T(8,128)S(1)} %get-tuple-element.64, f32[4,128]{1,0:T(4,128)S(1)} %get-tuple-element.62, bf16[1024,4,2,64]{0,3,1,2:T(8,128)(2,1)} %copy-done.2, f32[128,4]{0,1:T(4,128)S(1)} %bitcast_add_fusion.1, f32[128,4]{0,1:T(4,128)S(1)} %get-tuple-element.61), kind=kOutput, calls=%fused_computation.32 | convolution fusion | flops 68780032 | bytes 2693120 | tf_op jit(solution)/shard_map/while/body/eval_jaxpr/hqk,khd->hqd/dot_general | solution.py:102
  54.7 0.1 copy.31
  54.9 0.1 dot_general.22
  55.0 0.0 copy-done.1
  55.1 0.2 fusion.34
  55.3 0.3 collective-permute-start.10
  55.7 0.8 %collective-permute-start.11 = (f32[32,1024]{1,0:T(8,128)S(1)}, f32[32,1024]{1,0:T(8,128)S(1)}, u32[]{:S(2)}, u32[]{:S(2)}) collective-permute-start(f32[32,1024]{1,0:T(8,128)S(1)} %get-tuple-element.28), channel_id=1, source_target_pairs={{0,3},{1,0},{2,1},{3,2},{4,7},{5,4},{6,5},{7,6},{8,11},{9,8},{10,9... | collective-permute-start | bytes 393224 | tf_op jit(solution)/shard_map/ppermute | solution.py:41
  56.4 1.1 %collective-permute-start.9 = (f32[32,1024]{1,0:T(8,128)S(1)}, f32[32,1024]{1,0:T(8,128)S(1)}, u32[]{:S(2)}, u32[]{:S(2)}) collective-permute-start(f32[32,1024]{1,0:T(8,128)S(1)} %get-tuple-element.20), channel_id=1, source_target_pairs={{0,1},{1,2},{2,3},{3,0},{4,5},{5,6},{6,7},{7,4},{8,9},{9,10},{10,1... | collective-permute-start | bytes 393224 | tf_op jit(solution)/shard_map/ppermute | solution.py:41
  57.5 2.4 %collective-permute-done.10 = f32[32,1024]{1,0:T(8,128)S(1)} collective-permute-done((f32[32,1024]{1,0:T(8,128)S(1)}, f32[32,1024]{1,0:T(8,128)S(1)}, u32[]{:S(2)}, u32[]{:S(2)}) %collective-permute-start.10) | collective-permute-done | bytes 131104 | tf_op jit(solution)/shard_map/ppermute | solution.py:41
  60.0 3.5 %collective-permute-done.11 = f32[32,1024]{1,0:T(8,128)S(1)} collective-permute-done((f32[32,1024]{1,0:T(8,128)S(1)}, f32[32,1024]{1,0:T(8,128)S(1)}, u32[]{:S(2)}, u32[]{:S(2)}) %collective-permute-start.11) | collective-permute-done | bytes 131104 | tf_op jit(solution)/shard_map/ppermute | solution.py:41
  63.4 0.0 collective-permute-done.9
  63.5 0.7 %reshape.178 = bf16[1,16,2,1024]{3,2,1,0:T(2,128)(2,1)} reshape(bf16[32,1024]{1,0:T(8,128)(2,1)S(1)} %fusion.38) | data formatting | bytes 131072 | tf_op jit(solution)/shard_map/reshape | solution.py:125
  (13 shorter events, 0.4 us)
Async XLA Ops:
  0.0 23.5 %copy-start = (bf16[768,1024]{1,0:T(8,128)(2,1)S(1)}, bf16[768,1024]{1,0:T(8,128)(2,1)}, u32[]{:S(2)}) copy-start(bf16[768,1024]{1,0:T(8,128)(2,1)} %param.8) | copy-start | bytes 4718596
  1.0 7.9 %collective-permute-start = (bf16[1,16,2,1024]{3,1,2,0:T(8,128)(2,1)S(1)}, bf16[1,16,2,1024]{3,1,2,0:T(8,128)(2,1)S(1)}, u32[]{:S(2)}, u32[]{:S(2)}) collective-permute-start(bf16[1,16,2,1024]{3,1,2,0:T(8,128)(2,1)S(1)} %copy.23), channel_id=1, source_target_pairs={{0,4},{4,8},{8,12},{12,16},{16,20},{20,24},{24,28},{1,5},{5,9},{9,... | collective-permute-start | bytes 196616 | tf_op jit(solution)/shard_map/ppermute | solution.py:18
  4.1 5.9 %collective-permute-start.1 = (bf16[1,16,2,1024]{3,1,2,0:T(8,128)(2,1)S(1)}, bf16[1,16,2,1024]{3,1,2,0:T(8,128)(2,1)S(1)}, u32[]{:S(2)}, u32[]{:S(2)}) collective-permute-start(bf16[1,16,2,1024]{3,1,2,0:T(8,128)(2,1)S(1)} %copy.23), channel_id=1, source_target_pairs={{4,0},{8,4},{12,8},{16,12},{20,16},{24,20},{28,24},{5,1},{9,5},{13... | collective-permute-start | bytes 196616 | tf_op jit(solution)/shard_map/ppermute | solution.py:19
  10.1 10.7 %copy-start.3 = (f32[1024]{0:T(1024)S(1)}, f32[1024]{0:T(1024)}, u32[]{:S(2)}) copy-start(f32[1024]{0:T(1024)} %param.7) | copy-start | bytes 12292
  24.4 5.0 %collective-permute-start.2 = (bf16[128,4,2,64]{0,3,1,2:T(8,128)(2,1)S(1)}, bf16[128,4,2,64]{0,3,1,2:T(8,128)(2,1)S(1)}, u32[]{:S(2)}, u32[]{:S(2)}) collective-permute-start(bf16[128,4,2,64]{0,3,1,2:T(8,128)(2,1)S(1)} %get-tuple-element.32), channel_id=1, source_target_pairs={{0,4},{4,8},{8,12},{12,16},{16,20},{20,24},{24,28},{28,0},{1,5},{5... | collective-permute-start | bytes 393224 | tf_op jit(solution)/shard_map/ppermute | solution.py:29
  24.8 6.5 %collective-permute-start.3 = (bf16[128,4,2,64]{0,3,1,2:T(8,128)(2,1)S(1)}, bf16[128,4,2,64]{0,3,1,2:T(8,128)(2,1)S(1)}, u32[]{:S(2)}, u32[]{:S(2)}) collective-permute-start(bf16[128,4,2,64]{0,3,1,2:T(8,128)(2,1)S(1)} %get-tuple-element.32), channel_id=1, source_target_pairs={{0,8},{4,12},{8,16},{12,20},{16,24},{20,28},{24,0},{28,4},{1,9},{5... | collective-permute-start | bytes 393224 | tf_op jit(solution)/shard_map/ppermute | solution.py:29
  26.1 18.3 %collective-permute-start.4 = (bf16[128,4,2,64]{0,3,1,2:T(8,128)(2,1)S(1)}, bf16[128,4,2,64]{0,3,1,2:T(8,128)(2,1)S(1)}, u32[]{:S(2)}, u32[]{:S(2)}) collective-permute-start(bf16[128,4,2,64]{0,3,1,2:T(8,128)(2,1)S(1)} %get-tuple-element.32), channel_id=1, source_target_pairs={{0,12},{4,16},{8,20},{12,24},{16,28},{20,0},{24,4},{28,8},{1,13},{... | collective-permute-start | bytes 393224 | tf_op jit(solution)/shard_map/ppermute | solution.py:29
  27.9 19.3 %collective-permute-start.5 = (bf16[128,4,2,64]{0,3,1,2:T(8,128)(2,1)S(1)}, bf16[128,4,2,64]{0,3,1,2:T(8,128)(2,1)S(1)}, u32[]{:S(2)}, u32[]{:S(2)}) collective-permute-start(bf16[128,4,2,64]{0,3,1,2:T(8,128)(2,1)S(1)} %get-tuple-element.32), channel_id=1, source_target_pairs={{0,16},{4,20},{8,24},{12,28},{16,0},{20,4},{24,8},{28,12},{1,17},{... | collective-permute-start | bytes 393224 | tf_op jit(solution)/shard_map/ppermute | solution.py:29
  29.3 17.9 %collective-permute-start.6 = (bf16[128,4,2,64]{0,3,1,2:T(8,128)(2,1)S(1)}, bf16[128,4,2,64]{0,3,1,2:T(8,128)(2,1)S(1)}, u32[]{:S(2)}, u32[]{:S(2)}) collective-permute-start(bf16[128,4,2,64]{0,3,1,2:T(8,128)(2,1)S(1)} %get-tuple-element.32), channel_id=1, source_target_pairs={{0,20},{4,24},{8,28},{12,0},{16,4},{20,8},{24,12},{28,16},{1,21},{... | collective-permute-start | bytes 393224 | tf_op jit(solution)/shard_map/ppermute | solution.py:29
  29.4 20.0 %collective-permute-start.7 = (bf16[128,4,2,64]{0,3,1,2:T(8,128)(2,1)S(1)}, bf16[128,4,2,64]{0,3,1,2:T(8,128)(2,1)S(1)}, u32[]{:S(2)}, u32[]{:S(2)}) collective-permute-start(bf16[128,4,2,64]{0,3,1,2:T(8,128)(2,1)S(1)} %get-tuple-element.32), channel_id=1, source_target_pairs={{0,24},{4,28},{8,0},{12,4},{16,8},{20,12},{24,16},{28,20},{1,25},{... | collective-permute-start | bytes 393224 | tf_op jit(solution)/shard_map/ppermute | solution.py:29
  31.2 20.2 %collective-permute-start.8 = (bf16[128,4,2,64]{0,3,1,2:T(8,128)(2,1)S(1)}, bf16[128,4,2,64]{0,3,1,2:T(8,128)(2,1)S(1)}, u32[]{:S(2)}, u32[]{:S(2)}) collective-permute-start(bf16[128,4,2,64]{0,3,1,2:T(8,128)(2,1)S(1)} %get-tuple-element.32), channel_id=1, source_target_pairs={{0,28},{4,0},{8,4},{12,8},{16,12},{20,16},{24,20},{28,24},{1,29},{... | collective-permute-start | bytes 393224 | tf_op jit(solution)/shard_map/ppermute | solution.py:29
  51.5 1.0 %copy-start.2 = (bf16[1024,4,2,64]{0,3,1,2:T(8,128)(2,1)}, bf16[1024,4,2,64]{0,3,1,2:T(8,128)(2,1)S(1)}, u32[]{:S(2)}) copy-start(bf16[1024,4,2,64]{0,3,1,2:T(8,128)(2,1)S(1)} %constant_dynamic-update-slice_fusion) | copy-start | bytes 3145732
  53.0 2.0 %copy-start.1 = (bf16[256,1024]{1,0:T(8,128)(2,1)S(1)}, bf16[256,1024]{1,0:T(8,128)(2,1)}, u32[]{:S(2)}) copy-start(bf16[256,1024]{1,0:T(8,128)(2,1)} %param.9) | copy-start | bytes 1572868
  55.3 4.6 %collective-permute-start.10 = (f32[32,1024]{1,0:T(8,128)S(1)}, f32[32,1024]{1,0:T(8,128)S(1)}, u32[]{:S(2)}, u32[]{:S(2)}) collective-permute-start(f32[32,1024]{1,0:T(8,128)S(1)} %get-tuple-element.30), channel_id=1, source_target_pairs={{0,2},{1,3},{2,0},{3,1},{4,6},{5,7},{6,4},{7,5},{8,10},{9,11},{10,... | collective-permute-start | bytes 393224 | tf_op jit(solution)/shard_map/ppermute | solution.py:41
  55.7 7.8 %collective-permute-start.11 = (f32[32,1024]{1,0:T(8,128)S(1)}, f32[32,1024]{1,0:T(8,128)S(1)}, u32[]{:S(2)}, u32[]{:S(2)}) collective-permute-start(f32[32,1024]{1,0:T(8,128)S(1)} %get-tuple-element.28), channel_id=1, source_target_pairs={{0,3},{1,0},{2,1},{3,2},{4,7},{5,4},{6,5},{7,6},{8,11},{9,8},{10,9... | collective-permute-start | bytes 393224 | tf_op jit(solution)/shard_map/ppermute | solution.py:41
  56.4 7.0 %collective-permute-start.9 = (f32[32,1024]{1,0:T(8,128)S(1)}, f32[32,1024]{1,0:T(8,128)S(1)}, u32[]{:S(2)}, u32[]{:S(2)}) collective-permute-start(f32[32,1024]{1,0:T(8,128)S(1)} %get-tuple-element.20), channel_id=1, source_target_pairs={{0,1},{1,2},{2,3},{3,0},{4,5},{5,6},{6,7},{7,4},{8,9},{9,10},{10,1... | collective-permute-start | bytes 393224 | tf_op jit(solution)/shard_map/ppermute | solution.py:41

commit v4 on v3

--- a/solution.py
+++ b/solution.py
@@ -27,6 +27,21 @@
     for shift in range(1, size):
         pairs = [(i, (i + shift) % size) for i in range(size)]
         parts.append(lax.ppermute(piece, axis, pairs))
+    return jnp.concatenate(parts, axis=0)
+
+
+def relayed(piece, axis):
+    size = lax.axis_size(axis)
+    half = size // 2
+    if size % 2:
+        return gathered(piece, axis)
+    mirror = [(i, (i + half) % size) for i in range(size)]
+    crossed = lax.ppermute(piece, axis, mirror)
+    parts = [piece, crossed]
+    for shift in range(1, half):
+        pairs = [(i, (i // half) * half + (i % half + shift) % half) for i in range(size)]
+        parts.append(lax.ppermute(piece, axis, pairs))
+        parts.append(lax.ppermute(crossed, axis, pairs))
     return jnp.concatenate(parts, axis=0)
 
 
@@ -83,7 +98,7 @@
     projected = times_transposed(slab_rows, qkv_weight).astype(jnp.bfloat16)
     split_heads = projected.reshape(slab_tok, heads_here, 3, HS)
     queries = split_heads[:, :, 0]
-    key_value = gathered(split_heads[:, :, 1:], "blk")
+    key_value = relayed(split_heads[:, :, 1:], "blk")
     key_piece = key_value[:, :, 0]
     value_piece = key_value[:, :, 1]
     score_scale = 1.0 / math.sqrt(HS)

time: 64.6 us -> 56.2 us (0.87)
  the two profiles are of different devices: /device:TPU:13 before, /device:TPU:0 now
where the time goes in v4:
time: 56.2 us; the launch traced here: 55.4 us
  starting transfers between devices  18.4 us (33%)
  waiting for transfers between devices  16.2 us (29%)
  blocking collectives  8.6 us (15%)
  local copies, waits for them, and re-layouts  5.89 us (10%)
  matrix products  3.16 us (6%)
  other arithmetic  2.91 us (5%)
    all_gather x1, blocking collectives, on_device(): slab_in = lax.all_gather(with_halo, 'uly', axis=0, tiled=False)  8.6 us
    ppermute x3, waiting for transfers between devices, scattered_sum(): total = total + lax.ppermute(outgoing, axis, pairs)  5.75 us
    ppermute x3, waiting for transfers between devices, relayed(): parts.append(lax.ppermute(crossed, axis, pairs))  5.67 us
    ppermute x1, starting transfers between devices, padded_2(): before = lax.ppermute(last, axis, up)  4.87 us
    ppermute x3, starting transfers between devices, relayed(): parts.append(lax.ppermute(piece, axis, pairs))  4.5 us
    ppermute x3, starting transfers between devices, relayed(): parts.append(lax.ppermute(crossed, axis, pairs))  3.93 us
    ppermute x1, starting transfers between devices, relayed(): crossed = lax.ppermute(piece, axis, mirror)  2.66 us
    slice x2, local copies, waits for them, and re-layouts, on_device(): conv_weight[9 * step_z + 3 * step_x + step_y]  2.58 us
  transfers between devices with their start and end apart: 12, of which 7 were waited for; matrix products, arithmetic and copies ran while one was open for 5% of the time, Pallas kernels for 0%

profile of v4, /device:TPU:0, one launch (start us, length us, event | category | flops | bytes accessed | tf_op | source)
XLA Modules:
  0.0 55.4 jit_solution(15185441205694310477)
XLA Ops:
  0.0 0.0 copy-start
  0.0 1.0 %copy.23 = bf16[1,16,2,1024]{3,1,2,0:T(8,128)(2,1)S(1)} copy(bf16[1,16,2,1024]{3,2,1,0:T(2,128)(2,1)} %param.5) | data formatting | bytes 131072 | tf_op args[0]
  1.0 4.9 %collective-permute-start = (bf16[1,16,2,1024]{3,1,2,0:T(8,128)(2,1)S(1)}, bf16[1,16,2,1024]{3,1,2,0:T(8,128)(2,1)S(1)}, u32[]{:S(2)}, u32[]{:S(2)}) collective-permute-start(bf16[1,16,2,1024]{3,1,2,0:T(8,128)(2,1)S(1)} %copy.23), channel_id=1, source_target_pairs={{0,4},{4,8},{8,12},{12,16},{16,20},{20,24},{24,28},{1,5},{5,9},{9,... | collective-permute-start | bytes 196616 | tf_op jit(solution)/shard_map/ppermute | solution.py:18
  5.9 1.3 %collective-permute-start.1 = (bf16[1,16,2,1024]{3,1,2,0:T(8,128)(2,1)S(1)}, bf16[1,16,2,1024]{3,1,2,0:T(8,128)(2,1)S(1)}, u32[]{:S(2)}, u32[]{:S(2)}) collective-permute-start(bf16[1,16,2,1024]{3,1,2,0:T(8,128)(2,1)S(1)} %copy.23), channel_id=1, source_target_pairs={{4,0},{8,4},{12,8},{16,12},{20,16},{24,20},{28,24},{5,1},{9,5},{13... | collective-permute-start | bytes 196616 | tf_op jit(solution)/shard_map/ppermute | solution.py:19
  7.2 1.4 %fusion.42 = (f32[1,1024]{1,0:T(1,128)S(1)}, f32[1,1024]{1,0:T(1,128)S(1)}, f32[1,1024]{1,0:T(1,128)S(1)}, f32[1,1024]{1,0:T(1,128)S(1)}, f32[1,1024]{1,0:T(1,12...) fusion(f32[27,1024]{1,0:T(8,128)} %param.6), kind=kLoop, calls=%fused_computation.94 | loop fusion | bytes 155648 | tf_op jit(solution)/shard_map/slice | solution.py:82
  8.6 1.2 %fusion.43 = (f32[1,1024]{1,0:T(1,128)S(1)}, f32[1,1024]{1,0:T(1,128)S(1)}, f32[1,1024]{1,0:T(1,128)S(1)}, f32[1,1024]{1,0:T(1,128)S(1)}, f32[1,1024]{1,0:T(1,12...) fusion(f32[27,1024]{1,0:T(8,128)} %param.6), kind=kLoop, calls=%fused_computation.95 | loop fusion | bytes 65536 | tf_op jit(solution)/shard_map/slice | solution.py:82
  9.7 0.0 collective-permute-done
  9.8 2.3 %collective-permute-done.1 = bf16[1,16,2,1024]{3,1,2,0:T(8,128)(2,1)S(1)} collective-permute-done((bf16[1,16,2,1024]{3,1,2,0:T(8,128)(2,1)S(1)}, bf16[1,16,2,1024]{3,1,2,0:T(8,128)(2,1)S(1)}, u32[]{:S(2)}, u32[]{:S(2)}) %collective-permute-start.1) | collective-permute-done | bytes 65568 | tf_op jit(solution)/shard_map/ppermute | solution.py:19
  12.0 0.0 copy-start.3
  12.1 8.6 %all-gather = bf16[12,16,2,1024]{3,1,2,0:T(8,128)(2,1)S(1)} all-gather(bf16[3,16,2,1024]{3,1,2,0:T(8,128)(2,1)S(1)} %pad_maximum_fusion), channel_id=2, replica_groups=mesh['blk'=8,'uly'=4] {'uly'}, dimensions={0}, use_global_device_ids=true | all-gather | bytes 983040 | tf_op jit(solution)/shard_map/all_gather | solution.py:70
  20.7 0.1 fusion.40
  20.7 0.1 copy.26
  20.8 0.0 copy-done.3
  20.8 2.3 %add_convert_fusion = bf16[1,16,8,1024]{3,1,2,0:T(8,128)(2,1)S(1)} fusion(bf16[1,16,8,1024]{3,1,2,0:T(8,128)(2,1)S(1)} %bitcast.99, bf16[1,16,8,1024]{3,1,2,0:T(8,128)(2,1)S(1)} %bitcast.100, bf16[1,16,8,1024]{3,1,2,0:T(8,128)(2,1)S(1)} %bitcast.98, bf16[3,16,8,1024]{3,1,2,0:T(8,128)(2,1)S(1)} %bitcast.95, f32[1024]{0:T(1024)S(1)} %bitcast.128, ...), kind=kLoop, calls=%fused_computation.69 | loop fusion | flops 10878976 | bytes 1949696 | tf_op jit(solution)/shard_map/convert_element_type | solution.py:89
  23.1 0.3 copy.37
  23.4 0.1 reshape.176
  23.5 0.0 copy-done
  23.5 0.7 %convolution_convert_fusion = bf16[128,768]{1,0:T(8,128)(2,1)S(1)} fusion(bf16[128,1024]{1,0:T(8,128)(2,1)S(1)} %reshape.176, bf16[768,1024]{1,0:T(8,128)(2,1)S(1)} %copy-done), kind=kOutput, calls=%fused_computation.28 | convolution fusion | flops 201424896 | bytes 2031616 | tf_op jit(solution)/shard_map/dot_general | solution.py:61
  24.2 0.2 copy.28
  24.4 2.7 %collective-permute-start.2 = (bf16[128,4,2,64]{0,3,1,2:T(8,128)(2,1)S(1)}, bf16[128,4,2,64]{0,3,1,2:T(8,128)(2,1)S(1)}, u32[]{:S(2)}, u32[]{:S(2)}) collective-permute-start(bf16[128,4,2,64]{0,3,1,2:T(8,128)(2,1)S(1)} %get-tuple-element.32), channel_id=1, source_target_pairs={{0,16},{4,20},{8,24},{12,28},{16,0},{20,4},{24,8},{28,12},{1,17},{... | collective-permute-start | bytes 393224 | tf_op jit(solution)/shard_map/ppermute | solution.py:39
  27.1 2.4 %collective-permute-start.3 = (bf16[128,4,2,64]{0,3,1,2:T(8,128)(2,1)S(1)}, bf16[128,4,2,64]{0,3,1,2:T(8,128)(2,1)S(1)}, u32[]{:S(2)}, u32[]{:S(2)}) collective-permute-start(bf16[128,4,2,64]{0,3,1,2:T(8,128)(2,1)S(1)} %get-tuple-element.32), channel_id=1, source_target_pairs={{0,4},{4,8},{8,12},{12,0},{16,20},{20,24},{24,28},{28,16},{1,5},{5... | collective-permute-start | bytes 393224 | tf_op jit(solution)/shard_map/ppermute | solution.py:43
  29.5 0.0 collective-permute-start.5
  29.5 2.1 %collective-permute-start.7 = (bf16[128,4,2,64]{0,3,1,2:T(8,128)(2,1)S(1)}, bf16[128,4,2,64]{0,3,1,2:T(8,128)(2,1)S(1)}, u32[]{:S(2)}, u32[]{:S(2)}) collective-permute-start(bf16[128,4,2,64]{0,3,1,2:T(8,128)(2,1)S(1)} %get-tuple-element.32), channel_id=1, source_target_pairs={{0,12},{4,0},{8,4},{12,8},{16,28},{20,16},{24,20},{28,24},{1,13},{... | collective-permute-start | bytes 393224 | tf_op jit(solution)/shard_map/ppermute | solution.py:43
  31.6 2.5 %collective-permute-done.2 = bf16[128,4,2,64]{0,3,1,2:T(8,128)(2,1)S(1)} collective-permute-done((bf16[128,4,2,64]{0,3,1,2:T(8,128)(2,1)S(1)}, bf16[128,4,2,64]{0,3,1,2:T(8,128)(2,1)S(1)}, u32[]{:S(2)}, u32[]{:S(2)}) %collective-permute-start.2) | collective-permute-done | bytes 131104 | tf_op jit(solution)/shard_map/ppermute | solution.py:39
  34.0 2.4 %collective-permute-start.4 = (bf16[128,4,2,64]{0,3,1,2:T(8,128)(2,1)S(1)}, bf16[128,4,2,64]{0,3,1,2:T(8,128)(2,1)S(1)}, u32[]{:S(2)}, u32[]{:S(2)}) collective-permute-start(bf16[128,4,2,64]{0,3,1,2:T(8,128)(2,1)S(1)} %collective-permute-done.2), channel_id=1, source_target_pairs={{0,4},{4,8},{8,12},{12,0},{16,20},{20,24},{24,28},{28,16},{1,5},{5... | collective-permute-start | bytes 393224 | tf_op jit(solution)/shard_map/ppermute | solution.py:44
  36.5 0.0 collective-permute-start.6
  36.5 0.0 collective-permute-done.3
  36.5 1.5 %collective-permute-start.8 = (bf16[128,4,2,64]{0,3,1,2:T(8,128)(2,1)S(1)}, bf16[128,4,2,64]{0,3,1,2:T(8,128)(2,1)S(1)}, u32[]{:S(2)}, u32[]{:S(2)}) collective-permute-start(bf16[128,4,2,64]{0,3,1,2:T(8,128)(2,1)S(1)} %collective-permute-done.2), channel_id=1, source_target_pairs={{0,12},{4,0},{8,4},{12,8},{16,28},{20,16},{24,20},{28,24},{1,13},{... | collective-permute-start | bytes 393224 | tf_op jit(solution)/shard_map/ppermute | solution.py:44
  38.1 3.6 %collective-permute-done.4 = bf16[128,4,2,64]{0,3,1,2:T(8,128)(2,1)S(1)} collective-permute-done((bf16[128,4,2,64]{0,3,1,2:T(8,128)(2,1)S(1)}, bf16[128,4,2,64]{0,3,1,2:T(8,128)(2,1)S(1)}, u32[]{:S(2)}, u32[]{:S(2)}) %collective-permute-start.4) | collective-permute-done | bytes 131104 | tf_op jit(solution)/shard_map/ppermute | solution.py:44
  41.8 0.0 collective-permute-done.5
  41.8 1.1 %collective-permute-done.6 = bf16[128,4,2,64]{0,3,1,2:T(8,128)(2,1)S(1)} collective-permute-done((bf16[128,4,2,64]{0,3,1,2:T(8,128)(2,1)S(1)}, bf16[128,4,2,64]{0,3,1,2:T(8,128)(2,1)S(1)}, u32[]{:S(2)}, u32[]{:S(2)}) %collective-permute-start.6) | collective-permute-done | bytes 131104 | tf_op jit(solution)/shard_map/ppermute | solution.py:44
  42.9 0.0 collective-permute-done.7
  43.0 0.9 %collective-permute-done.8 = bf16[128,4,2,64]{0,3,1,2:T(8,128)(2,1)S(1)} collective-permute-done((bf16[128,4,2,64]{0,3,1,2:T(8,128)(2,1)S(1)}, bf16[128,4,2,64]{0,3,1,2:T(8,128)(2,1)S(1)}, u32[]{:S(2)}, u32[]{:S(2)}) %collective-permute-start.8) | collective-permute-done | bytes 131104 | tf_op jit(solution)/shard_map/ppermute | solution.py:44
  44.0 0.0 copy-start.2
  44.0 0.6 %multiply_reduce_fusion = (f32[4,128]{1,0:T(4,128)S(1)}, f32[4,128,1024]{2,1,0:T(8,128)S(1)}) fusion(bf16[1024,4,2,64]{0,3,1,2:T(8,128)(2,1)S(1)} %constant_dynamic-update-slice_fusion, bf16[128,4,3,64]{0,3,2,1:T(8,128)(2,1)S(1)} %bitcast.102), kind=kOutput, calls=%fused_computation.25 | convolution fusion | flops 68156928 | bytes 2689024 | tf_op jit(solution)/shard_map/while/body/eval_jaxpr/qhd,khd->hqk/dot_general | solution.py:110
  44.6 0.4 copy-done.2
  45.0 0.5 fusion
  45.5 0.0 copy-start.1
  45.5 1.7 %fusion.4 = bf16[128,4,64]{0,2,1:T(8,128)(2,1)S(1)} fusion(f32[4,128,1024]{2,1,0:T(8,128)S(1)} %get-tuple-element.64, f32[4,128]{1,0:T(4,128)S(1)} %get-tuple-element.62, bf16[1024,4,2,64]{0,3,1,2:T(8,128)(2,1)} %copy-done.2, f32[128,4]{0,1:T(4,128)S(1)} %bitcast_add_fusion.1, f32[128,4]{0,1:T(4,128)S(1)} %get-tuple-element.61), kind=kOutput, calls=%fused_computation.32 | convolution fusion | flops 68780032 | bytes 2693120 | tf_op jit(solution)/shard_map/while/body/eval_jaxpr/hqk,khd->hqd/dot_general | solution.py:117
  47.2 0.1 copy.31
  47.4 0.1 dot_general.22
  47.5 0.0 copy-done.1
  47.5 0.2 fusion.34
  47.8 0.6 %collective-permute-start.10 = (f32[32,1024]{1,0:T(8,128)S(1)}, f32[32,1024]{1,0:T(8,128)S(1)}, u32[]{:S(2)}, u32[]{:S(2)}) collective-permute-start(f32[32,1024]{1,0:T(8,128)S(1)} %get-tuple-element.30), channel_id=1, source_target_pairs={{0,2},{1,3},{2,0},{3,1},{4,6},{5,7},{6,4},{7,5},{8,10},{9,11},{10,... | collective-permute-start | bytes 393224 | tf_op jit(solution)/shard_map/ppermute | solution.py:56
  48.4 0.5 collective-permute-start.11
  48.9 0.0 collective-permute-start.9
  48.9 5.1 %collective-permute-done.10 = f32[32,1024]{1,0:T(8,128)S(1)} collective-permute-done((f32[32,1024]{1,0:T(8,128)S(1)}, f32[32,1024]{1,0:T(8,128)S(1)}, u32[]{:S(2)}, u32[]{:S(2)}) %collective-permute-start.10) | collective-permute-done | bytes 131104 | tf_op jit(solution)/shard_map/ppermute | solution.py:56
  54.0 0.0 collective-permute-done.11
  54.0 0.7 %collective-permute-done.9 = f32[32,1024]{1,0:T(8,128)S(1)} collective-permute-done((f32[32,1024]{1,0:T(8,128)S(1)}, f32[32,1024]{1,0:T(8,128)S(1)}, u32[]{:S(2)}, u32[]{:S(2)}) %collective-permute-start.9) | collective-permute-done | bytes 131104 | tf_op jit(solution)/shard_map/ppermute | solution.py:56
  54.7 0.7 %reshape.178 = bf16[1,16,2,1024]{3,2,1,0:T(2,128)(2,1)} reshape(bf16[32,1024]{1,0:T(8,128)(2,1)S(1)} %fusion.38) | data formatting | bytes 131072 | tf_op jit(solution)/shard_map/reshape | solution.py:140
  (13 shorter events, 0.4 us)
Async XLA Ops:
  0.0 23.5 %copy-start = (bf16[768,1024]{1,0:T(8,128)(2,1)S(1)}, bf16[768,1024]{1,0:T(8,128)(2,1)}, u32[]{:S(2)}) copy-start(bf16[768,1024]{1,0:T(8,128)(2,1)} %param.8) | copy-start | bytes 4718596
  1.0 8.8 %collective-permute-start = (bf16[1,16,2,1024]{3,1,2,0:T(8,128)(2,1)S(1)}, bf16[1,16,2,1024]{3,1,2,0:T(8,128)(2,1)S(1)}, u32[]{:S(2)}, u32[]{:S(2)}) collective-permute-start(bf16[1,16,2,1024]{3,1,2,0:T(8,128)(2,1)S(1)} %copy.23), channel_id=1, source_target_pairs={{0,4},{4,8},{8,12},{12,16},{16,20},{20,24},{24,28},{1,5},{5,9},{9,... | collective-permute-start | bytes 196616 | tf_op jit(solution)/shard_map/ppermute | solution.py:18
  5.9 6.2 %collective-permute-start.1 = (bf16[1,16,2,1024]{3,1,2,0:T(8,128)(2,1)S(1)}, bf16[1,16,2,1024]{3,1,2,0:T(8,128)(2,1)S(1)}, u32[]{:S(2)}, u32[]{:S(2)}) collective-permute-start(bf16[1,16,2,1024]{3,1,2,0:T(8,128)(2,1)S(1)} %copy.23), channel_id=1, source_target_pairs={{4,0},{8,4},{12,8},{16,12},{20,16},{24,20},{28,24},{5,1},{9,5},{13... | collective-permute-start | bytes 196616 | tf_op jit(solution)/shard_map/ppermute | solution.py:19
  12.0 8.7 %copy-start.3 = (f32[1024]{0:T(1024)S(1)}, f32[1024]{0:T(1024)}, u32[]{:S(2)}) copy-start(f32[1024]{0:T(1024)} %param.7) | copy-start | bytes 12292
  24.4 9.6 %collective-permute-start.2 = (bf16[128,4,2,64]{0,3,1,2:T(8,128)(2,1)S(1)}, bf16[128,4,2,64]{0,3,1,2:T(8,128)(2,1)S(1)}, u32[]{:S(2)}, u32[]{:S(2)}) collective-permute-start(bf16[128,4,2,64]{0,3,1,2:T(8,128)(2,1)S(1)} %get-tuple-element.32), channel_id=1, source_target_pairs={{0,16},{4,20},{8,24},{12,28},{16,0},{20,4},{24,8},{28,12},{1,17},{... | collective-permute-start | bytes 393224 | tf_op jit(solution)/shard_map/ppermute | solution.py:39
  27.1 9.4 %collective-permute-start.3 = (bf16[128,4,2,64]{0,3,1,2:T(8,128)(2,1)S(1)}, bf16[128,4,2,64]{0,3,1,2:T(8,128)(2,1)S(1)}, u32[]{:S(2)}, u32[]{:S(2)}) collective-permute-start(bf16[128,4,2,64]{0,3,1,2:T(8,128)(2,1)S(1)} %get-tuple-element.32), channel_id=1, source_target_pairs={{0,4},{4,8},{8,12},{12,0},{16,20},{20,24},{24,28},{28,16},{1,5},{5... | collective-permute-start | bytes 393224 | tf_op jit(solution)/shard_map/ppermute | solution.py:43
  29.5 12.3 %collective-permute-start.5 = (bf16[128,4,2,64]{0,3,1,2:T(8,128)(2,1)S(1)}, bf16[128,4,2,64]{0,3,1,2:T(8,128)(2,1)S(1)}, u32[]{:S(2)}, u32[]{:S(2)}) collective-permute-start(bf16[128,4,2,64]{0,3,1,2:T(8,128)(2,1)S(1)} %get-tuple-element.32), channel_id=1, source_target_pairs={{0,8},{4,12},{8,0},{12,4},{16,24},{20,28},{24,16},{28,20},{1,9},{5... | collective-permute-start | bytes 393224 | tf_op jit(solution)/shard_map/ppermute | solution.py:43
  29.5 13.5 %collective-permute-start.7 = (bf16[128,4,2,64]{0,3,1,2:T(8,128)(2,1)S(1)}, bf16[128,4,2,64]{0,3,1,2:T(8,128)(2,1)S(1)}, u32[]{:S(2)}, u32[]{:S(2)}) collective-permute-start(bf16[128,4,2,64]{0,3,1,2:T(8,128)(2,1)S(1)} %get-tuple-element.32), channel_id=1, source_target_pairs={{0,12},{4,0},{8,4},{12,8},{16,28},{20,16},{24,20},{28,24},{1,13},{... | collective-permute-start | bytes 393224 | tf_op jit(solution)/shard_map/ppermute | solution.py:43
  34.0 7.7 %collective-permute-start.4 = (bf16[128,4,2,64]{0,3,1,2:T(8,128)(2,1)S(1)}, bf16[128,4,2,64]{0,3,1,2:T(8,128)(2,1)S(1)}, u32[]{:S(2)}, u32[]{:S(2)}) collective-permute-start(bf16[128,4,2,64]{0,3,1,2:T(8,128)(2,1)S(1)} %collective-permute-done.2), channel_id=1, source_target_pairs={{0,4},{4,8},{8,12},{12,0},{16,20},{20,24},{24,28},{28,16},{1,5},{5... | collective-permute-start | bytes 393224 | tf_op jit(solution)/shard_map/ppermute | solution.py:44
  36.5 6.4 %collective-permute-start.6 = (bf16[128,4,2,64]{0,3,1,2:T(8,128)(2,1)S(1)}, bf16[128,4,2,64]{0,3,1,2:T(8,128)(2,1)S(1)}, u32[]{:S(2)}, u32[]{:S(2)}) collective-permute-start(bf16[128,4,2,64]{0,3,1,2:T(8,128)(2,1)S(1)} %collective-permute-done.2), channel_id=1, source_target_pairs={{0,8},{4,12},{8,0},{12,4},{16,24},{20,28},{24,16},{28,20},{1,9},{5... | collective-permute-start | bytes 393224 | tf_op jit(solution)/shard_map/ppermute | solution.py:44
  36.5 7.4 %collective-permute-start.8 = (bf16[128,4,2,64]{0,3,1,2:T(8,128)(2,1)S(1)}, bf16[128,4,2,64]{0,3,1,2:T(8,128)(2,1)S(1)}, u32[]{:S(2)}, u32[]{:S(2)}) collective-permute-start(bf16[128,4,2,64]{0,3,1,2:T(8,128)(2,1)S(1)} %collective-permute-done.2), channel_id=1, source_target_pairs={{0,12},{4,0},{8,4},{12,8},{16,28},{20,16},{24,20},{28,24},{1,13},{... | collective-permute-start | bytes 393224 | tf_op jit(solution)/shard_map/ppermute | solution.py:44
  44.0 1.0 %copy-start.2 = (bf16[1024,4,2,64]{0,3,1,2:T(8,128)(2,1)}, bf16[1024,4,2,64]{0,3,1,2:T(8,128)(2,1)S(1)}, u32[]{:S(2)}) copy-start(bf16[1024,4,2,64]{0,3,1,2:T(8,128)(2,1)S(1)} %constant_dynamic-update-slice_fusion) | copy-start | bytes 3145732
  45.5 2.0 %copy-start.1 = (bf16[256,1024]{1,0:T(8,128)(2,1)S(1)}, bf16[256,1024]{1,0:T(8,128)(2,1)}, u32[]{:S(2)}) copy-start(bf16[256,1024]{1,0:T(8,128)(2,1)} %param.9) | copy-start | bytes 1572868
  47.8 6.2 %collective-permute-start.10 = (f32[32,1024]{1,0:T(8,128)S(1)}, f32[32,1024]{1,0:T(8,128)S(1)}, u32[]{:S(2)}, u32[]{:S(2)}) collective-permute-start(f32[32,1024]{1,0:T(8,128)S(1)} %get-tuple-element.30), channel_id=1, source_target_pairs={{0,2},{1,3},{2,0},{3,1},{4,6},{5,7},{6,4},{7,5},{8,10},{9,11},{10,... | collective-permute-start | bytes 393224 | tf_op jit(solution)/shard_map/ppermute | solution.py:56
  48.4 5.6 %collective-permute-start.11 = (f32[32,1024]{1,0:T(8,128)S(1)}, f32[32,1024]{1,0:T(8,128)S(1)}, u32[]{:S(2)}, u32[]{:S(2)}) collective-permute-start(f32[32,1024]{1,0:T(8,128)S(1)} %get-tuple-element.28), channel_id=1, source_target_pairs={{0,3},{1,0},{2,1},{3,2},{4,7},{5,4},{6,5},{7,6},{8,11},{9,8},{10,9... | collective-permute-start | bytes 393224 | tf_op jit(solution)/shard_map/ppermute | solution.py:56
  48.9 5.8 %collective-permute-start.9 = (f32[32,1024]{1,0:T(8,128)S(1)}, f32[32,1024]{1,0:T(8,128)S(1)}, u32[]{:S(2)}, u32[]{:S(2)}) collective-permute-start(f32[32,1024]{1,0:T(8,128)S(1)} %get-tuple-element.20), channel_id=1, source_target_pairs={{0,1},{1,2},{2,3},{3,0},{4,5},{5,6},{6,7},{7,4},{8,9},{9,10},{10,1... | collective-permute-start | bytes 393224 | tf_op jit(solution)/shard_map/ppermute | solution.py:56

commit v5 on v4

--- a/solution.py
+++ b/solution.py
@@ -45,6 +45,44 @@
     return jnp.concatenate(parts, axis=0)
 
 
+def chip_shift(size, shift):
+    chips = size // 2
+    return [(i, ((i // 2 + shift) % chips) * 2 + i % 2) for i in range(size)]
+
+
+def gathered_by_chip(piece, axis):
+    size = lax.axis_size(axis)
+    rank = lax.axis_index(axis)
+    chips, core = size // 2, rank % 2
+    partner = [(i, i ^ 1) for i in range(size)]
+    stacked = jnp.zeros((size,) + piece.shape, piece.dtype)
+    stacked = lax.dynamic_update_index_in_dim(stacked, piece, rank, 0)
+    near = lax.ppermute(piece, axis, partner)
+    stacked = lax.dynamic_update_index_in_dim(stacked, near, rank ^ 1, 0)
+    for shift in range(1, chips):
+        source_chip = (rank // 2 - shift) % chips
+        far = lax.ppermute(piece, axis, chip_shift(size, shift))
+        stacked = lax.dynamic_update_index_in_dim(stacked, far, source_chip * 2 + core, 0)
+        handed = lax.ppermute(far, axis, partner)
+        stacked = lax.dynamic_update_index_in_dim(stacked, handed, source_chip * 2 + 1 - core, 0)
+    return stacked
+
+
+def scattered_sum_by_chip(whole, axis, shape):
+    size = lax.axis_size(axis)
+    rank = lax.axis_index(axis)
+    chips, core, chip = size // 2, rank % 2, rank // 2
+    blocks = whole.reshape(chips, 2, whole.shape[0] // size, *whole.shape[1:])
+    mine = lax.dynamic_index_in_dim(blocks, core, 1, keepdims=False)
+    theirs = lax.dynamic_index_in_dim(blocks, 1 - core, 1, keepdims=False)
+    chip_sum = mine + lax.ppermute(theirs, axis, [(i, i ^ 1) for i in range(size)])
+    total = lax.dynamic_index_in_dim(chip_sum, chip, 0, keepdims=False).reshape(shape)
+    for shift in range(1, chips):
+        outgoing = lax.dynamic_index_in_dim(chip_sum, (chip + shift) % chips, 0, keepdims=False)
+        total = total + lax.ppermute(outgoing, axis, chip_shift(size, shift)).reshape(shape)
+    return total
+
+
 def scattered_sum(whole, axis):
     size = lax.axis_size(axis)
     rank = lax.axis_index(axis)
@@ -67,7 +105,7 @@
     z_count, x_count, y_count, features = tokens.shape
     groups = lax.axis_size("uly")
     with_halo = padded_2(tokens, (("blk", 0),), 1)
-    slab_in = lax.all_gather(with_halo, "uly", axis=0, tiled=False)
+    slab_in = gathered_by_chip(with_halo, "uly")
     slab_in = slab_in.transpose(1, 2, 0, 3, 4).reshape(
         z_count + 2, x_count, groups * y_count, features
     )
@@ -136,8 +174,8 @@
     attended = (weighted / running_sum[:, :, None]).astype(jnp.bfloat16)
     head_rows = attended.transpose(1, 0, 2).reshape(slab_tok, heads_here * HS)
     partial = jnp.dot(head_rows, out_weight, preferred_element_type=jnp.float32)
-    result = scattered_sum(partial, "uly")
-    return result.astype(jnp.bfloat16).reshape(z_count, x_count, y_count, features)
+    result = scattered_sum_by_chip(partial, "uly", tokens.shape)
+    return result.astype(jnp.bfloat16)
 
 
 def solution(mesh):

time: 56.2 us -> 55.9 us (level)
  blocking collectives: 8.6 us -> 0 us
  waiting for transfers between devices: 16.2 us -> 21.5 us
  starting transfers between devices: 18.4 us -> 20.4 us
  other arithmetic: 2.91 us -> 3.6 us
    all_gather x1 -> x0, blocking collectives: 8.6 us -> none  [on_device(): slab_in = lax.all_gather(with_halo, 'uly', axis=0, tiled=False)]
    ppermute x3 -> x5, waiting for transfers between devices: 5.75 us -> 12.5 us  [the longest x1 5.63 us: gathered_by_chip(): far = lax.ppermute(piece, axis, chip_shift(size, shift))]
    ppermute x3 -> x5, starting transfers between devices: 1.11 us -> 3.2 us  [the longest x1 1.57 us: scattered_sum_by_chip(): lax.ppermute(outgoing, axis, chip_shift(size, shift)).reshape(shape)]
    ppermute x1, waiting for transfers between devices: 2.26 us -> 1.32 us  [padded_2(): after = lax.ppermute(initial, axis, down)]
    unnamed x16 -> x18, local copies, waits for them, and re-layouts: 1.65 us -> 2.51 us
    ppermute x3, starting transfers between devices: 3.93 us -> 3.09 us  [relayed(): parts.append(lax.ppermute(crossed, axis, pairs))]
    ppermute x1, starting transfers between devices: 2.66 us -> 3.46 us  [relayed(): crossed = lax.ppermute(piece, axis, mirror)]
    ppermute x3, waiting for transfers between devices: 5.67 us -> 4.92 us  [relayed(): parts.append(lax.ppermute(crossed, axis, pairs))]
  transfers between devices with their start and end apart: 12 -> 14, of which waited for: 7 -> 10; matrix products, arithmetic and copies ran while one was open for 5% -> 7% of each run, Pallas kernels for 0% -> 0%
where the time goes in v5:
time: 55.9 us; the launch traced here: 55.4 us
  waiting for transfers between devices  21.5 us (38%)
  starting transfers between devices  20.4 us (36%)
  local copies, waits for them, and re-layouts  6.37 us (11%)
  other arithmetic  3.6 us (6%)
  matrix products  3.15 us (6%)
    ppermute x1, waiting for transfers between devices, gathered_by_chip(): far = lax.ppermute(piece, axis, chip_shift(size, shift))  5.63 us
    ppermute x3, waiting for transfers between devices, relayed(): parts.append(lax.ppermute(crossed, axis, pairs))  4.92 us
    ppermute x1, starting transfers between devices, padded_2(): before = lax.ppermute(last, axis, up)  4.87 us
    ppermute x3, starting transfers between devices, relayed(): parts.append(lax.ppermute(piece, axis, pairs))  4.5 us
    ppermute x1, waiting for transfers between devices, scattered_sum_by_chip(): lax.ppermute(outgoing, axis, chip_shift(size, shift)).reshape(shape)  3.96 us
    ppermute x1, starting transfers between devices, relayed(): crossed = lax.ppermute(piece, axis, mirror)  3.46 us
    ppermute x3, starting transfers between devices, relayed(): parts.append(lax.ppermute(crossed, axis, pairs))  3.09 us
    slice x2, local copies, waits for them, and re-layouts, on_device(): conv_weight[9 * step_z + 3 * step_x + step_y]  2.58 us
  transfers between devices with their start and end apart: 14, of which 10 were waited for; matrix products, arithmetic and copies ran while one was open for 7% of the time, Pallas kernels for 0%

profile of v5, /device:TPU:0, one launch (start us, length us, event | category | flops | bytes accessed | tf_op | source)
XLA Modules:
  0.0 55.4 jit_solution(4348885578212167399)
XLA Ops:
  0.0 0.0 copy-start
  0.0 1.0 %copy.9 = bf16[1,16,2,1024]{3,1,2,0:T(8,128)(2,1)S(1)} copy(bf16[1,16,2,1024]{3,2,1,0:T(2,128)(2,1)} %param.5) | data formatting | bytes 131072 | tf_op args[0]
  1.0 4.9 %collective-permute-start = (bf16[1,16,2,1024]{3,1,2,0:T(8,128)(2,1)S(1)}, bf16[1,16,2,1024]{3,1,2,0:T(8,128)(2,1)S(1)}, u32[]{:S(2)}, u32[]{:S(2)}) collective-permute-start(bf16[1,16,2,1024]{3,1,2,0:T(8,128)(2,1)S(1)} %copy.9), channel_id=1, source_target_pairs={{0,4},{4,8},{8,12},{12,16},{16,20},{20,24},{24,28},{1,5},{5,9},{9,... | collective-permute-start | bytes 196616 | tf_op jit(solution)/shard_map/ppermute | solution.py:18
  5.9 1.3 %collective-permute-start.1 = (bf16[1,16,2,1024]{3,1,2,0:T(8,128)(2,1)S(1)}, bf16[1,16,2,1024]{3,1,2,0:T(8,128)(2,1)S(1)}, u32[]{:S(2)}, u32[]{:S(2)}) collective-permute-start(bf16[1,16,2,1024]{3,1,2,0:T(8,128)(2,1)S(1)} %copy.9), channel_id=1, source_target_pairs={{4,0},{8,4},{12,8},{16,12},{20,16},{24,20},{28,24},{5,1},{9,5},{13... | collective-permute-start | bytes 196616 | tf_op jit(solution)/shard_map/ppermute | solution.py:19
  7.2 1.4 %fusion.39 = (f32[1,1024]{1,0:T(1,128)S(1)}, f32[1,1024]{1,0:T(1,128)S(1)}, f32[1,1024]{1,0:T(1,128)S(1)}, f32[1,1024]{1,0:T(1,128)S(1)}, f32[1,1024]{1,0:T(1,12...) fusion(f32[27,1024]{1,0:T(8,128)} %param.6), kind=kLoop, calls=%fused_computation.98 | loop fusion | bytes 155648 | tf_op jit(solution)/shard_map/slice | solution.py:120
  8.6 1.2 %fusion.40 = (f32[1,1024]{1,0:T(1,128)S(1)}, f32[1,1024]{1,0:T(1,128)S(1)}, f32[1,1024]{1,0:T(1,128)S(1)}, f32[1,1024]{1,0:T(1,128)S(1)}, f32[1,1024]{1,0:T(1,12...) fusion(f32[27,1024]{1,0:T(8,128)} %param.6), kind=kLoop, calls=%fused_computation.99 | loop fusion | bytes 65536 | tf_op jit(solution)/shard_map/slice | solution.py:120
  9.8 0.0 collective-permute-done
  9.8 0.9 %constant_dynamic-update-slice_fusion.1 = bf16[3,16,2,1024]{3,1,2,0:T(8,128)(2,1)S(1)} fusion(bf16[3,16,2,1024]{3,1,2,0:T(8,128)(2,1)S(1)} %constant_dynamic-update-slice_fusion.2, bf16[1,16,2,1024]{3,2,1,0:T(2,128)(2,1)} %param.5), kind=kLoop, calls=%fused_computation.81 | loop fusion | bytes 131072
  10.7 0.0 copy-start.3
  10.7 1.3 %collective-permute-done.1 = bf16[1,16,2,1024]{3,1,2,0:T(8,128)(2,1)S(1)} collective-permute-done((bf16[1,16,2,1024]{3,1,2,0:T(8,128)(2,1)S(1)}, bf16[1,16,2,1024]{3,1,2,0:T(8,128)(2,1)S(1)}, u32[]{:S(2)}, u32[]{:S(2)}) %collective-permute-start.1) | collective-permute-done | bytes 65568 | tf_op jit(solution)/shard_map/ppermute | solution.py:19
  12.0 0.0 collective-permute-start.2
  12.0 1.6 %collective-permute-start.3 = (bf16[3,16,2,1024]{3,1,2,0:T(8,128)(2,1)S(1)}, bf16[3,16,2,1024]{3,1,2,0:T(8,128)(2,1)S(1)}, u32[]{:S(2)}, u32[]{:S(2)}) collective-permute-start(bf16[3,16,2,1024]{3,1,2,0:T(8,128)(2,1)S(1)} %constant_dynamic-update-slice_fusion), channel_id=1, source_target_pairs={{0,2},{1,3},{2,0},{3,1},{4,6},{5,7},{6,4},{7,5},{8,10},{9,11},{10,... | collective-permute-start | bytes 589832 | tf_op jit(solution)/shard_map/ppermute | solution.py:64
  13.6 0.1 broadcast_in_dim.31
  13.7 5.6 %collective-permute-done.3 = bf16[3,16,2,1024]{3,1,2,0:T(8,128)(2,1)S(1)} collective-permute-done((bf16[3,16,2,1024]{3,1,2,0:T(8,128)(2,1)S(1)}, bf16[3,16,2,1024]{3,1,2,0:T(8,128)(2,1)S(1)}, u32[]{:S(2)}, u32[]{:S(2)}) %collective-permute-start.3) | collective-permute-done | bytes 196640 | tf_op jit(solution)/shard_map/ppermute | solution.py:64
  19.3 0.0 collective-permute-start.4
  19.3 0.0 collective-permute-done.2
  19.4 1.4 %collective-permute-done.4 = bf16[3,16,2,1024]{3,1,2,0:T(8,128)(2,1)S(1)} collective-permute-done((bf16[3,16,2,1024]{3,1,2,0:T(8,128)(2,1)S(1)}, bf16[3,16,2,1024]{3,1,2,0:T(8,128)(2,1)S(1)}, u32[]{:S(2)}, u32[]{:S(2)}) %collective-permute-start.4) | collective-permute-done | bytes 196640 | tf_op jit(solution)/shard_map/ppermute | solution.py:66
  20.8 0.1 fusion.37
  20.9 0.0 copy-done.3
  20.9 2.3 %add_convert_fusion = bf16[1,16,8,1024]{3,1,2,0:T(8,128)(2,1)S(1)} fusion(bf16[1,16,8,1024]{3,1,2,0:T(8,128)(2,1)S(1)} %bitcast.106, bf16[1,16,8,1024]{3,1,2,0:T(8,128)(2,1)S(1)} %bitcast.105, bf16[1,16,8,1024]{3,1,2,0:T(8,128)(2,1)S(1)} %bitcast.104, bf16[3,16,8,1024]{3,1,2,0:T(8,128)(2,1)S(1)} %bitcast.101, f32[1024]{0:T(1024)S(1)} %bitcast.134, ...), kind=kLoop, calls=%fused_computation.69 | loop fusion | flops 10878976 | bytes 1949696 | tf_op jit(solution)/shard_map/convert_element_type | solution.py:127
  23.2 0.3 copy.27
  23.5 0.1 reshape.204
  23.6 0.0 copy-done
  23.6 0.7 %convolution_convert_fusion = bf16[128,768]{1,0:T(8,128)(2,1)S(1)} fusion(bf16[128,1024]{1,0:T(8,128)(2,1)S(1)} %reshape.204, bf16[768,1024]{1,0:T(8,128)(2,1)S(1)} %copy-done), kind=kOutput, calls=%fused_computation.28 | convolution fusion | flops 201424896 | bytes 2031616 | tf_op jit(solution)/shard_map/dot_general | solution.py:99
  24.3 0.2 copy.16
  24.5 3.5 %collective-permute-start.5 = (bf16[128,4,2,64]{0,3,1,2:T(8,128)(2,1)S(1)}, bf16[128,4,2,64]{0,3,1,2:T(8,128)(2,1)S(1)}, u32[]{:S(2)}, u32[]{:S(2)}) collective-permute-start(bf16[128,4,2,64]{0,3,1,2:T(8,128)(2,1)S(1)} %get-tuple-element.30), channel_id=1, source_target_pairs={{0,16},{4,20},{8,24},{12,28},{16,0},{20,4},{24,8},{28,12},{1,17},{... | collective-permute-start | bytes 393224 | tf_op jit(solution)/shard_map/ppermute | solution.py:39
  28.0 1.6 %collective-permute-start.6 = (bf16[128,4,2,64]{0,3,1,2:T(8,128)(2,1)S(1)}, bf16[128,4,2,64]{0,3,1,2:T(8,128)(2,1)S(1)}, u32[]{:S(2)}, u32[]{:S(2)}) collective-permute-start(bf16[128,4,2,64]{0,3,1,2:T(8,128)(2,1)S(1)} %get-tuple-element.30), channel_id=1, source_target_pairs={{0,4},{4,8},{8,12},{12,0},{16,20},{20,24},{24,28},{28,16},{1,5},{5... | collective-permute-start | bytes 393224 | tf_op jit(solution)/shard_map/ppermute | solution.py:43
  29.6 0.6 %collective-permute-start.8 = (bf16[128,4,2,64]{0,3,1,2:T(8,128)(2,1)S(1)}, bf16[128,4,2,64]{0,3,1,2:T(8,128)(2,1)S(1)}, u32[]{:S(2)}, u32[]{:S(2)}) collective-permute-start(bf16[128,4,2,64]{0,3,1,2:T(8,128)(2,1)S(1)} %get-tuple-element.30), channel_id=1, source_target_pairs={{0,8},{4,12},{8,0},{12,4},{16,24},{20,28},{24,16},{28,20},{1,9},{5... | collective-permute-start | bytes 393224 | tf_op jit(solution)/shard_map/ppermute | solution.py:43
  30.2 2.3 %collective-permute-start.10 = (bf16[128,4,2,64]{0,3,1,2:T(8,128)(2,1)S(1)}, bf16[128,4,2,64]{0,3,1,2:T(8,128)(2,1)S(1)}, u32[]{:S(2)}, u32[]{:S(2)}) collective-permute-start(bf16[128,4,2,64]{0,3,1,2:T(8,128)(2,1)S(1)} %get-tuple-element.30), channel_id=1, source_target_pairs={{0,12},{4,0},{8,4},{12,8},{16,28},{20,16},{24,20},{28,24},{1,13},{... | collective-permute-start | bytes 393224 | tf_op jit(solution)/shard_map/ppermute | solution.py:43
  32.5 2.2 %collective-permute-done.5 = bf16[128,4,2,64]{0,3,1,2:T(8,128)(2,1)S(1)} collective-permute-done((bf16[128,4,2,64]{0,3,1,2:T(8,128)(2,1)S(1)}, bf16[128,4,2,64]{0,3,1,2:T(8,128)(2,1)S(1)}, u32[]{:S(2)}, u32[]{:S(2)}) %collective-permute-start.5) | collective-permute-done | bytes 131104 | tf_op jit(solution)/shard_map/ppermute | solution.py:39
  34.7 1.7 %collective-permute-start.7 = (bf16[128,4,2,64]{0,3,1,2:T(8,128)(2,1)S(1)}, bf16[128,4,2,64]{0,3,1,2:T(8,128)(2,1)S(1)}, u32[]{:S(2)}, u32[]{:S(2)}) collective-permute-start(bf16[128,4,2,64]{0,3,1,2:T(8,128)(2,1)S(1)} %collective-permute-done.5), channel_id=1, source_target_pairs={{0,4},{4,8},{8,12},{12,0},{16,20},{20,24},{24,28},{28,16},{1,5},{5... | collective-permute-start | bytes 393224 | tf_op jit(solution)/shard_map/ppermute | solution.py:44
  36.4 0.0 collective-permute-start.9
  36.4 0.6 %collective-permute-done.6 = bf16[128,4,2,64]{0,3,1,2:T(8,128)(2,1)S(1)} collective-permute-done((bf16[128,4,2,64]{0,3,1,2:T(8,128)(2,1)S(1)}, bf16[128,4,2,64]{0,3,1,2:T(8,128)(2,1)S(1)}, u32[]{:S(2)}, u32[]{:S(2)}) %collective-permute-start.6) | collective-permute-done | bytes 131104 | tf_op jit(solution)/shard_map/ppermute | solution.py:43
  37.0 1.4 %collective-permute-start.11 = (bf16[128,4,2,64]{0,3,1,2:T(8,128)(2,1)S(1)}, bf16[128,4,2,64]{0,3,1,2:T(8,128)(2,1)S(1)}, u32[]{:S(2)}, u32[]{:S(2)}) collective-permute-start(bf16[128,4,2,64]{0,3,1,2:T(8,128)(2,1)S(1)} %collective-permute-done.5), channel_id=1, source_target_pairs={{0,12},{4,0},{8,4},{12,8},{16,28},{20,16},{24,20},{28,24},{1,13},{... | collective-permute-start | bytes 393224 | tf_op jit(solution)/shard_map/ppermute | solution.py:44
  38.4 4.0 %collective-permute-done.7 = bf16[128,4,2,64]{0,3,1,2:T(8,128)(2,1)S(1)} collective-permute-done((bf16[128,4,2,64]{0,3,1,2:T(8,128)(2,1)S(1)}, bf16[128,4,2,64]{0,3,1,2:T(8,128)(2,1)S(1)}, u32[]{:S(2)}, u32[]{:S(2)}) %collective-permute-start.7) | collective-permute-done | bytes 131104 | tf_op jit(solution)/shard_map/ppermute | solution.py:44
  42.4 0.0 collective-permute-done.8
  42.5 0.3 collective-permute-done.9
  42.8 0.0 collective-permute-done.10
  42.9 0.7 %collective-permute-done.11 = bf16[128,4,2,64]{0,3,1,2:T(8,128)(2,1)S(1)} collective-permute-done((bf16[128,4,2,64]{0,3,1,2:T(8,128)(2,1)S(1)}, bf16[128,4,2,64]{0,3,1,2:T(8,128)(2,1)S(1)}, u32[]{:S(2)}, u32[]{:S(2)}) %collective-permute-start.11) | collective-permute-done | bytes 131104 | tf_op jit(solution)/shard_map/ppermute | solution.py:44
  43.6 0.0 copy-start.2
  43.6 0.6 %multiply_reduce_fusion = (f32[4,128]{1,0:T(4,128)S(1)}, f32[4,128,1024]{2,1,0:T(8,128)S(1)}) fusion(bf16[1024,4,2,64]{0,3,1,2:T(8,128)(2,1)S(1)} %constant_dynamic-update-slice_fusion.3, bf16[128,4,3,64]{0,3,2,1:T(8,128)(2,1)S(1)} %bitcast.108), kind=kOutput, calls=%fused_computation.25 | convolution fusion | flops 68156928 | bytes 2689024 | tf_op jit(solution)/shard_map/while/body/eval_jaxpr/qhd,khd->hqk/dot_general | solution.py:148
  44.2 0.4 copy-done.2
  44.6 0.5 fusion
  45.1 0.0 copy-start.1
  45.1 1.7 %fusion.4 = bf16[128,4,64]{0,2,1:T(8,128)(2,1)S(1)} fusion(f32[4,128,1024]{2,1,0:T(8,128)S(1)} %get-tuple-element.63, f32[4,128]{1,0:T(4,128)S(1)} %get-tuple-element.61, bf16[1024,4,2,64]{0,3,1,2:T(8,128)(2,1)} %copy-done.2, f32[128,4]{0,1:T(4,128)S(1)} %bitcast_add_fusion.1, f32[128,4]{0,1:T(4,128)S(1)} %get-tuple-element.60), kind=kOutput, calls=%fused_computation.32 | convolution fusion | flops 68780032 | bytes 2693120 | tf_op jit(solution)/shard_map/while/body/eval_jaxpr/hqk,khd->hqd/dot_general | solution.py:155
  46.8 0.1 copy.19
  47.0 0.1 dot_general.22
  47.1 0.0 copy-done.1
  47.1 0.2 fusion.34
  47.4 0.1 collective-permute-start.12
  47.5 1.5 %collective-permute-done.12 = f32[2,32,1024]{2,1,0:T(8,128)S(1)} collective-permute-done((f32[2,32,1024]{2,1,0:T(8,128)S(1)}, f32[2,32,1024]{2,1,0:T(8,128)S(1)}, u32[]{:S(2)}, u32[]{:S(2)}) %collective-permute-start.12) | collective-permute-done | bytes 262176 | tf_op jit(solution)/shard_map/ppermute | solution.py:78
  49.1 1.6 %collective-permute-start.13 = (f32[32,1024]{1,0:T(8,128)S(1)}, f32[32,1024]{1,0:T(8,128)S(1)}, u32[]{:S(2)}, u32[]{:S(2)}) collective-permute-start(f32[32,1024]{1,0:T(8,128)S(1)} %get-tuple-element.20), channel_id=1, source_target_pairs={{0,2},{1,3},{2,0},{3,1},{4,6},{5,7},{6,4},{7,5},{8,10},{9,11},{10,... | collective-permute-start | bytes 393224 | tf_op jit(solution)/shard_map/ppermute | solution.py:82
  50.6 0.1 reshape.206
  50.7 4.0 %collective-permute-done.13 = f32[32,1024]{1,0:T(8,128)S(1)} collective-permute-done((f32[32,1024]{1,0:T(8,128)S(1)}, f32[32,1024]{1,0:T(8,128)S(1)}, u32[]{:S(2)}, u32[]{:S(2)}) %collective-permute-start.13) | collective-permute-done | bytes 131104 | tf_op jit(solution)/shard_map/ppermute | solution.py:82
  54.7 0.1 reshape.207
  54.7 0.7 %add_convert_fusion.1 = bf16[1,16,2,1024]{3,2,1,0:T(2,128)(2,1)} fusion(f32[1,16,2,1024]{3,2,1,0:T(2,128)S(1)} %reshape.206, f32[1,16,2,1024]{3,2,1,0:T(2,128)S(1)} %reshape.207), kind=kLoop, calls=%fused_computation.77 | loop fusion | flops 65536 | bytes 327680 | tf_op jit(solution)/shard_map/convert_element_type | solution.py:178
  (19 shorter events, 0.5 us)
Async XLA Ops:
  0.0 23.6 %copy-start = (bf16[768,1024]{1,0:T(8,128)(2,1)S(1)}, bf16[768,1024]{1,0:T(8,128)(2,1)}, u32[]{:S(2)}) copy-start(bf16[768,1024]{1,0:T(8,128)(2,1)} %param.8) | copy-start | bytes 4718596
  1.0 8.8 %collective-permute-start = (bf16[1,16,2,1024]{3,1,2,0:T(8,128)(2,1)S(1)}, bf16[1,16,2,1024]{3,1,2,0:T(8,128)(2,1)S(1)}, u32[]{:S(2)}, u32[]{:S(2)}) collective-permute-start(bf16[1,16,2,1024]{3,1,2,0:T(8,128)(2,1)S(1)} %copy.9), channel_id=1, source_target_pairs={{0,4},{4,8},{8,12},{12,16},{16,20},{20,24},{24,28},{1,5},{5,9},{9,... | collective-permute-start | bytes 196616 | tf_op jit(solution)/shard_map/ppermute | solution.py:18
  5.9 6.2 %collective-permute-start.1 = (bf16[1,16,2,1024]{3,1,2,0:T(8,128)(2,1)S(1)}, bf16[1,16,2,1024]{3,1,2,0:T(8,128)(2,1)S(1)}, u32[]{:S(2)}, u32[]{:S(2)}) collective-permute-start(bf16[1,16,2,1024]{3,1,2,0:T(8,128)(2,1)S(1)} %copy.9), channel_id=1, source_target_pairs={{4,0},{8,4},{12,8},{16,12},{20,16},{24,20},{28,24},{5,1},{9,5},{13... | collective-permute-start | bytes 196616 | tf_op jit(solution)/shard_map/ppermute | solution.py:19
  10.7 10.2 %copy-start.3 = (f32[1024]{0:T(1024)S(1)}, f32[1024]{0:T(1024)}, u32[]{:S(2)}) copy-start(f32[1024]{0:T(1024)} %param.7) | copy-start | bytes 12292
  12.0 7.3 %collective-permute-start.2 = (bf16[3,16,2,1024]{3,1,2,0:T(8,128)(2,1)S(1)}, bf16[3,16,2,1024]{3,1,2,0:T(8,128)(2,1)S(1)}, u32[]{:S(2)}, u32[]{:S(2)}) collective-permute-start(bf16[3,16,2,1024]{3,1,2,0:T(8,128)(2,1)S(1)} %constant_dynamic-update-slice_fusion), channel_id=1, source_target_pairs={{0,1},{1,0},{2,3},{3,2},{4,5},{5,4},{6,7},{7,6},{8,9},{9,8},{10,11... | collective-permute-start | bytes 589832 | tf_op jit(solution)/shard_map/ppermute | solution.py:60
  12.0 7.3 %collective-permute-start.3 = (bf16[3,16,2,1024]{3,1,2,0:T(8,128)(2,1)S(1)}, bf16[3,16,2,1024]{3,1,2,0:T(8,128)(2,1)S(1)}, u32[]{:S(2)}, u32[]{:S(2)}) collective-permute-start(bf16[3,16,2,1024]{3,1,2,0:T(8,128)(2,1)S(1)} %constant_dynamic-update-slice_fusion), channel_id=1, source_target_pairs={{0,2},{1,3},{2,0},{3,1},{4,6},{5,7},{6,4},{7,5},{8,10},{9,11},{10,... | collective-permute-start | bytes 589832 | tf_op jit(solution)/shard_map/ppermute | solution.py:64
  19.3 1.4 %collective-permute-start.4 = (bf16[3,16,2,1024]{3,1,2,0:T(8,128)(2,1)S(1)}, bf16[3,16,2,1024]{3,1,2,0:T(8,128)(2,1)S(1)}, u32[]{:S(2)}, u32[]{:S(2)}) collective-permute-start(bf16[3,16,2,1024]{3,1,2,0:T(8,128)(2,1)S(1)} %collective-permute-done.3), channel_id=1, source_target_pairs={{0,1},{1,0},{2,3},{3,2},{4,5},{5,4},{6,7},{7,6},{8,9},{9,8},{10,11... | collective-permute-start | bytes 589832 | tf_op jit(solution)/shard_map/ppermute | solution.py:66
  24.5 10.2 %collective-permute-start.5 = (bf16[128,4,2,64]{0,3,1,2:T(8,128)(2,1)S(1)}, bf16[128,4,2,64]{0,3,1,2:T(8,128)(2,1)S(1)}, u32[]{:S(2)}, u32[]{:S(2)}) collective-permute-start(bf16[128,4,2,64]{0,3,1,2:T(8,128)(2,1)S(1)} %get-tuple-element.30), channel_id=1, source_target_pairs={{0,16},{4,20},{8,24},{12,28},{16,0},{20,4},{24,8},{28,12},{1,17},{... | collective-permute-start | bytes 393224 | tf_op jit(solution)/shard_map/ppermute | solution.py:39
  28.0 9.0 %collective-permute-start.6 = (bf16[128,4,2,64]{0,3,1,2:T(8,128)(2,1)S(1)}, bf16[128,4,2,64]{0,3,1,2:T(8,128)(2,1)S(1)}, u32[]{:S(2)}, u32[]{:S(2)}) collective-permute-start(bf16[128,4,2,64]{0,3,1,2:T(8,128)(2,1)S(1)} %get-tuple-element.30), channel_id=1, source_target_pairs={{0,4},{4,8},{8,12},{12,0},{16,20},{20,24},{24,28},{28,16},{1,5},{5... | collective-permute-start | bytes 393224 | tf_op jit(solution)/shard_map/ppermute | solution.py:43
  29.6 12.8 %collective-permute-start.8 = (bf16[128,4,2,64]{0,3,1,2:T(8,128)(2,1)S(1)}, bf16[128,4,2,64]{0,3,1,2:T(8,128)(2,1)S(1)}, u32[]{:S(2)}, u32[]{:S(2)}) collective-permute-start(bf16[128,4,2,64]{0,3,1,2:T(8,128)(2,1)S(1)} %get-tuple-element.30), channel_id=1, source_target_pairs={{0,8},{4,12},{8,0},{12,4},{16,24},{20,28},{24,16},{28,20},{1,9},{5... | collective-permute-start | bytes 393224 | tf_op jit(solution)/shard_map/ppermute | solution.py:43
  30.2 12.7 %collective-permute-start.10 = (bf16[128,4,2,64]{0,3,1,2:T(8,128)(2,1)S(1)}, bf16[128,4,2,64]{0,3,1,2:T(8,128)(2,1)S(1)}, u32[]{:S(2)}, u32[]{:S(2)}) collective-permute-start(bf16[128,4,2,64]{0,3,1,2:T(8,128)(2,1)S(1)} %get-tuple-element.30), channel_id=1, source_target_pairs={{0,12},{4,0},{8,4},{12,8},{16,28},{20,16},{24,20},{28,24},{1,13},{... | collective-permute-start | bytes 393224 | tf_op jit(solution)/shard_map/ppermute | solution.py:43
  34.7 7.7 %collective-permute-start.7 = (bf16[128,4,2,64]{0,3,1,2:T(8,128)(2,1)S(1)}, bf16[128,4,2,64]{0,3,1,2:T(8,128)(2,1)S(1)}, u32[]{:S(2)}, u32[]{:S(2)}) collective-permute-start(bf16[128,4,2,64]{0,3,1,2:T(8,128)(2,1)S(1)} %collective-permute-done.5), channel_id=1, source_target_pairs={{0,4},{4,8},{8,12},{12,0},{16,20},{20,24},{24,28},{28,16},{1,5},{5... | collective-permute-start | bytes 393224 | tf_op jit(solution)/shard_map/ppermute | solution.py:44
  36.4 6.4 %collective-permute-start.9 = (bf16[128,4,2,64]{0,3,1,2:T(8,128)(2,1)S(1)}, bf16[128,4,2,64]{0,3,1,2:T(8,128)(2,1)S(1)}, u32[]{:S(2)}, u32[]{:S(2)}) collective-permute-start(bf16[128,4,2,64]{0,3,1,2:T(8,128)(2,1)S(1)} %collective-permute-done.5), channel_id=1, source_target_pairs={{0,8},{4,12},{8,0},{12,4},{16,24},{20,28},{24,16},{28,20},{1,9},{5... | collective-permute-start | bytes 393224 | tf_op jit(solution)/shard_map/ppermute | solution.py:44
  37.0 6.6 %collective-permute-start.11 = (bf16[128,4,2,64]{0,3,1,2:T(8,128)(2,1)S(1)}, bf16[128,4,2,64]{0,3,1,2:T(8,128)(2,1)S(1)}, u32[]{:S(2)}, u32[]{:S(2)}) collective-permute-start(bf16[128,4,2,64]{0,3,1,2:T(8,128)(2,1)S(1)} %collective-permute-done.5), channel_id=1, source_target_pairs={{0,12},{4,0},{8,4},{12,8},{16,28},{20,16},{24,20},{28,24},{1,13},{... | collective-permute-start | bytes 393224 | tf_op jit(solution)/shard_map/ppermute | solution.py:44
  43.6 1.0 %copy-start.2 = (bf16[1024,4,2,64]{0,3,1,2:T(8,128)(2,1)}, bf16[1024,4,2,64]{0,3,1,2:T(8,128)(2,1)S(1)}, u32[]{:S(2)}) copy-start(bf16[1024,4,2,64]{0,3,1,2:T(8,128)(2,1)S(1)} %constant_dynamic-update-slice_fusion.3) | copy-start | bytes 3145732
  45.1 2.0 %copy-start.1 = (bf16[256,1024]{1,0:T(8,128)(2,1)S(1)}, bf16[256,1024]{1,0:T(8,128)(2,1)}, u32[]{:S(2)}) copy-start(bf16[256,1024]{1,0:T(8,128)(2,1)} %param.9) | copy-start | bytes 1572868
  47.4 1.6 %collective-permute-start.12 = (f32[2,32,1024]{2,1,0:T(8,128)S(1)}, f32[2,32,1024]{2,1,0:T(8,128)S(1)}, u32[]{:S(2)}, u32[]{:S(2)}) collective-permute-start(f32[2,32,1024]{2,1,0:T(8,128)S(1)} %dynamic-slice_bitcast_fusion), channel_id=1, source_target_pairs={{0,1},{1,0},{2,3},{3,2},{4,5},{5,4},{6,7},{7,6},{8,9},{9,8},{10,11... | collective-permute-start | bytes 786440 | tf_op jit(solution)/shard_map/ppermute | solution.py:78
  49.1 5.6 %collective-permute-start.13 = (f32[32,1024]{1,0:T(8,128)S(1)}, f32[32,1024]{1,0:T(8,128)S(1)}, u32[]{:S(2)}, u32[]{:S(2)}) collective-permute-start(f32[32,1024]{1,0:T(8,128)S(1)} %get-tuple-element.20), channel_id=1, source_target_pairs={{0,2},{1,3},{2,0},{3,1},{4,6},{5,7},{6,4},{7,5},{8,10},{9,11},{10,... | collective-permute-start | bytes 393224 | tf_op jit(solution)/shard_map/ppermute | solution.py:82

commit v6 on v5

--- a/solution.py
+++ b/solution.py
@@ -79,7 +79,8 @@
     total = lax.dynamic_index_in_dim(chip_sum, chip, 0, keepdims=False).reshape(shape)
     for shift in range(1, chips):
         outgoing = lax.dynamic_index_in_dim(chip_sum, (chip + shift) % chips, 0, keepdims=False)
-        total = total + lax.ppermute(outgoing, axis, chip_shift(size, shift)).reshape(shape)
+        arrived = lax.ppermute(outgoing.astype(jnp.bfloat16), axis, chip_shift(size, shift))
+        total = total + arrived.astype(jnp.float32).reshape(shape)
     return total
 
 

time: 55.9 us -> 54.6 us (0.977)
  waiting for transfers between devices: 21.5 us -> 20.2 us
    ppermute x1, waiting for transfers between devices: 3.96 us -> 2.67 us  [scattered_sum_by_chip(): lax.ppermute(outgoing.astype(jnp.bfloat16), axis, chip_shift(size, shift))]
where the time goes in v6:
time: 54.6 us; the launch traced here: 54.2 us
  starting transfers between devices  20.4 us (37%)
  waiting for transfers between devices  20.2 us (37%)
  local copies, waits for them, and re-layouts  6.39 us (12%)
  other arithmetic  3.6 us (7%)
  matrix products  3.15 us (6%)
    ppermute x1, waiting for transfers between devices, gathered_by_chip(): far = lax.ppermute(piece, axis, chip_shift(size, shift))  5.63 us
    ppermute x3, waiting for transfers between devices, relayed(): parts.append(lax.ppermute(crossed, axis, pairs))  4.92 us
    ppermute x1, starting transfers between devices, padded_2(): before = lax.ppermute(last, axis, up)  4.87 us
    ppermute x3, starting transfers between devices, relayed(): parts.append(lax.ppermute(piece, axis, pairs))  4.5 us
    ppermute x1, starting transfers between devices, relayed(): crossed = lax.ppermute(piece, axis, mirror)  3.46 us
    ppermute x3, starting transfers between devices, relayed(): parts.append(lax.ppermute(crossed, axis, pairs))  3.09 us
    ppermute x1, waiting for transfers between devices, scattered_sum_by_chip(): lax.ppermute(outgoing.astype(jnp.bfloat16), axis, chip_shift(size, shift))  2.67 us
    slice x2, local copies, waits for them, and re-layouts, on_device(): conv_weight[9 * step_z + 3 * step_x + step_y]  2.58 us
  transfers between devices with their start and end apart: 14, of which 10 were waited for; matrix products, arithmetic and copies ran while one was open for 7% of the time, Pallas kernels for 0%

profile of v6, /device:TPU:0, one launch (start us, length us, event | category | flops | bytes accessed | tf_op | source)
XLA Modules:
  0.0 54.2 jit_solution(5586946109790079143)
XLA Ops:
  0.0 0.0 copy-start
  0.0 1.0 %copy.9 = bf16[1,16,2,1024]{3,1,2,0:T(8,128)(2,1)S(1)} copy(bf16[1,16,2,1024]{3,2,1,0:T(2,128)(2,1)} %param.5) | data formatting | bytes 131072 | tf_op args[0]
  1.0 4.9 %collective-permute-start = (bf16[1,16,2,1024]{3,1,2,0:T(8,128)(2,1)S(1)}, bf16[1,16,2,1024]{3,1,2,0:T(8,128)(2,1)S(1)}, u32[]{:S(2)}, u32[]{:S(2)}) collective-permute-start(bf16[1,16,2,1024]{3,1,2,0:T(8,128)(2,1)S(1)} %copy.9), channel_id=1, source_target_pairs={{0,4},{4,8},{8,12},{12,16},{16,20},{20,24},{24,28},{1,5},{5,9},{9,... | collective-permute-start | bytes 196616 | tf_op jit(solution)/shard_map/ppermute | solution.py:18
  5.9 1.3 %collective-permute-start.1 = (bf16[1,16,2,1024]{3,1,2,0:T(8,128)(2,1)S(1)}, bf16[1,16,2,1024]{3,1,2,0:T(8,128)(2,1)S(1)}, u32[]{:S(2)}, u32[]{:S(2)}) collective-permute-start(bf16[1,16,2,1024]{3,1,2,0:T(8,128)(2,1)S(1)} %copy.9), channel_id=1, source_target_pairs={{4,0},{8,4},{12,8},{16,12},{20,16},{24,20},{28,24},{5,1},{9,5},{13... | collective-permute-start | bytes 196616 | tf_op jit(solution)/shard_map/ppermute | solution.py:19
  7.2 1.4 %fusion.40 = (f32[1,1024]{1,0:T(1,128)S(1)}, f32[1,1024]{1,0:T(1,128)S(1)}, f32[1,1024]{1,0:T(1,128)S(1)}, f32[1,1024]{1,0:T(1,128)S(1)}, f32[1,1024]{1,0:T(1,12...) fusion(f32[27,1024]{1,0:T(8,128)} %param.6), kind=kLoop, calls=%fused_computation.99 | loop fusion | bytes 155648 | tf_op jit(solution)/shard_map/slice | solution.py:121
  8.6 1.2 %fusion.41 = (f32[1,1024]{1,0:T(1,128)S(1)}, f32[1,1024]{1,0:T(1,128)S(1)}, f32[1,1024]{1,0:T(1,128)S(1)}, f32[1,1024]{1,0:T(1,128)S(1)}, f32[1,1024]{1,0:T(1,12...) fusion(f32[27,1024]{1,0:T(8,128)} %param.6), kind=kLoop, calls=%fused_computation.100 | loop fusion | bytes 65536 | tf_op jit(solution)/shard_map/slice | solution.py:121
  9.8 0.0 collective-permute-done
  9.8 0.9 %constant_dynamic-update-slice_fusion.1 = bf16[3,16,2,1024]{3,1,2,0:T(8,128)(2,1)S(1)} fusion(bf16[3,16,2,1024]{3,1,2,0:T(8,128)(2,1)S(1)} %constant_dynamic-update-slice_fusion.2, bf16[1,16,2,1024]{3,2,1,0:T(2,128)(2,1)} %param.5), kind=kLoop, calls=%fused_computation.82 | loop fusion | bytes 131072
  10.7 0.0 copy-start.3
  10.7 1.3 %collective-permute-done.1 = bf16[1,16,2,1024]{3,1,2,0:T(8,128)(2,1)S(1)} collective-permute-done((bf16[1,16,2,1024]{3,1,2,0:T(8,128)(2,1)S(1)}, bf16[1,16,2,1024]{3,1,2,0:T(8,128)(2,1)S(1)}, u32[]{:S(2)}, u32[]{:S(2)}) %collective-permute-start.1) | collective-permute-done | bytes 65568 | tf_op jit(solution)/shard_map/ppermute | solution.py:19
  12.0 0.0 collective-permute-start.2
  12.0 1.6 %collective-permute-start.3 = (bf16[3,16,2,1024]{3,1,2,0:T(8,128)(2,1)S(1)}, bf16[3,16,2,1024]{3,1,2,0:T(8,128)(2,1)S(1)}, u32[]{:S(2)}, u32[]{:S(2)}) collective-permute-start(bf16[3,16,2,1024]{3,1,2,0:T(8,128)(2,1)S(1)} %constant_dynamic-update-slice_fusion), channel_id=1, source_target_pairs={{0,2},{1,3},{2,0},{3,1},{4,6},{5,7},{6,4},{7,5},{8,10},{9,11},{10,... | collective-permute-start | bytes 589832 | tf_op jit(solution)/shard_map/ppermute | solution.py:64
  13.6 0.1 broadcast_in_dim.31
  13.7 5.6 %collective-permute-done.3 = bf16[3,16,2,1024]{3,1,2,0:T(8,128)(2,1)S(1)} collective-permute-done((bf16[3,16,2,1024]{3,1,2,0:T(8,128)(2,1)S(1)}, bf16[3,16,2,1024]{3,1,2,0:T(8,128)(2,1)S(1)}, u32[]{:S(2)}, u32[]{:S(2)}) %collective-permute-start.3) | collective-permute-done | bytes 196640 | tf_op jit(solution)/shard_map/ppermute | solution.py:64
  19.3 0.0 collective-permute-start.4
  19.3 0.0 collective-permute-done.2
  19.4 1.4 %collective-permute-done.4 = bf16[3,16,2,1024]{3,1,2,0:T(8,128)(2,1)S(1)} collective-permute-done((bf16[3,16,2,1024]{3,1,2,0:T(8,128)(2,1)S(1)}, bf16[3,16,2,1024]{3,1,2,0:T(8,128)(2,1)S(1)}, u32[]{:S(2)}, u32[]{:S(2)}) %collective-permute-start.4) | collective-permute-done | bytes 196640 | tf_op jit(solution)/shard_map/ppermute | solution.py:66
  20.8 0.1 fusion.38
  20.9 0.0 copy-done.3
  20.9 2.3 %add_convert_fusion = bf16[1,16,8,1024]{3,1,2,0:T(8,128)(2,1)S(1)} fusion(bf16[1,16,8,1024]{3,1,2,0:T(8,128)(2,1)S(1)} %bitcast.106, bf16[1,16,8,1024]{3,1,2,0:T(8,128)(2,1)S(1)} %bitcast.105, bf16[1,16,8,1024]{3,1,2,0:T(8,128)(2,1)S(1)} %bitcast.104, bf16[3,16,8,1024]{3,1,2,0:T(8,128)(2,1)S(1)} %bitcast.101, f32[1024]{0:T(1024)S(1)} %bitcast.134, ...), kind=kLoop, calls=%fused_computation.69 | loop fusion | flops 10878976 | bytes 1949696 | tf_op jit(solution)/shard_map/convert_element_type | solution.py:128
  23.2 0.3 copy.27
  23.5 0.1 reshape.208
  23.6 0.0 copy-done
  23.6 0.7 %convolution_convert_fusion = bf16[128,768]{1,0:T(8,128)(2,1)S(1)} fusion(bf16[128,1024]{1,0:T(8,128)(2,1)S(1)} %reshape.208, bf16[768,1024]{1,0:T(8,128)(2,1)S(1)} %copy-done), kind=kOutput, calls=%fused_computation.28 | convolution fusion | flops 201424896 | bytes 2031616 | tf_op jit(solution)/shard_map/dot_general | solution.py:100
  24.3 0.2 copy.16
  24.5 3.5 %collective-permute-start.5 = (bf16[128,4,2,64]{0,3,1,2:T(8,128)(2,1)S(1)}, bf16[128,4,2,64]{0,3,1,2:T(8,128)(2,1)S(1)}, u32[]{:S(2)}, u32[]{:S(2)}) collective-permute-start(bf16[128,4,2,64]{0,3,1,2:T(8,128)(2,1)S(1)} %get-tuple-element.20), channel_id=1, source_target_pairs={{0,16},{4,20},{8,24},{12,28},{16,0},{20,4},{24,8},{28,12},{1,17},{... | collective-permute-start | bytes 393224 | tf_op jit(solution)/shard_map/ppermute | solution.py:39
  28.0 1.6 %collective-permute-start.6 = (bf16[128,4,2,64]{0,3,1,2:T(8,128)(2,1)S(1)}, bf16[128,4,2,64]{0,3,1,2:T(8,128)(2,1)S(1)}, u32[]{:S(2)}, u32[]{:S(2)}) collective-permute-start(bf16[128,4,2,64]{0,3,1,2:T(8,128)(2,1)S(1)} %get-tuple-element.20), channel_id=1, source_target_pairs={{0,4},{4,8},{8,12},{12,0},{16,20},{20,24},{24,28},{28,16},{1,5},{5... | collective-permute-start | bytes 393224 | tf_op jit(solution)/shard_map/ppermute | solution.py:43
  29.6 0.6 %collective-permute-start.8 = (bf16[128,4,2,64]{0,3,1,2:T(8,128)(2,1)S(1)}, bf16[128,4,2,64]{0,3,1,2:T(8,128)(2,1)S(1)}, u32[]{:S(2)}, u32[]{:S(2)}) collective-permute-start(bf16[128,4,2,64]{0,3,1,2:T(8,128)(2,1)S(1)} %get-tuple-element.20), channel_id=1, source_target_pairs={{0,8},{4,12},{8,0},{12,4},{16,24},{20,28},{24,16},{28,20},{1,9},{5... | collective-permute-start | bytes 393224 | tf_op jit(solution)/shard_map/ppermute | solution.py:43
  30.2 2.3 %collective-permute-start.10 = (bf16[128,4,2,64]{0,3,1,2:T(8,128)(2,1)S(1)}, bf16[128,4,2,64]{0,3,1,2:T(8,128)(2,1)S(1)}, u32[]{:S(2)}, u32[]{:S(2)}) collective-permute-start(bf16[128,4,2,64]{0,3,1,2:T(8,128)(2,1)S(1)} %get-tuple-element.20), channel_id=1, source_target_pairs={{0,12},{4,0},{8,4},{12,8},{16,28},{20,16},{24,20},{28,24},{1,13},{... | collective-permute-start | bytes 393224 | tf_op jit(solution)/shard_map/ppermute | solution.py:43
  32.5 2.2 %collective-permute-done.5 = bf16[128,4,2,64]{0,3,1,2:T(8,128)(2,1)S(1)} collective-permute-done((bf16[128,4,2,64]{0,3,1,2:T(8,128)(2,1)S(1)}, bf16[128,4,2,64]{0,3,1,2:T(8,128)(2,1)S(1)}, u32[]{:S(2)}, u32[]{:S(2)}) %collective-permute-start.5) | collective-permute-done | bytes 131104 | tf_op jit(solution)/shard_map/ppermute | solution.py:39
  34.7 1.7 %collective-permute-start.7 = (bf16[128,4,2,64]{0,3,1,2:T(8,128)(2,1)S(1)}, bf16[128,4,2,64]{0,3,1,2:T(8,128)(2,1)S(1)}, u32[]{:S(2)}, u32[]{:S(2)}) collective-permute-start(bf16[128,4,2,64]{0,3,1,2:T(8,128)(2,1)S(1)} %collective-permute-done.5), channel_id=1, source_target_pairs={{0,4},{4,8},{8,12},{12,0},{16,20},{20,24},{24,28},{28,16},{1,5},{5... | collective-permute-start | bytes 393224 | tf_op jit(solution)/shard_map/ppermute | solution.py:44
  36.4 0.0 collective-permute-start.9
  36.4 0.6 %collective-permute-done.6 = bf16[128,4,2,64]{0,3,1,2:T(8,128)(2,1)S(1)} collective-permute-done((bf16[128,4,2,64]{0,3,1,2:T(8,128)(2,1)S(1)}, bf16[128,4,2,64]{0,3,1,2:T(8,128)(2,1)S(1)}, u32[]{:S(2)}, u32[]{:S(2)}) %collective-permute-start.6) | collective-permute-done | bytes 131104 | tf_op jit(solution)/shard_map/ppermute | solution.py:43
  37.0 1.4 %collective-permute-start.11 = (bf16[128,4,2,64]{0,3,1,2:T(8,128)(2,1)S(1)}, bf16[128,4,2,64]{0,3,1,2:T(8,128)(2,1)S(1)}, u32[]{:S(2)}, u32[]{:S(2)}) collective-permute-start(bf16[128,4,2,64]{0,3,1,2:T(8,128)(2,1)S(1)} %collective-permute-done.5), channel_id=1, source_target_pairs={{0,12},{4,0},{8,4},{12,8},{16,28},{20,16},{24,20},{28,24},{1,13},{... | collective-permute-start | bytes 393224 | tf_op jit(solution)/shard_map/ppermute | solution.py:44
  38.4 4.0 %collective-permute-done.7 = bf16[128,4,2,64]{0,3,1,2:T(8,128)(2,1)S(1)} collective-permute-done((bf16[128,4,2,64]{0,3,1,2:T(8,128)(2,1)S(1)}, bf16[128,4,2,64]{0,3,1,2:T(8,128)(2,1)S(1)}, u32[]{:S(2)}, u32[]{:S(2)}) %collective-permute-start.7) | collective-permute-done | bytes 131104 | tf_op jit(solution)/shard_map/ppermute | solution.py:44
  42.4 0.0 collective-permute-done.8
  42.5 0.3 collective-permute-done.9
  42.8 0.0 collective-permute-done.10
  42.9 0.7 %collective-permute-done.11 = bf16[128,4,2,64]{0,3,1,2:T(8,128)(2,1)S(1)} collective-permute-done((bf16[128,4,2,64]{0,3,1,2:T(8,128)(2,1)S(1)}, bf16[128,4,2,64]{0,3,1,2:T(8,128)(2,1)S(1)}, u32[]{:S(2)}, u32[]{:S(2)}) %collective-permute-start.11) | collective-permute-done | bytes 131104 | tf_op jit(solution)/shard_map/ppermute | solution.py:44
  43.6 0.0 copy-start.2
  43.6 0.6 %multiply_reduce_fusion = (f32[4,128]{1,0:T(4,128)S(1)}, f32[4,128,1024]{2,1,0:T(8,128)S(1)}) fusion(bf16[1024,4,2,64]{0,3,1,2:T(8,128)(2,1)S(1)} %constant_dynamic-update-slice_fusion.3, bf16[128,4,3,64]{0,3,2,1:T(8,128)(2,1)S(1)} %bitcast.108), kind=kOutput, calls=%fused_computation.25 | convolution fusion | flops 68156928 | bytes 2689024 | tf_op jit(solution)/shard_map/while/body/eval_jaxpr/qhd,khd->hqk/dot_general | solution.py:149
  44.2 0.4 copy-done.2
  44.6 0.5 fusion
  45.1 0.0 copy-start.1
  45.1 1.7 %fusion.4 = bf16[128,4,64]{0,2,1:T(8,128)(2,1)S(1)} fusion(f32[4,128,1024]{2,1,0:T(8,128)S(1)} %get-tuple-element.61, f32[4,128]{1,0:T(4,128)S(1)} %get-tuple-element.59, bf16[1024,4,2,64]{0,3,1,2:T(8,128)(2,1)} %copy-done.2, f32[128,4]{0,1:T(4,128)S(1)} %bitcast_add_fusion.1, f32[128,4]{0,1:T(4,128)S(1)} %get-tuple-element.58), kind=kOutput, calls=%fused_computation.32 | convolution fusion | flops 68780032 | bytes 2693120 | tf_op jit(solution)/shard_map/while/body/eval_jaxpr/hqk,khd->hqd/dot_general | solution.py:156
  46.8 0.1 copy.19
  47.0 0.1 dot_general.22
  47.1 0.0 copy-done.1
  47.1 0.2 fusion.34
  47.4 0.1 collective-permute-start.12
  47.5 1.5 %collective-permute-done.12 = f32[2,32,1024]{2,1,0:T(8,128)S(1)} collective-permute-done((f32[2,32,1024]{2,1,0:T(8,128)S(1)}, f32[2,32,1024]{2,1,0:T(8,128)S(1)}, u32[]{:S(2)}, u32[]{:S(2)}) %collective-permute-start.12) | collective-permute-done | bytes 262176 | tf_op jit(solution)/shard_map/ppermute | solution.py:78
  49.1 1.6 %collective-permute-start.13 = (bf16[32,1024]{1,0:T(8,128)(2,1)S(1)}, bf16[32,1024]{1,0:T(8,128)(2,1)S(1)}, u32[]{:S(2)}, u32[]{:S(2)}) collective-permute-start(bf16[32,1024]{1,0:T(8,128)(2,1)S(1)} %fusion.36), channel_id=1, source_target_pairs={{0,2},{1,3},{2,0},{3,1},{4,6},{5,7},{6,4},{7,5},{8,10},{9,11},{10,... | collective-permute-start | bytes 196616 | tf_op jit(solution)/shard_map/ppermute | solution.py:82
  50.6 0.1 reshape.210
  50.7 2.7 %collective-permute-done.13 = bf16[32,1024]{1,0:T(8,128)(2,1)S(1)} collective-permute-done((bf16[32,1024]{1,0:T(8,128)(2,1)S(1)}, bf16[32,1024]{1,0:T(8,128)(2,1)S(1)}, u32[]{:S(2)}, u32[]{:S(2)}) %collective-permute-start.13) | collective-permute-done | bytes 65568 | tf_op jit(solution)/shard_map/ppermute | solution.py:82
  53.4 0.1 reshape.217
  53.5 0.7 %add_convert_fusion.1 = bf16[1,16,2,1024]{3,2,1,0:T(2,128)(2,1)} fusion(f32[1,16,2,1024]{3,2,1,0:T(2,128)S(1)} %reshape.210, f32[1,16,2,1024]{3,2,1,0:T(2,128)S(1)} %reshape.217), kind=kLoop, calls=%fused_computation.77 | loop fusion | flops 65536 | bytes 327680 | tf_op jit(solution)/shard_map/convert_element_type | solution.py:179
  (20 shorter events, 0.5 us)
Async XLA Ops:
  0.0 23.6 %copy-start = (bf16[768,1024]{1,0:T(8,128)(2,1)S(1)}, bf16[768,1024]{1,0:T(8,128)(2,1)}, u32[]{:S(2)}) copy-start(bf16[768,1024]{1,0:T(8,128)(2,1)} %param.8) | copy-start | bytes 4718596
  1.0 8.8 %collective-permute-start = (bf16[1,16,2,1024]{3,1,2,0:T(8,128)(2,1)S(1)}, bf16[1,16,2,1024]{3,1,2,0:T(8,128)(2,1)S(1)}, u32[]{:S(2)}, u32[]{:S(2)}) collective-permute-start(bf16[1,16,2,1024]{3,1,2,0:T(8,128)(2,1)S(1)} %copy.9), channel_id=1, source_target_pairs={{0,4},{4,8},{8,12},{12,16},{16,20},{20,24},{24,28},{1,5},{5,9},{9,... | collective-permute-start | bytes 196616 | tf_op jit(solution)/shard_map/ppermute | solution.py:18
  5.9 6.2 %collective-permute-start.1 = (bf16[1,16,2,1024]{3,1,2,0:T(8,128)(2,1)S(1)}, bf16[1,16,2,1024]{3,1,2,0:T(8,128)(2,1)S(1)}, u32[]{:S(2)}, u32[]{:S(2)}) collective-permute-start(bf16[1,16,2,1024]{3,1,2,0:T(8,128)(2,1)S(1)} %copy.9), channel_id=1, source_target_pairs={{4,0},{8,4},{12,8},{16,12},{20,16},{24,20},{28,24},{5,1},{9,5},{13... | collective-permute-start | bytes 196616 | tf_op jit(solution)/shard_map/ppermute | solution.py:19
  10.7 10.2 %copy-start.3 = (f32[1024]{0:T(1024)S(1)}, f32[1024]{0:T(1024)}, u32[]{:S(2)}) copy-start(f32[1024]{0:T(1024)} %param.7) | copy-start | bytes 12292
  12.0 7.3 %collective-permute-start.2 = (bf16[3,16,2,1024]{3,1,2,0:T(8,128)(2,1)S(1)}, bf16[3,16,2,1024]{3,1,2,0:T(8,128)(2,1)S(1)}, u32[]{:S(2)}, u32[]{:S(2)}) collective-permute-start(bf16[3,16,2,1024]{3,1,2,0:T(8,128)(2,1)S(1)} %constant_dynamic-update-slice_fusion), channel_id=1, source_target_pairs={{0,1},{1,0},{2,3},{3,2},{4,5},{5,4},{6,7},{7,6},{8,9},{9,8},{10,11... | collective-permute-start | bytes 589832 | tf_op jit(solution)/shard_map/ppermute | solution.py:60
  12.0 7.3 %collective-permute-start.3 = (bf16[3,16,2,1024]{3,1,2,0:T(8,128)(2,1)S(1)}, bf16[3,16,2,1024]{3,1,2,0:T(8,128)(2,1)S(1)}, u32[]{:S(2)}, u32[]{:S(2)}) collective-permute-start(bf16[3,16,2,1024]{3,1,2,0:T(8,128)(2,1)S(1)} %constant_dynamic-update-slice_fusion), channel_id=1, source_target_pairs={{0,2},{1,3},{2,0},{3,1},{4,6},{5,7},{6,4},{7,5},{8,10},{9,11},{10,... | collective-permute-start | bytes 589832 | tf_op jit(solution)/shard_map/ppermute | solution.py:64
  19.3 1.4 %collective-permute-start.4 = (bf16[3,16,2,1024]{3,1,2,0:T(8,128)(2,1)S(1)}, bf16[3,16,2,1024]{3,1,2,0:T(8,128)(2,1)S(1)}, u32[]{:S(2)}, u32[]{:S(2)}) collective-permute-start(bf16[3,16,2,1024]{3,1,2,0:T(8,128)(2,1)S(1)} %collective-permute-done.3), channel_id=1, source_target_pairs={{0,1},{1,0},{2,3},{3,2},{4,5},{5,4},{6,7},{7,6},{8,9},{9,8},{10,11... | collective-permute-start | bytes 589832 | tf_op jit(solution)/shard_map/ppermute | solution.py:66
  24.5 10.2 %collective-permute-start.5 = (bf16[128,4,2,64]{0,3,1,2:T(8,128)(2,1)S(1)}, bf16[128,4,2,64]{0,3,1,2:T(8,128)(2,1)S(1)}, u32[]{:S(2)}, u32[]{:S(2)}) collective-permute-start(bf16[128,4,2,64]{0,3,1,2:T(8,128)(2,1)S(1)} %get-tuple-element.20), channel_id=1, source_target_pairs={{0,16},{4,20},{8,24},{12,28},{16,0},{20,4},{24,8},{28,12},{1,17},{... | collective-permute-start | bytes 393224 | tf_op jit(solution)/shard_map/ppermute | solution.py:39
  28.0 9.0 %collective-permute-start.6 = (bf16[128,4,2,64]{0,3,1,2:T(8,128)(2,1)S(1)}, bf16[128,4,2,64]{0,3,1,2:T(8,128)(2,1)S(1)}, u32[]{:S(2)}, u32[]{:S(2)}) collective-permute-start(bf16[128,4,2,64]{0,3,1,2:T(8,128)(2,1)S(1)} %get-tuple-element.20), channel_id=1, source_target_pairs={{0,4},{4,8},{8,12},{12,0},{16,20},{20,24},{24,28},{28,16},{1,5},{5... | collective-permute-start | bytes 393224 | tf_op jit(solution)/shard_map/ppermute | solution.py:43
  29.6 12.8 %collective-permute-start.8 = (bf16[128,4,2,64]{0,3,1,2:T(8,128)(2,1)S(1)}, bf16[128,4,2,64]{0,3,1,2:T(8,128)(2,1)S(1)}, u32[]{:S(2)}, u32[]{:S(2)}) collective-permute-start(bf16[128,4,2,64]{0,3,1,2:T(8,128)(2,1)S(1)} %get-tuple-element.20), channel_id=1, source_target_pairs={{0,8},{4,12},{8,0},{12,4},{16,24},{20,28},{24,16},{28,20},{1,9},{5... | collective-permute-start | bytes 393224 | tf_op jit(solution)/shard_map/ppermute | solution.py:43
  30.2 12.7 %collective-permute-start.10 = (bf16[128,4,2,64]{0,3,1,2:T(8,128)(2,1)S(1)}, bf16[128,4,2,64]{0,3,1,2:T(8,128)(2,1)S(1)}, u32[]{:S(2)}, u32[]{:S(2)}) collective-permute-start(bf16[128,4,2,64]{0,3,1,2:T(8,128)(2,1)S(1)} %get-tuple-element.20), channel_id=1, source_target_pairs={{0,12},{4,0},{8,4},{12,8},{16,28},{20,16},{24,20},{28,24},{1,13},{... | collective-permute-start | bytes 393224 | tf_op jit(solution)/shard_map/ppermute | solution.py:43
  34.7 7.7 %collective-permute-start.7 = (bf16[128,4,2,64]{0,3,1,2:T(8,128)(2,1)S(1)}, bf16[128,4,2,64]{0,3,1,2:T(8,128)(2,1)S(1)}, u32[]{:S(2)}, u32[]{:S(2)}) collective-permute-start(bf16[128,4,2,64]{0,3,1,2:T(8,128)(2,1)S(1)} %collective-permute-done.5), channel_id=1, source_target_pairs={{0,4},{4,8},{8,12},{12,0},{16,20},{20,24},{24,28},{28,16},{1,5},{5... | collective-permute-start | bytes 393224 | tf_op jit(solution)/shard_map/ppermute | solution.py:44
  36.4 6.4 %collective-permute-start.9 = (bf16[128,4,2,64]{0,3,1,2:T(8,128)(2,1)S(1)}, bf16[128,4,2,64]{0,3,1,2:T(8,128)(2,1)S(1)}, u32[]{:S(2)}, u32[]{:S(2)}) collective-permute-start(bf16[128,4,2,64]{0,3,1,2:T(8,128)(2,1)S(1)} %collective-permute-done.5), channel_id=1, source_target_pairs={{0,8},{4,12},{8,0},{12,4},{16,24},{20,28},{24,16},{28,20},{1,9},{5... | collective-permute-start | bytes 393224 | tf_op jit(solution)/shard_map/ppermute | solution.py:44
  37.0 6.6 %collective-permute-start.11 = (bf16[128,4,2,64]{0,3,1,2:T(8,128)(2,1)S(1)}, bf16[128,4,2,64]{0,3,1,2:T(8,128)(2,1)S(1)}, u32[]{:S(2)}, u32[]{:S(2)}) collective-permute-start(bf16[128,4,2,64]{0,3,1,2:T(8,128)(2,1)S(1)} %collective-permute-done.5), channel_id=1, source_target_pairs={{0,12},{4,0},{8,4},{12,8},{16,28},{20,16},{24,20},{28,24},{1,13},{... | collective-permute-start | bytes 393224 | tf_op jit(solution)/shard_map/ppermute | solution.py:44
  43.6 1.0 %copy-start.2 = (bf16[1024,4,2,64]{0,3,1,2:T(8,128)(2,1)}, bf16[1024,4,2,64]{0,3,1,2:T(8,128)(2,1)S(1)}, u32[]{:S(2)}) copy-start(bf16[1024,4,2,64]{0,3,1,2:T(8,128)(2,1)S(1)} %constant_dynamic-update-slice_fusion.3) | copy-start | bytes 3145732
  45.1 2.0 %copy-start.1 = (bf16[256,1024]{1,0:T(8,128)(2,1)S(1)}, bf16[256,1024]{1,0:T(8,128)(2,1)}, u32[]{:S(2)}) copy-start(bf16[256,1024]{1,0:T(8,128)(2,1)} %param.9) | copy-start | bytes 1572868
  47.4 1.6 %collective-permute-start.12 = (f32[2,32,1024]{2,1,0:T(8,128)S(1)}, f32[2,32,1024]{2,1,0:T(8,128)S(1)}, u32[]{:S(2)}, u32[]{:S(2)}) collective-permute-start(f32[2,32,1024]{2,1,0:T(8,128)S(1)} %dynamic-slice_bitcast_fusion), channel_id=1, source_target_pairs={{0,1},{1,0},{2,3},{3,2},{4,5},{5,4},{6,7},{7,6},{8,9},{9,8},{10,11... | collective-permute-start | bytes 786440 | tf_op jit(solution)/shard_map/ppermute | solution.py:78
  49.1 4.3 %collective-permute-start.13 = (bf16[32,1024]{1,0:T(8,128)(2,1)S(1)}, bf16[32,1024]{1,0:T(8,128)(2,1)S(1)}, u32[]{:S(2)}, u32[]{:S(2)}) collective-permute-start(bf16[32,1024]{1,0:T(8,128)(2,1)S(1)} %fusion.36), channel_id=1, source_target_pairs={{0,2},{1,3},{2,0},{3,1},{4,6},{5,7},{6,4},{7,5},{8,10},{9,11},{10,... | collective-permute-start | bytes 196616 | tf_op jit(solution)/shard_map/ppermute | solution.py:82

commit v7 on v6

--- a/solution.py
+++ b/solution.py
@@ -141,41 +141,75 @@
     key_piece = key_value[:, :, 0]
     value_piece = key_value[:, :, 1]
     score_scale = 1.0 / math.sqrt(HS)
-
-    def key_block(carry_state, key_value):
-        running_max, running_sum, weighted = carry_state
-        key_part, value_part = key_value
-        scores = (
-            jnp.einsum("qhd,khd->hqk", queries, key_part, preferred_element_type=jnp.float32)
-            * score_scale
-        )
-        new_max = jnp.maximum(running_max, jnp.max(scores, axis=2))
-        shrink = jnp.exp(running_max - new_max)
-        weights = jnp.exp(scores - new_max[:, :, None])
-        running_sum = running_sum * shrink + jnp.sum(weights, axis=2)
-        weighted = weighted * shrink[:, :, None] + jnp.einsum(
-            "hqk,khd->hqd",
-            weights.astype(jnp.bfloat16),
-            value_part,
-            preferred_element_type=jnp.float32,
-        )
-        return ((new_max, running_sum, weighted), None)
-
-    start_state = (
-        jnp.full((heads_here, slab_tok), -1e30, jnp.float32),
-        jnp.zeros((heads_here, slab_tok), jnp.float32),
-        jnp.zeros((heads_here, slab_tok, HS), jnp.float32),
-    )
     key_count = key_piece.shape[0]
     block_len = min(1024, key_count)
     key_blocks = key_piece.reshape(key_count // block_len, block_len, heads_here, HS)
     value_blocks = value_piece.reshape(key_count // block_len, block_len, heads_here, HS)
-    folded, unused = lax.scan(key_block, start_state, (key_blocks, value_blocks))
-    running_max, running_sum, weighted = folded
-    attended = (weighted / running_sum[:, :, None]).astype(jnp.bfloat16)
-    head_rows = attended.transpose(1, 0, 2).reshape(slab_tok, heads_here * HS)
-    partial = jnp.dot(head_rows, out_weight, preferred_element_type=jnp.float32)
-    result = scattered_sum_by_chip(partial, "uly", tokens.shape)
+
+    def attend(query_rows):
+        rows = query_rows.shape[0]
+
+        def key_block(carry_state, key_value):
+            running_max, running_sum, weighted = carry_state
+            key_part, value_part = key_value
+            scores = (
+                jnp.einsum(
+                    "qhd,khd->hqk", query_rows, key_part, preferred_element_type=jnp.float32
+                )
+                * score_scale
+            )
+            new_max = jnp.maximum(running_max, jnp.max(scores, axis=2))
+            shrink = jnp.exp(running_max - new_max)
+            weights = jnp.exp(scores - new_max[:, :, None])
+            running_sum = running_sum * shrink + jnp.sum(weights, axis=2)
+            weighted = weighted * shrink[:, :, None] + jnp.einsum(
+                "hqk,khd->hqd",
+                weights.astype(jnp.bfloat16),
+                value_part,
+                preferred_element_type=jnp.float32,
+            )
+            return ((new_max, running_sum, weighted), None)
+
+        start_state = (
+            jnp.full((heads_here, rows), -1e30, jnp.float32),
+            jnp.zeros((heads_here, rows), jnp.float32),
+            jnp.zeros((heads_here, rows, HS), jnp.float32),
+        )
+        folded, unused = lax.scan(key_block, start_state, (key_blocks, value_blocks))
+        running_max, running_sum, weighted = folded
+        attended = (weighted / running_sum[:, :, None]).astype(jnp.bfloat16)
+        return attended.transpose(1, 0, 2).reshape(rows, heads_here * HS)
+
+    rank = lax.axis_index("uly")
+    chips, core, chip = groups // 2, rank % 2, rank // 2
+    pair_queries = queries.reshape(chips, 2 * local_tok, heads_here, HS)
+    total = None
+    for shift in range(1, chips):
+        far_rows = lax.dynamic_index_in_dim(pair_queries, (chip + shift) % chips, 0, keepdims=False)
+        far_partial = jnp.dot(attend(far_rows), out_weight, preferred_element_type=jnp.float32)
+        far_partial = far_partial.astype(jnp.bfloat16).reshape(2, local_tok, features)
+        same_core = lax.dynamic_index_in_dim(far_partial, core, 0, keepdims=False)
+        other_core = lax.dynamic_index_in_dim(far_partial, 1 - core, 0, keepdims=False)
+        far_sent = (same_core, other_core)
+        to_other_core = [
+            (i, ((i // 2 + shift) % chips) * 2 + 1 - i % 2) for i in range(groups)
+        ]
+        for arrived in (
+            lax.ppermute(same_core, "uly", chip_shift(groups, shift)),
+            lax.ppermute(other_core, "uly", to_other_core),
+        ):
+            arrived = arrived.astype(jnp.float32).reshape(tokens.shape)
+            total = arrived if total is None else total + arrived
+    near_rows = lax.dynamic_index_in_dim(pair_queries, chip, 0, keepdims=False)
+    if total is not None:
+        near_rows, unused = lax.optimization_barrier((near_rows, far_sent))
+    near_partial = jnp.dot(attend(near_rows), out_weight, preferred_element_type=jnp.float32)
+    near_partial = near_partial.reshape(2, local_tok, features)
+    own = lax.dynamic_index_in_dim(near_partial, core, 0, keepdims=False)
+    for_partner = lax.dynamic_index_in_dim(near_partial, 1 - core, 0, keepdims=False)
+    from_partner = lax.ppermute(for_partner, "uly", [(i, i ^ 1) for i in range(groups)])
+    near_sum = own.reshape(tokens.shape) + from_partner.reshape(tokens.shape)
+    result = near_sum if total is None else near_sum + total
     return result.astype(jnp.bfloat16)
 
 

time: 54.6 us -> 52.3 us (0.958)
  waiting for transfers between devices: 20.2 us -> 15.7 us
  local copies, waits for them, and re-layouts: 6.39 us -> 8.45 us
  matrix products: 3.15 us -> 2.5 us
    ppermute x2 -> x3, waiting for transfers between devices: 4.16 us -> 1.9 us  [the longest x1 1.4 us: on_device(): lax.ppermute(other_core, 'uly', to_other_core)]
    ppermute x3, waiting for transfers between devices: 4.92 us -> 3.23 us  [relayed(): parts.append(lax.ppermute(crossed, axis, pairs))]
    unnamed x18 -> x16, local copies, waits for them, and re-layouts: 2.51 us -> 4.1 us
    dot_general x1 -> x2, matrix products: 1.71 us -> 0.71 us  [key_block(): jnp.einsum('hqk,khd->hqd', weights.astype(jnp.bfloat16), value_part, pref...]
    ppermute x1, waiting for transfers between devices: 2.21 us -> 1.58 us  [relayed(): crossed = lax.ppermute(piece, axis, mirror)]
    ppermute x2 -> x3, starting transfers between devices: 1.64 us -> 2.27 us  [the longest x1 1.56 us: on_device(): lax.ppermute(same_core, 'uly', chip_shift(groups, shift))]
    dot_general x2 -> x4, matrix products: 0.79 us -> 1.13 us  [the longest x2 0.72 us: key_block(): jnp.einsum('qhd,khd->hqk', query_rows, key_part, preferred_element_type=j...]
  transfers between devices with their start and end apart: 14 -> 15, of which waited for: 10 -> 9; matrix products, arithmetic and copies ran while one was open for 7% -> 15% of each run, Pallas kernels for 0% -> 0%
where the time goes in v7:
time: 52.3 us; the launch traced here: 51.8 us
  starting transfers between devices  20.9 us (40%)
  waiting for transfers between devices  15.7 us (30%)
  local copies, waits for them, and re-layouts  8.45 us (16%)
  other arithmetic  3.75 us (7%)
  matrix products  2.5 us (5%)
    ppermute x1, waiting for transfers between devices, gathered_by_chip(): far = lax.ppermute(piece, axis, chip_shift(size, shift))  5.62 us
    ppermute x1, starting transfers between devices, padded_2(): before = lax.ppermute(last, axis, up)  4.87 us
    ppermute x3, starting transfers between devices, relayed(): parts.append(lax.ppermute(piece, axis, pairs))  4.5 us
    unnamed x16, local copies, waits for them, and re-layouts  4.1 us
    ppermute x3, starting transfers between devices, relayed(): parts.append(lax.ppermute(crossed, axis, pairs))  3.23 us
    ppermute x3, waiting for transfers between devices, relayed(): parts.append(lax.ppermute(crossed, axis, pairs))  3.23 us
    ppermute x1, starting transfers between devices, relayed(): crossed = lax.ppermute(piece, axis, mirror)  3.2 us
    convert_element_type x1, other arithmetic, on_device(): positioned = summed.astype(jnp.bfloat16)  2.34 us
  transfers between devices with their start and end apart: 15, of which 9 were waited for; matrix products, arithmetic and copies ran while one was open for 15% of the time, Pallas kernels for 0%

profile of v7, /device:TPU:0, one launch (start us, length us, event | category | flops | bytes accessed | tf_op | source)
XLA Modules:
  0.0 51.8 jit_solution(13982955516773312697)
XLA Ops:
  0.0 1.0 %copy.21 = bf16[1,16,2,1024]{3,1,2,0:T(8,128)(2,1)S(1)} copy(bf16[1,16,2,1024]{3,2,1,0:T(2,128)(2,1)} %param.5) | data formatting | bytes 131072 | tf_op args[0]
  1.0 4.9 %collective-permute-start = (bf16[1,16,2,1024]{3,1,2,0:T(8,128)(2,1)S(1)}, bf16[1,16,2,1024]{3,1,2,0:T(8,128)(2,1)S(1)}, u32[]{:S(2)}, u32[]{:S(2)}) collective-permute-start(bf16[1,16,2,1024]{3,1,2,0:T(8,128)(2,1)S(1)} %copy.21), channel_id=1, source_target_pairs={{0,4},{4,8},{8,12},{12,16},{16,20},{20,24},{24,28},{1,5},{5,9},{9,... | collective-permute-start | bytes 196616 | tf_op jit(solution)/shard_map/ppermute | solution.py:18
  5.9 1.3 %collective-permute-start.1 = (bf16[1,16,2,1024]{3,1,2,0:T(8,128)(2,1)S(1)}, bf16[1,16,2,1024]{3,1,2,0:T(8,128)(2,1)S(1)}, u32[]{:S(2)}, u32[]{:S(2)}) collective-permute-start(bf16[1,16,2,1024]{3,1,2,0:T(8,128)(2,1)S(1)} %copy.21), channel_id=1, source_target_pairs={{4,0},{8,4},{12,8},{16,12},{20,16},{24,20},{28,24},{5,1},{9,5},{13... | collective-permute-start | bytes 196616 | tf_op jit(solution)/shard_map/ppermute | solution.py:19
  7.2 1.3 %fusion.44 = (f32[1,1024]{1,0:T(1,128)S(1)}, f32[1,1024]{1,0:T(1,128)S(1)}, f32[1,1024]{1,0:T(1,128)S(1)}, f32[1,1024]{1,0:T(1,128)S(1)}, f32[1,1024]{1,0:T(1,12...) fusion(f32[27,1024]{1,0:T(8,128)} %param.6), kind=kLoop, calls=%fused_computation.111 | loop fusion | bytes 155648 | tf_op jit(solution)/shard_map/slice | solution.py:121
  8.5 1.0 %fusion.45 = (f32[1,1024]{1,0:T(1,128)S(1)}, f32[1,1024]{1,0:T(1,128)S(1)}, f32[1,1024]{1,0:T(1,128)S(1)}, f32[1,1024]{1,0:T(1,128)S(1)}, f32[1,1024]{1,0:T(1,12...) fusion(f32[27,1024]{1,0:T(8,128)} %param.6), kind=kLoop, calls=%fused_computation.112 | loop fusion | bytes 65536 | tf_op jit(solution)/shard_map/slice | solution.py:121
  9.6 0.0 collective-permute-done
  9.6 0.9 %constant_dynamic-update-slice_fusion.1 = bf16[3,16,2,1024]{3,1,2,0:T(8,128)(2,1)S(1)} fusion(bf16[3,16,2,1024]{3,1,2,0:T(8,128)(2,1)S(1)} %constant_dynamic-update-slice_fusion.2, bf16[1,16,2,1024]{3,2,1,0:T(2,128)(2,1)} %param.5), kind=kLoop, calls=%fused_computation.90 | loop fusion | bytes 131072
  10.4 1.6 %collective-permute-done.1 = bf16[1,16,2,1024]{3,1,2,0:T(8,128)(2,1)S(1)} collective-permute-done((bf16[1,16,2,1024]{3,1,2,0:T(8,128)(2,1)S(1)}, bf16[1,16,2,1024]{3,1,2,0:T(8,128)(2,1)S(1)}, u32[]{:S(2)}, u32[]{:S(2)}) %collective-permute-start.1) | collective-permute-done | bytes 65568 | tf_op jit(solution)/shard_map/ppermute | solution.py:19
  12.0 0.0 collective-permute-start.2
  12.0 1.6 %collective-permute-start.3 = (bf16[3,16,2,1024]{3,1,2,0:T(8,128)(2,1)S(1)}, bf16[3,16,2,1024]{3,1,2,0:T(8,128)(2,1)S(1)}, u32[]{:S(2)}, u32[]{:S(2)}) collective-permute-start(bf16[3,16,2,1024]{3,1,2,0:T(8,128)(2,1)S(1)} %constant_dynamic-update-slice_fusion), channel_id=1, source_target_pairs={{0,2},{1,3},{2,0},{3,1},{4,6},{5,7},{6,4},{7,5},{8,10},{9,11},{10,... | collective-permute-start | bytes 589832 | tf_op jit(solution)/shard_map/ppermute | solution.py:64
  13.6 0.1 broadcast_in_dim.27
  13.7 0.0 copy-start.2
  13.7 5.6 %collective-permute-done.3 = bf16[3,16,2,1024]{3,1,2,0:T(8,128)(2,1)S(1)} collective-permute-done((bf16[3,16,2,1024]{3,1,2,0:T(8,128)(2,1)S(1)}, bf16[3,16,2,1024]{3,1,2,0:T(8,128)(2,1)S(1)}, u32[]{:S(2)}, u32[]{:S(2)}) %collective-permute-start.3) | collective-permute-done | bytes 196640 | tf_op jit(solution)/shard_map/ppermute | solution.py:64
  19.3 0.0 collective-permute-start.4
  19.3 0.0 collective-permute-done.2
  19.4 1.4 %collective-permute-done.4 = bf16[3,16,2,1024]{3,1,2,0:T(8,128)(2,1)S(1)} collective-permute-done((bf16[3,16,2,1024]{3,1,2,0:T(8,128)(2,1)S(1)}, bf16[3,16,2,1024]{3,1,2,0:T(8,128)(2,1)S(1)}, u32[]{:S(2)}, u32[]{:S(2)}) %collective-permute-start.4) | collective-permute-done | bytes 196640 | tf_op jit(solution)/shard_map/ppermute | solution.py:66
  20.8 0.1 fusion.42
  20.9 2.3 %add_convert_fusion = bf16[1,16,8,1024]{3,1,2,0:T(8,128)(2,1)S(1)} fusion(bf16[1,16,8,1024]{3,1,2,0:T(8,128)(2,1)S(1)} %bitcast.129, bf16[1,16,8,1024]{3,1,2,0:T(8,128)(2,1)S(1)} %bitcast.128, bf16[1,16,8,1024]{3,1,2,0:T(8,128)(2,1)S(1)} %bitcast.127, bf16[3,16,8,1024]{3,1,2,0:T(8,128)(2,1)S(1)} %bitcast.124, f32[1024]{0:T(1024)S(1)} %bitcast.159, ...), kind=kLoop, calls=%fused_computation.77 | loop fusion | flops 10878976 | bytes 1949696 | tf_op jit(solution)/shard_map/convert_element_type | solution.py:128
  23.2 0.3 copy.39
  23.5 0.1 reshape.250
  23.6 0.7 %convolution_convert_fusion = bf16[128,768]{1,0:T(8,128)(2,1)S(1)} fusion(bf16[128,1024]{1,0:T(8,128)(2,1)S(1)} %reshape.250, bf16[768,1024]{1,0:T(8,128)(2,1)S(1)} %copy-done), kind=kOutput, calls=%fused_computation.26 | convolution fusion | flops 201424896 | bytes 2031616 | tf_op jit(solution)/shard_map/dot_general | solution.py:100
  24.3 0.2 copy.28
  24.5 3.2 %collective-permute-start.5 = (bf16[128,4,2,64]{0,3,1,2:T(8,128)(2,1)S(1)}, bf16[128,4,2,64]{0,3,1,2:T(8,128)(2,1)S(1)}, u32[]{:S(2)}, u32[]{:S(2)}) collective-permute-start(bf16[128,4,2,64]{0,3,1,2:T(8,128)(2,1)S(1)} %get-tuple-element.56), channel_id=1, source_target_pairs={{0,16},{4,20},{8,24},{12,28},{16,0},{20,4},{24,8},{28,12},{1,17},{... | collective-permute-start | bytes 393224 | tf_op jit(solution)/shard_map/ppermute | solution.py:39
  27.7 1.9 %collective-permute-start.6 = (bf16[128,4,2,64]{0,3,1,2:T(8,128)(2,1)S(1)}, bf16[128,4,2,64]{0,3,1,2:T(8,128)(2,1)}, u32[]{:S(2)}, u32[]{:S(2)}) collective-permute-start(bf16[128,4,2,64]{0,3,1,2:T(8,128)(2,1)S(1)} %get-tuple-element.56), channel_id=1, source_target_pairs={{0,4},{4,8},{8,12},{12,0},{16,20},{20,24},{24,28},{28,16},{1,5},{5... | collective-permute-start | bytes 393224 | tf_op jit(solution)/shard_map/ppermute | solution.py:43
  29.6 0.3 collective-permute-start.8
  29.9 2.3 %collective-permute-start.10 = (bf16[128,4,2,64]{0,3,1,2:T(8,128)(2,1)S(1)}, bf16[128,4,2,64]{0,3,1,2:T(8,128)(2,1)S(1)}, u32[]{:S(2)}, u32[]{:S(2)}) collective-permute-start(bf16[128,4,2,64]{0,3,1,2:T(8,128)(2,1)S(1)} %get-tuple-element.56), channel_id=1, source_target_pairs={{0,12},{4,0},{8,4},{12,8},{16,28},{20,16},{24,20},{28,24},{1,13},{... | collective-permute-start | bytes 393224 | tf_op jit(solution)/shard_map/ppermute | solution.py:43
  32.2 0.1 reshape_squeeze.2
  32.3 0.3 constant_dynamic-slice_fusion.2
  32.6 0.1 copy.30
  32.7 0.1 copy.29
  32.9 1.6 %collective-permute-done.5 = bf16[128,4,2,64]{0,3,1,2:T(8,128)(2,1)S(1)} collective-permute-done((bf16[128,4,2,64]{0,3,1,2:T(8,128)(2,1)S(1)}, bf16[128,4,2,64]{0,3,1,2:T(8,128)(2,1)S(1)}, u32[]{:S(2)}, u32[]{:S(2)}) %collective-permute-start.5) | collective-permute-done | bytes 131104 | tf_op jit(solution)/shard_map/ppermute | solution.py:39
  34.4 1.9 %collective-permute-start.7 = (bf16[128,4,2,64]{0,3,1,2:T(8,128)(2,1)S(1)}, bf16[128,4,2,64]{0,3,1,2:T(8,128)(2,1)S(1)}, u32[]{:S(2)}, u32[]{:S(2)}) collective-permute-start(bf16[128,4,2,64]{0,3,1,2:T(8,128)(2,1)S(1)} %collective-permute-done.5), channel_id=1, source_target_pairs={{0,4},{4,8},{8,12},{12,0},{16,20},{20,24},{24,28},{28,16},{1,5},{5... | collective-permute-start | bytes 393224 | tf_op jit(solution)/shard_map/ppermute | solution.py:44
  36.4 0.0 collective-permute-start.9
  36.4 0.4 collective-permute-done.6
  36.8 1.3 %collective-permute-start.11 = (bf16[128,4,2,64]{0,3,1,2:T(8,128)(2,1)S(1)}, bf16[128,4,2,64]{0,3,1,2:T(8,128)(2,1)S(1)}, u32[]{:S(2)}, u32[]{:S(2)}) collective-permute-start(bf16[128,4,2,64]{0,3,1,2:T(8,128)(2,1)S(1)} %collective-permute-done.5), channel_id=1, source_target_pairs={{0,12},{4,0},{8,4},{12,8},{16,28},{20,16},{24,20},{28,24},{1,13},{... | collective-permute-start | bytes 393224 | tf_op jit(solution)/shard_map/ppermute | solution.py:44
  38.1 0.9 %constant_dynamic-update-slice_fusion.8 = bf16[1024,4,2,64]{0,3,1,2:T(8,128)(2,1)S(1)} fusion(bf16[1024,4,2,64]{0,3,1,2:T(8,128)(2,1)S(1)} %constant_dynamic-update-slice_fusion.9, bf16[128,4,2,64]{0,3,1,2:T(8,128)(2,1)} %collective-permute-done.6), kind=kLoop, calls=%fused_computation.97 | loop fusion | bytes 262144
  39.1 3.2 %collective-permute-done.7 = bf16[128,4,2,64]{0,3,1,2:T(8,128)(2,1)S(1)} collective-permute-done((bf16[128,4,2,64]{0,3,1,2:T(8,128)(2,1)S(1)}, bf16[128,4,2,64]{0,3,1,2:T(8,128)(2,1)S(1)}, u32[]{:S(2)}, u32[]{:S(2)}) %collective-permute-start.7) | collective-permute-done | bytes 131104 | tf_op jit(solution)/shard_map/ppermute | solution.py:44
  42.3 0.9 %constant_dynamic-update-slice_fusion.6 = bf16[1024,4,2,64]{0,3,1,2:T(8,128)(2,1)S(1)} fusion(bf16[1024,4,2,64]{0,3,1,2:T(8,128)(2,1)S(1)} %constant_dynamic-update-slice_fusion.7, bf16[128,4,2,64]{0,3,1,2:T(8,128)(2,1)} %collective-permute-done.8), kind=kLoop, calls=%fused_computation.95 | loop fusion | bytes 262144
  43.2 0.0 collective-permute-done.9
  43.4 0.1 collective-permute-done.11
  43.5 0.4 fusion.46
  43.8 0.0 copy-start.1
  43.8 0.3 fusion.6
  44.2 0.4 fusion.5
  44.5 0.1 copy.32
  44.6 0.1 reshape.252
  44.7 0.2 copy-done.1
  44.9 0.2 convolution_convert_fusion.1
  45.1 1.6 %collective-permute-start.13 = (bf16[32,1024]{1,0:T(8,128)(2,1)S(1)}, bf16[32,1024]{1,0:T(8,128)(2,1)S(1)}, u32[]{:S(2)}, u32[]{:S(2)}) collective-permute-start(bf16[32,1024]{1,0:T(8,128)(2,1)S(1)} %get-tuple-element.47), channel_id=1, source_target_pairs={{0,2},{1,3},{2,0},{3,1},{4,6},{5,7},{6,4},{7,5},{8,10},{9,11},{10,... | collective-permute-start | bytes 196616 | tf_op jit(solution)/shard_map/ppermute | solution.py:198
  46.7 0.0 collective-permute-start.14
  46.7 0.4 fusion.47
  47.1 0.3 fusion.8
  47.4 0.4 fusion.4
  47.8 0.1 copy.33
  47.8 0.1 dot_general.39
  47.9 0.2 fusion.37
  48.2 0.7 %collective-permute-start.12 = (f32[32,1024]{1,0:T(8,128)S(1)}, f32[32,1024]{1,0:T(8,128)S(1)}, u32[]{:S(2)}, u32[]{:S(2)}) collective-permute-start(f32[32,1024]{1,0:T(8,128)S(1)} %get-tuple-element.43), channel_id=1, source_target_pairs={{0,1},{1,0},{2,3},{3,2},{4,5},{5,4},{6,7},{7,6},{8,9},{9,8},{10,11... | collective-permute-start | bytes 393224 | tf_op jit(solution)/shard_map/ppermute | solution.py:210
  48.9 0.1 reshape.254
  49.0 0.5 collective-permute-done.13
  49.5 1.4 %collective-permute-done.14 = bf16[32,1024]{1,0:T(8,128)(2,1)S(1)} collective-permute-done((bf16[32,1024]{1,0:T(8,128)(2,1)S(1)}, bf16[32,1024]{1,0:T(8,128)(2,1)S(1)}, u32[]{:S(2)}, u32[]{:S(2)}) %collective-permute-start.14) | collective-permute-done | bytes 65568 | tf_op jit(solution)/shard_map/ppermute | solution.py:199
  50.9 0.1 add.269
  51.0 0.0 collective-permute-done.12
  51.0 0.1 reshape.255
  51.1 0.7 %add_convert_fusion.1 = bf16[1,16,2,1024]{3,2,1,0:T(2,128)(2,1)} fusion(f32[1,16,2,1024]{3,2,1,0:T(2,128)S(1)} %add.269, f32[1,16,2,1024]{3,2,1,0:T(2,128)S(1)} %reshape.254, f32[1,16,2,1024]{3,2,1,0:T(2,128)S(1)} %reshape.255), kind=kLoop, calls=%fused_computation.83 | loop fusion | flops 98304 | bytes 458752 | tf_op jit(solution)/shard_map/convert_element_type | solution.py:213
  (25 shorter events, 0.4 us)
Async XLA Ops:
  0.0 23.6 %copy-start = (bf16[768,1024]{1,0:T(8,128)(2,1)S(1)}, bf16[768,1024]{1,0:T(8,128)(2,1)}, u32[]{:S(2)}) copy-start(bf16[768,1024]{1,0:T(8,128)(2,1)} %param.8) | copy-start | bytes 4718596
  1.0 8.6 %collective-permute-start = (bf16[1,16,2,1024]{3,1,2,0:T(8,128)(2,1)S(1)}, bf16[1,16,2,1024]{3,1,2,0:T(8,128)(2,1)S(1)}, u32[]{:S(2)}, u32[]{:S(2)}) collective-permute-start(bf16[1,16,2,1024]{3,1,2,0:T(8,128)(2,1)S(1)} %copy.21), channel_id=1, source_target_pairs={{0,4},{4,8},{8,12},{12,16},{16,20},{20,24},{24,28},{1,5},{5,9},{9,... | collective-permute-start | bytes 196616 | tf_op jit(solution)/shard_map/ppermute | solution.py:18
  5.9 6.2 %collective-permute-start.1 = (bf16[1,16,2,1024]{3,1,2,0:T(8,128)(2,1)S(1)}, bf16[1,16,2,1024]{3,1,2,0:T(8,128)(2,1)S(1)}, u32[]{:S(2)}, u32[]{:S(2)}) collective-permute-start(bf16[1,16,2,1024]{3,1,2,0:T(8,128)(2,1)S(1)} %copy.21), channel_id=1, source_target_pairs={{4,0},{8,4},{12,8},{16,12},{20,16},{24,20},{28,24},{5,1},{9,5},{13... | collective-permute-start | bytes 196616 | tf_op jit(solution)/shard_map/ppermute | solution.py:19
  12.0 7.3 %collective-permute-start.2 = (bf16[3,16,2,1024]{3,1,2,0:T(8,128)(2,1)S(1)}, bf16[3,16,2,1024]{3,1,2,0:T(8,128)(2,1)S(1)}, u32[]{:S(2)}, u32[]{:S(2)}) collective-permute-start(bf16[3,16,2,1024]{3,1,2,0:T(8,128)(2,1)S(1)} %constant_dynamic-update-slice_fusion), channel_id=1, source_target_pairs={{0,1},{1,0},{2,3},{3,2},{4,5},{5,4},{6,7},{7,6},{8,9},{9,8},{10,11... | collective-permute-start | bytes 589832 | tf_op jit(solution)/shard_map/ppermute | solution.py:60
  12.0 7.3 %collective-permute-start.3 = (bf16[3,16,2,1024]{3,1,2,0:T(8,128)(2,1)S(1)}, bf16[3,16,2,1024]{3,1,2,0:T(8,128)(2,1)S(1)}, u32[]{:S(2)}, u32[]{:S(2)}) collective-permute-start(bf16[3,16,2,1024]{3,1,2,0:T(8,128)(2,1)S(1)} %constant_dynamic-update-slice_fusion), channel_id=1, source_target_pairs={{0,2},{1,3},{2,0},{3,1},{4,6},{5,7},{6,4},{7,5},{8,10},{9,11},{10,... | collective-permute-start | bytes 589832 | tf_op jit(solution)/shard_map/ppermute | solution.py:64
  13.7 7.2 %copy-start.2 = (f32[1024]{0:T(1024)S(1)}, f32[1024]{0:T(1024)}, u32[]{:S(2)}) copy-start(f32[1024]{0:T(1024)} %param.7) | copy-start | bytes 12292
  19.3 1.4 %collective-permute-start.4 = (bf16[3,16,2,1024]{3,1,2,0:T(8,128)(2,1)S(1)}, bf16[3,16,2,1024]{3,1,2,0:T(8,128)(2,1)S(1)}, u32[]{:S(2)}, u32[]{:S(2)}) collective-permute-start(bf16[3,16,2,1024]{3,1,2,0:T(8,128)(2,1)S(1)} %collective-permute-done.3), channel_id=1, source_target_pairs={{0,1},{1,0},{2,3},{3,2},{4,5},{5,4},{6,7},{7,6},{8,9},{9,8},{10,11... | collective-permute-start | bytes 589832 | tf_op jit(solution)/shard_map/ppermute | solution.py:66
  24.5 9.9 %collective-permute-start.5 = (bf16[128,4,2,64]{0,3,1,2:T(8,128)(2,1)S(1)}, bf16[128,4,2,64]{0,3,1,2:T(8,128)(2,1)S(1)}, u32[]{:S(2)}, u32[]{:S(2)}) collective-permute-start(bf16[128,4,2,64]{0,3,1,2:T(8,128)(2,1)S(1)} %get-tuple-element.56), channel_id=1, source_target_pairs={{0,16},{4,20},{8,24},{12,28},{16,0},{20,4},{24,8},{28,12},{1,17},{... | collective-permute-start | bytes 393224 | tf_op jit(solution)/shard_map/ppermute | solution.py:39
  27.7 9.1 %collective-permute-start.6 = (bf16[128,4,2,64]{0,3,1,2:T(8,128)(2,1)S(1)}, bf16[128,4,2,64]{0,3,1,2:T(8,128)(2,1)}, u32[]{:S(2)}, u32[]{:S(2)}) collective-permute-start(bf16[128,4,2,64]{0,3,1,2:T(8,128)(2,1)S(1)} %get-tuple-element.56), channel_id=1, source_target_pairs={{0,4},{4,8},{8,12},{12,0},{16,20},{20,24},{24,28},{28,16},{1,5},{5... | collective-permute-start | bytes 393224 | tf_op jit(solution)/shard_map/ppermute | solution.py:43
  29.6 12.7 %collective-permute-start.8 = (bf16[128,4,2,64]{0,3,1,2:T(8,128)(2,1)S(1)}, bf16[128,4,2,64]{0,3,1,2:T(8,128)(2,1)}, u32[]{:S(2)}, u32[]{:S(2)}) collective-permute-start(bf16[128,4,2,64]{0,3,1,2:T(8,128)(2,1)S(1)} %get-tuple-element.56), channel_id=1, source_target_pairs={{0,8},{4,12},{8,0},{12,4},{16,24},{20,28},{24,16},{28,20},{1,9},{5... | collective-permute-start | bytes 393224 | tf_op jit(solution)/shard_map/ppermute | solution.py:43
  29.9 13.4 %collective-permute-start.10 = (bf16[128,4,2,64]{0,3,1,2:T(8,128)(2,1)S(1)}, bf16[128,4,2,64]{0,3,1,2:T(8,128)(2,1)S(1)}, u32[]{:S(2)}, u32[]{:S(2)}) collective-permute-start(bf16[128,4,2,64]{0,3,1,2:T(8,128)(2,1)S(1)} %get-tuple-element.56), channel_id=1, source_target_pairs={{0,12},{4,0},{8,4},{12,8},{16,28},{20,16},{24,20},{28,24},{1,13},{... | collective-permute-start | bytes 393224 | tf_op jit(solution)/shard_map/ppermute | solution.py:43
  34.4 7.8 %collective-permute-start.7 = (bf16[128,4,2,64]{0,3,1,2:T(8,128)(2,1)S(1)}, bf16[128,4,2,64]{0,3,1,2:T(8,128)(2,1)S(1)}, u32[]{:S(2)}, u32[]{:S(2)}) collective-permute-start(bf16[128,4,2,64]{0,3,1,2:T(8,128)(2,1)S(1)} %collective-permute-done.5), channel_id=1, source_target_pairs={{0,4},{4,8},{8,12},{12,0},{16,20},{20,24},{24,28},{28,16},{1,5},{5... | collective-permute-start | bytes 393224 | tf_op jit(solution)/shard_map/ppermute | solution.py:44
  36.4 6.9 %collective-permute-start.9 = (bf16[128,4,2,64]{0,3,1,2:T(8,128)(2,1)S(1)}, bf16[128,4,2,64]{0,3,1,2:T(8,128)(2,1)S(1)}, u32[]{:S(2)}, u32[]{:S(2)}) collective-permute-start(bf16[128,4,2,64]{0,3,1,2:T(8,128)(2,1)S(1)} %collective-permute-done.5), channel_id=1, source_target_pairs={{0,8},{4,12},{8,0},{12,4},{16,24},{20,28},{24,16},{28,20},{1,9},{5... | collective-permute-start | bytes 393224 | tf_op jit(solution)/shard_map/ppermute | solution.py:44
  36.8 6.6 %collective-permute-start.11 = (bf16[128,4,2,64]{0,3,1,2:T(8,128)(2,1)S(1)}, bf16[128,4,2,64]{0,3,1,2:T(8,128)(2,1)S(1)}, u32[]{:S(2)}, u32[]{:S(2)}) collective-permute-start(bf16[128,4,2,64]{0,3,1,2:T(8,128)(2,1)S(1)} %collective-permute-done.5), channel_id=1, source_target_pairs={{0,12},{4,0},{8,4},{12,8},{16,28},{20,16},{24,20},{28,24},{1,13},{... | collective-permute-start | bytes 393224 | tf_op jit(solution)/shard_map/ppermute | solution.py:44
  43.8 1.1 %copy-start.1 = (bf16[256,1024]{1,0:T(8,128)(2,1)S(1)}, bf16[256,1024]{1,0:T(8,128)(2,1)}, u32[]{:S(2)}) copy-start(bf16[256,1024]{1,0:T(8,128)(2,1)} %param.9) | copy-start | bytes 1572868
  45.1 4.3 %collective-permute-start.13 = (bf16[32,1024]{1,0:T(8,128)(2,1)S(1)}, bf16[32,1024]{1,0:T(8,128)(2,1)S(1)}, u32[]{:S(2)}, u32[]{:S(2)}) collective-permute-start(bf16[32,1024]{1,0:T(8,128)(2,1)S(1)} %get-tuple-element.47), channel_id=1, source_target_pairs={{0,2},{1,3},{2,0},{3,1},{4,6},{5,7},{6,4},{7,5},{8,10},{9,11},{10,... | collective-permute-start | bytes 196616 | tf_op jit(solution)/shard_map/ppermute | solution.py:198
  46.7 4.2 %collective-permute-start.14 = (bf16[32,1024]{1,0:T(8,128)(2,1)S(1)}, bf16[32,1024]{1,0:T(8,128)(2,1)S(1)}, u32[]{:S(2)}, u32[]{:S(2)}) collective-permute-start(bf16[32,1024]{1,0:T(8,128)(2,1)S(1)} %get-tuple-element.48), channel_id=1, source_target_pairs={{0,3},{1,2},{2,1},{3,0},{4,7},{5,6},{6,5},{7,4},{8,11},{9,10},{10,... | collective-permute-start | bytes 196616 | tf_op jit(solution)/shard_map/ppermute | solution.py:199
  48.2 2.8 %collective-permute-start.12 = (f32[32,1024]{1,0:T(8,128)S(1)}, f32[32,1024]{1,0:T(8,128)S(1)}, u32[]{:S(2)}, u32[]{:S(2)}) collective-permute-start(f32[32,1024]{1,0:T(8,128)S(1)} %get-tuple-element.43), channel_id=1, source_target_pairs={{0,1},{1,0},{2,3},{3,2},{4,5},{5,4},{6,7},{7,6},{8,9},{9,8},{10,11... | collective-permute-start | bytes 393224 | tf_op jit(solution)/shard_map/ppermute | solution.py:210

commit v8 on v7

--- a/solution.py
+++ b/solution.py
@@ -182,34 +182,31 @@
 
     rank = lax.axis_index("uly")
     chips, core, chip = groups // 2, rank % 2, rank // 2
-    pair_queries = queries.reshape(chips, 2 * local_tok, heads_here, HS)
-    total = None
+    rank_queries = queries.reshape(groups, local_tok, heads_here, HS)
+    partner = [(i, i ^ 1) for i in range(groups)]
+    plan = []
     for shift in range(1, chips):
-        far_rows = lax.dynamic_index_in_dim(pair_queries, (chip + shift) % chips, 0, keepdims=False)
-        far_partial = jnp.dot(attend(far_rows), out_weight, preferred_element_type=jnp.float32)
-        far_partial = far_partial.astype(jnp.bfloat16).reshape(2, local_tok, features)
-        same_core = lax.dynamic_index_in_dim(far_partial, core, 0, keepdims=False)
-        other_core = lax.dynamic_index_in_dim(far_partial, 1 - core, 0, keepdims=False)
-        far_sent = (same_core, other_core)
         to_other_core = [
             (i, ((i // 2 + shift) % chips) * 2 + 1 - i % 2) for i in range(groups)
         ]
-        for arrived in (
-            lax.ppermute(same_core, "uly", chip_shift(groups, shift)),
-            lax.ppermute(other_core, "uly", to_other_core),
-        ):
-            arrived = arrived.astype(jnp.float32).reshape(tokens.shape)
-            total = arrived if total is None else total + arrived
-    near_rows = lax.dynamic_index_in_dim(pair_queries, chip, 0, keepdims=False)
-    if total is not None:
-        near_rows, unused = lax.optimization_barrier((near_rows, far_sent))
-    near_partial = jnp.dot(attend(near_rows), out_weight, preferred_element_type=jnp.float32)
-    near_partial = near_partial.reshape(2, local_tok, features)
-    own = lax.dynamic_index_in_dim(near_partial, core, 0, keepdims=False)
-    for_partner = lax.dynamic_index_in_dim(near_partial, 1 - core, 0, keepdims=False)
-    from_partner = lax.ppermute(for_partner, "uly", [(i, i ^ 1) for i in range(groups)])
-    near_sum = own.reshape(tokens.shape) + from_partner.reshape(tokens.shape)
-    result = near_sum if total is None else near_sum + total
+        target_chip = (chip + shift) % chips
+        plan.append((target_chip * 2 + core, chip_shift(groups, shift), jnp.bfloat16))
+        plan.append((target_chip * 2 + 1 - core, to_other_core, jnp.bfloat16))
+    plan.append((rank ^ 1, partner, jnp.float32))
+    total = None
+    sent = None
+    for target, pairs, link_type in plan:
+        rows = lax.dynamic_index_in_dim(rank_queries, target, 0, keepdims=False)
+        if sent is not None:
+            rows, unused = lax.optimization_barrier((rows, sent))
+        part = jnp.dot(attend(rows), out_weight, preferred_element_type=jnp.float32)
+        sent = part.astype(link_type)
+        arrived = lax.ppermute(sent, "uly", pairs).astype(jnp.float32).reshape(tokens.shape)
+        total = arrived if total is None else total + arrived
+    rows = lax.dynamic_index_in_dim(rank_queries, rank, 0, keepdims=False)
+    rows, unused = lax.optimization_barrier((rows, sent))
+    own = jnp.dot(attend(rows), out_weight, preferred_element_type=jnp.float32)
+    result = own.reshape(tokens.shape) + total
     return result.astype(jnp.bfloat16)
 
 

time: 52.3 us -> 54.5 us (1.042)
  matrix products: 2.5 us -> 4.58 us
    unnamed x16 -> x22, local copies, waits for them, and re-layouts: 4.1 us -> 3.03 us
    dot_general x2 -> x4, matrix products: 0.41 us -> 1.41 us  [the longest x3 1.21 us: on_device(): part = jnp.dot(attend(rows), out_weight, preferred_element_type=jnp.float32)]
    ppermute x3, waiting for transfers between devices: 3.23 us -> 4.14 us  [relayed(): parts.append(lax.ppermute(crossed, axis, pairs))]
    add x1, other arithmetic: 0.02 us -> 0.89 us  [on_device(): total = arrived if total is None else total + arrived]
    ppermute x3, waiting for transfers between devices: 1.9 us -> 1.07 us  [on_device(): lax.ppermute(sent, 'uly', pairs).astype(jnp.float32).reshape(tokens.shape)]
    convert_element_type x1 -> x0, other arithmetic: 0.73 us -> none  [on_device(): return result.astype(jnp.bfloat16)]
    convert_element_type x0 -> x1, local copies, waits for them, and re-layouts: none -> 0.7 us  [on_device(): return result.astype(jnp.bfloat16)]
    dot_general x2 -> x4, matrix products: 0.71 us -> 1.34 us  [key_block(): jnp.einsum('hqk,khd->hqd', weights.astype(jnp.bfloat16), value_part, pref...]
  transfers between devices with their start and end apart: 15 -> 15, of which waited for: 9 -> 9; matrix products, arithmetic and copies ran while one was open for 15% -> 17% of each run, Pallas kernels for 0% -> 0%
where the time goes in v8:
time: 54.5 us; the launch traced here: 54 us
  starting transfers between devices  20.9 us (38%)
  waiting for transfers between devices  15.6 us (29%)
  local copies, waits for them, and re-layouts  8.21 us (15%)
  matrix products  4.58 us (8%)
  other arithmetic  4.25 us (8%)
    ppermute x1, waiting for transfers between devices, gathered_by_chip(): far = lax.ppermute(piece, axis, chip_shift(size, shift))  5.62 us
    ppermute x1, starting transfers between devices, padded_2(): before = lax.ppermute(last, axis, up)  4.87 us
    ppermute x3, starting transfers between devices, relayed(): parts.append(lax.ppermute(piece, axis, pairs))  4.5 us
    ppermute x3, waiting for transfers between devices, relayed(): parts.append(lax.ppermute(crossed, axis, pairs))  4.14 us
    ppermute x3, starting transfers between devices, relayed(): parts.append(lax.ppermute(crossed, axis, pairs))  3.23 us
    ppermute x1, starting transfers between devices, relayed(): crossed = lax.ppermute(piece, axis, mirror)  3.2 us
    unnamed x22, local copies, waits for them, and re-layouts  3.03 us
    convert_element_type x1, other arithmetic, on_device(): positioned = summed.astype(jnp.bfloat16)  2.34 us
  transfers between devices with their start and end apart: 15, of which 9 were waited for; matrix products, arithmetic and copies ran while one was open for 17% of the time, Pallas kernels for 0%

profile of v8, /device:TPU:0, one launch (start us, length us, event | category | flops | bytes accessed | tf_op | source)
XLA Modules:
  0.0 54.0 jit_solution(11868337517412675223)
XLA Ops:
  0.0 1.0 %copy.13 = bf16[1,16,2,1024]{3,1,2,0:T(8,128)(2,1)S(1)} copy(bf16[1,16,2,1024]{3,2,1,0:T(2,128)(2,1)} %param.5) | data formatting | bytes 131072 | tf_op args[0]
  1.0 4.9 %collective-permute-start = (bf16[1,16,2,1024]{3,1,2,0:T(8,128)(2,1)S(1)}, bf16[1,16,2,1024]{3,1,2,0:T(8,128)(2,1)S(1)}, u32[]{:S(2)}, u32[]{:S(2)}) collective-permute-start(bf16[1,16,2,1024]{3,1,2,0:T(8,128)(2,1)S(1)} %copy.13), channel_id=1, source_target_pairs={{0,4},{4,8},{8,12},{12,16},{16,20},{20,24},{24,28},{1,5},{5,9},{9,... | collective-permute-start | bytes 196616 | tf_op jit(solution)/shard_map/ppermute | solution.py:18
  5.9 1.3 %collective-permute-start.1 = (bf16[1,16,2,1024]{3,1,2,0:T(8,128)(2,1)S(1)}, bf16[1,16,2,1024]{3,1,2,0:T(8,128)(2,1)S(1)}, u32[]{:S(2)}, u32[]{:S(2)}) collective-permute-start(bf16[1,16,2,1024]{3,1,2,0:T(8,128)(2,1)S(1)} %copy.13), channel_id=1, source_target_pairs={{4,0},{8,4},{12,8},{16,12},{20,16},{24,20},{28,24},{5,1},{9,5},{13... | collective-permute-start | bytes 196616 | tf_op jit(solution)/shard_map/ppermute | solution.py:19
  7.2 1.3 %fusion.67 = (f32[1,1024]{1,0:T(1,128)S(1)}, f32[1,1024]{1,0:T(1,128)S(1)}, f32[1,1024]{1,0:T(1,128)S(1)}, f32[1,1024]{1,0:T(1,128)S(1)}, f32[1,1024]{1,0:T(1,12...) fusion(f32[27,1024]{1,0:T(8,128)} %param.6), kind=kLoop, calls=%fused_computation.138 | loop fusion | bytes 155648 | tf_op jit(solution)/shard_map/slice | solution.py:121
  8.5 1.0 %fusion.68 = (f32[1,1024]{1,0:T(1,128)S(1)}, f32[1,1024]{1,0:T(1,128)S(1)}, f32[1,1024]{1,0:T(1,128)S(1)}, f32[1,1024]{1,0:T(1,128)S(1)}, f32[1,1024]{1,0:T(1,12...) fusion(f32[27,1024]{1,0:T(8,128)} %param.6), kind=kLoop, calls=%fused_computation.139 | loop fusion | bytes 65536 | tf_op jit(solution)/shard_map/slice | solution.py:121
  9.6 0.0 collective-permute-done
  9.6 0.9 %constant_dynamic-update-slice_fusion.1 = bf16[3,16,2,1024]{3,1,2,0:T(8,128)(2,1)S(1)} fusion(bf16[3,16,2,1024]{3,1,2,0:T(8,128)(2,1)S(1)} %constant_dynamic-update-slice_fusion.2, bf16[1,16,2,1024]{3,2,1,0:T(2,128)(2,1)} %param.5), kind=kLoop, calls=%fused_computation.112 | loop fusion | bytes 131072
  10.4 1.6 %collective-permute-done.1 = bf16[1,16,2,1024]{3,1,2,0:T(8,128)(2,1)S(1)} collective-permute-done((bf16[1,16,2,1024]{3,1,2,0:T(8,128)(2,1)S(1)}, bf16[1,16,2,1024]{3,1,2,0:T(8,128)(2,1)S(1)}, u32[]{:S(2)}, u32[]{:S(2)}) %collective-permute-start.1) | collective-permute-done | bytes 65568 | tf_op jit(solution)/shard_map/ppermute | solution.py:19
  12.0 0.0 collective-permute-start.2
  12.0 1.6 %collective-permute-start.3 = (bf16[3,16,2,1024]{3,1,2,0:T(8,128)(2,1)S(1)}, bf16[3,16,2,1024]{3,1,2,0:T(8,128)(2,1)S(1)}, u32[]{:S(2)}, u32[]{:S(2)}) collective-permute-start(bf16[3,16,2,1024]{3,1,2,0:T(8,128)(2,1)S(1)} %constant_dynamic-update-slice_fusion), channel_id=1, source_target_pairs={{0,2},{1,3},{2,0},{3,1},{4,6},{5,7},{6,4},{7,5},{8,10},{9,11},{10,... | collective-permute-start | bytes 589832 | tf_op jit(solution)/shard_map/ppermute | solution.py:64
  13.6 0.1 broadcast_in_dim.37
  13.7 0.0 copy-start.5
  13.7 5.6 %collective-permute-done.3 = bf16[3,16,2,1024]{3,1,2,0:T(8,128)(2,1)S(1)} collective-permute-done((bf16[3,16,2,1024]{3,1,2,0:T(8,128)(2,1)S(1)}, bf16[3,16,2,1024]{3,1,2,0:T(8,128)(2,1)S(1)}, u32[]{:S(2)}, u32[]{:S(2)}) %collective-permute-start.3) | collective-permute-done | bytes 196640 | tf_op jit(solution)/shard_map/ppermute | solution.py:64
  19.4 1.4 %collective-permute-done.4 = bf16[3,16,2,1024]{3,1,2,0:T(8,128)(2,1)S(1)} collective-permute-done((bf16[3,16,2,1024]{3,1,2,0:T(8,128)(2,1)S(1)}, bf16[3,16,2,1024]{3,1,2,0:T(8,128)(2,1)S(1)}, u32[]{:S(2)}, u32[]{:S(2)}) %collective-permute-start.4) | collective-permute-done | bytes 196640 | tf_op jit(solution)/shard_map/ppermute | solution.py:66
  20.8 0.1 fusion.65
  20.9 2.3 %add_convert_fusion = bf16[1,16,8,1024]{3,1,2,0:T(8,128)(2,1)S(1)} fusion(bf16[1,16,8,1024]{3,1,2,0:T(8,128)(2,1)S(1)} %bitcast.169, bf16[1,16,8,1024]{3,1,2,0:T(8,128)(2,1)S(1)} %bitcast.168, bf16[1,16,8,1024]{3,1,2,0:T(8,128)(2,1)S(1)} %bitcast.167, bf16[3,16,8,1024]{3,1,2,0:T(8,128)(2,1)S(1)} %bitcast.164, f32[1024]{0:T(1024)S(1)} %bitcast.199, ...), kind=kLoop, calls=%fused_computation.84 | loop fusion | flops 10878976 | bytes 1949696 | tf_op jit(solution)/shard_map/convert_element_type | solution.py:128
  23.2 0.3 copy.44
  23.5 0.1 reshape.234
  23.6 0.7 %convolution_convert_fusion = bf16[128,768]{1,0:T(8,128)(2,1)S(1)} fusion(bf16[128,1024]{1,0:T(8,128)(2,1)S(1)} %reshape.234, bf16[768,1024]{1,0:T(8,128)(2,1)S(1)} %copy-done), kind=kOutput, calls=%fused_computation.28 | convolution fusion | flops 201424896 | bytes 2031616 | tf_op jit(solution)/shard_map/dot_general | solution.py:100
  24.3 0.2 copy.20
  24.5 3.2 %collective-permute-start.5 = (bf16[128,4,2,64]{0,3,1,2:T(8,128)(2,1)S(1)}, bf16[128,4,2,64]{0,3,1,2:T(8,128)(2,1)S(1)}, u32[]{:S(2)}, u32[]{:S(2)}) collective-permute-start(bf16[128,4,2,64]{0,3,1,2:T(8,128)(2,1)S(1)} %get-tuple-element.85), channel_id=1, source_target_pairs={{0,16},{4,20},{8,24},{12,28},{16,0},{20,4},{24,8},{28,12},{1,17},{... | collective-permute-start | bytes 393224 | tf_op jit(solution)/shard_map/ppermute | solution.py:39
  27.7 1.9 %collective-permute-start.6 = (bf16[128,4,2,64]{0,3,1,2:T(8,128)(2,1)S(1)}, bf16[128,4,2,64]{0,3,1,2:T(8,128)(2,1)}, u32[]{:S(2)}, u32[]{:S(2)}) collective-permute-start(bf16[128,4,2,64]{0,3,1,2:T(8,128)(2,1)S(1)} %get-tuple-element.85), channel_id=1, source_target_pairs={{0,4},{4,8},{8,12},{12,0},{16,20},{20,24},{24,28},{28,16},{1,5},{5... | collective-permute-start | bytes 393224 | tf_op jit(solution)/shard_map/ppermute | solution.py:43
  29.6 0.3 collective-permute-start.8
  29.9 2.3 %collective-permute-start.10 = (bf16[128,4,2,64]{0,3,1,2:T(8,128)(2,1)S(1)}, bf16[128,4,2,64]{0,3,1,2:T(8,128)(2,1)S(1)}, u32[]{:S(2)}, u32[]{:S(2)}) collective-permute-start(bf16[128,4,2,64]{0,3,1,2:T(8,128)(2,1)S(1)} %get-tuple-element.85), channel_id=1, source_target_pairs={{0,12},{4,0},{8,4},{12,8},{16,28},{20,16},{24,20},{28,24},{1,13},{... | collective-permute-start | bytes 393224 | tf_op jit(solution)/shard_map/ppermute | solution.py:43
  32.2 0.1 copy.21
  32.4 0.6 %dynamic-slice_bitcast_fusion.2 = (bf16[32,4,64]{2,0,1:T(8,128)(2,1)}, bf16[32,4,64]{2,0,1:T(8,128)(2,1)}, bf16[32,4,64]{2,0,1:T(8,128)(2,1)}) fusion(bf16[4,32,4,64]{3,1,0,2:T(8,128)(2,1)S(1)} %bitcast.172, s32[]{:T(128)S(6)} %select_n.44, s32[]{:T(128)S(6)} %select_n.52, s32[]{:T(128)S(6)} %select_n.45), kind=kLoop, calls=%fused_computation.110 | loop fusion | bytes 98316 | tf_op jit(solution)/shard_map/jit(dynamic_index_in_dim)/squeeze | solution.py:206
  33.0 1.4 %collective-permute-done.5 = bf16[128,4,2,64]{0,3,1,2:T(8,128)(2,1)S(1)} collective-permute-done((bf16[128,4,2,64]{0,3,1,2:T(8,128)(2,1)S(1)}, bf16[128,4,2,64]{0,3,1,2:T(8,128)(2,1)S(1)}, u32[]{:S(2)}, u32[]{:S(2)}) %collective-permute-start.5) | collective-permute-done | bytes 131104 | tf_op jit(solution)/shard_map/ppermute | solution.py:39
  34.4 1.9 %collective-permute-start.7 = (bf16[128,4,2,64]{0,3,1,2:T(8,128)(2,1)S(1)}, bf16[128,4,2,64]{0,3,1,2:T(8,128)(2,1)S(1)}, u32[]{:S(2)}, u32[]{:S(2)}) collective-permute-start(bf16[128,4,2,64]{0,3,1,2:T(8,128)(2,1)S(1)} %collective-permute-done.5), channel_id=1, source_target_pairs={{0,4},{4,8},{8,12},{12,0},{16,20},{20,24},{24,28},{28,16},{1,5},{5... | collective-permute-start | bytes 393224 | tf_op jit(solution)/shard_map/ppermute | solution.py:44
  36.4 0.0 collective-permute-start.9
  36.4 0.4 collective-permute-done.6
  36.8 1.3 %collective-permute-start.11 = (bf16[128,4,2,64]{0,3,1,2:T(8,128)(2,1)S(1)}, bf16[128,4,2,64]{0,3,1,2:T(8,128)(2,1)S(1)}, u32[]{:S(2)}, u32[]{:S(2)}) collective-permute-start(bf16[128,4,2,64]{0,3,1,2:T(8,128)(2,1)S(1)} %collective-permute-done.5), channel_id=1, source_target_pairs={{0,12},{4,0},{8,4},{12,8},{16,28},{20,16},{24,20},{28,24},{1,13},{... | collective-permute-start | bytes 393224 | tf_op jit(solution)/shard_map/ppermute | solution.py:44
  38.1 0.9 %constant_dynamic-update-slice_fusion.8 = bf16[1024,4,2,64]{0,3,1,2:T(8,128)(2,1)S(1)} fusion(bf16[1024,4,2,64]{0,3,1,2:T(8,128)(2,1)S(1)} %constant_dynamic-update-slice_fusion.9, bf16[128,4,2,64]{0,3,1,2:T(8,128)(2,1)} %collective-permute-done.6), kind=kLoop, calls=%fused_computation.119 | loop fusion | bytes 262144
  39.1 3.2 %collective-permute-done.7 = bf16[128,4,2,64]{0,3,1,2:T(8,128)(2,1)S(1)} collective-permute-done((bf16[128,4,2,64]{0,3,1,2:T(8,128)(2,1)S(1)}, bf16[128,4,2,64]{0,3,1,2:T(8,128)(2,1)S(1)}, u32[]{:S(2)}, u32[]{:S(2)}) %collective-permute-start.7) | collective-permute-done | bytes 131104 | tf_op jit(solution)/shard_map/ppermute | solution.py:44
  42.3 0.5 collective-permute-done.9
  42.8 0.0 collective-permute-done.10
  42.9 0.5 collective-permute-done.11
  43.5 0.0 copy-start.1
  43.5 0.0 copy-start.4
  43.5 0.3 fusion.69
  43.8 0.2 fusion.39
  44.0 0.3 fusion.8
  44.4 0.1 reshape.236
  44.5 0.2 convolution_convert_fusion.2
  44.7 1.5 %collective-permute-start.12 = (bf16[32,1024]{1,0:T(8,128)(2,1)S(1)}, bf16[32,1024]{1,0:T(8,128)(2,1)}, u32[]{:S(2)}, u32[]{:S(2)}) collective-permute-start(bf16[32,1024]{1,0:T(8,128)(2,1)S(1)} %convolution_convert_fusion.2), channel_id=1, source_target_pairs={{0,2},{1,3},{2,0},{3,1},{4,6},{5,7},{6,4},{7,5},{8,10},{9,11},{10,... | collective-permute-start | bytes 196616 | tf_op jit(solution)/shard_map/ppermute | solution.py:204
  46.3 0.3 fusion.70
  46.6 0.2 fusion.41
  46.8 0.3 fusion.9
  47.2 0.1 reshape.237
  47.3 0.8 %convolution_convert_fusion.1 = bf16[32,1024]{1,0:T(8,128)(2,1)} fusion(bf16[32,256]{1,0:T(8,128)(2,1)S(1)} %reshape.237, bf16[256,1024]{1,0:T(8,128)(2,1)S(1)} %copy-done.1), kind=kOutput, calls=%fused_computation.29 | convolution fusion | flops 16809984 | bytes 606208 | tf_op jit(solution)/shard_map/dot_general | solution.py:202
  48.1 0.3 fusion.71
  48.4 0.2 fusion.43
  48.7 0.3 fusion.10
  49.1 0.1 reshape.238
  49.2 0.2 fusion.73
  49.4 0.7 %collective-permute-start.14 = (f32[32,1024]{1,0:T(8,128)S(1)}, f32[32,1024]{1,0:T(8,128)S(1)}, u32[]{:S(2)}, u32[]{:S(2)}) collective-permute-start(f32[32,1024]{1,0:T(8,128)S(1)} %fusion.73), channel_id=1, source_target_pairs={{0,1},{1,0},{2,3},{3,2},{4,5},{5,4},{6,7},{7,6},{8,9},{9,8},{10,11... | collective-permute-start | bytes 393224 | tf_op jit(solution)/shard_map/ppermute | solution.py:204
  50.1 0.3 fusion.72
  50.4 0.2 fusion.45
  50.6 0.3 fusion.11
  51.0 0.1 dot_general.73
  51.1 1.1 %collective-permute-done.13 = bf16[32,1024]{1,0:T(8,128)(2,1)} collective-permute-done((bf16[32,1024]{1,0:T(8,128)(2,1)}, bf16[32,1024]{1,0:T(8,128)(2,1)}, u32[]{:S(2)}, u32[]{:S(2)}) %collective-permute-start.13) | collective-permute-done | bytes 65568 | tf_op jit(solution)/shard_map/ppermute | solution.py:204
  52.1 0.9 %add_add_fusion = f32[32,1024]{1,0:T(8,128)S(1)} fusion(f32[32,1024]{1,0:T(8,128)S(1)} %collective-permute-done.14, bf16[32,1024]{1,0:T(8,128)(2,1)} %collective-permute-done.13, bf16[32,1024]{1,0:T(8,128)(2,1)} %collective-permute-done.12), kind=kLoop, calls=%fused_computation.104 | loop fusion | flops 131072 | bytes 393216 | tf_op jit(solution)/shard_map/add | solution.py:205
  53.0 0.1 add.282
  53.1 0.2 fusion.56
  53.3 0.7 %copy.29 = bf16[1,16,2,1024]{3,2,1,0:T(2,128)(2,1)} copy(bf16[1,16,2,1024]{3,1,2,0:T(8,128)(2,1)S(1)} %fusion.56) | data formatting | bytes 131072 | tf_op jit(solution)/shard_map/convert_element_type | solution.py:210
  (41 shorter events, 0.5 us)
Async XLA Ops:
  0.0 23.6 %copy-start = (bf16[768,1024]{1,0:T(8,128)(2,1)S(1)}, bf16[768,1024]{1,0:T(8,128)(2,1)}, u32[]{:S(2)}) copy-start(bf16[768,1024]{1,0:T(8,128)(2,1)} %param.8) | copy-start | bytes 4718596
  1.0 8.6 %collective-permute-start = (bf16[1,16,2,1024]{3,1,2,0:T(8,128)(2,1)S(1)}, bf16[1,16,2,1024]{3,1,2,0:T(8,128)(2,1)S(1)}, u32[]{:S(2)}, u32[]{:S(2)}) collective-permute-start(bf16[1,16,2,1024]{3,1,2,0:T(8,128)(2,1)S(1)} %copy.13), channel_id=1, source_target_pairs={{0,4},{4,8},{8,12},{12,16},{16,20},{20,24},{24,28},{1,5},{5,9},{9,... | collective-permute-start | bytes 196616 | tf_op jit(solution)/shard_map/ppermute | solution.py:18
  5.9 6.2 %collective-permute-start.1 = (bf16[1,16,2,1024]{3,1,2,0:T(8,128)(2,1)S(1)}, bf16[1,16,2,1024]{3,1,2,0:T(8,128)(2,1)S(1)}, u32[]{:S(2)}, u32[]{:S(2)}) collective-permute-start(bf16[1,16,2,1024]{3,1,2,0:T(8,128)(2,1)S(1)} %copy.13), channel_id=1, source_target_pairs={{4,0},{8,4},{12,8},{16,12},{20,16},{24,20},{28,24},{5,1},{9,5},{13... | collective-permute-start | bytes 196616 | tf_op jit(solution)/shard_map/ppermute | solution.py:19
  12.0 7.3 %collective-permute-start.2 = (bf16[3,16,2,1024]{3,1,2,0:T(8,128)(2,1)S(1)}, bf16[3,16,2,1024]{3,1,2,0:T(8,128)(2,1)S(1)}, u32[]{:S(2)}, u32[]{:S(2)}) collective-permute-start(bf16[3,16,2,1024]{3,1,2,0:T(8,128)(2,1)S(1)} %constant_dynamic-update-slice_fusion), channel_id=1, source_target_pairs={{0,1},{1,0},{2,3},{3,2},{4,5},{5,4},{6,7},{7,6},{8,9},{9,8},{10,11... | collective-permute-start | bytes 589832 | tf_op jit(solution)/shard_map/ppermute | solution.py:60
  12.0 7.3 %collective-permute-start.3 = (bf16[3,16,2,1024]{3,1,2,0:T(8,128)(2,1)S(1)}, bf16[3,16,2,1024]{3,1,2,0:T(8,128)(2,1)S(1)}, u32[]{:S(2)}, u32[]{:S(2)}) collective-permute-start(bf16[3,16,2,1024]{3,1,2,0:T(8,128)(2,1)S(1)} %constant_dynamic-update-slice_fusion), channel_id=1, source_target_pairs={{0,2},{1,3},{2,0},{3,1},{4,6},{5,7},{6,4},{7,5},{8,10},{9,11},{10,... | collective-permute-start | bytes 589832 | tf_op jit(solution)/shard_map/ppermute | solution.py:64
  13.7 7.2 %copy-start.5 = (f32[1024]{0:T(1024)S(1)}, f32[1024]{0:T(1024)}, u32[]{:S(2)}) copy-start(f32[1024]{0:T(1024)} %param.7) | copy-start | bytes 12292
  19.3 1.4 %collective-permute-start.4 = (bf16[3,16,2,1024]{3,1,2,0:T(8,128)(2,1)S(1)}, bf16[3,16,2,1024]{3,1,2,0:T(8,128)(2,1)S(1)}, u32[]{:S(2)}, u32[]{:S(2)}) collective-permute-start(bf16[3,16,2,1024]{3,1,2,0:T(8,128)(2,1)S(1)} %collective-permute-done.3), channel_id=1, source_target_pairs={{0,1},{1,0},{2,3},{3,2},{4,5},{5,4},{6,7},{7,6},{8,9},{9,8},{10,11... | collective-permute-start | bytes 589832 | tf_op jit(solution)/shard_map/ppermute | solution.py:66
  24.5 9.9 %collective-permute-start.5 = (bf16[128,4,2,64]{0,3,1,2:T(8,128)(2,1)S(1)}, bf16[128,4,2,64]{0,3,1,2:T(8,128)(2,1)S(1)}, u32[]{:S(2)}, u32[]{:S(2)}) collective-permute-start(bf16[128,4,2,64]{0,3,1,2:T(8,128)(2,1)S(1)} %get-tuple-element.85), channel_id=1, source_target_pairs={{0,16},{4,20},{8,24},{12,28},{16,0},{20,4},{24,8},{28,12},{1,17},{... | collective-permute-start | bytes 393224 | tf_op jit(solution)/shard_map/ppermute | solution.py:39
  27.7 9.1 %collective-permute-start.6 = (bf16[128,4,2,64]{0,3,1,2:T(8,128)(2,1)S(1)}, bf16[128,4,2,64]{0,3,1,2:T(8,128)(2,1)}, u32[]{:S(2)}, u32[]{:S(2)}) collective-permute-start(bf16[128,4,2,64]{0,3,1,2:T(8,128)(2,1)S(1)} %get-tuple-element.85), channel_id=1, source_target_pairs={{0,4},{4,8},{8,12},{12,0},{16,20},{20,24},{24,28},{28,16},{1,5},{5... | collective-permute-start | bytes 393224 | tf_op jit(solution)/shard_map/ppermute | solution.py:43
  29.6 12.7 %collective-permute-start.8 = (bf16[128,4,2,64]{0,3,1,2:T(8,128)(2,1)S(1)}, bf16[128,4,2,64]{0,3,1,2:T(8,128)(2,1)S(1)}, u32[]{:S(2)}, u32[]{:S(2)}) collective-permute-start(bf16[128,4,2,64]{0,3,1,2:T(8,128)(2,1)S(1)} %get-tuple-element.85), channel_id=1, source_target_pairs={{0,8},{4,12},{8,0},{12,4},{16,24},{20,28},{24,16},{28,20},{1,9},{5... | collective-permute-start | bytes 393224 | tf_op jit(solution)/shard_map/ppermute | solution.py:43
  29.9 12.9 %collective-permute-start.10 = (bf16[128,4,2,64]{0,3,1,2:T(8,128)(2,1)S(1)}, bf16[128,4,2,64]{0,3,1,2:T(8,128)(2,1)S(1)}, u32[]{:S(2)}, u32[]{:S(2)}) collective-permute-start(bf16[128,4,2,64]{0,3,1,2:T(8,128)(2,1)S(1)} %get-tuple-element.85), channel_id=1, source_target_pairs={{0,12},{4,0},{8,4},{12,8},{16,28},{20,16},{24,20},{28,24},{1,13},{... | collective-permute-start | bytes 393224 | tf_op jit(solution)/shard_map/ppermute | solution.py:43
  34.4 7.8 %collective-permute-start.7 = (bf16[128,4,2,64]{0,3,1,2:T(8,128)(2,1)S(1)}, bf16[128,4,2,64]{0,3,1,2:T(8,128)(2,1)S(1)}, u32[]{:S(2)}, u32[]{:S(2)}) collective-permute-start(bf16[128,4,2,64]{0,3,1,2:T(8,128)(2,1)S(1)} %collective-permute-done.5), channel_id=1, source_target_pairs={{0,4},{4,8},{8,12},{12,0},{16,20},{20,24},{24,28},{28,16},{1,5},{5... | collective-permute-start | bytes 393224 | tf_op jit(solution)/shard_map/ppermute | solution.py:44
  36.4 6.4 %collective-permute-start.9 = (bf16[128,4,2,64]{0,3,1,2:T(8,128)(2,1)S(1)}, bf16[128,4,2,64]{0,3,1,2:T(8,128)(2,1)S(1)}, u32[]{:S(2)}, u32[]{:S(2)}) collective-permute-start(bf16[128,4,2,64]{0,3,1,2:T(8,128)(2,1)S(1)} %collective-permute-done.5), channel_id=1, source_target_pairs={{0,8},{4,12},{8,0},{12,4},{16,24},{20,28},{24,16},{28,20},{1,9},{5... | collective-permute-start | bytes 393224 | tf_op jit(solution)/shard_map/ppermute | solution.py:44
  36.8 6.6 %collective-permute-start.11 = (bf16[128,4,2,64]{0,3,1,2:T(8,128)(2,1)S(1)}, bf16[128,4,2,64]{0,3,1,2:T(8,128)(2,1)S(1)}, u32[]{:S(2)}, u32[]{:S(2)}) collective-permute-start(bf16[128,4,2,64]{0,3,1,2:T(8,128)(2,1)S(1)} %collective-permute-done.5), channel_id=1, source_target_pairs={{0,12},{4,0},{8,4},{12,8},{16,28},{20,16},{24,20},{28,24},{1,13},{... | collective-permute-start | bytes 393224 | tf_op jit(solution)/shard_map/ppermute | solution.py:44
  43.5 1.1 %copy-start.1 = (bf16[256,1024]{1,0:T(8,128)(2,1)S(1)}, bf16[256,1024]{1,0:T(8,128)(2,1)}, u32[]{:S(2)}) copy-start(bf16[256,1024]{1,0:T(8,128)(2,1)} %param.9) | copy-start | bytes 1572868
  43.5 2.8 %copy-start.4 = (bf16[32,4,64]{2,0,1:T(8,128)(2,1)S(1)}, bf16[32,4,64]{2,0,1:T(8,128)(2,1)}, u32[]{:S(2)}) copy-start(bf16[32,4,64]{2,0,1:T(8,128)(2,1)} %get-tuple-element.62) | copy-start | bytes 49156
  44.7 7.4 %collective-permute-start.12 = (bf16[32,1024]{1,0:T(8,128)(2,1)S(1)}, bf16[32,1024]{1,0:T(8,128)(2,1)}, u32[]{:S(2)}, u32[]{:S(2)}) collective-permute-start(bf16[32,1024]{1,0:T(8,128)(2,1)S(1)} %convolution_convert_fusion.2), channel_id=1, source_target_pairs={{0,2},{1,3},{2,0},{3,1},{4,6},{5,7},{6,4},{7,5},{8,10},{9,11},{10,... | collective-permute-start | bytes 196616 | tf_op jit(solution)/shard_map/ppermute | solution.py:204
  46.3 1.9 %copy-start.3 = (bf16[32,4,64]{2,0,1:T(8,128)(2,1)S(1)}, bf16[32,4,64]{2,0,1:T(8,128)(2,1)}, u32[]{:S(2)}) copy-start(bf16[32,4,64]{2,0,1:T(8,128)(2,1)} %get-tuple-element.70) | copy-start | bytes 49156
  48.1 4.0 %collective-permute-start.13 = (bf16[32,1024]{1,0:T(8,128)(2,1)}, bf16[32,1024]{1,0:T(8,128)(2,1)}, u32[]{:S(2)}, u32[]{:S(2)}) collective-permute-start(bf16[32,1024]{1,0:T(8,128)(2,1)} %convolution_convert_fusion.1), channel_id=1, source_target_pairs={{0,3},{1,2},{2,1},{3,0},{4,7},{5,6},{6,5},{7,4},{8,11},{9,10},{10,... | collective-permute-start | bytes 196616 | tf_op jit(solution)/shard_map/ppermute | solution.py:204
  48.4 1.6 %copy-start.2 = (bf16[32,4,64]{2,0,1:T(8,128)(2,1)S(1)}, bf16[32,4,64]{2,0,1:T(8,128)(2,1)}, u32[]{:S(2)}) copy-start(bf16[32,4,64]{2,0,1:T(8,128)(2,1)} %get-tuple-element.71) | copy-start | bytes 49156
  49.4 2.8 %collective-permute-start.14 = (f32[32,1024]{1,0:T(8,128)S(1)}, f32[32,1024]{1,0:T(8,128)S(1)}, u32[]{:S(2)}, u32[]{:S(2)}) collective-permute-start(f32[32,1024]{1,0:T(8,128)S(1)} %fusion.73), channel_id=1, source_target_pairs={{0,1},{1,0},{2,3},{3,2},{4,5},{5,4},{6,7},{7,6},{8,9},{9,8},{10,11... | collective-permute-start | bytes 393224 | tf_op jit(solution)/shard_map/ppermute | solution.py:204

commit v9 on v7

--- a/solution.py
+++ b/solution.py
@@ -128,11 +128,7 @@
     positioned = summed.astype(jnp.bfloat16)
     local_tok = z_count * x_count * y_count
     heads_here = qkv_weight.shape[0] // (3 * HS)
-    slab_rows = (
-        positioned.reshape(z_count, x_count, groups, y_count, features)
-        .transpose(2, 0, 1, 3, 4)
-        .reshape(groups * local_tok, features)
-    )
+    slab_rows = positioned.reshape(-1, features)
     slab_tok = slab_rows.shape[0]
     projected = times_transposed(slab_rows, qkv_weight).astype(jnp.bfloat16)
     split_heads = projected.reshape(slab_tok, heads_here, 3, HS)
@@ -182,14 +178,21 @@
 
     rank = lax.axis_index("uly")
     chips, core, chip = groups // 2, rank % 2, rank // 2
-    pair_queries = queries.reshape(chips, 2 * local_tok, heads_here, HS)
+    pair_queries = queries.reshape(z_count, x_count, chips, 2 * y_count, heads_here, HS)
+
+    def rows_of_chip(which):
+        picked = lax.dynamic_index_in_dim(pair_queries, which, 2, keepdims=False)
+        return picked.reshape(2 * local_tok, heads_here, HS)
+
+    def split_by_core(partial):
+        return partial.reshape(z_count, x_count, 2, y_count, features)
     total = None
     for shift in range(1, chips):
-        far_rows = lax.dynamic_index_in_dim(pair_queries, (chip + shift) % chips, 0, keepdims=False)
+        far_rows = rows_of_chip((chip + shift) % chips)
         far_partial = jnp.dot(attend(far_rows), out_weight, preferred_element_type=jnp.float32)
-        far_partial = far_partial.astype(jnp.bfloat16).reshape(2, local_tok, features)
-        same_core = lax.dynamic_index_in_dim(far_partial, core, 0, keepdims=False)
-        other_core = lax.dynamic_index_in_dim(far_partial, 1 - core, 0, keepdims=False)
+        far_partial = split_by_core(far_partial.astype(jnp.bfloat16))
+        same_core = lax.dynamic_index_in_dim(far_partial, core, 2, keepdims=False)
+        other_core = lax.dynamic_index_in_dim(far_partial, 1 - core, 2, keepdims=False)
         far_sent = (same_core, other_core)
         to_other_core = [
             (i, ((i // 2 + shift) % chips) * 2 + 1 - i % 2) for i in range(groups)
@@ -198,17 +201,17 @@
             lax.ppermute(same_core, "uly", chip_shift(groups, shift)),
             lax.ppermute(other_core, "uly", to_other_core),
         ):
-            arrived = arrived.astype(jnp.float32).reshape(tokens.shape)
+            arrived = arrived.astype(jnp.float32)
             total = arrived if total is None else total + arrived
-    near_rows = lax.dynamic_index_in_dim(pair_queries, chip, 0, keepdims=False)
+    near_rows = rows_of_chip(chip)
     if total is not None:
         near_rows, unused = lax.optimization_barrier((near_rows, far_sent))
     near_partial = jnp.dot(attend(near_rows), out_weight, preferred_element_type=jnp.float32)
-    near_partial = near_partial.reshape(2, local_tok, features)
-    own = lax.dynamic_index_in_dim(near_partial, core, 0, keepdims=False)
-    for_partner = lax.dynamic_index_in_dim(near_partial, 1 - core, 0, keepdims=False)
+    near_partial = split_by_core(near_partial)
+    own = lax.dynamic_index_in_dim(near_partial, core, 2, keepdims=False)
+    for_partner = lax.dynamic_index_in_dim(near_partial, 1 - core, 2, keepdims=False)
     from_partner = lax.ppermute(for_partner, "uly", [(i, i ^ 1) for i in range(groups)])
-    near_sum = own.reshape(tokens.shape) + from_partner.reshape(tokens.shape)
+    near_sum = own + from_partner
     result = near_sum if total is None else near_sum + total
     return result.astype(jnp.bfloat16)
 

time: 52.3 us -> 53.6 us (1.025)
  waiting for transfers between devices: 15.7 us -> 18 us
  other arithmetic: 3.75 us -> 3.04 us
    ppermute x1, starting transfers between devices: 0.01 us -> 1.6 us  [on_device(): lax.ppermute(other_core, 'uly', to_other_core)]
    ppermute x1, waiting for transfers between devices: 0.49 us -> 1.84 us  [on_device(): lax.ppermute(same_core, 'uly', chip_shift(groups, shift))]
    ppermute x1, starting transfers between devices: 1.56 us -> 0.55 us  [on_device(): lax.ppermute(same_core, 'uly', chip_shift(groups, shift))]
    convert_element_type x0 -> x1, local copies, waits for them, and re-layouts: none -> 0.7 us  [on_device(): return result.astype(jnp.bfloat16)]
    convert_element_type x1, other arithmetic: 0.73 us -> 0.03 us  [on_device(): return result.astype(jnp.bfloat16)]
    ppermute x1, starting transfers between devices: 0.71 us -> 0.07 us  [on_device(): lax.ppermute(for_partner, 'uly', [(i, i ^ 1) for i in range(groups)])]
  transfers between devices with their start and end apart: 15 -> 15, of which waited for: 9 -> 9; matrix products, arithmetic and copies ran while one was open for 15% -> 10% of each run, Pallas kernels for 0% -> 0%
where the time goes in v9:
time: 53.6 us; the launch traced here: 53.1 us
  starting transfers between devices  20.9 us (39%)
  waiting for transfers between devices  18 us (34%)
  local copies, waits for them, and re-layouts  8.28 us (15%)
  other arithmetic  3.04 us (6%)
  matrix products  2.54 us (5%)
    ppermute x1, waiting for transfers between devices, gathered_by_chip(): far = lax.ppermute(piece, axis, chip_shift(size, shift))  5.62 us
    ppermute x1, starting transfers between devices, padded_2(): before = lax.ppermute(last, axis, up)  4.87 us
    ppermute x3, starting transfers between devices, relayed(): parts.append(lax.ppermute(piece, axis, pairs))  4.5 us
    unnamed x16, local copies, waits for them, and re-layouts  4.09 us
    ppermute x3, starting transfers between devices, relayed(): parts.append(lax.ppermute(crossed, axis, pairs))  3.24 us
    ppermute x3, waiting for transfers between devices, relayed(): parts.append(lax.ppermute(crossed, axis, pairs))  3.23 us
    ppermute x1, starting transfers between devices, relayed(): crossed = lax.ppermute(piece, axis, mirror)  3.2 us
    convert_element_type x1, other arithmetic, on_device(): positioned = summed.astype(jnp.bfloat16)  2.34 us
  transfers between devices with their start and end apart: 15, of which 9 were waited for; matrix products, arithmetic and copies ran while one was open for 10% of the time, Pallas kernels for 0%

profile of v9, /device:TPU:0, one launch (start us, length us, event | category | flops | bytes accessed | tf_op | source)
XLA Modules:
  0.0 53.1 jit_solution(9390006678771021497)
XLA Ops:
  0.0 0.0 copy-start
  0.0 1.0 %copy.24 = bf16[1,16,2,1024]{3,1,2,0:T(8,128)(2,1)S(1)} copy(bf16[1,16,2,1024]{3,2,1,0:T(2,128)(2,1)} %param.5) | data formatting | bytes 131072 | tf_op args[0]
  1.0 4.9 %collective-permute-start = (bf16[1,16,2,1024]{3,1,2,0:T(8,128)(2,1)S(1)}, bf16[1,16,2,1024]{3,1,2,0:T(8,128)(2,1)S(1)}, u32[]{:S(2)}, u32[]{:S(2)}) collective-permute-start(bf16[1,16,2,1024]{3,1,2,0:T(8,128)(2,1)S(1)} %copy.24), channel_id=1, source_target_pairs={{0,4},{4,8},{8,12},{12,16},{16,20},{20,24},{24,28},{1,5},{5,9},{9,... | collective-permute-start | bytes 196616 | tf_op jit(solution)/shard_map/ppermute | solution.py:18
  5.9 1.3 %collective-permute-start.1 = (bf16[1,16,2,1024]{3,1,2,0:T(8,128)(2,1)S(1)}, bf16[1,16,2,1024]{3,1,2,0:T(8,128)(2,1)S(1)}, u32[]{:S(2)}, u32[]{:S(2)}) collective-permute-start(bf16[1,16,2,1024]{3,1,2,0:T(8,128)(2,1)S(1)} %copy.24), channel_id=1, source_target_pairs={{4,0},{8,4},{12,8},{16,12},{20,16},{24,20},{28,24},{5,1},{9,5},{13... | collective-permute-start | bytes 196616 | tf_op jit(solution)/shard_map/ppermute | solution.py:19
  7.2 1.3 %fusion.48 = (f32[1,1024]{1,0:T(1,128)S(1)}, f32[1,1024]{1,0:T(1,128)S(1)}, f32[1,1024]{1,0:T(1,128)S(1)}, f32[1,1024]{1,0:T(1,128)S(1)}, f32[1,1024]{1,0:T(1,12...) fusion(f32[27,1024]{1,0:T(8,128)} %param.6), kind=kLoop, calls=%fused_computation.114 | loop fusion | bytes 155648 | tf_op jit(solution)/shard_map/slice | solution.py:121
  8.5 1.0 %fusion.49 = (f32[1,1024]{1,0:T(1,128)S(1)}, f32[1,1024]{1,0:T(1,128)S(1)}, f32[1,1024]{1,0:T(1,128)S(1)}, f32[1,1024]{1,0:T(1,128)S(1)}, f32[1,1024]{1,0:T(1,12...) fusion(f32[27,1024]{1,0:T(8,128)} %param.6), kind=kLoop, calls=%fused_computation.115 | loop fusion | bytes 65536 | tf_op jit(solution)/shard_map/slice | solution.py:121
  9.6 0.0 collective-permute-done
  9.6 0.9 %constant_dynamic-update-slice_fusion.1 = bf16[3,16,2,1024]{3,1,2,0:T(8,128)(2,1)S(1)} fusion(bf16[3,16,2,1024]{3,1,2,0:T(8,128)(2,1)S(1)} %constant_dynamic-update-slice_fusion.2, bf16[1,16,2,1024]{3,2,1,0:T(2,128)(2,1)} %param.5), kind=kLoop, calls=%fused_computation.92 | loop fusion | bytes 131072
  10.4 1.6 %collective-permute-done.1 = bf16[1,16,2,1024]{3,1,2,0:T(8,128)(2,1)S(1)} collective-permute-done((bf16[1,16,2,1024]{3,1,2,0:T(8,128)(2,1)S(1)}, bf16[1,16,2,1024]{3,1,2,0:T(8,128)(2,1)S(1)}, u32[]{:S(2)}, u32[]{:S(2)}) %collective-permute-start.1) | collective-permute-done | bytes 65568 | tf_op jit(solution)/shard_map/ppermute | solution.py:19
  12.0 0.0 collective-permute-start.2
  12.0 1.6 %collective-permute-start.3 = (bf16[3,16,2,1024]{3,1,2,0:T(8,128)(2,1)S(1)}, bf16[3,16,2,1024]{3,1,2,0:T(8,128)(2,1)S(1)}, u32[]{:S(2)}, u32[]{:S(2)}) collective-permute-start(bf16[3,16,2,1024]{3,1,2,0:T(8,128)(2,1)S(1)} %constant_dynamic-update-slice_fusion), channel_id=1, source_target_pairs={{0,2},{1,3},{2,0},{3,1},{4,6},{5,7},{6,4},{7,5},{8,10},{9,11},{10,... | collective-permute-start | bytes 589832 | tf_op jit(solution)/shard_map/ppermute | solution.py:64
  13.6 0.1 broadcast_in_dim.27
  13.7 0.0 copy-start.2
  13.7 5.6 %collective-permute-done.3 = bf16[3,16,2,1024]{3,1,2,0:T(8,128)(2,1)S(1)} collective-permute-done((bf16[3,16,2,1024]{3,1,2,0:T(8,128)(2,1)S(1)}, bf16[3,16,2,1024]{3,1,2,0:T(8,128)(2,1)S(1)}, u32[]{:S(2)}, u32[]{:S(2)}) %collective-permute-start.3) | collective-permute-done | bytes 196640 | tf_op jit(solution)/shard_map/ppermute | solution.py:64
  19.3 0.0 collective-permute-start.4
  19.3 0.0 collective-permute-done.2
  19.4 1.4 %collective-permute-done.4 = bf16[3,16,2,1024]{3,1,2,0:T(8,128)(2,1)S(1)} collective-permute-done((bf16[3,16,2,1024]{3,1,2,0:T(8,128)(2,1)S(1)}, bf16[3,16,2,1024]{3,1,2,0:T(8,128)(2,1)S(1)}, u32[]{:S(2)}, u32[]{:S(2)}) %collective-permute-start.4) | collective-permute-done | bytes 196640 | tf_op jit(solution)/shard_map/ppermute | solution.py:66
  20.8 0.1 fusion.46
  20.9 0.0 copy-done.2
  20.9 2.3 %add_convert_fusion = bf16[1,16,8,1024]{3,1,2,0:T(8,128)(2,1)S(1)} fusion(bf16[1,16,8,1024]{3,1,2,0:T(8,128)(2,1)S(1)} %bitcast.125, bf16[1,16,8,1024]{3,1,2,0:T(8,128)(2,1)S(1)} %bitcast.124, bf16[1,16,8,1024]{3,1,2,0:T(8,128)(2,1)S(1)} %bitcast.123, bf16[3,16,8,1024]{3,1,2,0:T(8,128)(2,1)S(1)} %bitcast.122, f32[1024]{0:T(1024)S(1)} %bitcast.158, ...), kind=kLoop, calls=%fused_computation.77 | loop fusion | flops 10878976 | bytes 1949696 | tf_op jit(solution)/shard_map/convert_element_type | solution.py:128
  23.2 0.0 copy-done
  23.3 0.7 %convolution_convert_fusion = bf16[128,768]{1,0:T(8,128)(2,1)S(1)} fusion(bf16[768,1024]{1,0:T(8,128)(2,1)S(1)} %copy-done, bf16[1,16,8,1024]{3,1,2,0:T(8,128)(2,1)S(1)} %add_convert_fusion), kind=kOutput, calls=%fused_computation.26 | convolution fusion | flops 201424896 | bytes 2031616 | tf_op jit(solution)/shard_map/dot_general | solution.py:100
  23.9 0.2 copy.31
  24.2 3.2 %collective-permute-start.5 = (bf16[128,4,2,64]{0,3,1,2:T(8,128)(2,1)S(1)}, bf16[128,4,2,64]{0,3,1,2:T(8,128)(2,1)S(1)}, u32[]{:S(2)}, u32[]{:S(2)}) collective-permute-start(bf16[128,4,2,64]{0,3,1,2:T(8,128)(2,1)S(1)} %get-tuple-element.45), channel_id=1, source_target_pairs={{0,16},{4,20},{8,24},{12,28},{16,0},{20,4},{24,8},{28,12},{1,17},{... | collective-permute-start | bytes 393224 | tf_op jit(solution)/shard_map/ppermute | solution.py:39
  27.4 1.9 %collective-permute-start.6 = (bf16[128,4,2,64]{0,3,1,2:T(8,128)(2,1)S(1)}, bf16[128,4,2,64]{0,3,1,2:T(8,128)(2,1)}, u32[]{:S(2)}, u32[]{:S(2)}) collective-permute-start(bf16[128,4,2,64]{0,3,1,2:T(8,128)(2,1)S(1)} %get-tuple-element.45), channel_id=1, source_target_pairs={{0,4},{4,8},{8,12},{12,0},{16,20},{20,24},{24,28},{28,16},{1,5},{5... | collective-permute-start | bytes 393224 | tf_op jit(solution)/shard_map/ppermute | solution.py:43
  29.2 0.3 collective-permute-start.8
  29.6 2.3 %collective-permute-start.10 = (bf16[128,4,2,64]{0,3,1,2:T(8,128)(2,1)S(1)}, bf16[128,4,2,64]{0,3,1,2:T(8,128)(2,1)S(1)}, u32[]{:S(2)}, u32[]{:S(2)}) collective-permute-start(bf16[128,4,2,64]{0,3,1,2:T(8,128)(2,1)S(1)} %get-tuple-element.45), channel_id=1, source_target_pairs={{0,12},{4,0},{8,4},{12,8},{16,28},{20,16},{24,20},{28,24},{1,13},{... | collective-permute-start | bytes 393224 | tf_op jit(solution)/shard_map/ppermute | solution.py:43
  31.9 0.1 copy.32
  32.0 0.1 constant_dynamic-slice_fusion.2
  32.1 2.0 %collective-permute-done.5 = bf16[128,4,2,64]{0,3,1,2:T(8,128)(2,1)S(1)} collective-permute-done((bf16[128,4,2,64]{0,3,1,2:T(8,128)(2,1)S(1)}, bf16[128,4,2,64]{0,3,1,2:T(8,128)(2,1)S(1)}, u32[]{:S(2)}, u32[]{:S(2)}) %collective-permute-start.5) | collective-permute-done | bytes 131104 | tf_op jit(solution)/shard_map/ppermute | solution.py:39
  34.1 1.9 %collective-permute-start.7 = (bf16[128,4,2,64]{0,3,1,2:T(8,128)(2,1)S(1)}, bf16[128,4,2,64]{0,3,1,2:T(8,128)(2,1)S(1)}, u32[]{:S(2)}, u32[]{:S(2)}) collective-permute-start(bf16[128,4,2,64]{0,3,1,2:T(8,128)(2,1)S(1)} %collective-permute-done.5), channel_id=1, source_target_pairs={{0,4},{4,8},{8,12},{12,0},{16,20},{20,24},{24,28},{28,16},{1,5},{5... | collective-permute-start | bytes 393224 | tf_op jit(solution)/shard_map/ppermute | solution.py:44
  36.0 0.0 collective-permute-start.9
  36.0 0.4 collective-permute-done.6
  36.4 1.3 %collective-permute-start.11 = (bf16[128,4,2,64]{0,3,1,2:T(8,128)(2,1)S(1)}, bf16[128,4,2,64]{0,3,1,2:T(8,128)(2,1)S(1)}, u32[]{:S(2)}, u32[]{:S(2)}) collective-permute-start(bf16[128,4,2,64]{0,3,1,2:T(8,128)(2,1)S(1)} %collective-permute-done.5), channel_id=1, source_target_pairs={{0,12},{4,0},{8,4},{12,8},{16,28},{20,16},{24,20},{28,24},{1,13},{... | collective-permute-start | bytes 393224 | tf_op jit(solution)/shard_map/ppermute | solution.py:44
  37.8 0.9 %constant_dynamic-update-slice_fusion.8 = bf16[1024,4,2,64]{0,3,1,2:T(8,128)(2,1)S(1)} fusion(bf16[1024,4,2,64]{0,3,1,2:T(8,128)(2,1)S(1)} %constant_dynamic-update-slice_fusion.9, bf16[128,4,2,64]{0,3,1,2:T(8,128)(2,1)} %collective-permute-done.6), kind=kLoop, calls=%fused_computation.99 | loop fusion | bytes 262144
  38.7 3.2 %collective-permute-done.7 = bf16[128,4,2,64]{0,3,1,2:T(8,128)(2,1)S(1)} collective-permute-done((bf16[128,4,2,64]{0,3,1,2:T(8,128)(2,1)S(1)}, bf16[128,4,2,64]{0,3,1,2:T(8,128)(2,1)S(1)}, u32[]{:S(2)}, u32[]{:S(2)}) %collective-permute-start.7) | collective-permute-done | bytes 131104 | tf_op jit(solution)/shard_map/ppermute | solution.py:44
  41.9 0.0 collective-permute-done.8
  41.9 0.9 %constant_dynamic-update-slice_fusion.6 = bf16[1024,4,2,64]{0,3,1,2:T(8,128)(2,1)S(1)} fusion(bf16[1024,4,2,64]{0,3,1,2:T(8,128)(2,1)S(1)} %constant_dynamic-update-slice_fusion.7, bf16[128,4,2,64]{0,3,1,2:T(8,128)(2,1)} %collective-permute-done.8), kind=kLoop, calls=%fused_computation.97 | loop fusion | bytes 262144
  42.9 0.0 collective-permute-done.9
  42.9 0.0 collective-permute-done.10
  43.0 0.1 collective-permute-done.11
  43.1 0.4 fusion.50
  43.5 0.0 copy-start.1
  43.5 0.3 fusion.6
  43.8 0.4 fusion.5
  44.2 0.1 copy.34
  44.2 0.1 reshape.209
  44.4 0.2 copy-done.1
  44.5 0.2 convolution_convert_fusion.1
  44.7 0.1 reshape.210
  44.8 0.1 constant_dynamic-slice_fusion
  45.0 0.4 fusion.51
  45.3 0.3 fusion.8
  45.7 0.4 fusion.4
  46.0 0.1 copy.37
  46.1 0.1 reshape.211
  46.2 0.2 fusion.37
  46.4 0.1 collective-permute-start.12
  46.5 1.6 %collective-permute-start.14 = (bf16[1,16,2,1024]{3,1,2,0:T(8,128)(2,1)S(1)}, bf16[1,16,2,1024]{3,1,2,0:T(8,128)(2,1)S(1)}, u32[]{:S(2)}, u32[]{:S(2)}) collective-permute-start(bf16[1,16,2,1024]{3,1,2,0:T(8,128)(2,1)S(1)} %bitcast.132), channel_id=1, source_target_pairs={{0,3},{1,2},{2,1},{3,0},{4,7},{5,6},{6,5},{7,4},{8,11},{9,10},{10,... | collective-permute-start | bytes 196616 | tf_op jit(solution)/shard_map/ppermute | solution.py:202
  48.1 0.5 %collective-permute-start.13 = (bf16[1,16,2,1024]{3,1,2,0:T(8,128)(2,1)S(1)}, bf16[1,16,2,1024]{3,1,2,0:T(8,128)(2,1)S(1)}, u32[]{:S(2)}, u32[]{:S(2)}) collective-permute-start(bf16[1,16,2,1024]{3,1,2,0:T(8,128)(2,1)S(1)} %bitcast.131), channel_id=1, source_target_pairs={{0,2},{1,3},{2,0},{3,1},{4,6},{5,7},{6,4},{7,5},{8,10},{9,11},{10,... | collective-permute-start | bytes 196616 | tf_op jit(solution)/shard_map/ppermute | solution.py:201
  48.7 1.9 %collective-permute-done.14 = bf16[1,16,2,1024]{3,1,2,0:T(8,128)(2,1)S(1)} collective-permute-done((bf16[1,16,2,1024]{3,1,2,0:T(8,128)(2,1)S(1)}, bf16[1,16,2,1024]{3,1,2,0:T(8,128)(2,1)S(1)}, u32[]{:S(2)}, u32[]{:S(2)}) %collective-permute-start.14) | collective-permute-done | bytes 65568 | tf_op jit(solution)/shard_map/ppermute | solution.py:202
  50.5 1.8 %collective-permute-done.13 = bf16[1,16,2,1024]{3,1,2,0:T(8,128)(2,1)S(1)} collective-permute-done((bf16[1,16,2,1024]{3,1,2,0:T(8,128)(2,1)S(1)}, bf16[1,16,2,1024]{3,1,2,0:T(8,128)(2,1)S(1)}, u32[]{:S(2)}, u32[]{:S(2)}) %collective-permute-start.13) | collective-permute-done | bytes 65568 | tf_op jit(solution)/shard_map/ppermute | solution.py:201
  52.4 0.0 collective-permute-done.12
  52.4 0.7 %copy.39 = bf16[1,16,2,1024]{3,2,1,0:T(2,128)(2,1)} copy(bf16[1,16,2,1024]{3,1,2,0:T(8,128)(2,1)S(1)} %fusion.44) | data formatting | bytes 131072 | tf_op jit(solution)/shard_map/convert_element_type | solution.py:216
  (21 shorter events, 0.4 us)
Async XLA Ops:
  0.0 23.2 %copy-start = (bf16[768,1024]{1,0:T(8,128)(2,1)S(1)}, bf16[768,1024]{1,0:T(8,128)(2,1)}, u32[]{:S(2)}) copy-start(bf16[768,1024]{1,0:T(8,128)(2,1)} %param.8) | copy-start | bytes 4718596
  1.0 8.6 %collective-permute-start = (bf16[1,16,2,1024]{3,1,2,0:T(8,128)(2,1)S(1)}, bf16[1,16,2,1024]{3,1,2,0:T(8,128)(2,1)S(1)}, u32[]{:S(2)}, u32[]{:S(2)}) collective-permute-start(bf16[1,16,2,1024]{3,1,2,0:T(8,128)(2,1)S(1)} %copy.24), channel_id=1, source_target_pairs={{0,4},{4,8},{8,12},{12,16},{16,20},{20,24},{24,28},{1,5},{5,9},{9,... | collective-permute-start | bytes 196616 | tf_op jit(solution)/shard_map/ppermute | solution.py:18
  5.9 6.2 %collective-permute-start.1 = (bf16[1,16,2,1024]{3,1,2,0:T(8,128)(2,1)S(1)}, bf16[1,16,2,1024]{3,1,2,0:T(8,128)(2,1)S(1)}, u32[]{:S(2)}, u32[]{:S(2)}) collective-permute-start(bf16[1,16,2,1024]{3,1,2,0:T(8,128)(2,1)S(1)} %copy.24), channel_id=1, source_target_pairs={{4,0},{8,4},{12,8},{16,12},{20,16},{24,20},{28,24},{5,1},{9,5},{13... | collective-permute-start | bytes 196616 | tf_op jit(solution)/shard_map/ppermute | solution.py:19
  12.0 7.3 %collective-permute-start.2 = (bf16[3,16,2,1024]{3,1,2,0:T(8,128)(2,1)S(1)}, bf16[3,16,2,1024]{3,1,2,0:T(8,128)(2,1)S(1)}, u32[]{:S(2)}, u32[]{:S(2)}) collective-permute-start(bf16[3,16,2,1024]{3,1,2,0:T(8,128)(2,1)S(1)} %constant_dynamic-update-slice_fusion), channel_id=1, source_target_pairs={{0,1},{1,0},{2,3},{3,2},{4,5},{5,4},{6,7},{7,6},{8,9},{9,8},{10,11... | collective-permute-start | bytes 589832 | tf_op jit(solution)/shard_map/ppermute | solution.py:60
  12.0 7.3 %collective-permute-start.3 = (bf16[3,16,2,1024]{3,1,2,0:T(8,128)(2,1)S(1)}, bf16[3,16,2,1024]{3,1,2,0:T(8,128)(2,1)S(1)}, u32[]{:S(2)}, u32[]{:S(2)}) collective-permute-start(bf16[3,16,2,1024]{3,1,2,0:T(8,128)(2,1)S(1)} %constant_dynamic-update-slice_fusion), channel_id=1, source_target_pairs={{0,2},{1,3},{2,0},{3,1},{4,6},{5,7},{6,4},{7,5},{8,10},{9,11},{10,... | collective-permute-start | bytes 589832 | tf_op jit(solution)/shard_map/ppermute | solution.py:64
  13.7 7.2 %copy-start.2 = (f32[1024]{0:T(1024)S(1)}, f32[1024]{0:T(1024)}, u32[]{:S(2)}) copy-start(f32[1024]{0:T(1024)} %param.7) | copy-start | bytes 12292
  19.3 1.4 %collective-permute-start.4 = (bf16[3,16,2,1024]{3,1,2,0:T(8,128)(2,1)S(1)}, bf16[3,16,2,1024]{3,1,2,0:T(8,128)(2,1)S(1)}, u32[]{:S(2)}, u32[]{:S(2)}) collective-permute-start(bf16[3,16,2,1024]{3,1,2,0:T(8,128)(2,1)S(1)} %collective-permute-done.3), channel_id=1, source_target_pairs={{0,1},{1,0},{2,3},{3,2},{4,5},{5,4},{6,7},{7,6},{8,9},{9,8},{10,11... | collective-permute-start | bytes 589832 | tf_op jit(solution)/shard_map/ppermute | solution.py:66
  24.2 9.9 %collective-permute-start.5 = (bf16[128,4,2,64]{0,3,1,2:T(8,128)(2,1)S(1)}, bf16[128,4,2,64]{0,3,1,2:T(8,128)(2,1)S(1)}, u32[]{:S(2)}, u32[]{:S(2)}) collective-permute-start(bf16[128,4,2,64]{0,3,1,2:T(8,128)(2,1)S(1)} %get-tuple-element.45), channel_id=1, source_target_pairs={{0,16},{4,20},{8,24},{12,28},{16,0},{20,4},{24,8},{28,12},{1,17},{... | collective-permute-start | bytes 393224 | tf_op jit(solution)/shard_map/ppermute | solution.py:39
  27.4 9.1 %collective-permute-start.6 = (bf16[128,4,2,64]{0,3,1,2:T(8,128)(2,1)S(1)}, bf16[128,4,2,64]{0,3,1,2:T(8,128)(2,1)}, u32[]{:S(2)}, u32[]{:S(2)}) collective-permute-start(bf16[128,4,2,64]{0,3,1,2:T(8,128)(2,1)S(1)} %get-tuple-element.45), channel_id=1, source_target_pairs={{0,4},{4,8},{8,12},{12,0},{16,20},{20,24},{24,28},{28,16},{1,5},{5... | collective-permute-start | bytes 393224 | tf_op jit(solution)/shard_map/ppermute | solution.py:43
  29.2 12.7 %collective-permute-start.8 = (bf16[128,4,2,64]{0,3,1,2:T(8,128)(2,1)S(1)}, bf16[128,4,2,64]{0,3,1,2:T(8,128)(2,1)}, u32[]{:S(2)}, u32[]{:S(2)}) collective-permute-start(bf16[128,4,2,64]{0,3,1,2:T(8,128)(2,1)S(1)} %get-tuple-element.45), channel_id=1, source_target_pairs={{0,8},{4,12},{8,0},{12,4},{16,24},{20,28},{24,16},{28,20},{1,9},{5... | collective-permute-start | bytes 393224 | tf_op jit(solution)/shard_map/ppermute | solution.py:43
  29.6 13.4 %collective-permute-start.10 = (bf16[128,4,2,64]{0,3,1,2:T(8,128)(2,1)S(1)}, bf16[128,4,2,64]{0,3,1,2:T(8,128)(2,1)S(1)}, u32[]{:S(2)}, u32[]{:S(2)}) collective-permute-start(bf16[128,4,2,64]{0,3,1,2:T(8,128)(2,1)S(1)} %get-tuple-element.45), channel_id=1, source_target_pairs={{0,12},{4,0},{8,4},{12,8},{16,28},{20,16},{24,20},{28,24},{1,13},{... | collective-permute-start | bytes 393224 | tf_op jit(solution)/shard_map/ppermute | solution.py:43
  34.1 7.8 %collective-permute-start.7 = (bf16[128,4,2,64]{0,3,1,2:T(8,128)(2,1)S(1)}, bf16[128,4,2,64]{0,3,1,2:T(8,128)(2,1)S(1)}, u32[]{:S(2)}, u32[]{:S(2)}) collective-permute-start(bf16[128,4,2,64]{0,3,1,2:T(8,128)(2,1)S(1)} %collective-permute-done.5), channel_id=1, source_target_pairs={{0,4},{4,8},{8,12},{12,0},{16,20},{20,24},{24,28},{28,16},{1,5},{5... | collective-permute-start | bytes 393224 | tf_op jit(solution)/shard_map/ppermute | solution.py:44
  36.0 6.9 %collective-permute-start.9 = (bf16[128,4,2,64]{0,3,1,2:T(8,128)(2,1)S(1)}, bf16[128,4,2,64]{0,3,1,2:T(8,128)(2,1)S(1)}, u32[]{:S(2)}, u32[]{:S(2)}) collective-permute-start(bf16[128,4,2,64]{0,3,1,2:T(8,128)(2,1)S(1)} %collective-permute-done.5), channel_id=1, source_target_pairs={{0,8},{4,12},{8,0},{12,4},{16,24},{20,28},{24,16},{28,20},{1,9},{5... | collective-permute-start | bytes 393224 | tf_op jit(solution)/shard_map/ppermute | solution.py:44
  36.4 6.6 %collective-permute-start.11 = (bf16[128,4,2,64]{0,3,1,2:T(8,128)(2,1)S(1)}, bf16[128,4,2,64]{0,3,1,2:T(8,128)(2,1)S(1)}, u32[]{:S(2)}, u32[]{:S(2)}) collective-permute-start(bf16[128,4,2,64]{0,3,1,2:T(8,128)(2,1)S(1)} %collective-permute-done.5), channel_id=1, source_target_pairs={{0,12},{4,0},{8,4},{12,8},{16,28},{20,16},{24,20},{28,24},{1,13},{... | collective-permute-start | bytes 393224 | tf_op jit(solution)/shard_map/ppermute | solution.py:44
  43.5 1.1 %copy-start.1 = (bf16[256,1024]{1,0:T(8,128)(2,1)S(1)}, bf16[256,1024]{1,0:T(8,128)(2,1)}, u32[]{:S(2)}) copy-start(bf16[256,1024]{1,0:T(8,128)(2,1)} %param.9) | copy-start | bytes 1572868
  46.4 5.9 %collective-permute-start.12 = (f32[1,16,2,1024]{3,1,2,0:T(8,128)S(1)}, f32[1,16,2,1024]{3,1,2,0:T(8,128)S(1)}, u32[]{:S(2)}, u32[]{:S(2)}) collective-permute-start(f32[1,16,2,1024]{3,1,2,0:T(8,128)S(1)} %dynamic-slice_bitcast_fusion), channel_id=1, source_target_pairs={{0,1},{1,0},{2,3},{3,2},{4,5},{5,4},{6,7},{7,6},{8,9},{9,8},{10,11... | collective-permute-start | bytes 393224 | tf_op jit(solution)/shard_map/ppermute | solution.py:213
  46.5 4.0 %collective-permute-start.14 = (bf16[1,16,2,1024]{3,1,2,0:T(8,128)(2,1)S(1)}, bf16[1,16,2,1024]{3,1,2,0:T(8,128)(2,1)S(1)}, u32[]{:S(2)}, u32[]{:S(2)}) collective-permute-start(bf16[1,16,2,1024]{3,1,2,0:T(8,128)(2,1)S(1)} %bitcast.132), channel_id=1, source_target_pairs={{0,3},{1,2},{2,1},{3,0},{4,7},{5,6},{6,5},{7,4},{8,11},{9,10},{10,... | collective-permute-start | bytes 196616 | tf_op jit(solution)/shard_map/ppermute | solution.py:202
  48.1 4.3 %collective-permute-start.13 = (bf16[1,16,2,1024]{3,1,2,0:T(8,128)(2,1)S(1)}, bf16[1,16,2,1024]{3,1,2,0:T(8,128)(2,1)S(1)}, u32[]{:S(2)}, u32[]{:S(2)}) collective-permute-start(bf16[1,16,2,1024]{3,1,2,0:T(8,128)(2,1)S(1)} %bitcast.131), channel_id=1, source_target_pairs={{0,2},{1,3},{2,0},{3,1},{4,6},{5,7},{6,4},{7,5},{8,10},{9,11},{10,... | collective-permute-start | bytes 196616 | tf_op jit(solution)/shard_map/ppermute | solution.py:201

commit v10 on v7

--- a/solution.py
+++ b/solution.py
@@ -107,24 +107,28 @@
     groups = lax.axis_size("uly")
     with_halo = padded_2(tokens, (("blk", 0),), 1)
     slab_in = gathered_by_chip(with_halo, "uly")
+    lanes = 128 if features % 128 == 0 else features
+    tile_shape = (features // lanes, lanes)
     slab_in = slab_in.transpose(1, 2, 0, 3, 4).reshape(
-        z_count + 2, x_count, groups * y_count, features
+        z_count + 2, x_count, groups * y_count, *tile_shape
     )
     slab_y = groups * y_count
-    padded = jnp.pad(slab_in, ((0, 0), (1, 1), (1, 1), (0, 0)))
-    summed = slab_in[1 : 1 + z_count].astype(jnp.float32) + conv_bias
+    padded = jnp.pad(slab_in, ((0, 0), (1, 1), (1, 1), (0, 0), (0, 0)))
+    tap_weight = conv_weight.reshape(27, *tile_shape)
+    summed = slab_in[1 : 1 + z_count].astype(jnp.float32) + conv_bias.reshape(tile_shape)
     for step_z in range(3):
         for step_x in range(3):
             for step_y in range(3):
                 summed = (
                     summed
-                    + conv_weight[9 * step_z + 3 * step_x + step_y]
+                    + tap_weight[9 * step_z + 3 * step_x + step_y]
                     * padded[
                         step_z : step_z + z_count,
                         step_x : step_x + x_count,
                         step_y : step_y + slab_y,
                     ]
                 )
+    summed = summed.reshape(z_count, x_count, slab_y, features)
     positioned = summed.astype(jnp.bfloat16)
     local_tok = z_count * x_count * y_count
     heads_here = qkv_weight.shape[0] // (3 * HS)

time: 52.3 us -> 55.5 us (1.061)
  other arithmetic: 3.75 us -> 6.63 us
  local copies, waits for them, and re-layouts: 8.45 us -> 9.53 us
  waiting for transfers between devices: 15.7 us -> 14.7 us
    convert_element_type x0 -> x1, other arithmetic: none -> 2.63 us  [on_device(): tap_weight[9 * step_z + 3 * step_x + step_y]]
    unnamed x16 -> x15, local copies, waits for them, and re-layouts: 4.1 us -> 3.2 us
    ppermute x1, waiting for transfers between devices: 5.62 us -> 4.85 us  [gathered_by_chip(): far = lax.ppermute(piece, axis, chip_shift(size, shift))]
    slice x3 -> x2, local copies, waits for them, and re-layouts: 2.41 us -> 2.58 us  [on_device(): tap_weight[9 * step_z + 3 * step_x + step_y]]
  transfers between devices with their start and end apart: 15 -> 15, of which waited for: 9 -> 9; matrix products, arithmetic and copies ran while one was open for 15% -> 16% of each run, Pallas kernels for 0% -> 0%
where the time goes in v10:
time: 55.5 us; the launch traced here: 54.9 us
  starting transfers between devices  21.1 us (38%)
  waiting for transfers between devices  14.7 us (26%)
  local copies, waits for them, and re-layouts  9.53 us (17%)
  other arithmetic  6.63 us (12%)
  matrix products  2.51 us (5%)
    ppermute x1, starting transfers between devices, padded_2(): before = lax.ppermute(last, axis, up)  5 us
    ppermute x1, waiting for transfers between devices, gathered_by_chip(): far = lax.ppermute(piece, axis, chip_shift(size, shift))  4.85 us
    ppermute x3, starting transfers between devices, relayed(): parts.append(lax.ppermute(piece, axis, pairs))  4.5 us
    ppermute x1, starting transfers between devices, relayed(): crossed = lax.ppermute(piece, axis, mirror)  3.23 us
    ppermute x3, starting transfers between devices, relayed(): parts.append(lax.ppermute(crossed, axis, pairs))  3.22 us
    ppermute x3, waiting for transfers between devices, relayed(): parts.append(lax.ppermute(crossed, axis, pairs))  3.22 us
    unnamed x15, local copies, waits for them, and re-layouts  3.2 us
    convert_element_type x1, other arithmetic, on_device(): tap_weight[9 * step_z + 3 * step_x + step_y]  2.63 us
  transfers between devices with their start and end apart: 15, of which 9 were waited for; matrix products, arithmetic and copies ran while one was open for 16% of the time, Pallas kernels for 0%

profile of v10, /device:TPU:0, one launch (start us, length us, event | category | flops | bytes accessed | tf_op | source)
XLA Modules:
  0.0 54.9 jit_solution(17752376524857443978)
XLA Ops:
  0.0 5.0 %collective-permute-start = (bf16[1,16,2,1024]{3,2,1,0:T(2,128)(2,1)}, bf16[1,16,2,1024]{3,2,1,0:T(2,128)(2,1)S(1)}, u32[]{:S(2)}, u32[]{:S(2)}) collective-permute-start(bf16[1,16,2,1024]{3,2,1,0:T(2,128)(2,1)} %param.5), channel_id=1, source_target_pairs={{0,4},{4,8},{8,12},{12,16},{16,20},{20,24},{24,28},{1,5},{5,9},{9,... | collective-permute-start | bytes 196616 | tf_op jit(solution)/shard_map/ppermute | solution.py:18
  5.0 1.3 %collective-permute-start.1 = (bf16[1,16,2,1024]{3,2,1,0:T(2,128)(2,1)}, bf16[1,16,2,1024]{3,2,1,0:T(2,128)(2,1)S(1)}, u32[]{:S(2)}, u32[]{:S(2)}) collective-permute-start(bf16[1,16,2,1024]{3,2,1,0:T(2,128)(2,1)} %param.5), channel_id=1, source_target_pairs={{4,0},{8,4},{12,8},{16,12},{20,16},{24,20},{28,24},{5,1},{9,5},{13... | collective-permute-start | bytes 196616 | tf_op jit(solution)/shard_map/ppermute | solution.py:19
  6.3 1.4 %fusion.18 = (f32[1,1024]{1,0:T(1,128)S(1)}, f32[1,1024]{1,0:T(1,128)S(1)}, f32[1,1024]{1,0:T(1,128)S(1)}, f32[1,1024]{1,0:T(1,128)S(1)}, f32[1,1024]{1,0:T(1,12...) fusion(f32[27,1024]{1,0:T(8,128)} %param.6), kind=kLoop, calls=%fused_computation.84 | loop fusion | bytes 155648 | tf_op jit(solution)/shard_map/slice | solution.py:124
  7.7 1.2 %fusion.19 = (f32[1,1024]{1,0:T(1,128)S(1)}, f32[1,1024]{1,0:T(1,128)S(1)}, f32[1,1024]{1,0:T(1,128)S(1)}, f32[1,1024]{1,0:T(1,128)S(1)}, f32[1,1024]{1,0:T(1,12...) fusion(f32[27,1024]{1,0:T(8,128)} %param.6), kind=kLoop, calls=%fused_computation.85 | loop fusion | bytes 65536 | tf_op jit(solution)/shard_map/slice | solution.py:124
  9.0 0.9 %constant_dynamic-update-slice_fusion.1 = bf16[3,16,2,1024]{3,2,1,0:T(2,128)(2,1)S(1)} fusion(bf16[3,16,2,1024]{3,2,1,0:T(2,128)(2,1)S(1)} %constant_dynamic-update-slice_fusion.2, bf16[1,16,2,1024]{3,2,1,0:T(2,128)(2,1)} %param.5), kind=kLoop, calls=%fused_computation.64 | loop fusion | bytes 131072
  9.9 1.5 %collective-permute-done.1 = bf16[1,16,2,1024]{3,2,1,0:T(2,128)(2,1)S(1)} collective-permute-done((bf16[1,16,2,1024]{3,2,1,0:T(2,128)(2,1)}, bf16[1,16,2,1024]{3,2,1,0:T(2,128)(2,1)S(1)}, u32[]{:S(2)}, u32[]{:S(2)}) %collective-permute-start.1) | collective-permute-done | bytes 65568 | tf_op jit(solution)/shard_map/ppermute | solution.py:19
  11.4 0.1 constant_dynamic-update-slice_fusion
  11.4 0.1 collective-permute-start.2
  11.5 1.6 %collective-permute-start.3 = (bf16[3,16,2,1024]{3,2,1,0:T(2,128)(2,1)S(1)}, bf16[3,16,2,1024]{3,2,1,0:T(2,128)(2,1)S(1)}, u32[]{:S(2)}, u32[]{:S(2)}) collective-permute-start(bf16[3,16,2,1024]{3,2,1,0:T(2,128)(2,1)S(1)} %constant_dynamic-update-slice_fusion), channel_id=1, source_target_pairs={{0,2},{1,3},{2,0},{3,1},{4,6},{5,7},{6,4},{7,5},{8,10},{9,11},{10,... | collective-permute-start | bytes 589832 | tf_op jit(solution)/shard_map/ppermute | solution.py:64
  13.1 0.5 broadcast_in_dim.26
  13.6 0.2 copy_dynamic-update-slice_fusion.3
  13.8 0.0 collective-permute-done.2
  13.8 0.2 copy_dynamic-update-slice_fusion.2
  14.0 4.9 %collective-permute-done.3 = bf16[3,16,2,1024]{3,2,1,0:T(2,128)(2,1)S(1)} collective-permute-done((bf16[3,16,2,1024]{3,2,1,0:T(2,128)(2,1)S(1)}, bf16[3,16,2,1024]{3,2,1,0:T(2,128)(2,1)S(1)}, u32[]{:S(2)}, u32[]{:S(2)}) %collective-permute-start.3) | collective-permute-done | bytes 196640 | tf_op jit(solution)/shard_map/ppermute | solution.py:64
  18.8 0.0 collective-permute-start.4
  18.8 0.2 copy_dynamic-update-slice_fusion.1
  19.0 1.2 %collective-permute-done.4 = bf16[3,16,2,1024]{3,2,1,0:T(2,128)(2,1)S(1)} collective-permute-done((bf16[3,16,2,1024]{3,2,1,0:T(2,128)(2,1)S(1)}, bf16[3,16,2,1024]{3,2,1,0:T(2,128)(2,1)S(1)}, u32[]{:S(2)}, u32[]{:S(2)}) %collective-permute-start.4) | collective-permute-done | bytes 196640 | tf_op jit(solution)/shard_map/ppermute | solution.py:66
  20.3 0.2 copy_dynamic-update-slice_fusion
  20.5 2.6 %slice_convert_fusion.1 = (f32[1,16,4,2,1024]{4,0,3,2,1:T(1,128)}, f32[1,16,4,2,1024]{4,0,3,2,1:T(1,128)}, f32[1,16,4,2,1024]{4,0,3,2,1:T(1,128)}) fusion(bf16[3,16,4,2,1024]{4,0,3,2,1:T(4,128)(2,1)S(1)} %bitcast.114), kind=kLoop, calls=%fused_computation.45 | loop fusion | flops 393216 | bytes 2359296 | tf_op jit(solution)/shard_map/convert_element_type | solution.py:124
  23.1 0.7 %reshape.327 = bf16[3,16,8,8,128]{4,3,0,2,1:T(8,128)(2,1)S(1)} reshape(bf16[3,16,4,2,1024]{4,0,3,2,1:T(4,128)(2,1)S(1)} %bitcast.115) | data formatting | bytes 1572864 | tf_op jit(solution)/shard_map/reshape | solution.py:112
  23.8 2.6 %add_convert_fusion = bf16[1,16,8,8,128]{4,3,0,2,1:T(8,128)(2,1)S(1)} fusion(f32[1,16,8,8,128]{4,3,0,2,1:T(8,128)} %bitcast.117, f32[1,16,8,8,128]{4,3,0,2,1:T(8,128)} %bitcast.118, f32[1,16,8,8,128]{4,3,0,2,1:T(8,128)} %bitcast.116, bf16[3,16,8,8,128]{4,3,0,2,1:T(8,128)(2,1)S(1)} %reshape.327, f32[8,128]{1,0:T(8,128)S(1)} %bitcast.153, ...), kind=kLoop, calls=%fused_computation.51 | loop fusion | flops 10485760 | bytes 2736128 | tf_op jit(solution)/shard_map/convert_element_type | solution.py:132
  26.4 0.1 convert_element_type.201
  26.5 0.2 copy.43
  26.7 0.1 reshape.317
  26.8 0.7 %convolution_convert_fusion = bf16[128,768]{1,0:T(8,128)(2,1)S(1)} fusion(bf16[128,1024]{1,0:T(8,128)(2,1)S(1)} %reshape.317, bf16[768,1024]{1,0:T(8,128)(2,1)S(1)} %copy-done), kind=kOutput, calls=%fused_computation.26 | convolution fusion | flops 201424896 | bytes 2031616 | tf_op jit(solution)/shard_map/dot_general | solution.py:100
  27.4 0.2 copy.28
  27.6 3.2 %collective-permute-start.5 = (bf16[128,4,2,64]{0,3,1,2:T(8,128)(2,1)S(1)}, bf16[128,4,2,64]{0,3,1,2:T(8,128)(2,1)S(1)}, u32[]{:S(2)}, u32[]{:S(2)}) collective-permute-start(bf16[128,4,2,64]{0,3,1,2:T(8,128)(2,1)S(1)} %get-tuple-element.56), channel_id=1, source_target_pairs={{0,16},{4,20},{8,24},{12,28},{16,0},{20,4},{24,8},{28,12},{1,17},{... | collective-permute-start | bytes 393224 | tf_op jit(solution)/shard_map/ppermute | solution.py:39
  30.9 1.8 %collective-permute-start.6 = (bf16[128,4,2,64]{0,3,1,2:T(8,128)(2,1)S(1)}, bf16[128,4,2,64]{0,3,1,2:T(8,128)(2,1)}, u32[]{:S(2)}, u32[]{:S(2)}) collective-permute-start(bf16[128,4,2,64]{0,3,1,2:T(8,128)(2,1)S(1)} %get-tuple-element.56), channel_id=1, source_target_pairs={{0,4},{4,8},{8,12},{12,0},{16,20},{20,24},{24,28},{28,16},{1,5},{5... | collective-permute-start | bytes 393224 | tf_op jit(solution)/shard_map/ppermute | solution.py:43
  32.7 0.3 collective-permute-start.8
  33.1 2.3 %collective-permute-start.10 = (bf16[128,4,2,64]{0,3,1,2:T(8,128)(2,1)S(1)}, bf16[128,4,2,64]{0,3,1,2:T(8,128)(2,1)S(1)}, u32[]{:S(2)}, u32[]{:S(2)}) collective-permute-start(bf16[128,4,2,64]{0,3,1,2:T(8,128)(2,1)S(1)} %get-tuple-element.56), channel_id=1, source_target_pairs={{0,12},{4,0},{8,4},{12,8},{16,28},{20,16},{24,20},{28,24},{1,13},{... | collective-permute-start | bytes 393224 | tf_op jit(solution)/shard_map/ppermute | solution.py:43
  35.4 0.1 reshape_squeeze.2
  35.5 0.3 constant_dynamic-slice_fusion.2
  35.8 0.1 copy.30
  35.9 0.1 copy.29
  36.0 1.6 %collective-permute-done.5 = bf16[128,4,2,64]{0,3,1,2:T(8,128)(2,1)S(1)} collective-permute-done((bf16[128,4,2,64]{0,3,1,2:T(8,128)(2,1)S(1)}, bf16[128,4,2,64]{0,3,1,2:T(8,128)(2,1)S(1)}, u32[]{:S(2)}, u32[]{:S(2)}) %collective-permute-start.5) | collective-permute-done | bytes 131104 | tf_op jit(solution)/shard_map/ppermute | solution.py:39
  37.6 1.9 %collective-permute-start.7 = (bf16[128,4,2,64]{0,3,1,2:T(8,128)(2,1)S(1)}, bf16[128,4,2,64]{0,3,1,2:T(8,128)(2,1)S(1)}, u32[]{:S(2)}, u32[]{:S(2)}) collective-permute-start(bf16[128,4,2,64]{0,3,1,2:T(8,128)(2,1)S(1)} %collective-permute-done.5), channel_id=1, source_target_pairs={{0,4},{4,8},{8,12},{12,0},{16,20},{20,24},{24,28},{28,16},{1,5},{5... | collective-permute-start | bytes 393224 | tf_op jit(solution)/shard_map/ppermute | solution.py:44
  39.5 0.4 collective-permute-done.6
  40.0 1.3 %collective-permute-start.11 = (bf16[128,4,2,64]{0,3,1,2:T(8,128)(2,1)S(1)}, bf16[128,4,2,64]{0,3,1,2:T(8,128)(2,1)S(1)}, u32[]{:S(2)}, u32[]{:S(2)}) collective-permute-start(bf16[128,4,2,64]{0,3,1,2:T(8,128)(2,1)S(1)} %collective-permute-done.5), channel_id=1, source_target_pairs={{0,12},{4,0},{8,4},{12,8},{16,28},{20,16},{24,20},{28,24},{1,13},{... | collective-permute-start | bytes 393224 | tf_op jit(solution)/shard_map/ppermute | solution.py:44
  41.3 0.9 %constant_dynamic-update-slice_fusion.8 = bf16[1024,4,2,64]{0,3,1,2:T(8,128)(2,1)S(1)} fusion(bf16[1024,4,2,64]{0,3,1,2:T(8,128)(2,1)S(1)} %constant_dynamic-update-slice_fusion.9, bf16[128,4,2,64]{0,3,1,2:T(8,128)(2,1)} %collective-permute-done.6), kind=kLoop, calls=%fused_computation.71 | loop fusion | bytes 262144
  42.2 3.1 %collective-permute-done.7 = bf16[128,4,2,64]{0,3,1,2:T(8,128)(2,1)S(1)} collective-permute-done((bf16[128,4,2,64]{0,3,1,2:T(8,128)(2,1)S(1)}, bf16[128,4,2,64]{0,3,1,2:T(8,128)(2,1)S(1)}, u32[]{:S(2)}, u32[]{:S(2)}) %collective-permute-start.7) | collective-permute-done | bytes 131104 | tf_op jit(solution)/shard_map/ppermute | solution.py:44
  45.4 0.9 %constant_dynamic-update-slice_fusion.6 = bf16[1024,4,2,64]{0,3,1,2:T(8,128)(2,1)S(1)} fusion(bf16[1024,4,2,64]{0,3,1,2:T(8,128)(2,1)S(1)} %constant_dynamic-update-slice_fusion.7, bf16[128,4,2,64]{0,3,1,2:T(8,128)(2,1)} %collective-permute-done.8), kind=kLoop, calls=%fused_computation.69 | loop fusion | bytes 262144
  46.5 0.1 collective-permute-done.11
  46.6 0.4 fusion.20
  47.0 0.0 copy-start.1
  47.0 0.3 fusion.6
  47.3 0.4 fusion.5
  47.7 0.1 copy.32
  47.8 0.1 reshape.319
  47.9 0.2 copy-done.1
  48.0 0.2 convolution_convert_fusion.1
  48.3 1.6 %collective-permute-start.13 = (bf16[32,1024]{1,0:T(8,128)(2,1)S(1)}, bf16[32,1024]{1,0:T(8,128)(2,1)S(1)}, u32[]{:S(2)}, u32[]{:S(2)}) collective-permute-start(bf16[32,1024]{1,0:T(8,128)(2,1)S(1)} %get-tuple-element.47), channel_id=1, source_target_pairs={{0,2},{1,3},{2,0},{3,1},{4,6},{5,7},{6,4},{7,5},{8,10},{9,11},{10,... | collective-permute-start | bytes 196616 | tf_op jit(solution)/shard_map/ppermute | solution.py:202
  49.8 0.4 fusion.21
  50.2 0.3 fusion.8
  50.5 0.4 fusion.4
  50.9 0.1 copy.33
  51.0 0.1 dot_general.39
  51.1 0.2 fusion.12
  51.3 0.7 %collective-permute-start.12 = (f32[32,1024]{1,0:T(8,128)S(1)}, f32[32,1024]{1,0:T(8,128)S(1)}, u32[]{:S(2)}, u32[]{:S(2)}) collective-permute-start(f32[32,1024]{1,0:T(8,128)S(1)} %get-tuple-element.43), channel_id=1, source_target_pairs={{0,1},{1,0},{2,3},{3,2},{4,5},{5,4},{6,7},{7,6},{8,9},{9,8},{10,11... | collective-permute-start | bytes 393224 | tf_op jit(solution)/shard_map/ppermute | solution.py:214
  52.0 0.1 reshape.321
  52.1 0.5 collective-permute-done.13
  52.6 1.4 %collective-permute-done.14 = bf16[32,1024]{1,0:T(8,128)(2,1)S(1)} collective-permute-done((bf16[32,1024]{1,0:T(8,128)(2,1)S(1)}, bf16[32,1024]{1,0:T(8,128)(2,1)S(1)}, u32[]{:S(2)}, u32[]{:S(2)}) %collective-permute-start.14) | collective-permute-done | bytes 65568 | tf_op jit(solution)/shard_map/ppermute | solution.py:203
  54.0 0.1 add.272
  54.1 0.1 reshape.322
  54.2 0.7 %add_convert_fusion.1 = bf16[1,16,2,1024]{3,2,1,0:T(2,128)(2,1)} fusion(f32[1,16,2,1024]{3,2,1,0:T(2,128)S(1)} %add.272, f32[1,16,2,1024]{3,2,1,0:T(2,128)S(1)} %reshape.321, f32[1,16,2,1024]{3,2,1,0:T(2,128)S(1)} %reshape.322), kind=kLoop, calls=%fused_computation.57 | loop fusion | flops 98304 | bytes 458752 | tf_op jit(solution)/shard_map/convert_element_type | solution.py:217
  (26 shorter events, 0.4 us)
Async XLA Ops:
  0.0 26.8 %copy-start = (bf16[768,1024]{1,0:T(8,128)(2,1)S(1)}, bf16[768,1024]{1,0:T(8,128)(2,1)}, u32[]{:S(2)}) copy-start(bf16[768,1024]{1,0:T(8,128)(2,1)} %param.8) | copy-start | bytes 4718596
  0.0 9.0 %collective-permute-start = (bf16[1,16,2,1024]{3,2,1,0:T(2,128)(2,1)}, bf16[1,16,2,1024]{3,2,1,0:T(2,128)(2,1)S(1)}, u32[]{:S(2)}, u32[]{:S(2)}) collective-permute-start(bf16[1,16,2,1024]{3,2,1,0:T(2,128)(2,1)} %param.5), channel_id=1, source_target_pairs={{0,4},{4,8},{8,12},{12,16},{16,20},{20,24},{24,28},{1,5},{5,9},{9,... | collective-permute-start | bytes 196616 | tf_op jit(solution)/shard_map/ppermute | solution.py:18
  5.0 6.4 %collective-permute-start.1 = (bf16[1,16,2,1024]{3,2,1,0:T(2,128)(2,1)}, bf16[1,16,2,1024]{3,2,1,0:T(2,128)(2,1)S(1)}, u32[]{:S(2)}, u32[]{:S(2)}) collective-permute-start(bf16[1,16,2,1024]{3,2,1,0:T(2,128)(2,1)} %param.5), channel_id=1, source_target_pairs={{4,0},{8,4},{12,8},{16,12},{20,16},{24,20},{28,24},{5,1},{9,5},{13... | collective-permute-start | bytes 196616 | tf_op jit(solution)/shard_map/ppermute | solution.py:19
  11.4 2.3 %collective-permute-start.2 = (bf16[3,16,2,1024]{3,2,1,0:T(2,128)(2,1)S(1)}, bf16[3,16,2,1024]{3,2,1,0:T(2,128)(2,1)S(1)}, u32[]{:S(2)}, u32[]{:S(2)}) collective-permute-start(bf16[3,16,2,1024]{3,2,1,0:T(2,128)(2,1)S(1)} %constant_dynamic-update-slice_fusion), channel_id=1, source_target_pairs={{0,1},{1,0},{2,3},{3,2},{4,5},{5,4},{6,7},{7,6},{8,9},{9,8},{10,11... | collective-permute-start | bytes 589832 | tf_op jit(solution)/shard_map/ppermute | solution.py:60
  11.5 7.3 %collective-permute-start.3 = (bf16[3,16,2,1024]{3,2,1,0:T(2,128)(2,1)S(1)}, bf16[3,16,2,1024]{3,2,1,0:T(2,128)(2,1)S(1)}, u32[]{:S(2)}, u32[]{:S(2)}) collective-permute-start(bf16[3,16,2,1024]{3,2,1,0:T(2,128)(2,1)S(1)} %constant_dynamic-update-slice_fusion), channel_id=1, source_target_pairs={{0,2},{1,3},{2,0},{3,1},{4,6},{5,7},{6,4},{7,5},{8,10},{9,11},{10,... | collective-permute-start | bytes 589832 | tf_op jit(solution)/shard_map/ppermute | solution.py:64
  18.8 1.4 %collective-permute-start.4 = (bf16[3,16,2,1024]{3,2,1,0:T(2,128)(2,1)S(1)}, bf16[3,16,2,1024]{3,2,1,0:T(2,128)(2,1)S(1)}, u32[]{:S(2)}, u32[]{:S(2)}) collective-permute-start(bf16[3,16,2,1024]{3,2,1,0:T(2,128)(2,1)S(1)} %collective-permute-done.3), channel_id=1, source_target_pairs={{0,1},{1,0},{2,3},{3,2},{4,5},{5,4},{6,7},{7,6},{8,9},{9,8},{10,11... | collective-permute-start | bytes 589832 | tf_op jit(solution)/shard_map/ppermute | solution.py:66
  23.1 0.7 %copy-start.2 = (f32[1024]{0:T(1024)S(1)}, f32[1024]{0:T(1024)}, u32[]{:S(2)}) copy-start(f32[1024]{0:T(1024)} %param.7) | copy-start | bytes 12292
  27.6 9.9 %collective-permute-start.5 = (bf16[128,4,2,64]{0,3,1,2:T(8,128)(2,1)S(1)}, bf16[128,4,2,64]{0,3,1,2:T(8,128)(2,1)S(1)}, u32[]{:S(2)}, u32[]{:S(2)}) collective-permute-start(bf16[128,4,2,64]{0,3,1,2:T(8,128)(2,1)S(1)} %get-tuple-element.56), channel_id=1, source_target_pairs={{0,16},{4,20},{8,24},{12,28},{16,0},{20,4},{24,8},{28,12},{1,17},{... | collective-permute-start | bytes 393224 | tf_op jit(solution)/shard_map/ppermute | solution.py:39
  30.9 9.1 %collective-permute-start.6 = (bf16[128,4,2,64]{0,3,1,2:T(8,128)(2,1)S(1)}, bf16[128,4,2,64]{0,3,1,2:T(8,128)(2,1)}, u32[]{:S(2)}, u32[]{:S(2)}) collective-permute-start(bf16[128,4,2,64]{0,3,1,2:T(8,128)(2,1)S(1)} %get-tuple-element.56), channel_id=1, source_target_pairs={{0,4},{4,8},{8,12},{12,0},{16,20},{20,24},{24,28},{28,16},{1,5},{5... | collective-permute-start | bytes 393224 | tf_op jit(solution)/shard_map/ppermute | solution.py:43
  32.7 12.7 %collective-permute-start.8 = (bf16[128,4,2,64]{0,3,1,2:T(8,128)(2,1)S(1)}, bf16[128,4,2,64]{0,3,1,2:T(8,128)(2,1)}, u32[]{:S(2)}, u32[]{:S(2)}) collective-permute-start(bf16[128,4,2,64]{0,3,1,2:T(8,128)(2,1)S(1)} %get-tuple-element.56), channel_id=1, source_target_pairs={{0,8},{4,12},{8,0},{12,4},{16,24},{20,28},{24,16},{28,20},{1,9},{5... | collective-permute-start | bytes 393224 | tf_op jit(solution)/shard_map/ppermute | solution.py:43
  33.1 13.3 %collective-permute-start.10 = (bf16[128,4,2,64]{0,3,1,2:T(8,128)(2,1)S(1)}, bf16[128,4,2,64]{0,3,1,2:T(8,128)(2,1)S(1)}, u32[]{:S(2)}, u32[]{:S(2)}) collective-permute-start(bf16[128,4,2,64]{0,3,1,2:T(8,128)(2,1)S(1)} %get-tuple-element.56), channel_id=1, source_target_pairs={{0,12},{4,0},{8,4},{12,8},{16,28},{20,16},{24,20},{28,24},{1,13},{... | collective-permute-start | bytes 393224 | tf_op jit(solution)/shard_map/ppermute | solution.py:43
  37.6 7.8 %collective-permute-start.7 = (bf16[128,4,2,64]{0,3,1,2:T(8,128)(2,1)S(1)}, bf16[128,4,2,64]{0,3,1,2:T(8,128)(2,1)S(1)}, u32[]{:S(2)}, u32[]{:S(2)}) collective-permute-start(bf16[128,4,2,64]{0,3,1,2:T(8,128)(2,1)S(1)} %collective-permute-done.5), channel_id=1, source_target_pairs={{0,4},{4,8},{8,12},{12,0},{16,20},{20,24},{24,28},{28,16},{1,5},{5... | collective-permute-start | bytes 393224 | tf_op jit(solution)/shard_map/ppermute | solution.py:44
  39.5 6.9 %collective-permute-start.9 = (bf16[128,4,2,64]{0,3,1,2:T(8,128)(2,1)S(1)}, bf16[128,4,2,64]{0,3,1,2:T(8,128)(2,1)S(1)}, u32[]{:S(2)}, u32[]{:S(2)}) collective-permute-start(bf16[128,4,2,64]{0,3,1,2:T(8,128)(2,1)S(1)} %collective-permute-done.5), channel_id=1, source_target_pairs={{0,8},{4,12},{8,0},{12,4},{16,24},{20,28},{24,16},{28,20},{1,9},{5... | collective-permute-start | bytes 393224 | tf_op jit(solution)/shard_map/ppermute | solution.py:44
  40.0 6.6 %collective-permute-start.11 = (bf16[128,4,2,64]{0,3,1,2:T(8,128)(2,1)S(1)}, bf16[128,4,2,64]{0,3,1,2:T(8,128)(2,1)S(1)}, u32[]{:S(2)}, u32[]{:S(2)}) collective-permute-start(bf16[128,4,2,64]{0,3,1,2:T(8,128)(2,1)S(1)} %collective-permute-done.5), channel_id=1, source_target_pairs={{0,12},{4,0},{8,4},{12,8},{16,28},{20,16},{24,20},{28,24},{1,13},{... | collective-permute-start | bytes 393224 | tf_op jit(solution)/shard_map/ppermute | solution.py:44
  47.0 1.1 %copy-start.1 = (bf16[256,1024]{1,0:T(8,128)(2,1)S(1)}, bf16[256,1024]{1,0:T(8,128)(2,1)}, u32[]{:S(2)}) copy-start(bf16[256,1024]{1,0:T(8,128)(2,1)} %param.9) | copy-start | bytes 1572868
  48.3 4.3 %collective-permute-start.13 = (bf16[32,1024]{1,0:T(8,128)(2,1)S(1)}, bf16[32,1024]{1,0:T(8,128)(2,1)S(1)}, u32[]{:S(2)}, u32[]{:S(2)}) collective-permute-start(bf16[32,1024]{1,0:T(8,128)(2,1)S(1)} %get-tuple-element.47), channel_id=1, source_target_pairs={{0,2},{1,3},{2,0},{3,1},{4,6},{5,7},{6,4},{7,5},{8,10},{9,11},{10,... | collective-permute-start | bytes 196616 | tf_op jit(solution)/shard_map/ppermute | solution.py:202
  49.8 4.2 %collective-permute-start.14 = (bf16[32,1024]{1,0:T(8,128)(2,1)S(1)}, bf16[32,1024]{1,0:T(8,128)(2,1)S(1)}, u32[]{:S(2)}, u32[]{:S(2)}) collective-permute-start(bf16[32,1024]{1,0:T(8,128)(2,1)S(1)} %get-tuple-element.48), channel_id=1, source_target_pairs={{0,3},{1,2},{2,1},{3,0},{4,7},{5,6},{6,5},{7,4},{8,11},{9,10},{10,... | collective-permute-start | bytes 196616 | tf_op jit(solution)/shard_map/ppermute | solution.py:203
  51.3 2.8 %collective-permute-start.12 = (f32[32,1024]{1,0:T(8,128)S(1)}, f32[32,1024]{1,0:T(8,128)S(1)}, u32[]{:S(2)}, u32[]{:S(2)}) collective-permute-start(f32[32,1024]{1,0:T(8,128)S(1)} %get-tuple-element.43), channel_id=1, source_target_pairs={{0,1},{1,0},{2,3},{3,2},{4,5},{5,4},{6,7},{7,6},{8,9},{9,8},{10,11... | collective-permute-start | bytes 393224 | tf_op jit(solution)/shard_map/ppermute | solution.py:214

commit v11 on v7

--- a/solution.py
+++ b/solution.py
@@ -134,10 +134,13 @@
         .reshape(groups * local_tok, features)
     )
     slab_tok = slab_rows.shape[0]
-    projected = times_transposed(slab_rows, qkv_weight).astype(jnp.bfloat16)
-    split_heads = projected.reshape(slab_tok, heads_here, 3, HS)
-    queries = split_heads[:, :, 0]
-    key_value = relayed(split_heads[:, :, 1:], "blk")
+    head_weight = qkv_weight.reshape(heads_here, 3, HS, features)
+    kv_weight = head_weight[:, 1:].reshape(heads_here * 2 * HS, features)
+    q_weight = head_weight[:, 0].reshape(heads_here * HS, features)
+    kv_rows = times_transposed(slab_rows, kv_weight).astype(jnp.bfloat16)
+    key_value = relayed(kv_rows.reshape(slab_tok, heads_here, 2, HS), "blk")
+    queries = times_transposed(slab_rows, q_weight).astype(jnp.bfloat16)
+    queries = queries.reshape(slab_tok, heads_here, HS)
     key_piece = key_value[:, :, 0]
     value_piece = key_value[:, :, 1]
     score_scale = 1.0 / math.sqrt(HS)

time: 52.3 us -> 53.4 us (1.021)
  starting transfers between devices: 20.9 us -> 22.1 us
  local copies, waits for them, and re-layouts: 8.45 us -> 7.53 us
  waiting for transfers between devices: 15.7 us -> 16.4 us
    unnamed x16 -> x15, local copies, waits for them, and re-layouts: 4.1 us -> 1.17 us
    slice x1 -> x2, local copies, waits for them, and re-layouts: 0.01 us -> 2.45 us  [the longest x1 1.36 us: on_device(): kv_weight = head_weight[:, 1:].reshape(heads_here * 2 * HS, features)]
    ppermute x3, waiting for transfers between devices: 3.23 us -> 4.94 us  [relayed(): parts.append(lax.ppermute(crossed, axis, pairs))]
    ppermute x1, waiting for transfers between devices: 1.57 us -> 0.01 us  [padded_2(): after = lax.ppermute(initial, axis, down)]
    ppermute x1, starting transfers between devices: 3.2 us -> 4.67 us  [relayed(): crossed = lax.ppermute(piece, axis, mirror)]
  transfers between devices with their start and end apart: 15 -> 15, of which waited for: 9 -> 8; matrix products, arithmetic and copies ran while one was open for 15% -> 14% of each run, Pallas kernels for 0% -> 0%
where the time goes in v11:
time: 53.4 us; the launch traced here: 52.9 us
  starting transfers between devices  22.1 us (41%)
  waiting for transfers between devices  16.4 us (31%)
  local copies, waits for them, and re-layouts  7.53 us (14%)
  other arithmetic  3.76 us (7%)
  matrix products  2.64 us (5%)
  between operations  0.54 us (1%)
    ppermute x1, waiting for transfers between devices, gathered_by_chip(): far = lax.ppermute(piece, axis, chip_shift(size, shift))  5.63 us
    ppermute x3, waiting for transfers between devices, relayed(): parts.append(lax.ppermute(crossed, axis, pairs))  4.94 us
    ppermute x1, starting transfers between devices, padded_2(): before = lax.ppermute(last, axis, up)  4.87 us
    ppermute x1, starting transfers between devices, relayed(): crossed = lax.ppermute(piece, axis, mirror)  4.67 us
    ppermute x3, starting transfers between devices, relayed(): parts.append(lax.ppermute(piece, axis, pairs))  4.5 us
    ppermute x3, starting transfers between devices, relayed(): parts.append(lax.ppermute(crossed, axis, pairs))  2.82 us
    convert_element_type x1, other arithmetic, on_device(): positioned = summed.astype(jnp.bfloat16)  2.34 us
    slice x2, local copies, waits for them, and re-layouts, on_device(): conv_weight[9 * step_z + 3 * step_x + step_y]  2.34 us
  transfers between devices with their start and end apart: 15, of which 8 were waited for; matrix products, arithmetic and copies ran while one was open for 14% of the time, Pallas kernels for 0%

profile of v11, /device:TPU:0, one launch (start us, length us, event | category | flops | bytes accessed | tf_op | source)
XLA Modules:
  0.0 52.9 jit_solution(11595991807129648994)
XLA Ops:
  0.0 0.9 %copy.13 = bf16[1,16,2,1024]{3,1,2,0:T(8,128)(2,1)S(1)} copy(bf16[1,16,2,1024]{3,2,1,0:T(2,128)(2,1)} %param.5) | data formatting | bytes 131072 | tf_op args[0]
  0.9 4.9 %collective-permute-start = (bf16[1,16,2,1024]{3,1,2,0:T(8,128)(2,1)S(1)}, bf16[1,16,2,1024]{3,1,2,0:T(8,128)(2,1)S(1)}, u32[]{:S(2)}, u32[]{:S(2)}) collective-permute-start(bf16[1,16,2,1024]{3,1,2,0:T(8,128)(2,1)S(1)} %copy.13), channel_id=1, source_target_pairs={{0,4},{4,8},{8,12},{12,16},{16,20},{20,24},{24,28},{1,5},{5,9},{9,... | collective-permute-start | bytes 196616 | tf_op jit(solution)/shard_map/ppermute | solution.py:18
  5.8 1.3 %collective-permute-start.1 = (bf16[1,16,2,1024]{3,1,2,0:T(8,128)(2,1)S(1)}, bf16[1,16,2,1024]{3,1,2,0:T(8,128)(2,1)S(1)}, u32[]{:S(2)}, u32[]{:S(2)}) collective-permute-start(bf16[1,16,2,1024]{3,1,2,0:T(8,128)(2,1)S(1)} %copy.13), channel_id=1, source_target_pairs={{4,0},{8,4},{12,8},{16,12},{20,16},{24,20},{28,24},{5,1},{9,5},{13... | collective-permute-start | bytes 196616 | tf_op jit(solution)/shard_map/ppermute | solution.py:19
  7.1 1.3 %fusion.45 = (f32[1,1024]{1,0:T(1,128)S(1)}, f32[1,1024]{1,0:T(1,128)S(1)}, f32[1,1024]{1,0:T(1,128)S(1)}, f32[1,1024]{1,0:T(1,128)S(1)}, f32[1,1024]{1,0:T(1,12...) fusion(f32[27,1024]{1,0:T(8,128)} %param.6), kind=kLoop, calls=%fused_computation.114 | loop fusion | bytes 155648 | tf_op jit(solution)/shard_map/slice | solution.py:121
  8.4 1.0 %fusion.46 = (f32[1,1024]{1,0:T(1,128)S(1)}, f32[1,1024]{1,0:T(1,128)S(1)}, f32[1,1024]{1,0:T(1,128)S(1)}, f32[1,1024]{1,0:T(1,128)S(1)}, f32[1,1024]{1,0:T(1,12...) fusion(f32[27,1024]{1,0:T(8,128)} %param.6), kind=kLoop, calls=%fused_computation.115 | loop fusion | bytes 65536 | tf_op jit(solution)/shard_map/slice | solution.py:121
  9.5 0.0 copy-start.1
  9.5 1.4 %slice.244 = bf16[4,2,64,1024]{3,2,1,0:T(8,128)(2,1)S(1)} slice(bf16[4,3,64,1024]{3,2,1,0:T(8,128)(2,1)} %bitcast.130), slice={[0:4], [1:3], [0:64], [0:1024]} | slice | bytes 2097152 | tf_op jit(solution)/shard_map/slice | solution.py:138
  10.9 1.1 %slice.243 = bf16[4,1,64,1024]{3,2,1,0:T(8,128)(2,1)S(1)} slice(bf16[4,3,64,1024]{3,2,1,0:T(8,128)(2,1)} %bitcast.131), slice={[0:4], [0:1], [0:64], [0:1024]} | slice | bytes 1048576 | tf_op jit(solution)/shard_map/slice | solution.py:139
  12.0 0.0 collective-permute-done
  12.1 0.0 collective-permute-done.1
  12.1 0.1 collective-permute-start.2
  12.2 1.6 %collective-permute-start.3 = (bf16[3,16,2,1024]{3,1,2,0:T(8,128)(2,1)S(1)}, bf16[3,16,2,1024]{3,1,2,0:T(8,128)(2,1)S(1)}, u32[]{:S(2)}, u32[]{:S(2)}) collective-permute-start(bf16[3,16,2,1024]{3,1,2,0:T(8,128)(2,1)S(1)} %constant_dynamic-update-slice_fusion), channel_id=1, source_target_pairs={{0,2},{1,3},{2,0},{3,1},{4,6},{5,7},{6,4},{7,5},{8,10},{9,11},{10,... | collective-permute-start | bytes 589832 | tf_op jit(solution)/shard_map/ppermute | solution.py:64
  13.7 0.1 broadcast_in_dim.27
  13.8 0.0 copy-start.2
  13.9 5.6 %collective-permute-done.3 = bf16[3,16,2,1024]{3,1,2,0:T(8,128)(2,1)S(1)} collective-permute-done((bf16[3,16,2,1024]{3,1,2,0:T(8,128)(2,1)S(1)}, bf16[3,16,2,1024]{3,1,2,0:T(8,128)(2,1)S(1)}, u32[]{:S(2)}, u32[]{:S(2)}) %collective-permute-start.3) | collective-permute-done | bytes 196640 | tf_op jit(solution)/shard_map/ppermute | solution.py:64
  19.5 0.0 collective-permute-start.4
  19.5 0.0 collective-permute-done.2
  19.6 1.4 %collective-permute-done.4 = bf16[3,16,2,1024]{3,1,2,0:T(8,128)(2,1)S(1)} collective-permute-done((bf16[3,16,2,1024]{3,1,2,0:T(8,128)(2,1)S(1)}, bf16[3,16,2,1024]{3,1,2,0:T(8,128)(2,1)S(1)}, u32[]{:S(2)}, u32[]{:S(2)}) %collective-permute-start.4) | collective-permute-done | bytes 196640 | tf_op jit(solution)/shard_map/ppermute | solution.py:66
  21.0 0.1 fusion.43
  21.1 2.3 %add_convert_fusion = bf16[1,16,8,1024]{3,1,2,0:T(8,128)(2,1)S(1)} fusion(bf16[1,16,8,1024]{3,1,2,0:T(8,128)(2,1)S(1)} %bitcast.136, bf16[1,16,8,1024]{3,1,2,0:T(8,128)(2,1)S(1)} %bitcast.135, bf16[1,16,8,1024]{3,1,2,0:T(8,128)(2,1)S(1)} %bitcast.134, bf16[3,16,8,1024]{3,1,2,0:T(8,128)(2,1)S(1)} %bitcast.127, f32[1024]{0:T(1024)S(1)} %bitcast.165, ...), kind=kLoop, calls=%fused_computation.78 | loop fusion | flops 10878976 | bytes 1949696 | tf_op jit(solution)/shard_map/convert_element_type | solution.py:128
  23.4 0.3 copy.41
  23.7 0.1 reshape.256
  23.8 0.5 convolution_convert_fusion.1
  24.3 0.1 copy.22
  24.5 4.7 %collective-permute-start.5 = (bf16[128,4,2,64]{0,3,1,2:T(8,128)(2,1)S(1)}, bf16[128,4,2,64]{0,3,1,2:T(8,128)(2,1)S(1)}, u32[]{:S(2)}, u32[]{:S(2)}) collective-permute-start(bf16[128,4,2,64]{0,3,1,2:T(8,128)(2,1)S(1)} %get-tuple-element.56), channel_id=1, source_target_pairs={{0,16},{4,20},{8,24},{12,28},{16,0},{20,4},{24,8},{28,12},{1,17},{... | collective-permute-start | bytes 393224 | tf_op jit(solution)/shard_map/ppermute | solution.py:39
  29.1 0.6 %collective-permute-start.6 = (bf16[128,4,2,64]{0,3,1,2:T(8,128)(2,1)S(1)}, bf16[128,4,2,64]{0,3,1,2:T(8,128)(2,1)S(1)}, u32[]{:S(2)}, u32[]{:S(2)}) collective-permute-start(bf16[128,4,2,64]{0,3,1,2:T(8,128)(2,1)S(1)} %get-tuple-element.56), channel_id=1, source_target_pairs={{0,4},{4,8},{8,12},{12,0},{16,20},{20,24},{24,28},{28,16},{1,5},{5... | collective-permute-start | bytes 393224 | tf_op jit(solution)/shard_map/ppermute | solution.py:43
  29.8 1.6 %collective-permute-start.8 = (bf16[128,4,2,64]{0,3,1,2:T(8,128)(2,1)S(1)}, bf16[128,4,2,64]{0,3,1,2:T(8,128)(2,1)S(1)}, u32[]{:S(2)}, u32[]{:S(2)}) collective-permute-start(bf16[128,4,2,64]{0,3,1,2:T(8,128)(2,1)S(1)} %get-tuple-element.56), channel_id=1, source_target_pairs={{0,8},{4,12},{8,0},{12,4},{16,24},{20,28},{24,16},{28,20},{1,9},{5... | collective-permute-start | bytes 393224 | tf_op jit(solution)/shard_map/ppermute | solution.py:43
  31.3 2.3 %collective-permute-start.10 = (bf16[128,4,2,64]{0,3,1,2:T(8,128)(2,1)S(1)}, bf16[128,4,2,64]{0,3,1,2:T(8,128)(2,1)S(1)}, u32[]{:S(2)}, u32[]{:S(2)}) collective-permute-start(bf16[128,4,2,64]{0,3,1,2:T(8,128)(2,1)S(1)} %get-tuple-element.56), channel_id=1, source_target_pairs={{0,12},{4,0},{8,4},{12,8},{16,28},{20,16},{24,20},{28,24},{1,13},{... | collective-permute-start | bytes 393224 | tf_op jit(solution)/shard_map/ppermute | solution.py:43
  33.6 0.3 convolution_convert_fusion.2
  33.9 0.1 reshape_reshape.3
  34.1 0.1 constant_dynamic-slice_fusion.2
  34.2 1.7 %collective-permute-done.5 = bf16[128,4,2,64]{0,3,1,2:T(8,128)(2,1)S(1)} collective-permute-done((bf16[128,4,2,64]{0,3,1,2:T(8,128)(2,1)S(1)}, bf16[128,4,2,64]{0,3,1,2:T(8,128)(2,1)S(1)}, u32[]{:S(2)}, u32[]{:S(2)}) %collective-permute-start.5) | collective-permute-done | bytes 131104 | tf_op jit(solution)/shard_map/ppermute | solution.py:39
  35.8 0.7 %collective-permute-start.7 = (bf16[128,4,2,64]{0,3,1,2:T(8,128)(2,1)S(1)}, bf16[128,4,2,64]{0,3,1,2:T(8,128)(2,1)S(1)}, u32[]{:S(2)}, u32[]{:S(2)}) collective-permute-start(bf16[128,4,2,64]{0,3,1,2:T(8,128)(2,1)S(1)} %collective-permute-done.5), channel_id=1, source_target_pairs={{0,4},{4,8},{8,12},{12,0},{16,20},{20,24},{24,28},{28,16},{1,5},{5... | collective-permute-start | bytes 393224 | tf_op jit(solution)/shard_map/ppermute | solution.py:44
  36.5 0.6 %collective-permute-start.9 = (bf16[128,4,2,64]{0,3,1,2:T(8,128)(2,1)S(1)}, bf16[128,4,2,64]{0,3,1,2:T(8,128)(2,1)S(1)}, u32[]{:S(2)}, u32[]{:S(2)}) collective-permute-start(bf16[128,4,2,64]{0,3,1,2:T(8,128)(2,1)S(1)} %collective-permute-done.5), channel_id=1, source_target_pairs={{0,8},{4,12},{8,0},{12,4},{16,24},{20,28},{24,16},{28,20},{1,9},{5... | collective-permute-start | bytes 393224 | tf_op jit(solution)/shard_map/ppermute | solution.py:44
  37.2 0.8 %collective-permute-done.6 = bf16[128,4,2,64]{0,3,1,2:T(8,128)(2,1)S(1)} collective-permute-done((bf16[128,4,2,64]{0,3,1,2:T(8,128)(2,1)S(1)}, bf16[128,4,2,64]{0,3,1,2:T(8,128)(2,1)S(1)}, u32[]{:S(2)}, u32[]{:S(2)}) %collective-permute-start.6) | collective-permute-done | bytes 131104 | tf_op jit(solution)/shard_map/ppermute | solution.py:43
  38.0 1.5 %collective-permute-start.11 = (bf16[128,4,2,64]{0,3,1,2:T(8,128)(2,1)S(1)}, bf16[128,4,2,64]{0,3,1,2:T(8,128)(2,1)S(1)}, u32[]{:S(2)}, u32[]{:S(2)}) collective-permute-start(bf16[128,4,2,64]{0,3,1,2:T(8,128)(2,1)S(1)} %collective-permute-done.5), channel_id=1, source_target_pairs={{0,12},{4,0},{8,4},{12,8},{16,28},{20,16},{24,20},{28,24},{1,13},{... | collective-permute-start | bytes 393224 | tf_op jit(solution)/shard_map/ppermute | solution.py:44
  39.6 3.9 %collective-permute-done.7 = bf16[128,4,2,64]{0,3,1,2:T(8,128)(2,1)S(1)} collective-permute-done((bf16[128,4,2,64]{0,3,1,2:T(8,128)(2,1)S(1)}, bf16[128,4,2,64]{0,3,1,2:T(8,128)(2,1)S(1)}, u32[]{:S(2)}, u32[]{:S(2)}) %collective-permute-start.7) | collective-permute-done | bytes 131104 | tf_op jit(solution)/shard_map/ppermute | solution.py:44
  43.6 0.0 collective-permute-done.8
  43.6 0.0 collective-permute-done.9
  43.7 0.0 collective-permute-done.10
  43.7 1.0 %collective-permute-done.11 = bf16[128,4,2,64]{0,3,1,2:T(8,128)(2,1)S(1)} collective-permute-done((bf16[128,4,2,64]{0,3,1,2:T(8,128)(2,1)S(1)}, bf16[128,4,2,64]{0,3,1,2:T(8,128)(2,1)S(1)}, u32[]{:S(2)}, u32[]{:S(2)}) %collective-permute-start.11) | collective-permute-done | bytes 131104 | tf_op jit(solution)/shard_map/ppermute | solution.py:44
  44.8 0.4 fusion.47
  45.2 0.3 fusion.6
  45.5 0.4 fusion.5
  45.8 0.1 copy.28
  45.9 0.1 reshape.260
  46.0 0.0 copy-done
  46.0 0.2 convolution_convert_fusion
  46.3 1.6 %collective-permute-start.13 = (bf16[32,1024]{1,0:T(8,128)(2,1)S(1)}, bf16[32,1024]{1,0:T(8,128)(2,1)S(1)}, u32[]{:S(2)}, u32[]{:S(2)}) collective-permute-start(bf16[32,1024]{1,0:T(8,128)(2,1)S(1)} %get-tuple-element.47), channel_id=1, source_target_pairs={{0,2},{1,3},{2,0},{3,1},{4,6},{5,7},{6,4},{7,5},{8,10},{9,11},{10,... | collective-permute-start | bytes 196616 | tf_op jit(solution)/shard_map/ppermute | solution.py:201
  47.8 0.0 collective-permute-start.14
  47.8 0.4 fusion.48
  48.2 0.3 fusion.8
  48.5 0.4 fusion.4
  48.9 0.1 copy.29
  49.0 0.1 dot_general.43
  49.1 0.2 fusion.37
  49.3 0.7 %collective-permute-start.12 = (f32[32,1024]{1,0:T(8,128)S(1)}, f32[32,1024]{1,0:T(8,128)S(1)}, u32[]{:S(2)}, u32[]{:S(2)}) collective-permute-start(f32[32,1024]{1,0:T(8,128)S(1)} %get-tuple-element.43), channel_id=1, source_target_pairs={{0,1},{1,0},{2,3},{3,2},{4,5},{5,4},{6,7},{7,6},{8,9},{9,8},{10,11... | collective-permute-start | bytes 393224 | tf_op jit(solution)/shard_map/ppermute | solution.py:213
  50.0 0.1 reshape.262
  50.1 0.5 collective-permute-done.13
  50.6 1.4 %collective-permute-done.14 = bf16[32,1024]{1,0:T(8,128)(2,1)S(1)} collective-permute-done((bf16[32,1024]{1,0:T(8,128)(2,1)S(1)}, bf16[32,1024]{1,0:T(8,128)(2,1)S(1)}, u32[]{:S(2)}, u32[]{:S(2)}) %collective-permute-start.14) | collective-permute-done | bytes 65568 | tf_op jit(solution)/shard_map/ppermute | solution.py:202
  52.0 0.1 add.269
  52.1 0.0 collective-permute-done.12
  52.1 0.1 reshape.263
  52.2 0.7 %add_convert_fusion.1 = bf16[1,16,2,1024]{3,2,1,0:T(2,128)(2,1)} fusion(f32[1,16,2,1024]{3,2,1,0:T(2,128)S(1)} %add.269, f32[1,16,2,1024]{3,2,1,0:T(2,128)S(1)} %reshape.262, f32[1,16,2,1024]{3,2,1,0:T(2,128)S(1)} %reshape.263), kind=kLoop, calls=%fused_computation.84 | loop fusion | flops 98304 | bytes 458752 | tf_op jit(solution)/shard_map/convert_element_type | solution.py:216
  (26 shorter events, 0.5 us)
Async XLA Ops:
  0.0 46.0 %copy-start = (bf16[256,1024]{1,0:T(8,128)(2,1)S(1)}, bf16[256,1024]{1,0:T(8,128)(2,1)}, u32[]{:S(2)}) copy-start(bf16[256,1024]{1,0:T(8,128)(2,1)} %param.9) | copy-start | bytes 1572868
  0.9 11.1 %collective-permute-start = (bf16[1,16,2,1024]{3,1,2,0:T(8,128)(2,1)S(1)}, bf16[1,16,2,1024]{3,1,2,0:T(8,128)(2,1)S(1)}, u32[]{:S(2)}, u32[]{:S(2)}) collective-permute-start(bf16[1,16,2,1024]{3,1,2,0:T(8,128)(2,1)S(1)} %copy.13), channel_id=1, source_target_pairs={{0,4},{4,8},{8,12},{12,16},{16,20},{20,24},{24,28},{1,5},{5,9},{9,... | collective-permute-start | bytes 196616 | tf_op jit(solution)/shard_map/ppermute | solution.py:18
  5.8 6.3 %collective-permute-start.1 = (bf16[1,16,2,1024]{3,1,2,0:T(8,128)(2,1)S(1)}, bf16[1,16,2,1024]{3,1,2,0:T(8,128)(2,1)S(1)}, u32[]{:S(2)}, u32[]{:S(2)}) collective-permute-start(bf16[1,16,2,1024]{3,1,2,0:T(8,128)(2,1)S(1)} %copy.13), channel_id=1, source_target_pairs={{4,0},{8,4},{12,8},{16,12},{20,16},{24,20},{28,24},{5,1},{9,5},{13... | collective-permute-start | bytes 196616 | tf_op jit(solution)/shard_map/ppermute | solution.py:19
  9.5 2.6 %copy-start.1 = (bf16[1,16,2,1024]{3,2,1,0:T(2,128)(2,1)S(1)}, bf16[1,16,2,1024]{3,2,1,0:T(2,128)(2,1)}, u32[]{:S(2)}) copy-start(bf16[1,16,2,1024]{3,2,1,0:T(2,128)(2,1)} %param.5) | copy-start | bytes 196612
  12.1 7.4 %collective-permute-start.2 = (bf16[3,16,2,1024]{3,1,2,0:T(8,128)(2,1)S(1)}, bf16[3,16,2,1024]{3,1,2,0:T(8,128)(2,1)S(1)}, u32[]{:S(2)}, u32[]{:S(2)}) collective-permute-start(bf16[3,16,2,1024]{3,1,2,0:T(8,128)(2,1)S(1)} %constant_dynamic-update-slice_fusion), channel_id=1, source_target_pairs={{0,1},{1,0},{2,3},{3,2},{4,5},{5,4},{6,7},{7,6},{8,9},{9,8},{10,11... | collective-permute-start | bytes 589832 | tf_op jit(solution)/shard_map/ppermute | solution.py:60
  12.2 7.3 %collective-permute-start.3 = (bf16[3,16,2,1024]{3,1,2,0:T(8,128)(2,1)S(1)}, bf16[3,16,2,1024]{3,1,2,0:T(8,128)(2,1)S(1)}, u32[]{:S(2)}, u32[]{:S(2)}) collective-permute-start(bf16[3,16,2,1024]{3,1,2,0:T(8,128)(2,1)S(1)} %constant_dynamic-update-slice_fusion), channel_id=1, source_target_pairs={{0,2},{1,3},{2,0},{3,1},{4,6},{5,7},{6,4},{7,5},{8,10},{9,11},{10,... | collective-permute-start | bytes 589832 | tf_op jit(solution)/shard_map/ppermute | solution.py:64
  13.8 7.2 %copy-start.2 = (f32[1024]{0:T(1024)S(1)}, f32[1024]{0:T(1024)}, u32[]{:S(2)}) copy-start(f32[1024]{0:T(1024)} %param.7) | copy-start | bytes 12292
  19.5 1.4 %collective-permute-start.4 = (bf16[3,16,2,1024]{3,1,2,0:T(8,128)(2,1)S(1)}, bf16[3,16,2,1024]{3,1,2,0:T(8,128)(2,1)S(1)}, u32[]{:S(2)}, u32[]{:S(2)}) collective-permute-start(bf16[3,16,2,1024]{3,1,2,0:T(8,128)(2,1)S(1)} %collective-permute-done.3), channel_id=1, source_target_pairs={{0,1},{1,0},{2,3},{3,2},{4,5},{5,4},{6,7},{7,6},{8,9},{9,8},{10,11... | collective-permute-start | bytes 589832 | tf_op jit(solution)/shard_map/ppermute | solution.py:66
  24.5 11.4 %collective-permute-start.5 = (bf16[128,4,2,64]{0,3,1,2:T(8,128)(2,1)S(1)}, bf16[128,4,2,64]{0,3,1,2:T(8,128)(2,1)S(1)}, u32[]{:S(2)}, u32[]{:S(2)}) collective-permute-start(bf16[128,4,2,64]{0,3,1,2:T(8,128)(2,1)S(1)} %get-tuple-element.56), channel_id=1, source_target_pairs={{0,16},{4,20},{8,24},{12,28},{16,0},{20,4},{24,8},{28,12},{1,17},{... | collective-permute-start | bytes 393224 | tf_op jit(solution)/shard_map/ppermute | solution.py:39
  29.1 8.9 %collective-permute-start.6 = (bf16[128,4,2,64]{0,3,1,2:T(8,128)(2,1)S(1)}, bf16[128,4,2,64]{0,3,1,2:T(8,128)(2,1)S(1)}, u32[]{:S(2)}, u32[]{:S(2)}) collective-permute-start(bf16[128,4,2,64]{0,3,1,2:T(8,128)(2,1)S(1)} %get-tuple-element.56), channel_id=1, source_target_pairs={{0,4},{4,8},{8,12},{12,0},{16,20},{20,24},{24,28},{28,16},{1,5},{5... | collective-permute-start | bytes 393224 | tf_op jit(solution)/shard_map/ppermute | solution.py:43
  29.8 13.8 %collective-permute-start.8 = (bf16[128,4,2,64]{0,3,1,2:T(8,128)(2,1)S(1)}, bf16[128,4,2,64]{0,3,1,2:T(8,128)(2,1)S(1)}, u32[]{:S(2)}, u32[]{:S(2)}) collective-permute-start(bf16[128,4,2,64]{0,3,1,2:T(8,128)(2,1)S(1)} %get-tuple-element.56), channel_id=1, source_target_pairs={{0,8},{4,12},{8,0},{12,4},{16,24},{20,28},{24,16},{28,20},{1,9},{5... | collective-permute-start | bytes 393224 | tf_op jit(solution)/shard_map/ppermute | solution.py:43
  31.3 12.3 %collective-permute-start.10 = (bf16[128,4,2,64]{0,3,1,2:T(8,128)(2,1)S(1)}, bf16[128,4,2,64]{0,3,1,2:T(8,128)(2,1)S(1)}, u32[]{:S(2)}, u32[]{:S(2)}) collective-permute-start(bf16[128,4,2,64]{0,3,1,2:T(8,128)(2,1)S(1)} %get-tuple-element.56), channel_id=1, source_target_pairs={{0,12},{4,0},{8,4},{12,8},{16,28},{20,16},{24,20},{28,24},{1,13},{... | collective-permute-start | bytes 393224 | tf_op jit(solution)/shard_map/ppermute | solution.py:43
  35.8 7.7 %collective-permute-start.7 = (bf16[128,4,2,64]{0,3,1,2:T(8,128)(2,1)S(1)}, bf16[128,4,2,64]{0,3,1,2:T(8,128)(2,1)S(1)}, u32[]{:S(2)}, u32[]{:S(2)}) collective-permute-start(bf16[128,4,2,64]{0,3,1,2:T(8,128)(2,1)S(1)} %collective-permute-done.5), channel_id=1, source_target_pairs={{0,4},{4,8},{8,12},{12,0},{16,20},{20,24},{24,28},{28,16},{1,5},{5... | collective-permute-start | bytes 393224 | tf_op jit(solution)/shard_map/ppermute | solution.py:44
  36.5 7.1 %collective-permute-start.9 = (bf16[128,4,2,64]{0,3,1,2:T(8,128)(2,1)S(1)}, bf16[128,4,2,64]{0,3,1,2:T(8,128)(2,1)S(1)}, u32[]{:S(2)}, u32[]{:S(2)}) collective-permute-start(bf16[128,4,2,64]{0,3,1,2:T(8,128)(2,1)S(1)} %collective-permute-done.5), channel_id=1, source_target_pairs={{0,8},{4,12},{8,0},{12,4},{16,24},{20,28},{24,16},{28,20},{1,9},{5... | collective-permute-start | bytes 393224 | tf_op jit(solution)/shard_map/ppermute | solution.py:44
  38.0 6.7 %collective-permute-start.11 = (bf16[128,4,2,64]{0,3,1,2:T(8,128)(2,1)S(1)}, bf16[128,4,2,64]{0,3,1,2:T(8,128)(2,1)S(1)}, u32[]{:S(2)}, u32[]{:S(2)}) collective-permute-start(bf16[128,4,2,64]{0,3,1,2:T(8,128)(2,1)S(1)} %collective-permute-done.5), channel_id=1, source_target_pairs={{0,12},{4,0},{8,4},{12,8},{16,28},{20,16},{24,20},{28,24},{1,13},{... | collective-permute-start | bytes 393224 | tf_op jit(solution)/shard_map/ppermute | solution.py:44
  46.3 4.3 %collective-permute-start.13 = (bf16[32,1024]{1,0:T(8,128)(2,1)S(1)}, bf16[32,1024]{1,0:T(8,128)(2,1)S(1)}, u32[]{:S(2)}, u32[]{:S(2)}) collective-permute-start(bf16[32,1024]{1,0:T(8,128)(2,1)S(1)} %get-tuple-element.47), channel_id=1, source_target_pairs={{0,2},{1,3},{2,0},{3,1},{4,6},{5,7},{6,4},{7,5},{8,10},{9,11},{10,... | collective-permute-start | bytes 196616 | tf_op jit(solution)/shard_map/ppermute | solution.py:201
  47.8 4.2 %collective-permute-start.14 = (bf16[32,1024]{1,0:T(8,128)(2,1)S(1)}, bf16[32,1024]{1,0:T(8,128)(2,1)S(1)}, u32[]{:S(2)}, u32[]{:S(2)}) collective-permute-start(bf16[32,1024]{1,0:T(8,128)(2,1)S(1)} %get-tuple-element.48), channel_id=1, source_target_pairs={{0,3},{1,2},{2,1},{3,0},{4,7},{5,6},{6,5},{7,4},{8,11},{9,10},{10,... | collective-permute-start | bytes 196616 | tf_op jit(solution)/shard_map/ppermute | solution.py:202
  49.3 2.8 %collective-permute-start.12 = (f32[32,1024]{1,0:T(8,128)S(1)}, f32[32,1024]{1,0:T(8,128)S(1)}, u32[]{:S(2)}, u32[]{:S(2)}) collective-permute-start(f32[32,1024]{1,0:T(8,128)S(1)} %get-tuple-element.43), channel_id=1, source_target_pairs={{0,1},{1,0},{2,3},{3,2},{4,5},{5,4},{6,7},{7,6},{8,9},{9,8},{10,11... | collective-permute-start | bytes 393224 | tf_op jit(solution)/shard_map/ppermute | solution.py:213

commit v12 on v7

--- a/solution.py
+++ b/solution.py
@@ -184,22 +184,18 @@
     chips, core, chip = groups // 2, rank % 2, rank // 2
     pair_queries = queries.reshape(chips, 2 * local_tok, heads_here, HS)
     total = None
+    partner = [(i, i ^ 1) for i in range(groups)]
     for shift in range(1, chips):
         far_rows = lax.dynamic_index_in_dim(pair_queries, (chip + shift) % chips, 0, keepdims=False)
         far_partial = jnp.dot(attend(far_rows), out_weight, preferred_element_type=jnp.float32)
-        far_partial = far_partial.astype(jnp.bfloat16).reshape(2, local_tok, features)
-        same_core = lax.dynamic_index_in_dim(far_partial, core, 0, keepdims=False)
-        other_core = lax.dynamic_index_in_dim(far_partial, 1 - core, 0, keepdims=False)
-        far_sent = (same_core, other_core)
-        to_other_core = [
-            (i, ((i // 2 + shift) % chips) * 2 + 1 - i % 2) for i in range(groups)
-        ]
-        for arrived in (
-            lax.ppermute(same_core, "uly", chip_shift(groups, shift)),
-            lax.ppermute(other_core, "uly", to_other_core),
-        ):
-            arrived = arrived.astype(jnp.float32).reshape(tokens.shape)
-            total = arrived if total is None else total + arrived
+        far_partial = far_partial.reshape(2, local_tok, features)
+        mine = lax.dynamic_index_in_dim(far_partial, core, 0, keepdims=False)
+        for_partner = lax.dynamic_index_in_dim(far_partial, 1 - core, 0, keepdims=False)
+        far_sent = for_partner
+        chip_sum = mine + lax.ppermute(for_partner, "uly", partner)
+        arrived = lax.ppermute(chip_sum.astype(jnp.bfloat16), "uly", chip_shift(groups, shift))
+        arrived = arrived.astype(jnp.float32).reshape(tokens.shape)
+        total = arrived if total is None else total + arrived
     near_rows = lax.dynamic_index_in_dim(pair_queries, chip, 0, keepdims=False)
     if total is not None:
         near_rows, unused = lax.optimization_barrier((near_rows, far_sent))
@@ -207,7 +203,7 @@
     near_partial = near_partial.reshape(2, local_tok, features)
     own = lax.dynamic_index_in_dim(near_partial, core, 0, keepdims=False)
     for_partner = lax.dynamic_index_in_dim(near_partial, 1 - core, 0, keepdims=False)
-    from_partner = lax.ppermute(for_partner, "uly", [(i, i ^ 1) for i in range(groups)])
+    from_partner = lax.ppermute(for_partner, "uly", partner)
     near_sum = own.reshape(tokens.shape) + from_partner.reshape(tokens.shape)
     result = near_sum if total is None else near_sum + total
     return result.astype(jnp.bfloat16)

time: 52.3 us -> 54.4 us (1.040)
  other arithmetic: 3.75 us -> 4.65 us
  waiting for transfers between devices: 15.7 us -> 16.4 us
  local copies, waits for them, and re-layouts: 8.45 us -> 9.12 us
    convert_element_type x0 -> x1, other arithmetic: none -> 0.92 us  [on_device(): chip_sum.astype(jnp.bfloat16)]
    ppermute x3, waiting for transfers between devices: 1.9 us -> 2.61 us  [the longest x1 2.6 us: on_device(): lax.ppermute(chip_sum.astype(jnp.bfloat16), 'uly', chip_shift(groups, shi...]
    squeeze x1, local copies, waits for them, and re-layouts: 0.02 us -> 0.67 us  [on_device(): lax.dynamic_index_in_dim(far_partial, 1 - core, 0, keepdims=False)]
  transfers between devices with their start and end apart: 15 -> 15, of which waited for: 9 -> 8; matrix products, arithmetic and copies ran while one was open for 15% -> 16% of each run, Pallas kernels for 0% -> 0%
where the time goes in v12:
time: 54.4 us; the launch traced here: 53.9 us
  starting transfers between devices  20.8 us (38%)
  waiting for transfers between devices  16.4 us (30%)
  local copies, waits for them, and re-layouts  9.12 us (17%)
  other arithmetic  4.65 us (9%)
  matrix products  2.49 us (5%)
    ppermute x1, waiting for transfers between devices, gathered_by_chip(): far = lax.ppermute(piece, axis, chip_shift(size, shift))  5.62 us
    ppermute x1, starting transfers between devices, padded_2(): before = lax.ppermute(last, axis, up)  4.87 us
    ppermute x3, starting transfers between devices, relayed(): parts.append(lax.ppermute(piece, axis, pairs))  4.5 us
    unnamed x16, local copies, waits for them, and re-layouts  4.1 us
    ppermute x3, starting transfers between devices, relayed(): parts.append(lax.ppermute(crossed, axis, pairs))  3.23 us
    ppermute x3, waiting for transfers between devices, relayed(): parts.append(lax.ppermute(crossed, axis, pairs))  3.23 us
    ppermute x1, starting transfers between devices, relayed(): crossed = lax.ppermute(piece, axis, mirror)  3.2 us
    ppermute x1, waiting for transfers between devices, on_device(): lax.ppermute(chip_sum.astype(jnp.bfloat16), 'uly', chip_shift(groups, shi...  2.6 us
  transfers between devices with their start and end apart: 15, of which 8 were waited for; matrix products, arithmetic and copies ran while one was open for 16% of the time, Pallas kernels for 0%

profile of v12, /device:TPU:0, one launch (start us, length us, event | category | flops | bytes accessed | tf_op | source)
XLA Modules:
  0.0 53.9 jit_solution(11553026014197786454)
XLA Ops:
  0.0 1.0 %copy.21 = bf16[1,16,2,1024]{3,1,2,0:T(8,128)(2,1)S(1)} copy(bf16[1,16,2,1024]{3,2,1,0:T(2,128)(2,1)} %param.5) | data formatting | bytes 131072 | tf_op args[0]
  1.0 4.9 %collective-permute-start = (bf16[1,16,2,1024]{3,1,2,0:T(8,128)(2,1)S(1)}, bf16[1,16,2,1024]{3,1,2,0:T(8,128)(2,1)S(1)}, u32[]{:S(2)}, u32[]{:S(2)}) collective-permute-start(bf16[1,16,2,1024]{3,1,2,0:T(8,128)(2,1)S(1)} %copy.21), channel_id=1, source_target_pairs={{0,4},{4,8},{8,12},{12,16},{16,20},{20,24},{24,28},{1,5},{5,9},{9,... | collective-permute-start | bytes 196616 | tf_op jit(solution)/shard_map/ppermute | solution.py:18
  5.9 1.3 %collective-permute-start.1 = (bf16[1,16,2,1024]{3,1,2,0:T(8,128)(2,1)S(1)}, bf16[1,16,2,1024]{3,1,2,0:T(8,128)(2,1)S(1)}, u32[]{:S(2)}, u32[]{:S(2)}) collective-permute-start(bf16[1,16,2,1024]{3,1,2,0:T(8,128)(2,1)S(1)} %copy.21), channel_id=1, source_target_pairs={{4,0},{8,4},{12,8},{16,12},{20,16},{24,20},{28,24},{5,1},{9,5},{13... | collective-permute-start | bytes 196616 | tf_op jit(solution)/shard_map/ppermute | solution.py:19
  7.2 1.3 %fusion.47 = (f32[1,1024]{1,0:T(1,128)S(1)}, f32[1,1024]{1,0:T(1,128)S(1)}, f32[1,1024]{1,0:T(1,128)S(1)}, f32[1,1024]{1,0:T(1,128)S(1)}, f32[1,1024]{1,0:T(1,12...) fusion(f32[27,1024]{1,0:T(8,128)} %param.6), kind=kLoop, calls=%fused_computation.112 | loop fusion | bytes 155648 | tf_op jit(solution)/shard_map/slice | solution.py:121
  8.5 1.0 %fusion.48 = (f32[1,1024]{1,0:T(1,128)S(1)}, f32[1,1024]{1,0:T(1,128)S(1)}, f32[1,1024]{1,0:T(1,128)S(1)}, f32[1,1024]{1,0:T(1,128)S(1)}, f32[1,1024]{1,0:T(1,12...) fusion(f32[27,1024]{1,0:T(8,128)} %param.6), kind=kLoop, calls=%fused_computation.113 | loop fusion | bytes 65536 | tf_op jit(solution)/shard_map/slice | solution.py:121
  9.6 0.0 collective-permute-done
  9.6 0.9 %constant_dynamic-update-slice_fusion.1 = bf16[3,16,2,1024]{3,1,2,0:T(8,128)(2,1)S(1)} fusion(bf16[3,16,2,1024]{3,1,2,0:T(8,128)(2,1)S(1)} %constant_dynamic-update-slice_fusion.2, bf16[1,16,2,1024]{3,2,1,0:T(2,128)(2,1)} %param.5), kind=kLoop, calls=%fused_computation.91 | loop fusion | bytes 131072
  10.4 1.6 %collective-permute-done.1 = bf16[1,16,2,1024]{3,1,2,0:T(8,128)(2,1)S(1)} collective-permute-done((bf16[1,16,2,1024]{3,1,2,0:T(8,128)(2,1)S(1)}, bf16[1,16,2,1024]{3,1,2,0:T(8,128)(2,1)S(1)}, u32[]{:S(2)}, u32[]{:S(2)}) %collective-permute-start.1) | collective-permute-done | bytes 65568 | tf_op jit(solution)/shard_map/ppermute | solution.py:19
  12.0 0.0 collective-permute-start.2
  12.0 1.6 %collective-permute-start.3 = (bf16[3,16,2,1024]{3,1,2,0:T(8,128)(2,1)S(1)}, bf16[3,16,2,1024]{3,1,2,0:T(8,128)(2,1)S(1)}, u32[]{:S(2)}, u32[]{:S(2)}) collective-permute-start(bf16[3,16,2,1024]{3,1,2,0:T(8,128)(2,1)S(1)} %constant_dynamic-update-slice_fusion), channel_id=1, source_target_pairs={{0,2},{1,3},{2,0},{3,1},{4,6},{5,7},{6,4},{7,5},{8,10},{9,11},{10,... | collective-permute-start | bytes 589832 | tf_op jit(solution)/shard_map/ppermute | solution.py:64
  13.6 0.1 broadcast_in_dim.27
  13.7 0.0 copy-start.2
  13.7 5.6 %collective-permute-done.3 = bf16[3,16,2,1024]{3,1,2,0:T(8,128)(2,1)S(1)} collective-permute-done((bf16[3,16,2,1024]{3,1,2,0:T(8,128)(2,1)S(1)}, bf16[3,16,2,1024]{3,1,2,0:T(8,128)(2,1)S(1)}, u32[]{:S(2)}, u32[]{:S(2)}) %collective-permute-start.3) | collective-permute-done | bytes 196640 | tf_op jit(solution)/shard_map/ppermute | solution.py:64
  19.3 0.0 collective-permute-start.4
  19.3 0.0 collective-permute-done.2
  19.4 1.4 %collective-permute-done.4 = bf16[3,16,2,1024]{3,1,2,0:T(8,128)(2,1)S(1)} collective-permute-done((bf16[3,16,2,1024]{3,1,2,0:T(8,128)(2,1)S(1)}, bf16[3,16,2,1024]{3,1,2,0:T(8,128)(2,1)S(1)}, u32[]{:S(2)}, u32[]{:S(2)}) %collective-permute-start.4) | collective-permute-done | bytes 196640 | tf_op jit(solution)/shard_map/ppermute | solution.py:66
  20.8 0.1 fusion.45
  20.9 2.3 %add_convert_fusion = bf16[1,16,8,1024]{3,1,2,0:T(8,128)(2,1)S(1)} fusion(bf16[1,16,8,1024]{3,1,2,0:T(8,128)(2,1)S(1)} %bitcast.131, bf16[1,16,8,1024]{3,1,2,0:T(8,128)(2,1)S(1)} %bitcast.130, bf16[1,16,8,1024]{3,1,2,0:T(8,128)(2,1)S(1)} %bitcast.129, bf16[3,16,8,1024]{3,1,2,0:T(8,128)(2,1)S(1)} %bitcast.126, f32[1024]{0:T(1024)S(1)} %bitcast.160, ...), kind=kLoop, calls=%fused_computation.78 | loop fusion | flops 10878976 | bytes 1949696 | tf_op jit(solution)/shard_map/convert_element_type | solution.py:128
  23.2 0.3 copy.39
  23.5 0.1 reshape.239
  23.6 0.7 %convolution_convert_fusion = bf16[128,768]{1,0:T(8,128)(2,1)S(1)} fusion(bf16[128,1024]{1,0:T(8,128)(2,1)S(1)} %reshape.239, bf16[768,1024]{1,0:T(8,128)(2,1)S(1)} %copy-done), kind=kOutput, calls=%fused_computation.26 | convolution fusion | flops 201424896 | bytes 2031616 | tf_op jit(solution)/shard_map/dot_general | solution.py:100
  24.3 0.2 copy.28
  24.5 3.2 %collective-permute-start.5 = (bf16[128,4,2,64]{0,3,1,2:T(8,128)(2,1)S(1)}, bf16[128,4,2,64]{0,3,1,2:T(8,128)(2,1)S(1)}, u32[]{:S(2)}, u32[]{:S(2)}) collective-permute-start(bf16[128,4,2,64]{0,3,1,2:T(8,128)(2,1)S(1)} %get-tuple-element.47), channel_id=1, source_target_pairs={{0,16},{4,20},{8,24},{12,28},{16,0},{20,4},{24,8},{28,12},{1,17},{... | collective-permute-start | bytes 393224 | tf_op jit(solution)/shard_map/ppermute | solution.py:39
  27.7 1.9 %collective-permute-start.6 = (bf16[128,4,2,64]{0,3,1,2:T(8,128)(2,1)S(1)}, bf16[128,4,2,64]{0,3,1,2:T(8,128)(2,1)}, u32[]{:S(2)}, u32[]{:S(2)}) collective-permute-start(bf16[128,4,2,64]{0,3,1,2:T(8,128)(2,1)S(1)} %get-tuple-element.47), channel_id=1, source_target_pairs={{0,4},{4,8},{8,12},{12,0},{16,20},{20,24},{24,28},{28,16},{1,5},{5... | collective-permute-start | bytes 393224 | tf_op jit(solution)/shard_map/ppermute | solution.py:43
  29.6 0.3 collective-permute-start.8
  29.9 2.3 %collective-permute-start.10 = (bf16[128,4,2,64]{0,3,1,2:T(8,128)(2,1)S(1)}, bf16[128,4,2,64]{0,3,1,2:T(8,128)(2,1)S(1)}, u32[]{:S(2)}, u32[]{:S(2)}) collective-permute-start(bf16[128,4,2,64]{0,3,1,2:T(8,128)(2,1)S(1)} %get-tuple-element.47), channel_id=1, source_target_pairs={{0,12},{4,0},{8,4},{12,8},{16,28},{20,16},{24,20},{28,24},{1,13},{... | collective-permute-start | bytes 393224 | tf_op jit(solution)/shard_map/ppermute | solution.py:43
  32.2 0.1 reshape_squeeze.2
  32.3 0.3 constant_dynamic-slice_fusion.2
  32.6 0.1 copy.30
  32.7 0.1 copy.29
  32.9 1.6 %collective-permute-done.5 = bf16[128,4,2,64]{0,3,1,2:T(8,128)(2,1)S(1)} collective-permute-done((bf16[128,4,2,64]{0,3,1,2:T(8,128)(2,1)S(1)}, bf16[128,4,2,64]{0,3,1,2:T(8,128)(2,1)S(1)}, u32[]{:S(2)}, u32[]{:S(2)}) %collective-permute-start.5) | collective-permute-done | bytes 131104 | tf_op jit(solution)/shard_map/ppermute | solution.py:39
  34.4 1.9 %collective-permute-start.7 = (bf16[128,4,2,64]{0,3,1,2:T(8,128)(2,1)S(1)}, bf16[128,4,2,64]{0,3,1,2:T(8,128)(2,1)S(1)}, u32[]{:S(2)}, u32[]{:S(2)}) collective-permute-start(bf16[128,4,2,64]{0,3,1,2:T(8,128)(2,1)S(1)} %collective-permute-done.5), channel_id=1, source_target_pairs={{0,4},{4,8},{8,12},{12,0},{16,20},{20,24},{24,28},{28,16},{1,5},{5... | collective-permute-start | bytes 393224 | tf_op jit(solution)/shard_map/ppermute | solution.py:44
  36.4 0.0 collective-permute-start.9
  36.4 0.4 collective-permute-done.6
  36.8 1.3 %collective-permute-start.11 = (bf16[128,4,2,64]{0,3,1,2:T(8,128)(2,1)S(1)}, bf16[128,4,2,64]{0,3,1,2:T(8,128)(2,1)S(1)}, u32[]{:S(2)}, u32[]{:S(2)}) collective-permute-start(bf16[128,4,2,64]{0,3,1,2:T(8,128)(2,1)S(1)} %collective-permute-done.5), channel_id=1, source_target_pairs={{0,12},{4,0},{8,4},{12,8},{16,28},{20,16},{24,20},{28,24},{1,13},{... | collective-permute-start | bytes 393224 | tf_op jit(solution)/shard_map/ppermute | solution.py:44
  38.1 0.9 %constant_dynamic-update-slice_fusion.8 = bf16[1024,4,2,64]{0,3,1,2:T(8,128)(2,1)S(1)} fusion(bf16[1024,4,2,64]{0,3,1,2:T(8,128)(2,1)S(1)} %constant_dynamic-update-slice_fusion.9, bf16[128,4,2,64]{0,3,1,2:T(8,128)(2,1)} %collective-permute-done.6), kind=kLoop, calls=%fused_computation.98 | loop fusion | bytes 262144
  39.1 3.2 %collective-permute-done.7 = bf16[128,4,2,64]{0,3,1,2:T(8,128)(2,1)S(1)} collective-permute-done((bf16[128,4,2,64]{0,3,1,2:T(8,128)(2,1)S(1)}, bf16[128,4,2,64]{0,3,1,2:T(8,128)(2,1)S(1)}, u32[]{:S(2)}, u32[]{:S(2)}) %collective-permute-start.7) | collective-permute-done | bytes 131104 | tf_op jit(solution)/shard_map/ppermute | solution.py:44
  42.3 0.9 %constant_dynamic-update-slice_fusion.6 = bf16[1024,4,2,64]{0,3,1,2:T(8,128)(2,1)S(1)} fusion(bf16[1024,4,2,64]{0,3,1,2:T(8,128)(2,1)S(1)} %constant_dynamic-update-slice_fusion.7, bf16[128,4,2,64]{0,3,1,2:T(8,128)(2,1)} %collective-permute-done.8), kind=kLoop, calls=%fused_computation.96 | loop fusion | bytes 262144
  43.4 0.1 collective-permute-done.11
  43.5 0.4 fusion.49
  43.8 0.0 copy-start.1
  43.8 0.3 fusion.6
  44.2 0.4 fusion.5
  44.5 0.1 copy.32
  44.6 0.1 dot_general.37
  44.7 0.2 copy-done.1
  44.9 0.2 fusion.39
  45.1 0.7 %dynamic-slice_bitcast_fusion.1 = f32[32,1024]{1,0:T(8,128)} fusion(f32[2,32,1024]{2,1,0:T(8,128)S(1)} %fusion.39, s32[]{:T(128)S(6)} %select_n.61), kind=kLoop, calls=%fused_computation.88 | loop fusion | bytes 262148 | tf_op jit(solution)/shard_map/jit(dynamic_index_in_dim)/squeeze | solution.py:193
  45.8 0.0 collective-permute-start.13
  45.8 0.4 fusion.50
  46.1 0.3 fusion.8
  46.5 0.4 fusion.4
  46.8 0.1 copy.33
  46.9 0.1 dot_general.42
  47.0 0.2 fusion.37
  47.3 0.6 %collective-permute-start.12 = (f32[32,1024]{1,0:T(8,128)S(1)}, f32[32,1024]{1,0:T(8,128)S(1)}, u32[]{:S(2)}, u32[]{:S(2)}) collective-permute-start(f32[32,1024]{1,0:T(8,128)S(1)} %get-tuple-element.43), channel_id=1, source_target_pairs={{0,1},{1,0},{2,3},{3,2},{4,5},{5,4},{6,7},{7,6},{8,9},{9,8},{10,11... | collective-permute-start | bytes 393224 | tf_op jit(solution)/shard_map/ppermute | solution.py:206
  47.8 0.0 collective-permute-done.13
  47.8 0.9 %fusion.43 = bf16[32,1024]{1,0:T(8,128)(2,1)S(1)} fusion(f32[32,1024]{1,0:T(8,128)} %collective-permute-done.13, f32[2,32,1024]{2,1,0:T(8,128)S(1)} %fusion.39, s32[]{:T(128)S(6)} %select_n.62), kind=kLoop, calls=%fused_computation.85 | loop fusion | flops 65536 | bytes 327684 | tf_op jit(solution)/shard_map/convert_element_type | solution.py:196
  48.8 1.6 %collective-permute-start.14 = (bf16[32,1024]{1,0:T(8,128)(2,1)S(1)}, bf16[32,1024]{1,0:T(8,128)(2,1)S(1)}, u32[]{:S(2)}, u32[]{:S(2)}) collective-permute-start(bf16[32,1024]{1,0:T(8,128)(2,1)S(1)} %fusion.43), channel_id=1, source_target_pairs={{0,2},{1,3},{2,0},{3,1},{4,6},{5,7},{6,4},{7,5},{8,10},{9,11},{10,... | collective-permute-start | bytes 196616 | tf_op jit(solution)/shard_map/ppermute | solution.py:196
  50.3 0.1 reshape.241
  50.4 0.1 reshape.242
  50.5 2.6 %collective-permute-done.14 = bf16[32,1024]{1,0:T(8,128)(2,1)S(1)} collective-permute-done((bf16[32,1024]{1,0:T(8,128)(2,1)S(1)}, bf16[32,1024]{1,0:T(8,128)(2,1)S(1)}, u32[]{:S(2)}, u32[]{:S(2)}) %collective-permute-start.14) | collective-permute-done | bytes 65568 | tf_op jit(solution)/shard_map/ppermute | solution.py:196
  53.1 0.1 reshape.249
  53.2 0.7 %add_convert_fusion.1 = bf16[1,16,2,1024]{3,2,1,0:T(2,128)(2,1)} fusion(f32[1,16,2,1024]{3,2,1,0:T(2,128)S(1)} %reshape.249, f32[1,16,2,1024]{3,2,1,0:T(2,128)S(1)} %reshape.241, f32[1,16,2,1024]{3,2,1,0:T(2,128)S(1)} %reshape.242), kind=kLoop, calls=%fused_computation.86 | loop fusion | flops 98304 | bytes 458752 | tf_op jit(solution)/shard_map/convert_element_type | solution.py:209
  (25 shorter events, 0.4 us)
Async XLA Ops:
  0.0 23.6 %copy-start = (bf16[768,1024]{1,0:T(8,128)(2,1)S(1)}, bf16[768,1024]{1,0:T(8,128)(2,1)}, u32[]{:S(2)}) copy-start(bf16[768,1024]{1,0:T(8,128)(2,1)} %param.8) | copy-start | bytes 4718596
  1.0 8.6 %collective-permute-start = (bf16[1,16,2,1024]{3,1,2,0:T(8,128)(2,1)S(1)}, bf16[1,16,2,1024]{3,1,2,0:T(8,128)(2,1)S(1)}, u32[]{:S(2)}, u32[]{:S(2)}) collective-permute-start(bf16[1,16,2,1024]{3,1,2,0:T(8,128)(2,1)S(1)} %copy.21), channel_id=1, source_target_pairs={{0,4},{4,8},{8,12},{12,16},{16,20},{20,24},{24,28},{1,5},{5,9},{9,... | collective-permute-start | bytes 196616 | tf_op jit(solution)/shard_map/ppermute | solution.py:18
  5.9 6.2 %collective-permute-start.1 = (bf16[1,16,2,1024]{3,1,2,0:T(8,128)(2,1)S(1)}, bf16[1,16,2,1024]{3,1,2,0:T(8,128)(2,1)S(1)}, u32[]{:S(2)}, u32[]{:S(2)}) collective-permute-start(bf16[1,16,2,1024]{3,1,2,0:T(8,128)(2,1)S(1)} %copy.21), channel_id=1, source_target_pairs={{4,0},{8,4},{12,8},{16,12},{20,16},{24,20},{28,24},{5,1},{9,5},{13... | collective-permute-start | bytes 196616 | tf_op jit(solution)/shard_map/ppermute | solution.py:19
  12.0 7.3 %collective-permute-start.2 = (bf16[3,16,2,1024]{3,1,2,0:T(8,128)(2,1)S(1)}, bf16[3,16,2,1024]{3,1,2,0:T(8,128)(2,1)S(1)}, u32[]{:S(2)}, u32[]{:S(2)}) collective-permute-start(bf16[3,16,2,1024]{3,1,2,0:T(8,128)(2,1)S(1)} %constant_dynamic-update-slice_fusion), channel_id=1, source_target_pairs={{0,1},{1,0},{2,3},{3,2},{4,5},{5,4},{6,7},{7,6},{8,9},{9,8},{10,11... | collective-permute-start | bytes 589832 | tf_op jit(solution)/shard_map/ppermute | solution.py:60
  12.0 7.3 %collective-permute-start.3 = (bf16[3,16,2,1024]{3,1,2,0:T(8,128)(2,1)S(1)}, bf16[3,16,2,1024]{3,1,2,0:T(8,128)(2,1)S(1)}, u32[]{:S(2)}, u32[]{:S(2)}) collective-permute-start(bf16[3,16,2,1024]{3,1,2,0:T(8,128)(2,1)S(1)} %constant_dynamic-update-slice_fusion), channel_id=1, source_target_pairs={{0,2},{1,3},{2,0},{3,1},{4,6},{5,7},{6,4},{7,5},{8,10},{9,11},{10,... | collective-permute-start | bytes 589832 | tf_op jit(solution)/shard_map/ppermute | solution.py:64
  13.7 7.2 %copy-start.2 = (f32[1024]{0:T(1024)S(1)}, f32[1024]{0:T(1024)}, u32[]{:S(2)}) copy-start(f32[1024]{0:T(1024)} %param.7) | copy-start | bytes 12292
  19.3 1.4 %collective-permute-start.4 = (bf16[3,16,2,1024]{3,1,2,0:T(8,128)(2,1)S(1)}, bf16[3,16,2,1024]{3,1,2,0:T(8,128)(2,1)S(1)}, u32[]{:S(2)}, u32[]{:S(2)}) collective-permute-start(bf16[3,16,2,1024]{3,1,2,0:T(8,128)(2,1)S(1)} %collective-permute-done.3), channel_id=1, source_target_pairs={{0,1},{1,0},{2,3},{3,2},{4,5},{5,4},{6,7},{7,6},{8,9},{9,8},{10,11... | collective-permute-start | bytes 589832 | tf_op jit(solution)/shard_map/ppermute | solution.py:66
  24.5 9.9 %collective-permute-start.5 = (bf16[128,4,2,64]{0,3,1,2:T(8,128)(2,1)S(1)}, bf16[128,4,2,64]{0,3,1,2:T(8,128)(2,1)S(1)}, u32[]{:S(2)}, u32[]{:S(2)}) collective-permute-start(bf16[128,4,2,64]{0,3,1,2:T(8,128)(2,1)S(1)} %get-tuple-element.47), channel_id=1, source_target_pairs={{0,16},{4,20},{8,24},{12,28},{16,0},{20,4},{24,8},{28,12},{1,17},{... | collective-permute-start | bytes 393224 | tf_op jit(solution)/shard_map/ppermute | solution.py:39
  27.7 9.1 %collective-permute-start.6 = (bf16[128,4,2,64]{0,3,1,2:T(8,128)(2,1)S(1)}, bf16[128,4,2,64]{0,3,1,2:T(8,128)(2,1)}, u32[]{:S(2)}, u32[]{:S(2)}) collective-permute-start(bf16[128,4,2,64]{0,3,1,2:T(8,128)(2,1)S(1)} %get-tuple-element.47), channel_id=1, source_target_pairs={{0,4},{4,8},{8,12},{12,0},{16,20},{20,24},{24,28},{28,16},{1,5},{5... | collective-permute-start | bytes 393224 | tf_op jit(solution)/shard_map/ppermute | solution.py:43
  29.6 12.7 %collective-permute-start.8 = (bf16[128,4,2,64]{0,3,1,2:T(8,128)(2,1)S(1)}, bf16[128,4,2,64]{0,3,1,2:T(8,128)(2,1)}, u32[]{:S(2)}, u32[]{:S(2)}) collective-permute-start(bf16[128,4,2,64]{0,3,1,2:T(8,128)(2,1)S(1)} %get-tuple-element.47), channel_id=1, source_target_pairs={{0,8},{4,12},{8,0},{12,4},{16,24},{20,28},{24,16},{28,20},{1,9},{5... | collective-permute-start | bytes 393224 | tf_op jit(solution)/shard_map/ppermute | solution.py:43
  29.9 13.4 %collective-permute-start.10 = (bf16[128,4,2,64]{0,3,1,2:T(8,128)(2,1)S(1)}, bf16[128,4,2,64]{0,3,1,2:T(8,128)(2,1)S(1)}, u32[]{:S(2)}, u32[]{:S(2)}) collective-permute-start(bf16[128,4,2,64]{0,3,1,2:T(8,128)(2,1)S(1)} %get-tuple-element.47), channel_id=1, source_target_pairs={{0,12},{4,0},{8,4},{12,8},{16,28},{20,16},{24,20},{28,24},{1,13},{... | collective-permute-start | bytes 393224 | tf_op jit(solution)/shard_map/ppermute | solution.py:43
  34.4 7.8 %collective-permute-start.7 = (bf16[128,4,2,64]{0,3,1,2:T(8,128)(2,1)S(1)}, bf16[128,4,2,64]{0,3,1,2:T(8,128)(2,1)S(1)}, u32[]{:S(2)}, u32[]{:S(2)}) collective-permute-start(bf16[128,4,2,64]{0,3,1,2:T(8,128)(2,1)S(1)} %collective-permute-done.5), channel_id=1, source_target_pairs={{0,4},{4,8},{8,12},{12,0},{16,20},{20,24},{24,28},{28,16},{1,5},{5... | collective-permute-start | bytes 393224 | tf_op jit(solution)/shard_map/ppermute | solution.py:44
  36.4 6.9 %collective-permute-start.9 = (bf16[128,4,2,64]{0,3,1,2:T(8,128)(2,1)S(1)}, bf16[128,4,2,64]{0,3,1,2:T(8,128)(2,1)S(1)}, u32[]{:S(2)}, u32[]{:S(2)}) collective-permute-start(bf16[128,4,2,64]{0,3,1,2:T(8,128)(2,1)S(1)} %collective-permute-done.5), channel_id=1, source_target_pairs={{0,8},{4,12},{8,0},{12,4},{16,24},{20,28},{24,16},{28,20},{1,9},{5... | collective-permute-start | bytes 393224 | tf_op jit(solution)/shard_map/ppermute | solution.py:44
  36.8 6.6 %collective-permute-start.11 = (bf16[128,4,2,64]{0,3,1,2:T(8,128)(2,1)S(1)}, bf16[128,4,2,64]{0,3,1,2:T(8,128)(2,1)S(1)}, u32[]{:S(2)}, u32[]{:S(2)}) collective-permute-start(bf16[128,4,2,64]{0,3,1,2:T(8,128)(2,1)S(1)} %collective-permute-done.5), channel_id=1, source_target_pairs={{0,12},{4,0},{8,4},{12,8},{16,28},{20,16},{24,20},{28,24},{1,13},{... | collective-permute-start | bytes 393224 | tf_op jit(solution)/shard_map/ppermute | solution.py:44
  43.8 1.1 %copy-start.1 = (bf16[256,1024]{1,0:T(8,128)(2,1)S(1)}, bf16[256,1024]{1,0:T(8,128)(2,1)}, u32[]{:S(2)}) copy-start(bf16[256,1024]{1,0:T(8,128)(2,1)} %param.9) | copy-start | bytes 1572868
  45.8 2.1 %collective-permute-start.13 = (f32[32,1024]{1,0:T(8,128)}, f32[32,1024]{1,0:T(8,128)}, u32[]{:S(2)}, u32[]{:S(2)}) collective-permute-start(f32[32,1024]{1,0:T(8,128)} %dynamic-slice_bitcast_fusion.1), channel_id=1, source_target_pairs={{0,1},{1,0},{2,3},{3,2},{4,5},{5,4},{6,7},{7,6},{8,9},{9,8},{10,11... | collective-permute-start | bytes 393224 | tf_op jit(solution)/shard_map/ppermute | solution.py:195
  47.3 3.1 %collective-permute-start.12 = (f32[32,1024]{1,0:T(8,128)S(1)}, f32[32,1024]{1,0:T(8,128)S(1)}, u32[]{:S(2)}, u32[]{:S(2)}) collective-permute-start(f32[32,1024]{1,0:T(8,128)S(1)} %get-tuple-element.43), channel_id=1, source_target_pairs={{0,1},{1,0},{2,3},{3,2},{4,5},{5,4},{6,7},{7,6},{8,9},{9,8},{10,11... | collective-permute-start | bytes 393224 | tf_op jit(solution)/shard_map/ppermute | solution.py:206
  48.8 4.3 %collective-permute-start.14 = (bf16[32,1024]{1,0:T(8,128)(2,1)S(1)}, bf16[32,1024]{1,0:T(8,128)(2,1)S(1)}, u32[]{:S(2)}, u32[]{:S(2)}) collective-permute-start(bf16[32,1024]{1,0:T(8,128)(2,1)S(1)} %fusion.43), channel_id=1, source_target_pairs={{0,2},{1,3},{2,0},{3,1},{4,6},{5,7},{6,4},{7,5},{8,10},{9,11},{10,... | collective-permute-start | bytes 196616 | tf_op jit(solution)/shard_map/ppermute | solution.py:196

commit v13 on v7

--- a/solution.py
+++ b/solution.py
@@ -59,12 +59,19 @@
     stacked = lax.dynamic_update_index_in_dim(stacked, piece, rank, 0)
     near = lax.ppermute(piece, axis, partner)
     stacked = lax.dynamic_update_index_in_dim(stacked, near, rank ^ 1, 0)
+    halves = 2 if piece.ndim > 1 and piece.shape[1] % 2 == 0 else 1
+    width = piece.shape[1] // halves
+    zeros = (0,) * (piece.ndim - 1)
     for shift in range(1, chips):
         source_chip = (rank // 2 - shift) % chips
-        far = lax.ppermute(piece, axis, chip_shift(size, shift))
-        stacked = lax.dynamic_update_index_in_dim(stacked, far, source_chip * 2 + core, 0)
-        handed = lax.ppermute(far, axis, partner)
-        stacked = lax.dynamic_update_index_in_dim(stacked, handed, source_chip * 2 + 1 - core, 0)
+        for half in range(halves):
+            part = lax.slice_in_dim(piece, half * width, (half + 1) * width, axis=1)
+            far = lax.ppermute(part, axis, chip_shift(size, shift))
+            start = (source_chip * 2 + core, 0, half * width) + zeros[1:]
+            stacked = lax.dynamic_update_slice(stacked, far[None], start)
+            handed = lax.ppermute(far, axis, partner)
+            start = (source_chip * 2 + 1 - core, 0, half * width) + zeros[1:]
+            stacked = lax.dynamic_update_slice(stacked, handed[None], start)
     return stacked
 
 

time: 52.3 us -> 52.2 us (level)
  waiting for transfers between devices: 15.7 us -> 15 us
  starting transfers between devices: 20.9 us -> 21.5 us
    ppermute x1 -> x2, starting transfers between devices: 1.56 us -> 2.09 us  [gathered_by_chip(): far = lax.ppermute(part, axis, chip_shift(size, shift))]
    ppermute x1 -> x2, waiting for transfers between devices: 5.62 us -> 5.14 us  [gathered_by_chip(): far = lax.ppermute(part, axis, chip_shift(size, shift))]
    ppermute x1 -> x2, waiting for transfers between devices: 1.39 us -> 1.2 us  [gathered_by_chip(): handed = lax.ppermute(far, axis, partner)]
  transfers between devices with their start and end apart: 15 -> 17, of which waited for: 9 -> 10; matrix products, arithmetic and copies ran while one was open for 15% -> 15% of each run, Pallas kernels for 0% -> 0%
where the time goes in v13:
time: 52.2 us; the launch traced here: 51.7 us
  starting transfers between devices  21.5 us (41%)
  waiting for transfers between devices  15 us (29%)
  local copies, waits for them, and re-layouts  8.47 us (16%)
  other arithmetic  3.75 us (7%)
  matrix products  2.5 us (5%)
    ppermute x2, waiting for transfers between devices, gathered_by_chip(): far = lax.ppermute(part, axis, chip_shift(size, shift))  5.14 us
    ppermute x1, starting transfers between devices, padded_2(): before = lax.ppermute(last, axis, up)  4.87 us
    ppermute x3, starting transfers between devices, relayed(): parts.append(lax.ppermute(piece, axis, pairs))  4.5 us
    unnamed x16, local copies, waits for them, and re-layouts  4.1 us
    ppermute x3, starting transfers between devices, relayed(): parts.append(lax.ppermute(crossed, axis, pairs))  3.28 us
    ppermute x3, waiting for transfers between devices, relayed(): parts.append(lax.ppermute(crossed, axis, pairs))  3.23 us
    ppermute x1, starting transfers between devices, relayed(): crossed = lax.ppermute(piece, axis, mirror)  3.19 us
    convert_element_type x1, other arithmetic, on_device(): positioned = summed.astype(jnp.bfloat16)  2.34 us
  transfers between devices with their start and end apart: 17, of which 10 were waited for; matrix products, arithmetic and copies ran while one was open for 15% of the time, Pallas kernels for 0%

profile of v13, /device:TPU:0, one launch (start us, length us, event | category | flops | bytes accessed | tf_op | source)
XLA Modules:
  0.0 51.7 jit_solution(3328686710412706691)
XLA Ops:
  0.0 1.0 %copy.23 = bf16[1,16,2,1024]{3,1,2,0:T(8,128)(2,1)S(1)} copy(bf16[1,16,2,1024]{3,2,1,0:T(2,128)(2,1)} %param.5) | data formatting | bytes 131072 | tf_op args[0]
  1.0 4.9 %collective-permute-start = (bf16[1,16,2,1024]{3,1,2,0:T(8,128)(2,1)S(1)}, bf16[1,16,2,1024]{3,1,2,0:T(8,128)(2,1)S(1)}, u32[]{:S(2)}, u32[]{:S(2)}) collective-permute-start(bf16[1,16,2,1024]{3,1,2,0:T(8,128)(2,1)S(1)} %copy.23), channel_id=1, source_target_pairs={{0,4},{4,8},{8,12},{12,16},{16,20},{20,24},{24,28},{1,5},{5,9},{9,... | collective-permute-start | bytes 196616 | tf_op jit(solution)/shard_map/ppermute | solution.py:18
  5.9 1.3 %collective-permute-start.1 = (bf16[1,16,2,1024]{3,1,2,0:T(8,128)(2,1)S(1)}, bf16[1,16,2,1024]{3,1,2,0:T(8,128)(2,1)S(1)}, u32[]{:S(2)}, u32[]{:S(2)}) collective-permute-start(bf16[1,16,2,1024]{3,1,2,0:T(8,128)(2,1)S(1)} %copy.23), channel_id=1, source_target_pairs={{4,0},{8,4},{12,8},{16,12},{20,16},{24,20},{28,24},{5,1},{9,5},{13... | collective-permute-start | bytes 196616 | tf_op jit(solution)/shard_map/ppermute | solution.py:19
  7.2 1.3 %fusion.45 = (f32[1,1024]{1,0:T(1,128)S(1)}, f32[1,1024]{1,0:T(1,128)S(1)}, f32[1,1024]{1,0:T(1,128)S(1)}, f32[1,1024]{1,0:T(1,128)S(1)}, f32[1,1024]{1,0:T(1,12...) fusion(f32[27,1024]{1,0:T(8,128)} %param.6), kind=kLoop, calls=%fused_computation.114 | loop fusion | bytes 155648 | tf_op jit(solution)/shard_map/slice | solution.py:128
  8.5 1.0 %fusion.46 = (f32[1,1024]{1,0:T(1,128)S(1)}, f32[1,1024]{1,0:T(1,128)S(1)}, f32[1,1024]{1,0:T(1,128)S(1)}, f32[1,1024]{1,0:T(1,128)S(1)}, f32[1,1024]{1,0:T(1,12...) fusion(f32[27,1024]{1,0:T(8,128)} %param.6), kind=kLoop, calls=%fused_computation.115 | loop fusion | bytes 65536 | tf_op jit(solution)/shard_map/slice | solution.py:128
  9.6 0.0 collective-permute-done
  9.6 0.9 %constant_dynamic-update-slice_fusion.1 = bf16[3,16,2,1024]{3,1,2,0:T(8,128)(2,1)S(1)} fusion(bf16[3,16,2,1024]{3,1,2,0:T(8,128)(2,1)S(1)} %constant_dynamic-update-slice_fusion.2, bf16[1,16,2,1024]{3,2,1,0:T(2,128)(2,1)} %param.5), kind=kLoop, calls=%fused_computation.92 | loop fusion | bytes 131072
  10.4 1.6 %collective-permute-done.1 = bf16[1,16,2,1024]{3,1,2,0:T(8,128)(2,1)S(1)} collective-permute-done((bf16[1,16,2,1024]{3,1,2,0:T(8,128)(2,1)S(1)}, bf16[1,16,2,1024]{3,1,2,0:T(8,128)(2,1)S(1)}, u32[]{:S(2)}, u32[]{:S(2)}) %collective-permute-start.1) | collective-permute-done | bytes 65568 | tf_op jit(solution)/shard_map/ppermute | solution.py:19
  12.0 0.0 collective-permute-start.2
  12.1 1.6 %collective-permute-start.3 = (bf16[3,8,2,1024]{3,1,2,0:T(8,128)(2,1)S(1)}, bf16[3,8,2,1024]{3,1,2,0:T(8,128)(2,1)S(1)}, u32[]{:S(2)}, u32[]{:S(2)}) collective-permute-start(bf16[3,8,2,1024]{3,1,2,0:T(8,128)(2,1)S(1)} %get-tuple-element.46), channel_id=1, source_target_pairs={{0,2},{1,3},{2,0},{3,1},{4,6},{5,7},{6,4},{7,5},{8,10},{9,11},{10,... | collective-permute-start | bytes 294920 | tf_op jit(solution)/shard_map/ppermute | solution.py:69
  13.6 0.5 %collective-permute-start.5 = (bf16[3,8,2,1024]{3,1,2,0:T(8,128)(2,1)S(1)}, bf16[3,8,2,1024]{3,1,2,0:T(8,128)(2,1)S(1)}, u32[]{:S(2)}, u32[]{:S(2)}) collective-permute-start(bf16[3,8,2,1024]{3,1,2,0:T(8,128)(2,1)S(1)} %get-tuple-element.45), channel_id=1, source_target_pairs={{0,2},{1,3},{2,0},{3,1},{4,6},{5,7},{6,4},{7,5},{8,10},{9,11},{10,... | collective-permute-start | bytes 294920 | tf_op jit(solution)/shard_map/ppermute | solution.py:69
  14.2 0.1 broadcast_in_dim.33
  14.2 0.0 copy-start.2
  14.3 3.4 %collective-permute-done.3 = bf16[3,8,2,1024]{3,1,2,0:T(8,128)(2,1)S(1)} collective-permute-done((bf16[3,8,2,1024]{3,1,2,0:T(8,128)(2,1)S(1)}, bf16[3,8,2,1024]{3,1,2,0:T(8,128)(2,1)S(1)}, u32[]{:S(2)}, u32[]{:S(2)}) %collective-permute-start.3) | collective-permute-done | bytes 98336 | tf_op jit(solution)/shard_map/ppermute | solution.py:69
  17.7 0.0 collective-permute-start.4
  17.7 1.7 %collective-permute-done.5 = bf16[3,8,2,1024]{3,1,2,0:T(8,128)(2,1)S(1)} collective-permute-done((bf16[3,8,2,1024]{3,1,2,0:T(8,128)(2,1)S(1)}, bf16[3,8,2,1024]{3,1,2,0:T(8,128)(2,1)S(1)}, u32[]{:S(2)}, u32[]{:S(2)}) %collective-permute-start.5) | collective-permute-done | bytes 98336 | tf_op jit(solution)/shard_map/ppermute | solution.py:69
  19.4 0.0 collective-permute-start.6
  19.5 0.0 collective-permute-done.4
  19.5 1.2 %collective-permute-done.6 = bf16[3,8,2,1024]{3,1,2,0:T(8,128)(2,1)S(1)} collective-permute-done((bf16[3,8,2,1024]{3,1,2,0:T(8,128)(2,1)S(1)}, bf16[3,8,2,1024]{3,1,2,0:T(8,128)(2,1)S(1)}, u32[]{:S(2)}, u32[]{:S(2)}) %collective-permute-start.6) | collective-permute-done | bytes 98336 | tf_op jit(solution)/shard_map/ppermute | solution.py:72
  20.7 0.1 fusion.42
  20.8 2.3 %add_convert_fusion = bf16[1,16,8,1024]{3,1,2,0:T(8,128)(2,1)S(1)} fusion(bf16[1,16,8,1024]{3,1,2,0:T(8,128)(2,1)S(1)} %bitcast.137, bf16[1,16,8,1024]{3,1,2,0:T(8,128)(2,1)S(1)} %bitcast.136, bf16[1,16,8,1024]{3,1,2,0:T(8,128)(2,1)S(1)} %bitcast.135, bf16[3,16,8,1024]{3,1,2,0:T(8,128)(2,1)S(1)} %bitcast.132, f32[1024]{0:T(1024)S(1)} %bitcast.167, ...), kind=kLoop, calls=%fused_computation.77 | loop fusion | flops 10878976 | bytes 1949696 | tf_op jit(solution)/shard_map/convert_element_type | solution.py:135
  23.2 0.3 copy.43
  23.5 0.1 reshape.250
  23.6 0.7 %convolution_convert_fusion = bf16[128,768]{1,0:T(8,128)(2,1)S(1)} fusion(bf16[128,1024]{1,0:T(8,128)(2,1)S(1)} %reshape.250, bf16[768,1024]{1,0:T(8,128)(2,1)S(1)} %copy-done), kind=kOutput, calls=%fused_computation.26 | convolution fusion | flops 201424896 | bytes 2031616 | tf_op jit(solution)/shard_map/dot_general | solution.py:107
  24.2 0.2 copy.32
  24.4 3.2 %collective-permute-start.7 = (bf16[128,4,2,64]{0,3,1,2:T(8,128)(2,1)S(1)}, bf16[128,4,2,64]{0,3,1,2:T(8,128)(2,1)S(1)}, u32[]{:S(2)}, u32[]{:S(2)}) collective-permute-start(bf16[128,4,2,64]{0,3,1,2:T(8,128)(2,1)S(1)} %get-tuple-element.60), channel_id=1, source_target_pairs={{0,16},{4,20},{8,24},{12,28},{16,0},{20,4},{24,8},{28,12},{1,17},{... | collective-permute-start | bytes 393224 | tf_op jit(solution)/shard_map/ppermute | solution.py:39
  27.6 1.9 %collective-permute-start.8 = (bf16[128,4,2,64]{0,3,1,2:T(8,128)(2,1)S(1)}, bf16[128,4,2,64]{0,3,1,2:T(8,128)(2,1)}, u32[]{:S(2)}, u32[]{:S(2)}) collective-permute-start(bf16[128,4,2,64]{0,3,1,2:T(8,128)(2,1)S(1)} %get-tuple-element.60), channel_id=1, source_target_pairs={{0,4},{4,8},{8,12},{12,0},{16,20},{20,24},{24,28},{28,16},{1,5},{5... | collective-permute-start | bytes 393224 | tf_op jit(solution)/shard_map/ppermute | solution.py:43
  29.5 0.3 collective-permute-start.10
  29.8 2.3 %collective-permute-start.12 = (bf16[128,4,2,64]{0,3,1,2:T(8,128)(2,1)S(1)}, bf16[128,4,2,64]{0,3,1,2:T(8,128)(2,1)S(1)}, u32[]{:S(2)}, u32[]{:S(2)}) collective-permute-start(bf16[128,4,2,64]{0,3,1,2:T(8,128)(2,1)S(1)} %get-tuple-element.60), channel_id=1, source_target_pairs={{0,12},{4,0},{8,4},{12,8},{16,28},{20,16},{24,20},{28,24},{1,13},{... | collective-permute-start | bytes 393224 | tf_op jit(solution)/shard_map/ppermute | solution.py:43
  32.1 0.1 reshape_squeeze.2
  32.3 0.3 constant_dynamic-slice_fusion.2
  32.5 0.1 copy.34
  32.7 0.1 copy.33
  32.8 1.6 %collective-permute-done.7 = bf16[128,4,2,64]{0,3,1,2:T(8,128)(2,1)S(1)} collective-permute-done((bf16[128,4,2,64]{0,3,1,2:T(8,128)(2,1)S(1)}, bf16[128,4,2,64]{0,3,1,2:T(8,128)(2,1)S(1)}, u32[]{:S(2)}, u32[]{:S(2)}) %collective-permute-start.7) | collective-permute-done | bytes 131104 | tf_op jit(solution)/shard_map/ppermute | solution.py:39
  34.4 1.9 %collective-permute-start.9 = (bf16[128,4,2,64]{0,3,1,2:T(8,128)(2,1)S(1)}, bf16[128,4,2,64]{0,3,1,2:T(8,128)(2,1)S(1)}, u32[]{:S(2)}, u32[]{:S(2)}) collective-permute-start(bf16[128,4,2,64]{0,3,1,2:T(8,128)(2,1)S(1)} %collective-permute-done.7), channel_id=1, source_target_pairs={{0,4},{4,8},{8,12},{12,0},{16,20},{20,24},{24,28},{28,16},{1,5},{5... | collective-permute-start | bytes 393224 | tf_op jit(solution)/shard_map/ppermute | solution.py:44
  36.3 0.0 collective-permute-start.11
  36.3 0.4 collective-permute-done.8
  36.7 1.4 %collective-permute-start.13 = (bf16[128,4,2,64]{0,3,1,2:T(8,128)(2,1)S(1)}, bf16[128,4,2,64]{0,3,1,2:T(8,128)(2,1)S(1)}, u32[]{:S(2)}, u32[]{:S(2)}) collective-permute-start(bf16[128,4,2,64]{0,3,1,2:T(8,128)(2,1)S(1)} %collective-permute-done.7), channel_id=1, source_target_pairs={{0,12},{4,0},{8,4},{12,8},{16,28},{20,16},{24,20},{28,24},{1,13},{... | collective-permute-start | bytes 393224 | tf_op jit(solution)/shard_map/ppermute | solution.py:44
  38.1 0.9 %constant_dynamic-update-slice_fusion.8 = bf16[1024,4,2,64]{0,3,1,2:T(8,128)(2,1)S(1)} fusion(bf16[1024,4,2,64]{0,3,1,2:T(8,128)(2,1)S(1)} %constant_dynamic-update-slice_fusion.9, bf16[128,4,2,64]{0,3,1,2:T(8,128)(2,1)} %collective-permute-done.8), kind=kLoop, calls=%fused_computation.99 | loop fusion | bytes 262144
  39.0 3.1 %collective-permute-done.9 = bf16[128,4,2,64]{0,3,1,2:T(8,128)(2,1)S(1)} collective-permute-done((bf16[128,4,2,64]{0,3,1,2:T(8,128)(2,1)S(1)}, bf16[128,4,2,64]{0,3,1,2:T(8,128)(2,1)S(1)}, u32[]{:S(2)}, u32[]{:S(2)}) %collective-permute-start.9) | collective-permute-done | bytes 131104 | tf_op jit(solution)/shard_map/ppermute | solution.py:44
  42.2 0.9 %constant_dynamic-update-slice_fusion.6 = bf16[1024,4,2,64]{0,3,1,2:T(8,128)(2,1)S(1)} fusion(bf16[1024,4,2,64]{0,3,1,2:T(8,128)(2,1)S(1)} %constant_dynamic-update-slice_fusion.7, bf16[128,4,2,64]{0,3,1,2:T(8,128)(2,1)} %collective-permute-done.10), kind=kLoop, calls=%fused_computation.97 | loop fusion | bytes 262144
  43.3 0.1 collective-permute-done.13
  43.4 0.4 fusion.47
  43.8 0.0 copy-start.1
  43.8 0.3 fusion.6
  44.1 0.4 fusion.5
  44.5 0.1 copy.36
  44.5 0.1 reshape.252
  44.7 0.2 copy-done.1
  44.8 0.2 convolution_convert_fusion.1
  45.1 1.6 %collective-permute-start.15 = (bf16[32,1024]{1,0:T(8,128)(2,1)S(1)}, bf16[32,1024]{1,0:T(8,128)(2,1)S(1)}, u32[]{:S(2)}, u32[]{:S(2)}) collective-permute-start(bf16[32,1024]{1,0:T(8,128)(2,1)S(1)} %get-tuple-element.56), channel_id=1, source_target_pairs={{0,2},{1,3},{2,0},{3,1},{4,6},{5,7},{6,4},{7,5},{8,10},{9,11},{10,... | collective-permute-start | bytes 196616 | tf_op jit(solution)/shard_map/ppermute | solution.py:205
  46.7 0.4 fusion.48
  47.0 0.3 fusion.8
  47.4 0.4 fusion.4
  47.7 0.1 copy.37
  47.8 0.1 dot_general.39
  47.9 0.2 fusion.37
  48.1 0.7 %collective-permute-start.14 = (f32[32,1024]{1,0:T(8,128)S(1)}, f32[32,1024]{1,0:T(8,128)S(1)}, u32[]{:S(2)}, u32[]{:S(2)}) collective-permute-start(f32[32,1024]{1,0:T(8,128)S(1)} %get-tuple-element.43), channel_id=1, source_target_pairs={{0,1},{1,0},{2,3},{3,2},{4,5},{5,4},{6,7},{7,6},{8,9},{9,8},{10,11... | collective-permute-start | bytes 393224 | tf_op jit(solution)/shard_map/ppermute | solution.py:217
  48.8 0.1 reshape.254
  48.9 0.5 collective-permute-done.15
  49.4 1.4 %collective-permute-done.16 = bf16[32,1024]{1,0:T(8,128)(2,1)S(1)} collective-permute-done((bf16[32,1024]{1,0:T(8,128)(2,1)S(1)}, bf16[32,1024]{1,0:T(8,128)(2,1)S(1)}, u32[]{:S(2)}, u32[]{:S(2)}) %collective-permute-start.16) | collective-permute-done | bytes 65568 | tf_op jit(solution)/shard_map/ppermute | solution.py:206
  50.8 0.1 add.273
  50.9 0.1 reshape.255
  51.0 0.7 %add_convert_fusion.1 = bf16[1,16,2,1024]{3,2,1,0:T(2,128)(2,1)} fusion(f32[1,16,2,1024]{3,2,1,0:T(2,128)S(1)} %add.273, f32[1,16,2,1024]{3,2,1,0:T(2,128)S(1)} %reshape.254, f32[1,16,2,1024]{3,2,1,0:T(2,128)S(1)} %reshape.255), kind=kLoop, calls=%fused_computation.81 | loop fusion | flops 98304 | bytes 458752 | tf_op jit(solution)/shard_map/convert_element_type | solution.py:220
  (32 shorter events, 0.5 us)
Async XLA Ops:
  0.0 23.6 %copy-start = (bf16[768,1024]{1,0:T(8,128)(2,1)S(1)}, bf16[768,1024]{1,0:T(8,128)(2,1)}, u32[]{:S(2)}) copy-start(bf16[768,1024]{1,0:T(8,128)(2,1)} %param.8) | copy-start | bytes 4718596
  1.0 8.6 %collective-permute-start = (bf16[1,16,2,1024]{3,1,2,0:T(8,128)(2,1)S(1)}, bf16[1,16,2,1024]{3,1,2,0:T(8,128)(2,1)S(1)}, u32[]{:S(2)}, u32[]{:S(2)}) collective-permute-start(bf16[1,16,2,1024]{3,1,2,0:T(8,128)(2,1)S(1)} %copy.23), channel_id=1, source_target_pairs={{0,4},{4,8},{8,12},{12,16},{16,20},{20,24},{24,28},{1,5},{5,9},{9,... | collective-permute-start | bytes 196616 | tf_op jit(solution)/shard_map/ppermute | solution.py:18
  5.9 6.2 %collective-permute-start.1 = (bf16[1,16,2,1024]{3,1,2,0:T(8,128)(2,1)S(1)}, bf16[1,16,2,1024]{3,1,2,0:T(8,128)(2,1)S(1)}, u32[]{:S(2)}, u32[]{:S(2)}) collective-permute-start(bf16[1,16,2,1024]{3,1,2,0:T(8,128)(2,1)S(1)} %copy.23), channel_id=1, source_target_pairs={{4,0},{8,4},{12,8},{16,12},{20,16},{24,20},{28,24},{5,1},{9,5},{13... | collective-permute-start | bytes 196616 | tf_op jit(solution)/shard_map/ppermute | solution.py:19
  12.0 7.4 %collective-permute-start.2 = (bf16[3,16,2,1024]{3,1,2,0:T(8,128)(2,1)S(1)}, bf16[3,16,2,1024]{3,1,2,0:T(8,128)(2,1)S(1)}, u32[]{:S(2)}, u32[]{:S(2)}) collective-permute-start(bf16[3,16,2,1024]{3,1,2,0:T(8,128)(2,1)S(1)} %constant_dynamic-update-slice_fusion), channel_id=1, source_target_pairs={{0,1},{1,0},{2,3},{3,2},{4,5},{5,4},{6,7},{7,6},{8,9},{9,8},{10,11... | collective-permute-start | bytes 589832 | tf_op jit(solution)/shard_map/ppermute | solution.py:60
  12.1 5.7 %collective-permute-start.3 = (bf16[3,8,2,1024]{3,1,2,0:T(8,128)(2,1)S(1)}, bf16[3,8,2,1024]{3,1,2,0:T(8,128)(2,1)S(1)}, u32[]{:S(2)}, u32[]{:S(2)}) collective-permute-start(bf16[3,8,2,1024]{3,1,2,0:T(8,128)(2,1)S(1)} %get-tuple-element.46), channel_id=1, source_target_pairs={{0,2},{1,3},{2,0},{3,1},{4,6},{5,7},{6,4},{7,5},{8,10},{9,11},{10,... | collective-permute-start | bytes 294920 | tf_op jit(solution)/shard_map/ppermute | solution.py:69
  13.6 5.8 %collective-permute-start.5 = (bf16[3,8,2,1024]{3,1,2,0:T(8,128)(2,1)S(1)}, bf16[3,8,2,1024]{3,1,2,0:T(8,128)(2,1)S(1)}, u32[]{:S(2)}, u32[]{:S(2)}) collective-permute-start(bf16[3,8,2,1024]{3,1,2,0:T(8,128)(2,1)S(1)} %get-tuple-element.45), channel_id=1, source_target_pairs={{0,2},{1,3},{2,0},{3,1},{4,6},{5,7},{6,4},{7,5},{8,10},{9,11},{10,... | collective-permute-start | bytes 294920 | tf_op jit(solution)/shard_map/ppermute | solution.py:69
  14.2 6.6 %copy-start.2 = (f32[1024]{0:T(1024)S(1)}, f32[1024]{0:T(1024)}, u32[]{:S(2)}) copy-start(f32[1024]{0:T(1024)} %param.7) | copy-start | bytes 12292
  17.7 1.8 %collective-permute-start.4 = (bf16[3,8,2,1024]{3,1,2,0:T(8,128)(2,1)S(1)}, bf16[3,8,2,1024]{3,1,2,0:T(8,128)(2,1)S(1)}, u32[]{:S(2)}, u32[]{:S(2)}) collective-permute-start(bf16[3,8,2,1024]{3,1,2,0:T(8,128)(2,1)S(1)} %collective-permute-done.3), channel_id=1, source_target_pairs={{0,1},{1,0},{2,3},{3,2},{4,5},{5,4},{6,7},{7,6},{8,9},{9,8},{10,11... | collective-permute-start | bytes 294920 | tf_op jit(solution)/shard_map/ppermute | solution.py:72
  19.4 1.3 %collective-permute-start.6 = (bf16[3,8,2,1024]{3,1,2,0:T(8,128)(2,1)S(1)}, bf16[3,8,2,1024]{3,1,2,0:T(8,128)(2,1)S(1)}, u32[]{:S(2)}, u32[]{:S(2)}) collective-permute-start(bf16[3,8,2,1024]{3,1,2,0:T(8,128)(2,1)S(1)} %collective-permute-done.5), channel_id=1, source_target_pairs={{0,1},{1,0},{2,3},{3,2},{4,5},{5,4},{6,7},{7,6},{8,9},{9,8},{10,11... | collective-permute-start | bytes 294920 | tf_op jit(solution)/shard_map/ppermute | solution.py:72
  24.4 9.9 %collective-permute-start.7 = (bf16[128,4,2,64]{0,3,1,2:T(8,128)(2,1)S(1)}, bf16[128,4,2,64]{0,3,1,2:T(8,128)(2,1)S(1)}, u32[]{:S(2)}, u32[]{:S(2)}) collective-permute-start(bf16[128,4,2,64]{0,3,1,2:T(8,128)(2,1)S(1)} %get-tuple-element.60), channel_id=1, source_target_pairs={{0,16},{4,20},{8,24},{12,28},{16,0},{20,4},{24,8},{28,12},{1,17},{... | collective-permute-start | bytes 393224 | tf_op jit(solution)/shard_map/ppermute | solution.py:39
  27.6 9.1 %collective-permute-start.8 = (bf16[128,4,2,64]{0,3,1,2:T(8,128)(2,1)S(1)}, bf16[128,4,2,64]{0,3,1,2:T(8,128)(2,1)}, u32[]{:S(2)}, u32[]{:S(2)}) collective-permute-start(bf16[128,4,2,64]{0,3,1,2:T(8,128)(2,1)S(1)} %get-tuple-element.60), channel_id=1, source_target_pairs={{0,4},{4,8},{8,12},{12,0},{16,20},{20,24},{24,28},{28,16},{1,5},{5... | collective-permute-start | bytes 393224 | tf_op jit(solution)/shard_map/ppermute | solution.py:43
  29.5 12.7 %collective-permute-start.10 = (bf16[128,4,2,64]{0,3,1,2:T(8,128)(2,1)S(1)}, bf16[128,4,2,64]{0,3,1,2:T(8,128)(2,1)}, u32[]{:S(2)}, u32[]{:S(2)}) collective-permute-start(bf16[128,4,2,64]{0,3,1,2:T(8,128)(2,1)S(1)} %get-tuple-element.60), channel_id=1, source_target_pairs={{0,8},{4,12},{8,0},{12,4},{16,24},{20,28},{24,16},{28,20},{1,9},{5... | collective-permute-start | bytes 393224 | tf_op jit(solution)/shard_map/ppermute | solution.py:43
  29.8 13.4 %collective-permute-start.12 = (bf16[128,4,2,64]{0,3,1,2:T(8,128)(2,1)S(1)}, bf16[128,4,2,64]{0,3,1,2:T(8,128)(2,1)S(1)}, u32[]{:S(2)}, u32[]{:S(2)}) collective-permute-start(bf16[128,4,2,64]{0,3,1,2:T(8,128)(2,1)S(1)} %get-tuple-element.60), channel_id=1, source_target_pairs={{0,12},{4,0},{8,4},{12,8},{16,28},{20,16},{24,20},{28,24},{1,13},{... | collective-permute-start | bytes 393224 | tf_op jit(solution)/shard_map/ppermute | solution.py:43
  34.4 7.8 %collective-permute-start.9 = (bf16[128,4,2,64]{0,3,1,2:T(8,128)(2,1)S(1)}, bf16[128,4,2,64]{0,3,1,2:T(8,128)(2,1)S(1)}, u32[]{:S(2)}, u32[]{:S(2)}) collective-permute-start(bf16[128,4,2,64]{0,3,1,2:T(8,128)(2,1)S(1)} %collective-permute-done.7), channel_id=1, source_target_pairs={{0,4},{4,8},{8,12},{12,0},{16,20},{20,24},{24,28},{28,16},{1,5},{5... | collective-permute-start | bytes 393224 | tf_op jit(solution)/shard_map/ppermute | solution.py:44
  36.3 6.9 %collective-permute-start.11 = (bf16[128,4,2,64]{0,3,1,2:T(8,128)(2,1)S(1)}, bf16[128,4,2,64]{0,3,1,2:T(8,128)(2,1)S(1)}, u32[]{:S(2)}, u32[]{:S(2)}) collective-permute-start(bf16[128,4,2,64]{0,3,1,2:T(8,128)(2,1)S(1)} %collective-permute-done.7), channel_id=1, source_target_pairs={{0,8},{4,12},{8,0},{12,4},{16,24},{20,28},{24,16},{28,20},{1,9},{5... | collective-permute-start | bytes 393224 | tf_op jit(solution)/shard_map/ppermute | solution.py:44
  36.7 6.7 %collective-permute-start.13 = (bf16[128,4,2,64]{0,3,1,2:T(8,128)(2,1)S(1)}, bf16[128,4,2,64]{0,3,1,2:T(8,128)(2,1)S(1)}, u32[]{:S(2)}, u32[]{:S(2)}) collective-permute-start(bf16[128,4,2,64]{0,3,1,2:T(8,128)(2,1)S(1)} %collective-permute-done.7), channel_id=1, source_target_pairs={{0,12},{4,0},{8,4},{12,8},{16,28},{20,16},{24,20},{28,24},{1,13},{... | collective-permute-start | bytes 393224 | tf_op jit(solution)/shard_map/ppermute | solution.py:44
  43.8 1.1 %copy-start.1 = (bf16[256,1024]{1,0:T(8,128)(2,1)S(1)}, bf16[256,1024]{1,0:T(8,128)(2,1)}, u32[]{:S(2)}) copy-start(bf16[256,1024]{1,0:T(8,128)(2,1)} %param.9) | copy-start | bytes 1572868
  45.1 4.3 %collective-permute-start.15 = (bf16[32,1024]{1,0:T(8,128)(2,1)S(1)}, bf16[32,1024]{1,0:T(8,128)(2,1)S(1)}, u32[]{:S(2)}, u32[]{:S(2)}) collective-permute-start(bf16[32,1024]{1,0:T(8,128)(2,1)S(1)} %get-tuple-element.56), channel_id=1, source_target_pairs={{0,2},{1,3},{2,0},{3,1},{4,6},{5,7},{6,4},{7,5},{8,10},{9,11},{10,... | collective-permute-start | bytes 196616 | tf_op jit(solution)/shard_map/ppermute | solution.py:205
  46.6 4.2 %collective-permute-start.16 = (bf16[32,1024]{1,0:T(8,128)(2,1)S(1)}, bf16[32,1024]{1,0:T(8,128)(2,1)S(1)}, u32[]{:S(2)}, u32[]{:S(2)}) collective-permute-start(bf16[32,1024]{1,0:T(8,128)(2,1)S(1)} %get-tuple-element.58), channel_id=1, source_target_pairs={{0,3},{1,2},{2,1},{3,0},{4,7},{5,6},{6,5},{7,4},{8,11},{9,10},{10,... | collective-permute-start | bytes 196616 | tf_op jit(solution)/shard_map/ppermute | solution.py:206
  48.1 2.8 %collective-permute-start.14 = (f32[32,1024]{1,0:T(8,128)S(1)}, f32[32,1024]{1,0:T(8,128)S(1)}, u32[]{:S(2)}, u32[]{:S(2)}) collective-permute-start(f32[32,1024]{1,0:T(8,128)S(1)} %get-tuple-element.43), channel_id=1, source_target_pairs={{0,1},{1,0},{2,3},{3,2},{4,5},{5,4},{6,7},{7,6},{8,9},{9,8},{10,11... | collective-permute-start | bytes 393224 | tf_op jit(solution)/shard_map/ppermute | solution.py:217

commit v14 on v7

--- a/solution.py
+++ b/solution.py
@@ -106,7 +106,7 @@
     z_count, x_count, y_count, features = tokens.shape
     groups = lax.axis_size("uly")
     with_halo = padded_2(tokens, (("blk", 0),), 1)
-    slab_in = gathered_by_chip(with_halo, "uly")
+    slab_in = lax.all_gather(with_halo, "uly", axis=0, tiled=False)
     slab_in = slab_in.transpose(1, 2, 0, 3, 4).reshape(
         z_count + 2, x_count, groups * y_count, features
     )

time: 52.3 us -> 52.6 us (level)
  blocking collectives: 0 us -> 8.6 us
  waiting for transfers between devices: 15.7 us -> 9.37 us
  starting transfers between devices: 20.9 us -> 19.5 us
    all_gather x0 -> x1, blocking collectives: none -> 8.6 us  [on_device(): slab_in = lax.all_gather(with_halo, 'uly', axis=0, tiled=False)]
    ppermute x3 -> x0, waiting for transfers between devices: 7.01 us -> none  [the longest x1 5.62 us: gathered_by_chip(): far = lax.ppermute(piece, axis, chip_shift(size, shift))]
    ppermute x3 -> x0, starting transfers between devices: 1.56 us -> none  [the longest x1 1.56 us: gathered_by_chip(): far = lax.ppermute(piece, axis, chip_shift(size, shift))]
    ppermute x1, waiting for transfers between devices: 1.4 us -> 0.01 us  [on_device(): lax.ppermute(other_core, 'uly', to_other_core)]
    ppermute x1, starting transfers between devices: 1.56 us -> 0.6 us  [on_device(): lax.ppermute(same_core, 'uly', chip_shift(groups, shift))]
    ppermute x1, waiting for transfers between devices: 1.57 us -> 2.5 us  [padded_2(): after = lax.ppermute(initial, axis, down)]
    ppermute x3, starting transfers between devices: 3.23 us -> 3.93 us  [relayed(): parts.append(lax.ppermute(crossed, axis, pairs))]
    ppermute x1, waiting for transfers between devices: 0.49 us -> 1.16 us  [on_device(): lax.ppermute(same_core, 'uly', chip_shift(groups, shift))]
  transfers between devices with their start and end apart: 15 -> 12, of which waited for: 9 -> 6; matrix products, arithmetic and copies ran while one was open for 15% -> 13% of each run, Pallas kernels for 0% -> 0%
where the time goes in v14:
time: 52.6 us; the launch traced here: 52 us
  starting transfers between devices  19.5 us (37%)
  waiting for transfers between devices  9.37 us (18%)
  blocking collectives  8.6 us (16%)
  local copies, waits for them, and re-layouts  8.02 us (15%)
  other arithmetic  3.69 us (7%)
  matrix products  2.51 us (5%)
    all_gather x1, blocking collectives, on_device(): slab_in = lax.all_gather(with_halo, 'uly', axis=0, tiled=False)  8.6 us
    ppermute x1, starting transfers between devices, padded_2(): before = lax.ppermute(last, axis, up)  4.87 us
    ppermute x3, starting transfers between devices, relayed(): parts.append(lax.ppermute(piece, axis, pairs))  4.5 us
    ppermute x3, starting transfers between devices, relayed(): parts.append(lax.ppermute(crossed, axis, pairs))  3.93 us
    ppermute x3, waiting for transfers between devices, relayed(): parts.append(lax.ppermute(crossed, axis, pairs))  3.86 us
    unnamed x14, local copies, waits for them, and re-layouts  3.8 us
    ppermute x1, starting transfers between devices, relayed(): crossed = lax.ppermute(piece, axis, mirror)  2.66 us
    ppermute x1, waiting for transfers between devices, padded_2(): after = lax.ppermute(initial, axis, down)  2.5 us
  transfers between devices with their start and end apart: 12, of which 6 were waited for; matrix products, arithmetic and copies ran while one was open for 13% of the time, Pallas kernels for 0%

profile of v14, /device:TPU:0, one launch (start us, length us, event | category | flops | bytes accessed | tf_op | source)
XLA Modules:
  0.0 52.0 jit_solution(16189058926392645326)
XLA Ops:
  0.0 0.0 copy-start
  0.0 1.0 %copy.26 = bf16[1,16,2,1024]{3,1,2,0:T(8,128)(2,1)S(1)} copy(bf16[1,16,2,1024]{3,2,1,0:T(2,128)(2,1)} %param.5) | data formatting | bytes 131072 | tf_op args[0]
  1.0 4.9 %collective-permute-start = (bf16[1,16,2,1024]{3,1,2,0:T(8,128)(2,1)S(1)}, bf16[1,16,2,1024]{3,1,2,0:T(8,128)(2,1)S(1)}, u32[]{:S(2)}, u32[]{:S(2)}) collective-permute-start(bf16[1,16,2,1024]{3,1,2,0:T(8,128)(2,1)S(1)} %copy.26), channel_id=1, source_target_pairs={{0,4},{4,8},{8,12},{12,16},{16,20},{20,24},{24,28},{1,5},{5,9},{9,... | collective-permute-start | bytes 196616 | tf_op jit(solution)/shard_map/ppermute | solution.py:18
  5.9 1.3 %collective-permute-start.1 = (bf16[1,16,2,1024]{3,1,2,0:T(8,128)(2,1)S(1)}, bf16[1,16,2,1024]{3,1,2,0:T(8,128)(2,1)S(1)}, u32[]{:S(2)}, u32[]{:S(2)}) collective-permute-start(bf16[1,16,2,1024]{3,1,2,0:T(8,128)(2,1)S(1)} %copy.26), channel_id=1, source_target_pairs={{4,0},{8,4},{12,8},{16,12},{20,16},{24,20},{28,24},{5,1},{9,5},{13... | collective-permute-start | bytes 196616 | tf_op jit(solution)/shard_map/ppermute | solution.py:19
  7.2 1.3 %fusion.44 = (f32[1,1024]{1,0:T(1,128)S(1)}, f32[1,1024]{1,0:T(1,128)S(1)}, f32[1,1024]{1,0:T(1,128)S(1)}, f32[1,1024]{1,0:T(1,128)S(1)}, f32[1,1024]{1,0:T(1,12...) fusion(f32[27,1024]{1,0:T(8,128)} %param.6), kind=kLoop, calls=%fused_computation.105 | loop fusion | bytes 155648 | tf_op jit(solution)/shard_map/slice | solution.py:121
  8.5 1.0 %fusion.45 = (f32[1,1024]{1,0:T(1,128)S(1)}, f32[1,1024]{1,0:T(1,128)S(1)}, f32[1,1024]{1,0:T(1,128)S(1)}, f32[1,1024]{1,0:T(1,128)S(1)}, f32[1,1024]{1,0:T(1,12...) fusion(f32[27,1024]{1,0:T(8,128)} %param.6), kind=kLoop, calls=%fused_computation.106 | loop fusion | bytes 65536 | tf_op jit(solution)/shard_map/slice | solution.py:121
  9.5 0.0 collective-permute-done
  9.5 2.5 %collective-permute-done.1 = bf16[1,16,2,1024]{3,1,2,0:T(8,128)(2,1)S(1)} collective-permute-done((bf16[1,16,2,1024]{3,1,2,0:T(8,128)(2,1)S(1)}, bf16[1,16,2,1024]{3,1,2,0:T(8,128)(2,1)S(1)}, u32[]{:S(2)}, u32[]{:S(2)}) %collective-permute-start.1) | collective-permute-done | bytes 65568 | tf_op jit(solution)/shard_map/ppermute | solution.py:19
  12.0 8.6 %all-gather = bf16[12,16,2,1024]{3,1,2,0:T(8,128)(2,1)S(1)} all-gather(bf16[3,16,2,1024]{3,1,2,0:T(8,128)(2,1)S(1)} %pad_maximum_fusion), channel_id=2, replica_groups=mesh['blk'=8,'uly'=4] {'uly'}, dimensions={0}, use_global_device_ids=true | all-gather | bytes 983040 | tf_op jit(solution)/shard_map/all_gather | solution.py:109
  20.6 0.0 copy-start.2
  20.6 0.1 fusion.42
  20.7 0.1 copy.29
  20.8 0.6 %copy-done.2 = f32[1024]{0:T(1024)S(1)} copy-done((f32[1024]{0:T(1024)S(1)}, f32[1024]{0:T(1024)}, u32[]{:S(2)}) %copy-start.2) | copy-done | bytes 4120
  21.3 2.3 %add_convert_fusion = bf16[1,16,8,1024]{3,1,2,0:T(8,128)(2,1)S(1)} fusion(bf16[1,16,8,1024]{3,1,2,0:T(8,128)(2,1)S(1)} %bitcast.116, bf16[1,16,8,1024]{3,1,2,0:T(8,128)(2,1)S(1)} %bitcast.117, bf16[1,16,8,1024]{3,1,2,0:T(8,128)(2,1)S(1)} %bitcast.115, bf16[3,16,8,1024]{3,1,2,0:T(8,128)(2,1)S(1)} %bitcast.112, f32[1024]{0:T(1024)S(1)} %bitcast.147, ...), kind=kLoop, calls=%fused_computation.77 | loop fusion | flops 10878976 | bytes 1949696 | tf_op jit(solution)/shard_map/convert_element_type | solution.py:128
  23.6 0.3 copy.41
  23.9 0.1 reshape.250
  24.0 0.0 copy-done
  24.0 0.7 %convolution_convert_fusion = bf16[128,768]{1,0:T(8,128)(2,1)S(1)} fusion(bf16[128,1024]{1,0:T(8,128)(2,1)S(1)} %reshape.250, bf16[768,1024]{1,0:T(8,128)(2,1)S(1)} %copy-done), kind=kOutput, calls=%fused_computation.26 | convolution fusion | flops 201424896 | bytes 2031616 | tf_op jit(solution)/shard_map/dot_general | solution.py:100
  24.7 0.2 copy.31
  24.9 2.7 %collective-permute-start.2 = (bf16[128,4,2,64]{0,3,1,2:T(8,128)(2,1)S(1)}, bf16[128,4,2,64]{0,3,1,2:T(8,128)(2,1)S(1)}, u32[]{:S(2)}, u32[]{:S(2)}) collective-permute-start(bf16[128,4,2,64]{0,3,1,2:T(8,128)(2,1)S(1)} %get-tuple-element.56), channel_id=1, source_target_pairs={{0,16},{4,20},{8,24},{12,28},{16,0},{20,4},{24,8},{28,12},{1,17},{... | collective-permute-start | bytes 393224 | tf_op jit(solution)/shard_map/ppermute | solution.py:39
  27.5 2.4 %collective-permute-start.3 = (bf16[128,4,2,64]{0,3,1,2:T(8,128)(2,1)S(1)}, bf16[128,4,2,64]{0,3,1,2:T(8,128)(2,1)}, u32[]{:S(2)}, u32[]{:S(2)}) collective-permute-start(bf16[128,4,2,64]{0,3,1,2:T(8,128)(2,1)S(1)} %get-tuple-element.56), channel_id=1, source_target_pairs={{0,4},{4,8},{8,12},{12,0},{16,20},{20,24},{24,28},{28,16},{1,5},{5... | collective-permute-start | bytes 393224 | tf_op jit(solution)/shard_map/ppermute | solution.py:43
  29.9 0.0 collective-permute-start.5
  30.0 2.1 %collective-permute-start.7 = (bf16[128,4,2,64]{0,3,1,2:T(8,128)(2,1)S(1)}, bf16[128,4,2,64]{0,3,1,2:T(8,128)(2,1)S(1)}, u32[]{:S(2)}, u32[]{:S(2)}) collective-permute-start(bf16[128,4,2,64]{0,3,1,2:T(8,128)(2,1)S(1)} %get-tuple-element.56), channel_id=1, source_target_pairs={{0,12},{4,0},{8,4},{12,8},{16,28},{20,16},{24,20},{28,24},{1,13},{... | collective-permute-start | bytes 393224 | tf_op jit(solution)/shard_map/ppermute | solution.py:43
  32.0 0.1 reshape_squeeze.2
  32.1 0.3 constant_dynamic-slice_fusion.2
  32.4 0.1 copy.33
  32.6 0.1 copy.32
  32.7 1.8 %collective-permute-done.2 = bf16[128,4,2,64]{0,3,1,2:T(8,128)(2,1)S(1)} collective-permute-done((bf16[128,4,2,64]{0,3,1,2:T(8,128)(2,1)S(1)}, bf16[128,4,2,64]{0,3,1,2:T(8,128)(2,1)S(1)}, u32[]{:S(2)}, u32[]{:S(2)}) %collective-permute-start.2) | collective-permute-done | bytes 131104 | tf_op jit(solution)/shard_map/ppermute | solution.py:39
  34.5 2.4 %collective-permute-start.4 = (bf16[128,4,2,64]{0,3,1,2:T(8,128)(2,1)S(1)}, bf16[128,4,2,64]{0,3,1,2:T(8,128)(2,1)S(1)}, u32[]{:S(2)}, u32[]{:S(2)}) collective-permute-start(bf16[128,4,2,64]{0,3,1,2:T(8,128)(2,1)S(1)} %collective-permute-done.2), channel_id=1, source_target_pairs={{0,4},{4,8},{8,12},{12,0},{16,20},{20,24},{24,28},{28,16},{1,5},{5... | collective-permute-start | bytes 393224 | tf_op jit(solution)/shard_map/ppermute | solution.py:44
  36.9 0.0 collective-permute-start.6
  37.0 0.0 collective-permute-done.3
  37.0 1.5 %collective-permute-start.8 = (bf16[128,4,2,64]{0,3,1,2:T(8,128)(2,1)S(1)}, bf16[128,4,2,64]{0,3,1,2:T(8,128)(2,1)S(1)}, u32[]{:S(2)}, u32[]{:S(2)}) collective-permute-start(bf16[128,4,2,64]{0,3,1,2:T(8,128)(2,1)S(1)} %collective-permute-done.2), channel_id=1, source_target_pairs={{0,12},{4,0},{8,4},{12,8},{16,28},{20,16},{24,20},{28,24},{1,13},{... | collective-permute-start | bytes 393224 | tf_op jit(solution)/shard_map/ppermute | solution.py:44
  38.5 0.9 %constant_dynamic-update-slice_fusion.5 = bf16[1024,4,2,64]{0,3,1,2:T(8,128)(2,1)S(1)} fusion(bf16[1024,4,2,64]{0,3,1,2:T(8,128)(2,1)S(1)} %constant_dynamic-update-slice_fusion.6, bf16[128,4,2,64]{0,3,1,2:T(8,128)(2,1)} %collective-permute-done.3), kind=kLoop, calls=%fused_computation.91 | loop fusion | bytes 262144
  39.4 2.7 %collective-permute-done.4 = bf16[128,4,2,64]{0,3,1,2:T(8,128)(2,1)S(1)} collective-permute-done((bf16[128,4,2,64]{0,3,1,2:T(8,128)(2,1)S(1)}, bf16[128,4,2,64]{0,3,1,2:T(8,128)(2,1)S(1)}, u32[]{:S(2)}, u32[]{:S(2)}) %collective-permute-start.4) | collective-permute-done | bytes 131104 | tf_op jit(solution)/shard_map/ppermute | solution.py:44
  42.2 0.0 collective-permute-done.5
  42.2 0.9 %constant_dynamic-update-slice_fusion.3 = bf16[1024,4,2,64]{0,3,1,2:T(8,128)(2,1)S(1)} fusion(bf16[1024,4,2,64]{0,3,1,2:T(8,128)(2,1)S(1)} %constant_dynamic-update-slice_fusion.4, bf16[128,4,2,64]{0,3,1,2:T(8,128)(2,1)} %collective-permute-done.5), kind=kLoop, calls=%fused_computation.89 | loop fusion | bytes 262144
  43.2 0.2 collective-permute-done.6
  43.4 0.0 collective-permute-done.7
  43.5 0.9 %collective-permute-done.8 = bf16[128,4,2,64]{0,3,1,2:T(8,128)(2,1)S(1)} collective-permute-done((bf16[128,4,2,64]{0,3,1,2:T(8,128)(2,1)S(1)}, bf16[128,4,2,64]{0,3,1,2:T(8,128)(2,1)S(1)}, u32[]{:S(2)}, u32[]{:S(2)}) %collective-permute-start.8) | collective-permute-done | bytes 131104 | tf_op jit(solution)/shard_map/ppermute | solution.py:44
  44.4 0.4 fusion.46
  44.8 0.0 copy-start.1
  44.8 0.3 fusion.6
  45.2 0.4 fusion.5
  45.5 0.1 copy.35
  45.6 0.1 reshape.252
  45.7 0.2 copy-done.1
  45.9 0.2 convolution_convert_fusion.1
  46.1 0.6 %collective-permute-start.10 = (bf16[32,1024]{1,0:T(8,128)(2,1)S(1)}, bf16[32,1024]{1,0:T(8,128)(2,1)S(1)}, u32[]{:S(2)}, u32[]{:S(2)}) collective-permute-start(bf16[32,1024]{1,0:T(8,128)(2,1)S(1)} %get-tuple-element.47), channel_id=1, source_target_pairs={{0,2},{1,3},{2,0},{3,1},{4,6},{5,7},{6,4},{7,5},{8,10},{9,11},{10,... | collective-permute-start | bytes 196616 | tf_op jit(solution)/shard_map/ppermute | solution.py:198
  46.7 0.5 collective-permute-start.11
  47.2 0.4 fusion.47
  47.6 0.3 fusion.8
  47.9 0.4 fusion.4
  48.2 0.1 copy.36
  48.3 0.1 dot_general.39
  48.4 0.2 fusion.37
  48.7 1.2 %collective-permute-start.9 = (f32[32,1024]{1,0:T(8,128)S(1)}, f32[32,1024]{1,0:T(8,128)S(1)}, u32[]{:S(2)}, u32[]{:S(2)}) collective-permute-start(f32[32,1024]{1,0:T(8,128)S(1)} %get-tuple-element.43), channel_id=1, source_target_pairs={{0,1},{1,0},{2,3},{3,2},{4,5},{5,4},{6,7},{7,6},{8,9},{9,8},{10,11... | collective-permute-start | bytes 393224 | tf_op jit(solution)/shard_map/ppermute | solution.py:210
  49.9 0.1 reshape.254
  50.0 1.2 %collective-permute-done.10 = bf16[32,1024]{1,0:T(8,128)(2,1)S(1)} collective-permute-done((bf16[32,1024]{1,0:T(8,128)(2,1)S(1)}, bf16[32,1024]{1,0:T(8,128)(2,1)S(1)}, u32[]{:S(2)}, u32[]{:S(2)}) %collective-permute-start.10) | collective-permute-done | bytes 65568 | tf_op jit(solution)/shard_map/ppermute | solution.py:198
  51.1 0.0 collective-permute-done.11
  51.1 0.1 add.238
  51.2 0.0 collective-permute-done.9
  51.2 0.1 reshape.255
  51.3 0.7 %add_convert_fusion.1 = bf16[1,16,2,1024]{3,2,1,0:T(2,128)(2,1)} fusion(f32[1,16,2,1024]{3,2,1,0:T(2,128)S(1)} %add.238, f32[1,16,2,1024]{3,2,1,0:T(2,128)S(1)} %reshape.254, f32[1,16,2,1024]{3,2,1,0:T(2,128)S(1)} %reshape.255), kind=kLoop, calls=%fused_computation.80 | loop fusion | flops 98304 | bytes 458752 | tf_op jit(solution)/shard_map/convert_element_type | solution.py:213
  (15 shorter events, 0.4 us)
Async XLA Ops:
  0.0 24.0 %copy-start = (bf16[768,1024]{1,0:T(8,128)(2,1)S(1)}, bf16[768,1024]{1,0:T(8,128)(2,1)}, u32[]{:S(2)}) copy-start(bf16[768,1024]{1,0:T(8,128)(2,1)} %param.8) | copy-start | bytes 4718596
  1.0 8.5 %collective-permute-start = (bf16[1,16,2,1024]{3,1,2,0:T(8,128)(2,1)S(1)}, bf16[1,16,2,1024]{3,1,2,0:T(8,128)(2,1)S(1)}, u32[]{:S(2)}, u32[]{:S(2)}) collective-permute-start(bf16[1,16,2,1024]{3,1,2,0:T(8,128)(2,1)S(1)} %copy.26), channel_id=1, source_target_pairs={{0,4},{4,8},{8,12},{12,16},{16,20},{20,24},{24,28},{1,5},{5,9},{9,... | collective-permute-start | bytes 196616 | tf_op jit(solution)/shard_map/ppermute | solution.py:18
  5.9 6.2 %collective-permute-start.1 = (bf16[1,16,2,1024]{3,1,2,0:T(8,128)(2,1)S(1)}, bf16[1,16,2,1024]{3,1,2,0:T(8,128)(2,1)S(1)}, u32[]{:S(2)}, u32[]{:S(2)}) collective-permute-start(bf16[1,16,2,1024]{3,1,2,0:T(8,128)(2,1)S(1)} %copy.26), channel_id=1, source_target_pairs={{4,0},{8,4},{12,8},{16,12},{20,16},{24,20},{28,24},{5,1},{9,5},{13... | collective-permute-start | bytes 196616 | tf_op jit(solution)/shard_map/ppermute | solution.py:19
  20.6 0.7 %copy-start.2 = (f32[1024]{0:T(1024)S(1)}, f32[1024]{0:T(1024)}, u32[]{:S(2)}) copy-start(f32[1024]{0:T(1024)} %param.7) | copy-start | bytes 12292
  24.9 9.6 %collective-permute-start.2 = (bf16[128,4,2,64]{0,3,1,2:T(8,128)(2,1)S(1)}, bf16[128,4,2,64]{0,3,1,2:T(8,128)(2,1)S(1)}, u32[]{:S(2)}, u32[]{:S(2)}) collective-permute-start(bf16[128,4,2,64]{0,3,1,2:T(8,128)(2,1)S(1)} %get-tuple-element.56), channel_id=1, source_target_pairs={{0,16},{4,20},{8,24},{12,28},{16,0},{20,4},{24,8},{28,12},{1,17},{... | collective-permute-start | bytes 393224 | tf_op jit(solution)/shard_map/ppermute | solution.py:39
  27.5 9.4 %collective-permute-start.3 = (bf16[128,4,2,64]{0,3,1,2:T(8,128)(2,1)S(1)}, bf16[128,4,2,64]{0,3,1,2:T(8,128)(2,1)}, u32[]{:S(2)}, u32[]{:S(2)}) collective-permute-start(bf16[128,4,2,64]{0,3,1,2:T(8,128)(2,1)S(1)} %get-tuple-element.56), channel_id=1, source_target_pairs={{0,4},{4,8},{8,12},{12,0},{16,20},{20,24},{24,28},{28,16},{1,5},{5... | collective-permute-start | bytes 393224 | tf_op jit(solution)/shard_map/ppermute | solution.py:43
  29.9 12.3 %collective-permute-start.5 = (bf16[128,4,2,64]{0,3,1,2:T(8,128)(2,1)S(1)}, bf16[128,4,2,64]{0,3,1,2:T(8,128)(2,1)}, u32[]{:S(2)}, u32[]{:S(2)}) collective-permute-start(bf16[128,4,2,64]{0,3,1,2:T(8,128)(2,1)S(1)} %get-tuple-element.56), channel_id=1, source_target_pairs={{0,8},{4,12},{8,0},{12,4},{16,24},{20,28},{24,16},{28,20},{1,9},{5... | collective-permute-start | bytes 393224 | tf_op jit(solution)/shard_map/ppermute | solution.py:43
  30.0 13.5 %collective-permute-start.7 = (bf16[128,4,2,64]{0,3,1,2:T(8,128)(2,1)S(1)}, bf16[128,4,2,64]{0,3,1,2:T(8,128)(2,1)S(1)}, u32[]{:S(2)}, u32[]{:S(2)}) collective-permute-start(bf16[128,4,2,64]{0,3,1,2:T(8,128)(2,1)S(1)} %get-tuple-element.56), channel_id=1, source_target_pairs={{0,12},{4,0},{8,4},{12,8},{16,28},{20,16},{24,20},{28,24},{1,13},{... | collective-permute-start | bytes 393224 | tf_op jit(solution)/shard_map/ppermute | solution.py:43
  34.5 7.7 %collective-permute-start.4 = (bf16[128,4,2,64]{0,3,1,2:T(8,128)(2,1)S(1)}, bf16[128,4,2,64]{0,3,1,2:T(8,128)(2,1)S(1)}, u32[]{:S(2)}, u32[]{:S(2)}) collective-permute-start(bf16[128,4,2,64]{0,3,1,2:T(8,128)(2,1)S(1)} %collective-permute-done.2), channel_id=1, source_target_pairs={{0,4},{4,8},{8,12},{12,0},{16,20},{20,24},{24,28},{28,16},{1,5},{5... | collective-permute-start | bytes 393224 | tf_op jit(solution)/shard_map/ppermute | solution.py:44
  36.9 6.4 %collective-permute-start.6 = (bf16[128,4,2,64]{0,3,1,2:T(8,128)(2,1)S(1)}, bf16[128,4,2,64]{0,3,1,2:T(8,128)(2,1)S(1)}, u32[]{:S(2)}, u32[]{:S(2)}) collective-permute-start(bf16[128,4,2,64]{0,3,1,2:T(8,128)(2,1)S(1)} %collective-permute-done.2), channel_id=1, source_target_pairs={{0,8},{4,12},{8,0},{12,4},{16,24},{20,28},{24,16},{28,20},{1,9},{5... | collective-permute-start | bytes 393224 | tf_op jit(solution)/shard_map/ppermute | solution.py:44
  37.0 7.4 %collective-permute-start.8 = (bf16[128,4,2,64]{0,3,1,2:T(8,128)(2,1)S(1)}, bf16[128,4,2,64]{0,3,1,2:T(8,128)(2,1)S(1)}, u32[]{:S(2)}, u32[]{:S(2)}) collective-permute-start(bf16[128,4,2,64]{0,3,1,2:T(8,128)(2,1)S(1)} %collective-permute-done.2), channel_id=1, source_target_pairs={{0,12},{4,0},{8,4},{12,8},{16,28},{20,16},{24,20},{28,24},{1,13},{... | collective-permute-start | bytes 393224 | tf_op jit(solution)/shard_map/ppermute | solution.py:44
  44.8 1.1 %copy-start.1 = (bf16[256,1024]{1,0:T(8,128)(2,1)S(1)}, bf16[256,1024]{1,0:T(8,128)(2,1)}, u32[]{:S(2)}) copy-start(bf16[256,1024]{1,0:T(8,128)(2,1)} %param.9) | copy-start | bytes 1572868
  46.1 5.0 %collective-permute-start.10 = (bf16[32,1024]{1,0:T(8,128)(2,1)S(1)}, bf16[32,1024]{1,0:T(8,128)(2,1)S(1)}, u32[]{:S(2)}, u32[]{:S(2)}) collective-permute-start(bf16[32,1024]{1,0:T(8,128)(2,1)S(1)} %get-tuple-element.47), channel_id=1, source_target_pairs={{0,2},{1,3},{2,0},{3,1},{4,6},{5,7},{6,4},{7,5},{8,10},{9,11},{10,... | collective-permute-start | bytes 196616 | tf_op jit(solution)/shard_map/ppermute | solution.py:198
  46.7 4.4 %collective-permute-start.11 = (bf16[32,1024]{1,0:T(8,128)(2,1)S(1)}, bf16[32,1024]{1,0:T(8,128)(2,1)S(1)}, u32[]{:S(2)}, u32[]{:S(2)}) collective-permute-start(bf16[32,1024]{1,0:T(8,128)(2,1)S(1)} %get-tuple-element.48), channel_id=1, source_target_pairs={{0,3},{1,2},{2,1},{3,0},{4,7},{5,6},{6,5},{7,4},{8,11},{9,10},{10,... | collective-permute-start | bytes 196616 | tf_op jit(solution)/shard_map/ppermute | solution.py:199
  48.7 2.6 %collective-permute-start.9 = (f32[32,1024]{1,0:T(8,128)S(1)}, f32[32,1024]{1,0:T(8,128)S(1)}, u32[]{:S(2)}, u32[]{:S(2)}) collective-permute-start(f32[32,1024]{1,0:T(8,128)S(1)} %get-tuple-element.43), channel_id=1, source_target_pairs={{0,1},{1,0},{2,3},{3,2},{4,5},{5,4},{6,7},{7,6},{8,9},{9,8},{10,11... | collective-permute-start | bytes 393224 | tf_op jit(solution)/shard_map/ppermute | solution.py:210

commit v15 on v7

--- a/solution.py
+++ b/solution.py
@@ -169,6 +169,25 @@
                 preferred_element_type=jnp.float32,
             )
             return ((new_max, running_sum, weighted), None)
+
+        if key_blocks.shape[0] == 1:
+            scores = (
+                jnp.einsum(
+                    "qhd,khd->hqk", query_rows, key_piece, preferred_element_type=jnp.float32
+                )
+                * score_scale
+            )
+            row_max = jnp.max(scores, axis=2, keepdims=True)
+            weights = jnp.exp(scores - row_max)
+            row_sum = jnp.sum(weights, axis=2, keepdims=True)
+            mixed = jnp.einsum(
+                "hqk,khd->hqd",
+                weights.astype(jnp.bfloat16),
+                value_piece,
+                preferred_element_type=jnp.float32,
+            )
+            attended = (mixed / row_sum).astype(jnp.bfloat16)
+            return attended.transpose(1, 0, 2).reshape(rows, heads_here * HS)
 
         start_state = (
             jnp.full((heads_here, rows), -1e30, jnp.float32),

time: 52.3 us -> 52.3 us (level)
  no operation moved by 1% of the time
where the time goes in v15:
time: 52.3 us; the launch traced here: 51.8 us
  starting transfers between devices  20.9 us (40%)
  waiting for transfers between devices  15.7 us (30%)
  local copies, waits for them, and re-layouts  8.44 us (16%)
  other arithmetic  3.71 us (7%)
  matrix products  2.52 us (5%)
    ppermute x1, waiting for transfers between devices, gathered_by_chip(): far = lax.ppermute(piece, axis, chip_shift(size, shift))  5.62 us
    ppermute x1, starting transfers between devices, padded_2(): before = lax.ppermute(last, axis, up)  4.87 us
    ppermute x3, starting transfers between devices, relayed(): parts.append(lax.ppermute(piece, axis, pairs))  4.5 us
    unnamed x16, local copies, waits for them, and re-layouts  4.1 us
    ppermute x3, starting transfers between devices, relayed(): parts.append(lax.ppermute(crossed, axis, pairs))  3.23 us
    ppermute x3, waiting for transfers between devices, relayed(): parts.append(lax.ppermute(crossed, axis, pairs))  3.23 us
    ppermute x1, starting transfers between devices, relayed(): crossed = lax.ppermute(piece, axis, mirror)  3.2 us
    convert_element_type x1, other arithmetic, on_device(): positioned = summed.astype(jnp.bfloat16)  2.34 us
  transfers between devices with their start and end apart: 15, of which 9 were waited for; matrix products, arithmetic and copies ran while one was open for 15% of the time, Pallas kernels for 0%

profile of v15, /device:TPU:0, one launch (start us, length us, event | category | flops | bytes accessed | tf_op | source)
XLA Modules:
  0.0 51.8 jit_solution(7302979305084032717)
XLA Ops:
  0.0 1.0 %copy.21 = bf16[1,16,2,1024]{3,1,2,0:T(8,128)(2,1)S(1)} copy(bf16[1,16,2,1024]{3,2,1,0:T(2,128)(2,1)} %param.5) | data formatting | bytes 131072 | tf_op args[0]
  1.0 4.9 %collective-permute-start = (bf16[1,16,2,1024]{3,1,2,0:T(8,128)(2,1)S(1)}, bf16[1,16,2,1024]{3,1,2,0:T(8,128)(2,1)S(1)}, u32[]{:S(2)}, u32[]{:S(2)}) collective-permute-start(bf16[1,16,2,1024]{3,1,2,0:T(8,128)(2,1)S(1)} %copy.21), channel_id=1, source_target_pairs={{0,4},{4,8},{8,12},{12,16},{16,20},{20,24},{24,28},{1,5},{5,9},{9,... | collective-permute-start | bytes 196616 | tf_op jit(solution)/shard_map/ppermute | solution.py:18
  5.9 1.3 %collective-permute-start.1 = (bf16[1,16,2,1024]{3,1,2,0:T(8,128)(2,1)S(1)}, bf16[1,16,2,1024]{3,1,2,0:T(8,128)(2,1)S(1)}, u32[]{:S(2)}, u32[]{:S(2)}) collective-permute-start(bf16[1,16,2,1024]{3,1,2,0:T(8,128)(2,1)S(1)} %copy.21), channel_id=1, source_target_pairs={{4,0},{8,4},{12,8},{16,12},{20,16},{24,20},{28,24},{5,1},{9,5},{13... | collective-permute-start | bytes 196616 | tf_op jit(solution)/shard_map/ppermute | solution.py:19
  7.2 1.3 %fusion.42 = (f32[1,1024]{1,0:T(1,128)S(1)}, f32[1,1024]{1,0:T(1,128)S(1)}, f32[1,1024]{1,0:T(1,128)S(1)}, f32[1,1024]{1,0:T(1,128)S(1)}, f32[1,1024]{1,0:T(1,12...) fusion(f32[27,1024]{1,0:T(8,128)} %param.6), kind=kLoop, calls=%fused_computation.103 | loop fusion | bytes 155648 | tf_op jit(solution)/shard_map/slice | solution.py:121
  8.5 1.0 %fusion.43 = (f32[1,1024]{1,0:T(1,128)S(1)}, f32[1,1024]{1,0:T(1,128)S(1)}, f32[1,1024]{1,0:T(1,128)S(1)}, f32[1,1024]{1,0:T(1,128)S(1)}, f32[1,1024]{1,0:T(1,12...) fusion(f32[27,1024]{1,0:T(8,128)} %param.6), kind=kLoop, calls=%fused_computation.104 | loop fusion | bytes 65536 | tf_op jit(solution)/shard_map/slice | solution.py:121
  9.6 0.0 collective-permute-done
  9.6 0.9 %constant_dynamic-update-slice_fusion.1 = bf16[3,16,2,1024]{3,1,2,0:T(8,128)(2,1)S(1)} fusion(bf16[3,16,2,1024]{3,1,2,0:T(8,128)(2,1)S(1)} %constant_dynamic-update-slice_fusion.2, bf16[1,16,2,1024]{3,2,1,0:T(2,128)(2,1)} %param.5), kind=kLoop, calls=%fused_computation.88 | loop fusion | bytes 131072
  10.4 1.6 %collective-permute-done.1 = bf16[1,16,2,1024]{3,1,2,0:T(8,128)(2,1)S(1)} collective-permute-done((bf16[1,16,2,1024]{3,1,2,0:T(8,128)(2,1)S(1)}, bf16[1,16,2,1024]{3,1,2,0:T(8,128)(2,1)S(1)}, u32[]{:S(2)}, u32[]{:S(2)}) %collective-permute-start.1) | collective-permute-done | bytes 65568 | tf_op jit(solution)/shard_map/ppermute | solution.py:19
  12.0 0.0 collective-permute-start.2
  12.0 1.6 %collective-permute-start.3 = (bf16[3,16,2,1024]{3,1,2,0:T(8,128)(2,1)S(1)}, bf16[3,16,2,1024]{3,1,2,0:T(8,128)(2,1)S(1)}, u32[]{:S(2)}, u32[]{:S(2)}) collective-permute-start(bf16[3,16,2,1024]{3,1,2,0:T(8,128)(2,1)S(1)} %constant_dynamic-update-slice_fusion), channel_id=1, source_target_pairs={{0,2},{1,3},{2,0},{3,1},{4,6},{5,7},{6,4},{7,5},{8,10},{9,11},{10,... | collective-permute-start | bytes 589832 | tf_op jit(solution)/shard_map/ppermute | solution.py:64
  13.6 0.1 broadcast_in_dim.21
  13.7 0.0 copy-start.2
  13.7 5.6 %collective-permute-done.3 = bf16[3,16,2,1024]{3,1,2,0:T(8,128)(2,1)S(1)} collective-permute-done((bf16[3,16,2,1024]{3,1,2,0:T(8,128)(2,1)S(1)}, bf16[3,16,2,1024]{3,1,2,0:T(8,128)(2,1)S(1)}, u32[]{:S(2)}, u32[]{:S(2)}) %collective-permute-start.3) | collective-permute-done | bytes 196640 | tf_op jit(solution)/shard_map/ppermute | solution.py:64
  19.3 0.0 collective-permute-start.4
  19.3 0.0 collective-permute-done.2
  19.4 1.4 %collective-permute-done.4 = bf16[3,16,2,1024]{3,1,2,0:T(8,128)(2,1)S(1)} collective-permute-done((bf16[3,16,2,1024]{3,1,2,0:T(8,128)(2,1)S(1)}, bf16[3,16,2,1024]{3,1,2,0:T(8,128)(2,1)S(1)}, u32[]{:S(2)}, u32[]{:S(2)}) %collective-permute-start.4) | collective-permute-done | bytes 196640 | tf_op jit(solution)/shard_map/ppermute | solution.py:66
  20.8 0.1 fusion.40
  20.9 2.3 %add_convert_fusion = bf16[1,16,8,1024]{3,1,2,0:T(8,128)(2,1)S(1)} fusion(bf16[1,16,8,1024]{3,1,2,0:T(8,128)(2,1)S(1)} %bitcast.115, bf16[1,16,8,1024]{3,1,2,0:T(8,128)(2,1)S(1)} %bitcast.114, bf16[1,16,8,1024]{3,1,2,0:T(8,128)(2,1)S(1)} %bitcast.113, bf16[3,16,8,1024]{3,1,2,0:T(8,128)(2,1)S(1)} %bitcast.110, f32[1024]{0:T(1024)S(1)} %bitcast.145, ...), kind=kLoop, calls=%fused_computation.75 | loop fusion | flops 10878976 | bytes 1949696 | tf_op jit(solution)/shard_map/convert_element_type | solution.py:128
  23.2 0.3 copy.39
  23.5 0.1 reshape.226
  23.6 0.7 %convolution_convert_fusion = bf16[128,768]{1,0:T(8,128)(2,1)S(1)} fusion(bf16[128,1024]{1,0:T(8,128)(2,1)S(1)} %reshape.226, bf16[768,1024]{1,0:T(8,128)(2,1)S(1)} %copy-done), kind=kOutput, calls=%fused_computation.26 | convolution fusion | flops 201424896 | bytes 2031616 | tf_op jit(solution)/shard_map/dot_general | solution.py:100
  24.3 0.2 copy.28
  24.5 3.2 %collective-permute-start.5 = (bf16[128,4,2,64]{0,3,1,2:T(8,128)(2,1)S(1)}, bf16[128,4,2,64]{0,3,1,2:T(8,128)(2,1)S(1)}, u32[]{:S(2)}, u32[]{:S(2)}) collective-permute-start(bf16[128,4,2,64]{0,3,1,2:T(8,128)(2,1)S(1)} %get-tuple-element.16), channel_id=1, source_target_pairs={{0,16},{4,20},{8,24},{12,28},{16,0},{20,4},{24,8},{28,12},{1,17},{... | collective-permute-start | bytes 393224 | tf_op jit(solution)/shard_map/ppermute | solution.py:39
  27.7 1.9 %collective-permute-start.6 = (bf16[128,4,2,64]{0,3,1,2:T(8,128)(2,1)S(1)}, bf16[128,4,2,64]{0,3,1,2:T(8,128)(2,1)}, u32[]{:S(2)}, u32[]{:S(2)}) collective-permute-start(bf16[128,4,2,64]{0,3,1,2:T(8,128)(2,1)S(1)} %get-tuple-element.16), channel_id=1, source_target_pairs={{0,4},{4,8},{8,12},{12,0},{16,20},{20,24},{24,28},{28,16},{1,5},{5... | collective-permute-start | bytes 393224 | tf_op jit(solution)/shard_map/ppermute | solution.py:43
  29.6 0.3 collective-permute-start.8
  29.9 2.3 %collective-permute-start.10 = (bf16[128,4,2,64]{0,3,1,2:T(8,128)(2,1)S(1)}, bf16[128,4,2,64]{0,3,1,2:T(8,128)(2,1)S(1)}, u32[]{:S(2)}, u32[]{:S(2)}) collective-permute-start(bf16[128,4,2,64]{0,3,1,2:T(8,128)(2,1)S(1)} %get-tuple-element.16), channel_id=1, source_target_pairs={{0,12},{4,0},{8,4},{12,8},{16,28},{20,16},{24,20},{28,24},{1,13},{... | collective-permute-start | bytes 393224 | tf_op jit(solution)/shard_map/ppermute | solution.py:43
  32.2 0.1 reshape_squeeze.3
  32.3 0.3 constant_dynamic-slice_fusion.2
  32.6 0.1 copy.30
  32.7 0.1 copy.29
  32.9 1.6 %collective-permute-done.5 = bf16[128,4,2,64]{0,3,1,2:T(8,128)(2,1)S(1)} collective-permute-done((bf16[128,4,2,64]{0,3,1,2:T(8,128)(2,1)S(1)}, bf16[128,4,2,64]{0,3,1,2:T(8,128)(2,1)S(1)}, u32[]{:S(2)}, u32[]{:S(2)}) %collective-permute-start.5) | collective-permute-done | bytes 131104 | tf_op jit(solution)/shard_map/ppermute | solution.py:39
  34.4 1.9 %collective-permute-start.7 = (bf16[128,4,2,64]{0,3,1,2:T(8,128)(2,1)S(1)}, bf16[128,4,2,64]{0,3,1,2:T(8,128)(2,1)S(1)}, u32[]{:S(2)}, u32[]{:S(2)}) collective-permute-start(bf16[128,4,2,64]{0,3,1,2:T(8,128)(2,1)S(1)} %collective-permute-done.5), channel_id=1, source_target_pairs={{0,4},{4,8},{8,12},{12,0},{16,20},{20,24},{24,28},{28,16},{1,5},{5... | collective-permute-start | bytes 393224 | tf_op jit(solution)/shard_map/ppermute | solution.py:44
  36.4 0.0 collective-permute-start.9
  36.4 0.4 collective-permute-done.6
  36.8 1.3 %collective-permute-start.11 = (bf16[128,4,2,64]{0,3,1,2:T(8,128)(2,1)S(1)}, bf16[128,4,2,64]{0,3,1,2:T(8,128)(2,1)S(1)}, u32[]{:S(2)}, u32[]{:S(2)}) collective-permute-start(bf16[128,4,2,64]{0,3,1,2:T(8,128)(2,1)S(1)} %collective-permute-done.5), channel_id=1, source_target_pairs={{0,12},{4,0},{8,4},{12,8},{16,28},{20,16},{24,20},{28,24},{1,13},{... | collective-permute-start | bytes 393224 | tf_op jit(solution)/shard_map/ppermute | solution.py:44
  38.1 0.9 %constant_dynamic-update-slice_fusion.8 = bf16[1024,4,2,64]{0,3,1,2:T(8,128)(2,1)S(1)} fusion(bf16[1024,4,2,64]{0,3,1,2:T(8,128)(2,1)S(1)} %constant_dynamic-update-slice_fusion.9, bf16[128,4,2,64]{0,3,1,2:T(8,128)(2,1)} %collective-permute-done.6), kind=kLoop, calls=%fused_computation.95 | loop fusion | bytes 262144
  39.1 3.2 %collective-permute-done.7 = bf16[128,4,2,64]{0,3,1,2:T(8,128)(2,1)S(1)} collective-permute-done((bf16[128,4,2,64]{0,3,1,2:T(8,128)(2,1)S(1)}, bf16[128,4,2,64]{0,3,1,2:T(8,128)(2,1)S(1)}, u32[]{:S(2)}, u32[]{:S(2)}) %collective-permute-start.7) | collective-permute-done | bytes 131104 | tf_op jit(solution)/shard_map/ppermute | solution.py:44
  42.3 0.0 collective-permute-done.8
  42.3 0.9 %constant_dynamic-update-slice_fusion.6 = bf16[1024,4,2,64]{0,3,1,2:T(8,128)(2,1)S(1)} fusion(bf16[1024,4,2,64]{0,3,1,2:T(8,128)(2,1)S(1)} %constant_dynamic-update-slice_fusion.7, bf16[128,4,2,64]{0,3,1,2:T(8,128)(2,1)} %collective-permute-done.8), kind=kLoop, calls=%fused_computation.93 | loop fusion | bytes 262144
  43.3 0.0 collective-permute-done.10
  43.4 0.1 collective-permute-done.11
  43.5 0.4 fusion.44
  43.8 0.0 copy-start.1
  43.8 0.3 fusion.4
  44.1 0.4 fusion.3
  44.5 0.1 copy.32
  44.6 0.1 reshape.228
  44.7 0.2 copy-done.1
  44.9 0.2 convolution_convert_fusion.1
  45.1 1.6 %collective-permute-start.13 = (bf16[32,1024]{1,0:T(8,128)(2,1)S(1)}, bf16[32,1024]{1,0:T(8,128)(2,1)S(1)}, u32[]{:S(2)}, u32[]{:S(2)}) collective-permute-start(bf16[32,1024]{1,0:T(8,128)(2,1)S(1)} %get-tuple-element.14), channel_id=1, source_target_pairs={{0,2},{1,3},{2,0},{3,1},{4,6},{5,7},{6,4},{7,5},{8,10},{9,11},{10,... | collective-permute-start | bytes 196616 | tf_op jit(solution)/shard_map/ppermute | solution.py:217
  46.7 0.4 fusion.45
  47.0 0.3 fusion.6
  47.4 0.4 fusion.2
  47.7 0.1 copy.33
  47.8 0.1 dot_general.35
  47.9 0.2 fusion.35
  48.1 0.7 %collective-permute-start.12 = (f32[32,1024]{1,0:T(8,128)S(1)}, f32[32,1024]{1,0:T(8,128)S(1)}, u32[]{:S(2)}, u32[]{:S(2)}) collective-permute-start(f32[32,1024]{1,0:T(8,128)S(1)} %get-tuple-element.10), channel_id=1, source_target_pairs={{0,1},{1,0},{2,3},{3,2},{4,5},{5,4},{6,7},{7,6},{8,9},{9,8},{10,11... | collective-permute-start | bytes 393224 | tf_op jit(solution)/shard_map/ppermute | solution.py:229
  48.8 0.1 reshape.230
  48.9 0.5 %collective-permute-done.13 = bf16[32,1024]{1,0:T(8,128)(2,1)S(1)} collective-permute-done((bf16[32,1024]{1,0:T(8,128)(2,1)S(1)}, bf16[32,1024]{1,0:T(8,128)(2,1)S(1)}, u32[]{:S(2)}, u32[]{:S(2)}) %collective-permute-start.13) | collective-permute-done | bytes 65568 | tf_op jit(solution)/shard_map/ppermute | solution.py:217
  49.4 1.4 %collective-permute-done.14 = bf16[32,1024]{1,0:T(8,128)(2,1)S(1)} collective-permute-done((bf16[32,1024]{1,0:T(8,128)(2,1)S(1)}, bf16[32,1024]{1,0:T(8,128)(2,1)S(1)}, u32[]{:S(2)}, u32[]{:S(2)}) %collective-permute-start.14) | collective-permute-done | bytes 65568 | tf_op jit(solution)/shard_map/ppermute | solution.py:218
  50.9 0.1 add.233
  51.0 0.0 collective-permute-done.12
  51.0 0.1 reshape.231
  51.0 0.7 %add_convert_fusion.1 = bf16[1,16,2,1024]{3,2,1,0:T(2,128)(2,1)} fusion(f32[1,16,2,1024]{3,2,1,0:T(2,128)S(1)} %add.233, f32[1,16,2,1024]{3,2,1,0:T(2,128)S(1)} %reshape.230, f32[1,16,2,1024]{3,2,1,0:T(2,128)S(1)} %reshape.231), kind=kLoop, calls=%fused_computation.81 | loop fusion | flops 98304 | bytes 458752 | tf_op jit(solution)/shard_map/convert_element_type | solution.py:232
  (21 shorter events, 0.4 us)
Async XLA Ops:
  0.0 23.6 %copy-start = (bf16[768,1024]{1,0:T(8,128)(2,1)S(1)}, bf16[768,1024]{1,0:T(8,128)(2,1)}, u32[]{:S(2)}) copy-start(bf16[768,1024]{1,0:T(8,128)(2,1)} %param.8) | copy-start | bytes 4718596
  1.0 8.6 %collective-permute-start = (bf16[1,16,2,1024]{3,1,2,0:T(8,128)(2,1)S(1)}, bf16[1,16,2,1024]{3,1,2,0:T(8,128)(2,1)S(1)}, u32[]{:S(2)}, u32[]{:S(2)}) collective-permute-start(bf16[1,16,2,1024]{3,1,2,0:T(8,128)(2,1)S(1)} %copy.21), channel_id=1, source_target_pairs={{0,4},{4,8},{8,12},{12,16},{16,20},{20,24},{24,28},{1,5},{5,9},{9,... | collective-permute-start | bytes 196616 | tf_op jit(solution)/shard_map/ppermute | solution.py:18
  5.9 6.2 %collective-permute-start.1 = (bf16[1,16,2,1024]{3,1,2,0:T(8,128)(2,1)S(1)}, bf16[1,16,2,1024]{3,1,2,0:T(8,128)(2,1)S(1)}, u32[]{:S(2)}, u32[]{:S(2)}) collective-permute-start(bf16[1,16,2,1024]{3,1,2,0:T(8,128)(2,1)S(1)} %copy.21), channel_id=1, source_target_pairs={{4,0},{8,4},{12,8},{16,12},{20,16},{24,20},{28,24},{5,1},{9,5},{13... | collective-permute-start | bytes 196616 | tf_op jit(solution)/shard_map/ppermute | solution.py:19
  12.0 7.3 %collective-permute-start.2 = (bf16[3,16,2,1024]{3,1,2,0:T(8,128)(2,1)S(1)}, bf16[3,16,2,1024]{3,1,2,0:T(8,128)(2,1)S(1)}, u32[]{:S(2)}, u32[]{:S(2)}) collective-permute-start(bf16[3,16,2,1024]{3,1,2,0:T(8,128)(2,1)S(1)} %constant_dynamic-update-slice_fusion), channel_id=1, source_target_pairs={{0,1},{1,0},{2,3},{3,2},{4,5},{5,4},{6,7},{7,6},{8,9},{9,8},{10,11... | collective-permute-start | bytes 589832 | tf_op jit(solution)/shard_map/ppermute | solution.py:60
  12.0 7.3 %collective-permute-start.3 = (bf16[3,16,2,1024]{3,1,2,0:T(8,128)(2,1)S(1)}, bf16[3,16,2,1024]{3,1,2,0:T(8,128)(2,1)S(1)}, u32[]{:S(2)}, u32[]{:S(2)}) collective-permute-start(bf16[3,16,2,1024]{3,1,2,0:T(8,128)(2,1)S(1)} %constant_dynamic-update-slice_fusion), channel_id=1, source_target_pairs={{0,2},{1,3},{2,0},{3,1},{4,6},{5,7},{6,4},{7,5},{8,10},{9,11},{10,... | collective-permute-start | bytes 589832 | tf_op jit(solution)/shard_map/ppermute | solution.py:64
  13.7 7.2 %copy-start.2 = (f32[1024]{0:T(1024)S(1)}, f32[1024]{0:T(1024)}, u32[]{:S(2)}) copy-start(f32[1024]{0:T(1024)} %param.7) | copy-start | bytes 12292
  19.3 1.4 %collective-permute-start.4 = (bf16[3,16,2,1024]{3,1,2,0:T(8,128)(2,1)S(1)}, bf16[3,16,2,1024]{3,1,2,0:T(8,128)(2,1)S(1)}, u32[]{:S(2)}, u32[]{:S(2)}) collective-permute-start(bf16[3,16,2,1024]{3,1,2,0:T(8,128)(2,1)S(1)} %collective-permute-done.3), channel_id=1, source_target_pairs={{0,1},{1,0},{2,3},{3,2},{4,5},{5,4},{6,7},{7,6},{8,9},{9,8},{10,11... | collective-permute-start | bytes 589832 | tf_op jit(solution)/shard_map/ppermute | solution.py:66
  24.5 9.9 %collective-permute-start.5 = (bf16[128,4,2,64]{0,3,1,2:T(8,128)(2,1)S(1)}, bf16[128,4,2,64]{0,3,1,2:T(8,128)(2,1)S(1)}, u32[]{:S(2)}, u32[]{:S(2)}) collective-permute-start(bf16[128,4,2,64]{0,3,1,2:T(8,128)(2,1)S(1)} %get-tuple-element.16), channel_id=1, source_target_pairs={{0,16},{4,20},{8,24},{12,28},{16,0},{20,4},{24,8},{28,12},{1,17},{... | collective-permute-start | bytes 393224 | tf_op jit(solution)/shard_map/ppermute | solution.py:39
  27.7 9.1 %collective-permute-start.6 = (bf16[128,4,2,64]{0,3,1,2:T(8,128)(2,1)S(1)}, bf16[128,4,2,64]{0,3,1,2:T(8,128)(2,1)}, u32[]{:S(2)}, u32[]{:S(2)}) collective-permute-start(bf16[128,4,2,64]{0,3,1,2:T(8,128)(2,1)S(1)} %get-tuple-element.16), channel_id=1, source_target_pairs={{0,4},{4,8},{8,12},{12,0},{16,20},{20,24},{24,28},{28,16},{1,5},{5... | collective-permute-start | bytes 393224 | tf_op jit(solution)/shard_map/ppermute | solution.py:43
  29.6 12.7 %collective-permute-start.8 = (bf16[128,4,2,64]{0,3,1,2:T(8,128)(2,1)S(1)}, bf16[128,4,2,64]{0,3,1,2:T(8,128)(2,1)}, u32[]{:S(2)}, u32[]{:S(2)}) collective-permute-start(bf16[128,4,2,64]{0,3,1,2:T(8,128)(2,1)S(1)} %get-tuple-element.16), channel_id=1, source_target_pairs={{0,8},{4,12},{8,0},{12,4},{16,24},{20,28},{24,16},{28,20},{1,9},{5... | collective-permute-start | bytes 393224 | tf_op jit(solution)/shard_map/ppermute | solution.py:43
  29.9 13.4 %collective-permute-start.10 = (bf16[128,4,2,64]{0,3,1,2:T(8,128)(2,1)S(1)}, bf16[128,4,2,64]{0,3,1,2:T(8,128)(2,1)S(1)}, u32[]{:S(2)}, u32[]{:S(2)}) collective-permute-start(bf16[128,4,2,64]{0,3,1,2:T(8,128)(2,1)S(1)} %get-tuple-element.16), channel_id=1, source_target_pairs={{0,12},{4,0},{8,4},{12,8},{16,28},{20,16},{24,20},{28,24},{1,13},{... | collective-permute-start | bytes 393224 | tf_op jit(solution)/shard_map/ppermute | solution.py:43
  34.4 7.8 %collective-permute-start.7 = (bf16[128,4,2,64]{0,3,1,2:T(8,128)(2,1)S(1)}, bf16[128,4,2,64]{0,3,1,2:T(8,128)(2,1)S(1)}, u32[]{:S(2)}, u32[]{:S(2)}) collective-permute-start(bf16[128,4,2,64]{0,3,1,2:T(8,128)(2,1)S(1)} %collective-permute-done.5), channel_id=1, source_target_pairs={{0,4},{4,8},{8,12},{12,0},{16,20},{20,24},{24,28},{28,16},{1,5},{5... | collective-permute-start | bytes 393224 | tf_op jit(solution)/shard_map/ppermute | solution.py:44
  36.4 6.9 %collective-permute-start.9 = (bf16[128,4,2,64]{0,3,1,2:T(8,128)(2,1)S(1)}, bf16[128,4,2,64]{0,3,1,2:T(8,128)(2,1)S(1)}, u32[]{:S(2)}, u32[]{:S(2)}) collective-permute-start(bf16[128,4,2,64]{0,3,1,2:T(8,128)(2,1)S(1)} %collective-permute-done.5), channel_id=1, source_target_pairs={{0,8},{4,12},{8,0},{12,4},{16,24},{20,28},{24,16},{28,20},{1,9},{5... | collective-permute-start | bytes 393224 | tf_op jit(solution)/shard_map/ppermute | solution.py:44
  36.8 6.6 %collective-permute-start.11 = (bf16[128,4,2,64]{0,3,1,2:T(8,128)(2,1)S(1)}, bf16[128,4,2,64]{0,3,1,2:T(8,128)(2,1)S(1)}, u32[]{:S(2)}, u32[]{:S(2)}) collective-permute-start(bf16[128,4,2,64]{0,3,1,2:T(8,128)(2,1)S(1)} %collective-permute-done.5), channel_id=1, source_target_pairs={{0,12},{4,0},{8,4},{12,8},{16,28},{20,16},{24,20},{28,24},{1,13},{... | collective-permute-start | bytes 393224 | tf_op jit(solution)/shard_map/ppermute | solution.py:44
  43.8 1.0 %copy-start.1 = (bf16[256,1024]{1,0:T(8,128)(2,1)S(1)}, bf16[256,1024]{1,0:T(8,128)(2,1)}, u32[]{:S(2)}) copy-start(bf16[256,1024]{1,0:T(8,128)(2,1)} %param.9) | copy-start | bytes 1572868
  45.1 4.3 %collective-permute-start.13 = (bf16[32,1024]{1,0:T(8,128)(2,1)S(1)}, bf16[32,1024]{1,0:T(8,128)(2,1)S(1)}, u32[]{:S(2)}, u32[]{:S(2)}) collective-permute-start(bf16[32,1024]{1,0:T(8,128)(2,1)S(1)} %get-tuple-element.14), channel_id=1, source_target_pairs={{0,2},{1,3},{2,0},{3,1},{4,6},{5,7},{6,4},{7,5},{8,10},{9,11},{10,... | collective-permute-start | bytes 196616 | tf_op jit(solution)/shard_map/ppermute | solution.py:217
  46.7 4.2 %collective-permute-start.14 = (bf16[32,1024]{1,0:T(8,128)(2,1)S(1)}, bf16[32,1024]{1,0:T(8,128)(2,1)S(1)}, u32[]{:S(2)}, u32[]{:S(2)}) collective-permute-start(bf16[32,1024]{1,0:T(8,128)(2,1)S(1)} %get-tuple-element.15), channel_id=1, source_target_pairs={{0,3},{1,2},{2,1},{3,0},{4,7},{5,6},{6,5},{7,4},{8,11},{9,10},{10,... | collective-permute-start | bytes 196616 | tf_op jit(solution)/shard_map/ppermute | solution.py:218
  48.1 2.8 %collective-permute-start.12 = (f32[32,1024]{1,0:T(8,128)S(1)}, f32[32,1024]{1,0:T(8,128)S(1)}, u32[]{:S(2)}, u32[]{:S(2)}) collective-permute-start(f32[32,1024]{1,0:T(8,128)S(1)} %get-tuple-element.10), channel_id=1, source_target_pairs={{0,1},{1,0},{2,3},{3,2},{4,5},{5,4},{6,7},{7,6},{8,9},{9,8},{10,11... | collective-permute-start | bytes 393224 | tf_op jit(solution)/shard_map/ppermute | solution.py:229

commit v16 on v7

--- a/solution.py
+++ b/solution.py
@@ -3,18 +3,22 @@
 import jax
 import jax.numpy as jnp
 from jax import lax
+from jax.experimental.layout import Layout, with_layout_constraint
 from jax.sharding import PartitionSpec as P
 
 HS = 64
 
 
-def padded_2(shard, sides, width):
+def padded_2(shard, sides, width, keep=None):
     for axis, dim in sides:
         size, length = (lax.axis_size(axis), shard.shape[dim])
         up = [(i, (i + 1) % size) for i in range(size - 1)]
         down = [(j, i) for i, j in up]
         last = lax.slice_in_dim(shard, length - width, length, axis=dim)
         initial = lax.slice_in_dim(shard, 0, width, axis=dim)
+        if keep is not None:
+            last = with_layout_constraint(last, keep)
+            initial = with_layout_constraint(initial, keep)
         before = lax.ppermute(last, axis, up)
         after = lax.ppermute(initial, axis, down)
         shard = jnp.concatenate([before, shard, after], axis=dim)
@@ -105,7 +109,8 @@
 def on_device(tokens, conv_weight, conv_bias, qkv_weight, out_weight):
     z_count, x_count, y_count, features = tokens.shape
     groups = lax.axis_size("uly")
-    with_halo = padded_2(tokens, (("blk", 0),), 1)
+    arrival = Layout(major_to_minor=tuple(range(tokens.ndim)))
+    with_halo = padded_2(tokens, (("blk", 0),), 1, arrival if y_count == 2 else None)
     slab_in = gathered_by_chip(with_halo, "uly")
     slab_in = slab_in.transpose(1, 2, 0, 3, 4).reshape(
         z_count + 2, x_count, groups * y_count, features

time: 52.3 us -> 51.8 us (level)
  local copies, waits for them, and re-layouts: 8.45 us -> 7.7 us
    unnamed x16 -> x15, local copies, waits for them, and re-layouts: 4.1 us -> 3.21 us
where the time goes in v16:
time: 51.8 us; the launch traced here: 51.3 us
  starting transfers between devices  21.1 us (41%)
  waiting for transfers between devices  15.8 us (31%)
  local copies, waits for them, and re-layouts  7.7 us (15%)
  other arithmetic  3.75 us (7%)
  matrix products  2.5 us (5%)
    ppermute x1, waiting for transfers between devices, gathered_by_chip(): far = lax.ppermute(piece, axis, chip_shift(size, shift))  5.55 us
    ppermute x1, starting transfers between devices, padded_2(): before = lax.ppermute(last, axis, up)  5 us
    ppermute x3, starting transfers between devices, relayed(): parts.append(lax.ppermute(piece, axis, pairs))  4.5 us
    ppermute x3, waiting for transfers between devices, relayed(): parts.append(lax.ppermute(crossed, axis, pairs))  3.47 us
    ppermute x3, starting transfers between devices, relayed(): parts.append(lax.ppermute(crossed, axis, pairs))  3.46 us
    unnamed x15, local copies, waits for them, and re-layouts  3.21 us
    ppermute x1, starting transfers between devices, relayed(): crossed = lax.ppermute(piece, axis, mirror)  2.99 us
    convert_element_type x1, other arithmetic, on_device(): positioned = summed.astype(jnp.bfloat16)  2.34 us
  transfers between devices with their start and end apart: 15, of which 9 were waited for; matrix products, arithmetic and copies ran while one was open for 15% of the time, Pallas kernels for 0%

profile of v16, /device:TPU:0, one launch (start us, length us, event | category | flops | bytes accessed | tf_op | source)
XLA Modules:
  0.0 51.3 jit_solution(3624441731219388550)
XLA Ops:
  0.0 5.0 %collective-permute-start = (bf16[1,16,2,1024]{3,2,1,0:T(2,128)(2,1)}, bf16[1,16,2,1024]{3,2,1,0:T(2,128)(2,1)S(1)}, u32[]{:S(2)}, u32[]{:S(2)}) collective-permute-start(bf16[1,16,2,1024]{3,2,1,0:T(2,128)(2,1)} %param.5), channel_id=1, source_target_pairs={{0,4},{4,8},{8,12},{12,16},{16,20},{20,24},{24,28},{1,5},{5,9},{9,... | collective-permute-start | bytes 196616 | tf_op jit(solution)/shard_map/ppermute | solution.py:22
  5.0 1.3 %collective-permute-start.1 = (bf16[1,16,2,1024]{3,2,1,0:T(2,128)(2,1)}, bf16[1,16,2,1024]{3,2,1,0:T(2,128)(2,1)S(1)}, u32[]{:S(2)}, u32[]{:S(2)}) collective-permute-start(bf16[1,16,2,1024]{3,2,1,0:T(2,128)(2,1)} %param.5), channel_id=1, source_target_pairs={{4,0},{8,4},{12,8},{16,12},{20,16},{24,20},{28,24},{5,1},{9,5},{13... | collective-permute-start | bytes 196616 | tf_op jit(solution)/shard_map/ppermute | solution.py:23
  6.3 1.3 %fusion.44 = (f32[1,1024]{1,0:T(1,128)S(1)}, f32[1,1024]{1,0:T(1,128)S(1)}, f32[1,1024]{1,0:T(1,128)S(1)}, f32[1,1024]{1,0:T(1,128)S(1)}, f32[1,1024]{1,0:T(1,12...) fusion(f32[27,1024]{1,0:T(8,128)} %param.6), kind=kLoop, calls=%fused_computation.111 | loop fusion | bytes 155648 | tf_op jit(solution)/shard_map/slice | solution.py:126
  7.6 1.0 %fusion.45 = (f32[1,1024]{1,0:T(1,128)S(1)}, f32[1,1024]{1,0:T(1,128)S(1)}, f32[1,1024]{1,0:T(1,128)S(1)}, f32[1,1024]{1,0:T(1,128)S(1)}, f32[1,1024]{1,0:T(1,12...) fusion(f32[27,1024]{1,0:T(8,128)} %param.6), kind=kLoop, calls=%fused_computation.112 | loop fusion | bytes 65536 | tf_op jit(solution)/shard_map/slice | solution.py:126
  8.7 0.0 collective-permute-done
  8.8 0.9 %constant_dynamic-update-slice_fusion.1 = bf16[3,16,2,1024]{3,2,1,0:T(2,128)(2,1)S(1)} fusion(bf16[3,16,2,1024]{3,2,1,0:T(2,128)(2,1)S(1)} %constant_dynamic-update-slice_fusion.2, bf16[1,16,2,1024]{3,2,1,0:T(2,128)(2,1)} %param.5), kind=kLoop, calls=%fused_computation.90 | loop fusion | bytes 131072
  9.7 1.7 %collective-permute-done.1 = bf16[1,16,2,1024]{3,2,1,0:T(2,128)(2,1)S(1)} collective-permute-done((bf16[1,16,2,1024]{3,2,1,0:T(2,128)(2,1)}, bf16[1,16,2,1024]{3,2,1,0:T(2,128)(2,1)S(1)}, u32[]{:S(2)}, u32[]{:S(2)}) %collective-permute-start.1) | collective-permute-done | bytes 65568 | tf_op jit(solution)/shard_map/ppermute | solution.py:23
  11.4 0.1 constant_dynamic-update-slice_fusion
  11.4 0.1 collective-permute-start.2
  11.5 1.6 %collective-permute-start.3 = (bf16[3,16,2,1024]{3,2,1,0:T(2,128)(2,1)S(1)}, bf16[3,16,2,1024]{3,2,1,0:T(2,128)(2,1)S(1)}, u32[]{:S(2)}, u32[]{:S(2)}) collective-permute-start(bf16[3,16,2,1024]{3,2,1,0:T(2,128)(2,1)S(1)} %constant_dynamic-update-slice_fusion), channel_id=1, source_target_pairs={{0,2},{1,3},{2,0},{3,1},{4,6},{5,7},{6,4},{7,5},{8,10},{9,11},{10,... | collective-permute-start | bytes 589832 | tf_op jit(solution)/shard_map/ppermute | solution.py:68
  13.1 0.1 broadcast_in_dim.27
  13.2 0.0 copy-start.2
  13.2 0.0 collective-permute-done.2
  13.3 5.5 %collective-permute-done.3 = bf16[3,16,2,1024]{3,2,1,0:T(2,128)(2,1)S(1)} collective-permute-done((bf16[3,16,2,1024]{3,2,1,0:T(2,128)(2,1)S(1)}, bf16[3,16,2,1024]{3,2,1,0:T(2,128)(2,1)S(1)}, u32[]{:S(2)}, u32[]{:S(2)}) %collective-permute-start.3) | collective-permute-done | bytes 196640 | tf_op jit(solution)/shard_map/ppermute | solution.py:68
  18.8 0.0 collective-permute-start.4
  18.9 1.4 %collective-permute-done.4 = bf16[3,16,2,1024]{3,2,1,0:T(2,128)(2,1)S(1)} collective-permute-done((bf16[3,16,2,1024]{3,2,1,0:T(2,128)(2,1)S(1)}, bf16[3,16,2,1024]{3,2,1,0:T(2,128)(2,1)S(1)}, u32[]{:S(2)}, u32[]{:S(2)}) %collective-permute-start.4) | collective-permute-done | bytes 196640 | tf_op jit(solution)/shard_map/ppermute | solution.py:70
  20.3 0.1 fusion.42
  20.4 2.3 %add_convert_fusion = bf16[1,16,8,1024]{3,1,2,0:T(8,128)(2,1)S(1)} fusion(bf16[1,16,8,1024]{3,1,2,0:T(8,128)(2,1)S(1)} %bitcast.119, bf16[1,16,8,1024]{3,1,2,0:T(8,128)(2,1)S(1)} %bitcast.118, bf16[1,16,8,1024]{3,1,2,0:T(8,128)(2,1)S(1)} %bitcast.117, bf16[3,16,8,1024]{3,1,2,0:T(8,128)(2,1)S(1)} %bitcast.114, f32[1024]{0:T(1024)S(1)} %bitcast.153, ...), kind=kLoop, calls=%fused_computation.77 | loop fusion | flops 10878976 | bytes 1949696 | tf_op jit(solution)/shard_map/convert_element_type | solution.py:133
  22.8 0.3 copy.38
  23.0 0.1 reshape.250
  23.2 0.7 %convolution_convert_fusion = bf16[128,768]{1,0:T(8,128)(2,1)S(1)} fusion(bf16[128,1024]{1,0:T(8,128)(2,1)S(1)} %reshape.250, bf16[768,1024]{1,0:T(8,128)(2,1)S(1)} %copy-done), kind=kOutput, calls=%fused_computation.26 | convolution fusion | flops 201424896 | bytes 2031616 | tf_op jit(solution)/shard_map/dot_general | solution.py:104
  23.8 0.2 copy.24
  24.0 3.0 %collective-permute-start.5 = (bf16[128,4,2,64]{0,3,1,2:T(8,128)(2,1)S(1)}, bf16[128,4,2,64]{0,3,1,2:T(8,128)(2,1)S(1)}, u32[]{:S(2)}, u32[]{:S(2)}) collective-permute-start(bf16[128,4,2,64]{0,3,1,2:T(8,128)(2,1)S(1)} %get-tuple-element.56), channel_id=1, source_target_pairs={{0,16},{4,20},{8,24},{12,28},{16,0},{20,4},{24,8},{28,12},{1,17},{... | collective-permute-start | bytes 393224 | tf_op jit(solution)/shard_map/ppermute | solution.py:43
  27.0 2.1 %collective-permute-start.6 = (bf16[128,4,2,64]{0,3,1,2:T(8,128)(2,1)S(1)}, bf16[128,4,2,64]{0,3,1,2:T(8,128)(2,1)}, u32[]{:S(2)}, u32[]{:S(2)}) collective-permute-start(bf16[128,4,2,64]{0,3,1,2:T(8,128)(2,1)S(1)} %get-tuple-element.56), channel_id=1, source_target_pairs={{0,4},{4,8},{8,12},{12,0},{16,20},{20,24},{24,28},{28,16},{1,5},{5... | collective-permute-start | bytes 393224 | tf_op jit(solution)/shard_map/ppermute | solution.py:47
  29.1 0.1 collective-permute-start.8
  29.2 2.3 %collective-permute-start.10 = (bf16[128,4,2,64]{0,3,1,2:T(8,128)(2,1)S(1)}, bf16[128,4,2,64]{0,3,1,2:T(8,128)(2,1)S(1)}, u32[]{:S(2)}, u32[]{:S(2)}) collective-permute-start(bf16[128,4,2,64]{0,3,1,2:T(8,128)(2,1)S(1)} %get-tuple-element.56), channel_id=1, source_target_pairs={{0,12},{4,0},{8,4},{12,8},{16,28},{20,16},{24,20},{28,24},{1,13},{... | collective-permute-start | bytes 393224 | tf_op jit(solution)/shard_map/ppermute | solution.py:47
  31.5 0.1 reshape_squeeze.2
  31.6 0.3 constant_dynamic-slice_fusion.2
  31.9 0.1 copy.26
  32.0 0.1 copy.25
  32.2 1.6 %collective-permute-done.5 = bf16[128,4,2,64]{0,3,1,2:T(8,128)(2,1)S(1)} collective-permute-done((bf16[128,4,2,64]{0,3,1,2:T(8,128)(2,1)S(1)}, bf16[128,4,2,64]{0,3,1,2:T(8,128)(2,1)S(1)}, u32[]{:S(2)}, u32[]{:S(2)}) %collective-permute-start.5) | collective-permute-done | bytes 131104 | tf_op jit(solution)/shard_map/ppermute | solution.py:43
  33.7 2.1 %collective-permute-start.7 = (bf16[128,4,2,64]{0,3,1,2:T(8,128)(2,1)S(1)}, bf16[128,4,2,64]{0,3,1,2:T(8,128)(2,1)S(1)}, u32[]{:S(2)}, u32[]{:S(2)}) collective-permute-start(bf16[128,4,2,64]{0,3,1,2:T(8,128)(2,1)S(1)} %collective-permute-done.5), channel_id=1, source_target_pairs={{0,4},{4,8},{8,12},{12,0},{16,20},{20,24},{24,28},{28,16},{1,5},{5... | collective-permute-start | bytes 393224 | tf_op jit(solution)/shard_map/ppermute | solution.py:48
  35.9 0.0 collective-permute-start.9
  35.9 0.2 collective-permute-done.6
  36.1 1.3 %collective-permute-start.11 = (bf16[128,4,2,64]{0,3,1,2:T(8,128)(2,1)S(1)}, bf16[128,4,2,64]{0,3,1,2:T(8,128)(2,1)S(1)}, u32[]{:S(2)}, u32[]{:S(2)}) collective-permute-start(bf16[128,4,2,64]{0,3,1,2:T(8,128)(2,1)S(1)} %collective-permute-done.5), channel_id=1, source_target_pairs={{0,12},{4,0},{8,4},{12,8},{16,28},{20,16},{24,20},{28,24},{1,13},{... | collective-permute-start | bytes 393224 | tf_op jit(solution)/shard_map/ppermute | solution.py:48
  37.4 0.9 %constant_dynamic-update-slice_fusion.8 = bf16[1024,4,2,64]{0,3,1,2:T(8,128)(2,1)S(1)} fusion(bf16[1024,4,2,64]{0,3,1,2:T(8,128)(2,1)S(1)} %constant_dynamic-update-slice_fusion.9, bf16[128,4,2,64]{0,3,1,2:T(8,128)(2,1)} %collective-permute-done.6), kind=kLoop, calls=%fused_computation.97 | loop fusion | bytes 262144
  38.4 3.3 %collective-permute-done.7 = bf16[128,4,2,64]{0,3,1,2:T(8,128)(2,1)S(1)} collective-permute-done((bf16[128,4,2,64]{0,3,1,2:T(8,128)(2,1)S(1)}, bf16[128,4,2,64]{0,3,1,2:T(8,128)(2,1)S(1)}, u32[]{:S(2)}, u32[]{:S(2)}) %collective-permute-start.7) | collective-permute-done | bytes 131104 | tf_op jit(solution)/shard_map/ppermute | solution.py:48
  41.7 0.0 collective-permute-done.8
  41.7 0.9 %constant_dynamic-update-slice_fusion.6 = bf16[1024,4,2,64]{0,3,1,2:T(8,128)(2,1)S(1)} fusion(bf16[1024,4,2,64]{0,3,1,2:T(8,128)(2,1)S(1)} %constant_dynamic-update-slice_fusion.7, bf16[128,4,2,64]{0,3,1,2:T(8,128)(2,1)} %collective-permute-done.8), kind=kLoop, calls=%fused_computation.95 | loop fusion | bytes 262144
  42.7 0.0 collective-permute-done.9
  42.8 0.2 collective-permute-done.11
  43.0 0.4 fusion.46
  43.4 0.0 copy-start.1
  43.4 0.3 fusion.6
  43.7 0.4 fusion.5
  44.1 0.1 copy.28
  44.1 0.1 reshape.252
  44.2 0.2 copy-done.1
  44.4 0.2 convolution_convert_fusion.1
  44.7 1.6 %collective-permute-start.13 = (bf16[32,1024]{1,0:T(8,128)(2,1)S(1)}, bf16[32,1024]{1,0:T(8,128)(2,1)S(1)}, u32[]{:S(2)}, u32[]{:S(2)}) collective-permute-start(bf16[32,1024]{1,0:T(8,128)(2,1)S(1)} %get-tuple-element.47), channel_id=1, source_target_pairs={{0,2},{1,3},{2,0},{3,1},{4,6},{5,7},{6,4},{7,5},{8,10},{9,11},{10,... | collective-permute-start | bytes 196616 | tf_op jit(solution)/shard_map/ppermute | solution.py:203
  46.2 0.0 collective-permute-start.14
  46.2 0.4 fusion.47
  46.6 0.3 fusion.8
  46.9 0.4 fusion.4
  47.3 0.1 copy.29
  47.4 0.1 dot_general.39
  47.5 0.2 fusion.37
  47.7 0.7 %collective-permute-start.12 = (f32[32,1024]{1,0:T(8,128)S(1)}, f32[32,1024]{1,0:T(8,128)S(1)}, u32[]{:S(2)}, u32[]{:S(2)}) collective-permute-start(f32[32,1024]{1,0:T(8,128)S(1)} %get-tuple-element.43), channel_id=1, source_target_pairs={{0,1},{1,0},{2,3},{3,2},{4,5},{5,4},{6,7},{7,6},{8,9},{9,8},{10,11... | collective-permute-start | bytes 393224 | tf_op jit(solution)/shard_map/ppermute | solution.py:215
  48.4 0.1 reshape.254
  48.5 0.5 collective-permute-done.13
  49.0 1.4 %collective-permute-done.14 = bf16[32,1024]{1,0:T(8,128)(2,1)S(1)} collective-permute-done((bf16[32,1024]{1,0:T(8,128)(2,1)S(1)}, bf16[32,1024]{1,0:T(8,128)(2,1)S(1)}, u32[]{:S(2)}, u32[]{:S(2)}) %collective-permute-start.14) | collective-permute-done | bytes 65568 | tf_op jit(solution)/shard_map/ppermute | solution.py:204
  50.4 0.1 add.269
  50.5 0.1 reshape.255
  50.6 0.7 %add_convert_fusion.1 = bf16[1,16,2,1024]{3,2,1,0:T(2,128)(2,1)} fusion(f32[1,16,2,1024]{3,2,1,0:T(2,128)S(1)} %add.269, f32[1,16,2,1024]{3,2,1,0:T(2,128)S(1)} %reshape.254, f32[1,16,2,1024]{3,2,1,0:T(2,128)S(1)} %reshape.255), kind=kLoop, calls=%fused_computation.83 | loop fusion | flops 98304 | bytes 458752 | tf_op jit(solution)/shard_map/convert_element_type | solution.py:218
  (24 shorter events, 0.6 us)
Async XLA Ops:
  0.0 23.1 %copy-start = (bf16[768,1024]{1,0:T(8,128)(2,1)S(1)}, bf16[768,1024]{1,0:T(8,128)(2,1)}, u32[]{:S(2)}) copy-start(bf16[768,1024]{1,0:T(8,128)(2,1)} %param.8) | copy-start | bytes 4718596
  0.0 8.7 %collective-permute-start = (bf16[1,16,2,1024]{3,2,1,0:T(2,128)(2,1)}, bf16[1,16,2,1024]{3,2,1,0:T(2,128)(2,1)S(1)}, u32[]{:S(2)}, u32[]{:S(2)}) collective-permute-start(bf16[1,16,2,1024]{3,2,1,0:T(2,128)(2,1)} %param.5), channel_id=1, source_target_pairs={{0,4},{4,8},{8,12},{12,16},{16,20},{20,24},{24,28},{1,5},{5,9},{9,... | collective-permute-start | bytes 196616 | tf_op jit(solution)/shard_map/ppermute | solution.py:22
  5.0 6.4 %collective-permute-start.1 = (bf16[1,16,2,1024]{3,2,1,0:T(2,128)(2,1)}, bf16[1,16,2,1024]{3,2,1,0:T(2,128)(2,1)S(1)}, u32[]{:S(2)}, u32[]{:S(2)}) collective-permute-start(bf16[1,16,2,1024]{3,2,1,0:T(2,128)(2,1)} %param.5), channel_id=1, source_target_pairs={{4,0},{8,4},{12,8},{16,12},{20,16},{24,20},{28,24},{5,1},{9,5},{13... | collective-permute-start | bytes 196616 | tf_op jit(solution)/shard_map/ppermute | solution.py:23
  11.4 1.8 %collective-permute-start.2 = (bf16[3,16,2,1024]{3,2,1,0:T(2,128)(2,1)S(1)}, bf16[3,16,2,1024]{3,2,1,0:T(2,128)(2,1)S(1)}, u32[]{:S(2)}, u32[]{:S(2)}) collective-permute-start(bf16[3,16,2,1024]{3,2,1,0:T(2,128)(2,1)S(1)} %constant_dynamic-update-slice_fusion), channel_id=1, source_target_pairs={{0,1},{1,0},{2,3},{3,2},{4,5},{5,4},{6,7},{7,6},{8,9},{9,8},{10,11... | collective-permute-start | bytes 589832 | tf_op jit(solution)/shard_map/ppermute | solution.py:64
  11.5 7.3 %collective-permute-start.3 = (bf16[3,16,2,1024]{3,2,1,0:T(2,128)(2,1)S(1)}, bf16[3,16,2,1024]{3,2,1,0:T(2,128)(2,1)S(1)}, u32[]{:S(2)}, u32[]{:S(2)}) collective-permute-start(bf16[3,16,2,1024]{3,2,1,0:T(2,128)(2,1)S(1)} %constant_dynamic-update-slice_fusion), channel_id=1, source_target_pairs={{0,2},{1,3},{2,0},{3,1},{4,6},{5,7},{6,4},{7,5},{8,10},{9,11},{10,... | collective-permute-start | bytes 589832 | tf_op jit(solution)/shard_map/ppermute | solution.py:68
  13.2 7.2 %copy-start.2 = (f32[1024]{0:T(1024)S(1)}, f32[1024]{0:T(1024)}, u32[]{:S(2)}) copy-start(f32[1024]{0:T(1024)} %param.7) | copy-start | bytes 12292
  18.8 1.4 %collective-permute-start.4 = (bf16[3,16,2,1024]{3,2,1,0:T(2,128)(2,1)S(1)}, bf16[3,16,2,1024]{3,2,1,0:T(2,128)(2,1)S(1)}, u32[]{:S(2)}, u32[]{:S(2)}) collective-permute-start(bf16[3,16,2,1024]{3,2,1,0:T(2,128)(2,1)S(1)} %collective-permute-done.3), channel_id=1, source_target_pairs={{0,1},{1,0},{2,3},{3,2},{4,5},{5,4},{6,7},{7,6},{8,9},{9,8},{10,11... | collective-permute-start | bytes 589832 | tf_op jit(solution)/shard_map/ppermute | solution.py:70
  24.0 9.7 %collective-permute-start.5 = (bf16[128,4,2,64]{0,3,1,2:T(8,128)(2,1)S(1)}, bf16[128,4,2,64]{0,3,1,2:T(8,128)(2,1)S(1)}, u32[]{:S(2)}, u32[]{:S(2)}) collective-permute-start(bf16[128,4,2,64]{0,3,1,2:T(8,128)(2,1)S(1)} %get-tuple-element.56), channel_id=1, source_target_pairs={{0,16},{4,20},{8,24},{12,28},{16,0},{20,4},{24,8},{28,12},{1,17},{... | collective-permute-start | bytes 393224 | tf_op jit(solution)/shard_map/ppermute | solution.py:43
  27.0 9.1 %collective-permute-start.6 = (bf16[128,4,2,64]{0,3,1,2:T(8,128)(2,1)S(1)}, bf16[128,4,2,64]{0,3,1,2:T(8,128)(2,1)}, u32[]{:S(2)}, u32[]{:S(2)}) collective-permute-start(bf16[128,4,2,64]{0,3,1,2:T(8,128)(2,1)S(1)} %get-tuple-element.56), channel_id=1, source_target_pairs={{0,4},{4,8},{8,12},{12,0},{16,20},{20,24},{24,28},{28,16},{1,5},{5... | collective-permute-start | bytes 393224 | tf_op jit(solution)/shard_map/ppermute | solution.py:47
  29.1 12.6 %collective-permute-start.8 = (bf16[128,4,2,64]{0,3,1,2:T(8,128)(2,1)S(1)}, bf16[128,4,2,64]{0,3,1,2:T(8,128)(2,1)}, u32[]{:S(2)}, u32[]{:S(2)}) collective-permute-start(bf16[128,4,2,64]{0,3,1,2:T(8,128)(2,1)S(1)} %get-tuple-element.56), channel_id=1, source_target_pairs={{0,8},{4,12},{8,0},{12,4},{16,24},{20,28},{24,16},{28,20},{1,9},{5... | collective-permute-start | bytes 393224 | tf_op jit(solution)/shard_map/ppermute | solution.py:47
  29.2 13.5 %collective-permute-start.10 = (bf16[128,4,2,64]{0,3,1,2:T(8,128)(2,1)S(1)}, bf16[128,4,2,64]{0,3,1,2:T(8,128)(2,1)S(1)}, u32[]{:S(2)}, u32[]{:S(2)}) collective-permute-start(bf16[128,4,2,64]{0,3,1,2:T(8,128)(2,1)S(1)} %get-tuple-element.56), channel_id=1, source_target_pairs={{0,12},{4,0},{8,4},{12,8},{16,28},{20,16},{24,20},{28,24},{1,13},{... | collective-permute-start | bytes 393224 | tf_op jit(solution)/shard_map/ppermute | solution.py:47
  33.7 7.9 %collective-permute-start.7 = (bf16[128,4,2,64]{0,3,1,2:T(8,128)(2,1)S(1)}, bf16[128,4,2,64]{0,3,1,2:T(8,128)(2,1)S(1)}, u32[]{:S(2)}, u32[]{:S(2)}) collective-permute-start(bf16[128,4,2,64]{0,3,1,2:T(8,128)(2,1)S(1)} %collective-permute-done.5), channel_id=1, source_target_pairs={{0,4},{4,8},{8,12},{12,0},{16,20},{20,24},{24,28},{28,16},{1,5},{5... | collective-permute-start | bytes 393224 | tf_op jit(solution)/shard_map/ppermute | solution.py:48
  35.9 6.8 %collective-permute-start.9 = (bf16[128,4,2,64]{0,3,1,2:T(8,128)(2,1)S(1)}, bf16[128,4,2,64]{0,3,1,2:T(8,128)(2,1)S(1)}, u32[]{:S(2)}, u32[]{:S(2)}) collective-permute-start(bf16[128,4,2,64]{0,3,1,2:T(8,128)(2,1)S(1)} %collective-permute-done.5), channel_id=1, source_target_pairs={{0,8},{4,12},{8,0},{12,4},{16,24},{20,28},{24,16},{28,20},{1,9},{5... | collective-permute-start | bytes 393224 | tf_op jit(solution)/shard_map/ppermute | solution.py:48
  36.1 6.9 %collective-permute-start.11 = (bf16[128,4,2,64]{0,3,1,2:T(8,128)(2,1)S(1)}, bf16[128,4,2,64]{0,3,1,2:T(8,128)(2,1)S(1)}, u32[]{:S(2)}, u32[]{:S(2)}) collective-permute-start(bf16[128,4,2,64]{0,3,1,2:T(8,128)(2,1)S(1)} %collective-permute-done.5), channel_id=1, source_target_pairs={{0,12},{4,0},{8,4},{12,8},{16,28},{20,16},{24,20},{28,24},{1,13},{... | collective-permute-start | bytes 393224 | tf_op jit(solution)/shard_map/ppermute | solution.py:48
  43.4 1.1 %copy-start.1 = (bf16[256,1024]{1,0:T(8,128)(2,1)S(1)}, bf16[256,1024]{1,0:T(8,128)(2,1)}, u32[]{:S(2)}) copy-start(bf16[256,1024]{1,0:T(8,128)(2,1)} %param.9) | copy-start | bytes 1572868
  44.7 4.3 %collective-permute-start.13 = (bf16[32,1024]{1,0:T(8,128)(2,1)S(1)}, bf16[32,1024]{1,0:T(8,128)(2,1)S(1)}, u32[]{:S(2)}, u32[]{:S(2)}) collective-permute-start(bf16[32,1024]{1,0:T(8,128)(2,1)S(1)} %get-tuple-element.47), channel_id=1, source_target_pairs={{0,2},{1,3},{2,0},{3,1},{4,6},{5,7},{6,4},{7,5},{8,10},{9,11},{10,... | collective-permute-start | bytes 196616 | tf_op jit(solution)/shard_map/ppermute | solution.py:203
  46.2 4.2 %collective-permute-start.14 = (bf16[32,1024]{1,0:T(8,128)(2,1)S(1)}, bf16[32,1024]{1,0:T(8,128)(2,1)S(1)}, u32[]{:S(2)}, u32[]{:S(2)}) collective-permute-start(bf16[32,1024]{1,0:T(8,128)(2,1)S(1)} %get-tuple-element.48), channel_id=1, source_target_pairs={{0,3},{1,2},{2,1},{3,0},{4,7},{5,6},{6,5},{7,4},{8,11},{9,10},{10,... | collective-permute-start | bytes 196616 | tf_op jit(solution)/shard_map/ppermute | solution.py:204
  47.7 2.8 %collective-permute-start.12 = (f32[32,1024]{1,0:T(8,128)S(1)}, f32[32,1024]{1,0:T(8,128)S(1)}, u32[]{:S(2)}, u32[]{:S(2)}) collective-permute-start(f32[32,1024]{1,0:T(8,128)S(1)} %get-tuple-element.43), channel_id=1, source_target_pairs={{0,1},{1,0},{2,3},{3,2},{4,5},{5,4},{6,7},{7,6},{8,9},{9,8},{10,11... | collective-permute-start | bytes 393224 | tf_op jit(solution)/shard_map/ppermute | solution.py:215

commit v17 on v16

--- a/solution.py
+++ b/solution.py
@@ -214,6 +214,7 @@
     for_partner = lax.dynamic_index_in_dim(near_partial, 1 - core, 0, keepdims=False)
     from_partner = lax.ppermute(for_partner, "uly", [(i, i ^ 1) for i in range(groups)])
     near_sum = own.reshape(tokens.shape) + from_partner.reshape(tokens.shape)
+    near_sum = with_layout_constraint(near_sum, Layout(major_to_minor=tuple(range(tokens.ndim))))
     result = near_sum if total is None else near_sum + total
     return result.astype(jnp.bfloat16)
 

time: 51.8 us -> 51.8 us (level)
  no operation moved by 1% of the time
where the time goes in v17:
time: 51.8 us; the launch traced here: 51.3 us
  starting transfers between devices  21.1 us (41%)
  waiting for transfers between devices  15.8 us (31%)
  local copies, waits for them, and re-layouts  7.7 us (15%)
  other arithmetic  3.75 us (7%)
  matrix products  2.5 us (5%)
    ppermute x1, waiting for transfers between devices, gathered_by_chip(): far = lax.ppermute(piece, axis, chip_shift(size, shift))  5.55 us
    ppermute x1, starting transfers between devices, padded_2(): before = lax.ppermute(last, axis, up)  5 us
    ppermute x3, starting transfers between devices, relayed(): parts.append(lax.ppermute(piece, axis, pairs))  4.5 us
    ppermute x3, waiting for transfers between devices, relayed(): parts.append(lax.ppermute(crossed, axis, pairs))  3.47 us
    ppermute x3, starting transfers between devices, relayed(): parts.append(lax.ppermute(crossed, axis, pairs))  3.46 us
    unnamed x15, local copies, waits for them, and re-layouts  3.21 us
    ppermute x1, starting transfers between devices, relayed(): crossed = lax.ppermute(piece, axis, mirror)  2.99 us
    convert_element_type x1, other arithmetic, on_device(): positioned = summed.astype(jnp.bfloat16)  2.34 us
  transfers between devices with their start and end apart: 15, of which 9 were waited for; matrix products, arithmetic and copies ran while one was open for 15% of the time, Pallas kernels for 0%

profile of v17, /device:TPU:0, one launch (start us, length us, event | category | flops | bytes accessed | tf_op | source)
XLA Modules:
  0.0 51.3 jit_solution(3624441731219388550)
XLA Ops:
  0.0 5.0 %collective-permute-start = (bf16[1,16,2,1024]{3,2,1,0:T(2,128)(2,1)}, bf16[1,16,2,1024]{3,2,1,0:T(2,128)(2,1)S(1)}, u32[]{:S(2)}, u32[]{:S(2)}) collective-permute-start(bf16[1,16,2,1024]{3,2,1,0:T(2,128)(2,1)} %param.5), channel_id=1, source_target_pairs={{0,4},{4,8},{8,12},{12,16},{16,20},{20,24},{24,28},{1,5},{5,9},{9,... | collective-permute-start | bytes 196616 | tf_op jit(solution)/shard_map/ppermute | solution.py:22
  5.0 1.3 %collective-permute-start.1 = (bf16[1,16,2,1024]{3,2,1,0:T(2,128)(2,1)}, bf16[1,16,2,1024]{3,2,1,0:T(2,128)(2,1)S(1)}, u32[]{:S(2)}, u32[]{:S(2)}) collective-permute-start(bf16[1,16,2,1024]{3,2,1,0:T(2,128)(2,1)} %param.5), channel_id=1, source_target_pairs={{4,0},{8,4},{12,8},{16,12},{20,16},{24,20},{28,24},{5,1},{9,5},{13... | collective-permute-start | bytes 196616 | tf_op jit(solution)/shard_map/ppermute | solution.py:23
  6.3 1.3 %fusion.44 = (f32[1,1024]{1,0:T(1,128)S(1)}, f32[1,1024]{1,0:T(1,128)S(1)}, f32[1,1024]{1,0:T(1,128)S(1)}, f32[1,1024]{1,0:T(1,128)S(1)}, f32[1,1024]{1,0:T(1,12...) fusion(f32[27,1024]{1,0:T(8,128)} %param.6), kind=kLoop, calls=%fused_computation.111 | loop fusion | bytes 155648 | tf_op jit(solution)/shard_map/slice | solution.py:126
  7.6 1.0 %fusion.45 = (f32[1,1024]{1,0:T(1,128)S(1)}, f32[1,1024]{1,0:T(1,128)S(1)}, f32[1,1024]{1,0:T(1,128)S(1)}, f32[1,1024]{1,0:T(1,128)S(1)}, f32[1,1024]{1,0:T(1,12...) fusion(f32[27,1024]{1,0:T(8,128)} %param.6), kind=kLoop, calls=%fused_computation.112 | loop fusion | bytes 65536 | tf_op jit(solution)/shard_map/slice | solution.py:126
  8.7 0.0 collective-permute-done
  8.8 0.9 %constant_dynamic-update-slice_fusion.1 = bf16[3,16,2,1024]{3,2,1,0:T(2,128)(2,1)S(1)} fusion(bf16[3,16,2,1024]{3,2,1,0:T(2,128)(2,1)S(1)} %constant_dynamic-update-slice_fusion.2, bf16[1,16,2,1024]{3,2,1,0:T(2,128)(2,1)} %param.5), kind=kLoop, calls=%fused_computation.90 | loop fusion | bytes 131072
  9.7 1.7 %collective-permute-done.1 = bf16[1,16,2,1024]{3,2,1,0:T(2,128)(2,1)S(1)} collective-permute-done((bf16[1,16,2,1024]{3,2,1,0:T(2,128)(2,1)}, bf16[1,16,2,1024]{3,2,1,0:T(2,128)(2,1)S(1)}, u32[]{:S(2)}, u32[]{:S(2)}) %collective-permute-start.1) | collective-permute-done | bytes 65568 | tf_op jit(solution)/shard_map/ppermute | solution.py:23
  11.4 0.1 constant_dynamic-update-slice_fusion
  11.4 0.1 collective-permute-start.2
  11.5 1.6 %collective-permute-start.3 = (bf16[3,16,2,1024]{3,2,1,0:T(2,128)(2,1)S(1)}, bf16[3,16,2,1024]{3,2,1,0:T(2,128)(2,1)S(1)}, u32[]{:S(2)}, u32[]{:S(2)}) collective-permute-start(bf16[3,16,2,1024]{3,2,1,0:T(2,128)(2,1)S(1)} %constant_dynamic-update-slice_fusion), channel_id=1, source_target_pairs={{0,2},{1,3},{2,0},{3,1},{4,6},{5,7},{6,4},{7,5},{8,10},{9,11},{10,... | collective-permute-start | bytes 589832 | tf_op jit(solution)/shard_map/ppermute | solution.py:68
  13.1 0.1 broadcast_in_dim.27
  13.2 0.0 copy-start.2
  13.2 0.0 collective-permute-done.2
  13.3 5.5 %collective-permute-done.3 = bf16[3,16,2,1024]{3,2,1,0:T(2,128)(2,1)S(1)} collective-permute-done((bf16[3,16,2,1024]{3,2,1,0:T(2,128)(2,1)S(1)}, bf16[3,16,2,1024]{3,2,1,0:T(2,128)(2,1)S(1)}, u32[]{:S(2)}, u32[]{:S(2)}) %collective-permute-start.3) | collective-permute-done | bytes 196640 | tf_op jit(solution)/shard_map/ppermute | solution.py:68
  18.8 0.0 collective-permute-start.4
  18.9 1.4 %collective-permute-done.4 = bf16[3,16,2,1024]{3,2,1,0:T(2,128)(2,1)S(1)} collective-permute-done((bf16[3,16,2,1024]{3,2,1,0:T(2,128)(2,1)S(1)}, bf16[3,16,2,1024]{3,2,1,0:T(2,128)(2,1)S(1)}, u32[]{:S(2)}, u32[]{:S(2)}) %collective-permute-start.4) | collective-permute-done | bytes 196640 | tf_op jit(solution)/shard_map/ppermute | solution.py:70
  20.3 0.1 fusion.42
  20.4 2.3 %add_convert_fusion = bf16[1,16,8,1024]{3,1,2,0:T(8,128)(2,1)S(1)} fusion(bf16[1,16,8,1024]{3,1,2,0:T(8,128)(2,1)S(1)} %bitcast.119, bf16[1,16,8,1024]{3,1,2,0:T(8,128)(2,1)S(1)} %bitcast.118, bf16[1,16,8,1024]{3,1,2,0:T(8,128)(2,1)S(1)} %bitcast.117, bf16[3,16,8,1024]{3,1,2,0:T(8,128)(2,1)S(1)} %bitcast.114, f32[1024]{0:T(1024)S(1)} %bitcast.153, ...), kind=kLoop, calls=%fused_computation.77 | loop fusion | flops 10878976 | bytes 1949696 | tf_op jit(solution)/shard_map/convert_element_type | solution.py:133
  22.8 0.3 copy.38
  23.0 0.1 reshape.242
  23.2 0.7 %convolution_convert_fusion = bf16[128,768]{1,0:T(8,128)(2,1)S(1)} fusion(bf16[128,1024]{1,0:T(8,128)(2,1)S(1)} %reshape.242, bf16[768,1024]{1,0:T(8,128)(2,1)S(1)} %copy-done), kind=kOutput, calls=%fused_computation.26 | convolution fusion | flops 201424896 | bytes 2031616 | tf_op jit(solution)/shard_map/dot_general | solution.py:104
  23.8 0.2 copy.24
  24.0 3.0 %collective-permute-start.5 = (bf16[128,4,2,64]{0,3,1,2:T(8,128)(2,1)S(1)}, bf16[128,4,2,64]{0,3,1,2:T(8,128)(2,1)S(1)}, u32[]{:S(2)}, u32[]{:S(2)}) collective-permute-start(bf16[128,4,2,64]{0,3,1,2:T(8,128)(2,1)S(1)} %get-tuple-element.56), channel_id=1, source_target_pairs={{0,16},{4,20},{8,24},{12,28},{16,0},{20,4},{24,8},{28,12},{1,17},{... | collective-permute-start | bytes 393224 | tf_op jit(solution)/shard_map/ppermute | solution.py:43
  27.0 2.1 %collective-permute-start.6 = (bf16[128,4,2,64]{0,3,1,2:T(8,128)(2,1)S(1)}, bf16[128,4,2,64]{0,3,1,2:T(8,128)(2,1)}, u32[]{:S(2)}, u32[]{:S(2)}) collective-permute-start(bf16[128,4,2,64]{0,3,1,2:T(8,128)(2,1)S(1)} %get-tuple-element.56), channel_id=1, source_target_pairs={{0,4},{4,8},{8,12},{12,0},{16,20},{20,24},{24,28},{28,16},{1,5},{5... | collective-permute-start | bytes 393224 | tf_op jit(solution)/shard_map/ppermute | solution.py:47
  29.1 0.1 collective-permute-start.8
  29.2 2.3 %collective-permute-start.10 = (bf16[128,4,2,64]{0,3,1,2:T(8,128)(2,1)S(1)}, bf16[128,4,2,64]{0,3,1,2:T(8,128)(2,1)S(1)}, u32[]{:S(2)}, u32[]{:S(2)}) collective-permute-start(bf16[128,4,2,64]{0,3,1,2:T(8,128)(2,1)S(1)} %get-tuple-element.56), channel_id=1, source_target_pairs={{0,12},{4,0},{8,4},{12,8},{16,28},{20,16},{24,20},{28,24},{1,13},{... | collective-permute-start | bytes 393224 | tf_op jit(solution)/shard_map/ppermute | solution.py:47
  31.5 0.1 reshape_squeeze.2
  31.6 0.3 constant_dynamic-slice_fusion.2
  31.9 0.1 copy.26
  32.0 0.1 copy.25
  32.2 1.6 %collective-permute-done.5 = bf16[128,4,2,64]{0,3,1,2:T(8,128)(2,1)S(1)} collective-permute-done((bf16[128,4,2,64]{0,3,1,2:T(8,128)(2,1)S(1)}, bf16[128,4,2,64]{0,3,1,2:T(8,128)(2,1)S(1)}, u32[]{:S(2)}, u32[]{:S(2)}) %collective-permute-start.5) | collective-permute-done | bytes 131104 | tf_op jit(solution)/shard_map/ppermute | solution.py:43
  33.7 2.1 %collective-permute-start.7 = (bf16[128,4,2,64]{0,3,1,2:T(8,128)(2,1)S(1)}, bf16[128,4,2,64]{0,3,1,2:T(8,128)(2,1)S(1)}, u32[]{:S(2)}, u32[]{:S(2)}) collective-permute-start(bf16[128,4,2,64]{0,3,1,2:T(8,128)(2,1)S(1)} %collective-permute-done.5), channel_id=1, source_target_pairs={{0,4},{4,8},{8,12},{12,0},{16,20},{20,24},{24,28},{28,16},{1,5},{5... | collective-permute-start | bytes 393224 | tf_op jit(solution)/shard_map/ppermute | solution.py:48
  35.9 0.0 collective-permute-start.9
  35.9 0.2 collective-permute-done.6
  36.1 1.3 %collective-permute-start.11 = (bf16[128,4,2,64]{0,3,1,2:T(8,128)(2,1)S(1)}, bf16[128,4,2,64]{0,3,1,2:T(8,128)(2,1)S(1)}, u32[]{:S(2)}, u32[]{:S(2)}) collective-permute-start(bf16[128,4,2,64]{0,3,1,2:T(8,128)(2,1)S(1)} %collective-permute-done.5), channel_id=1, source_target_pairs={{0,12},{4,0},{8,4},{12,8},{16,28},{20,16},{24,20},{28,24},{1,13},{... | collective-permute-start | bytes 393224 | tf_op jit(solution)/shard_map/ppermute | solution.py:48
  37.4 0.9 %constant_dynamic-update-slice_fusion.8 = bf16[1024,4,2,64]{0,3,1,2:T(8,128)(2,1)S(1)} fusion(bf16[1024,4,2,64]{0,3,1,2:T(8,128)(2,1)S(1)} %constant_dynamic-update-slice_fusion.9, bf16[128,4,2,64]{0,3,1,2:T(8,128)(2,1)} %collective-permute-done.6), kind=kLoop, calls=%fused_computation.97 | loop fusion | bytes 262144
  38.4 3.3 %collective-permute-done.7 = bf16[128,4,2,64]{0,3,1,2:T(8,128)(2,1)S(1)} collective-permute-done((bf16[128,4,2,64]{0,3,1,2:T(8,128)(2,1)S(1)}, bf16[128,4,2,64]{0,3,1,2:T(8,128)(2,1)S(1)}, u32[]{:S(2)}, u32[]{:S(2)}) %collective-permute-start.7) | collective-permute-done | bytes 131104 | tf_op jit(solution)/shard_map/ppermute | solution.py:48
  41.7 0.0 collective-permute-done.8
  41.7 0.9 %constant_dynamic-update-slice_fusion.6 = bf16[1024,4,2,64]{0,3,1,2:T(8,128)(2,1)S(1)} fusion(bf16[1024,4,2,64]{0,3,1,2:T(8,128)(2,1)S(1)} %constant_dynamic-update-slice_fusion.7, bf16[128,4,2,64]{0,3,1,2:T(8,128)(2,1)} %collective-permute-done.8), kind=kLoop, calls=%fused_computation.95 | loop fusion | bytes 262144
  42.7 0.0 collective-permute-done.9
  42.8 0.2 collective-permute-done.11
  43.0 0.4 fusion.46
  43.4 0.0 copy-start.1
  43.4 0.3 fusion.6
  43.7 0.4 fusion.5
  44.1 0.1 copy.28
  44.1 0.1 reshape.244
  44.2 0.2 copy-done.1
  44.4 0.2 convolution_convert_fusion.1
  44.7 1.6 %collective-permute-start.13 = (bf16[32,1024]{1,0:T(8,128)(2,1)S(1)}, bf16[32,1024]{1,0:T(8,128)(2,1)S(1)}, u32[]{:S(2)}, u32[]{:S(2)}) collective-permute-start(bf16[32,1024]{1,0:T(8,128)(2,1)S(1)} %get-tuple-element.47), channel_id=1, source_target_pairs={{0,2},{1,3},{2,0},{3,1},{4,6},{5,7},{6,4},{7,5},{8,10},{9,11},{10,... | collective-permute-start | bytes 196616 | tf_op jit(solution)/shard_map/ppermute | solution.py:203
  46.2 0.0 collective-permute-start.14
  46.2 0.4 fusion.47
  46.6 0.3 fusion.8
  46.9 0.4 fusion.4
  47.3 0.1 copy.29
  47.4 0.1 dot_general.39
  47.5 0.2 fusion.37
  47.7 0.7 %collective-permute-start.12 = (f32[32,1024]{1,0:T(8,128)S(1)}, f32[32,1024]{1,0:T(8,128)S(1)}, u32[]{:S(2)}, u32[]{:S(2)}) collective-permute-start(f32[32,1024]{1,0:T(8,128)S(1)} %get-tuple-element.43), channel_id=1, source_target_pairs={{0,1},{1,0},{2,3},{3,2},{4,5},{5,4},{6,7},{7,6},{8,9},{9,8},{10,11... | collective-permute-start | bytes 393224 | tf_op jit(solution)/shard_map/ppermute | solution.py:215
  48.4 0.1 reshape.246
  48.5 0.5 collective-permute-done.13
  49.0 1.4 %collective-permute-done.14 = bf16[32,1024]{1,0:T(8,128)(2,1)S(1)} collective-permute-done((bf16[32,1024]{1,0:T(8,128)(2,1)S(1)}, bf16[32,1024]{1,0:T(8,128)(2,1)S(1)}, u32[]{:S(2)}, u32[]{:S(2)}) %collective-permute-start.14) | collective-permute-done | bytes 65568 | tf_op jit(solution)/shard_map/ppermute | solution.py:204
  50.4 0.1 add.261
  50.5 0.1 reshape.247
  50.6 0.7 %add_convert_fusion.1 = bf16[1,16,2,1024]{3,2,1,0:T(2,128)(2,1)} fusion(f32[1,16,2,1024]{3,2,1,0:T(2,128)S(1)} %add.261, f32[1,16,2,1024]{3,2,1,0:T(2,128)S(1)} %reshape.246, f32[1,16,2,1024]{3,2,1,0:T(2,128)S(1)} %reshape.247), kind=kLoop, calls=%fused_computation.83 | loop fusion | flops 98304 | bytes 458752 | tf_op jit(solution)/shard_map/convert_element_type | solution.py:219
  (24 shorter events, 0.6 us)
Async XLA Ops:
  0.0 23.1 %copy-start = (bf16[768,1024]{1,0:T(8,128)(2,1)S(1)}, bf16[768,1024]{1,0:T(8,128)(2,1)}, u32[]{:S(2)}) copy-start(bf16[768,1024]{1,0:T(8,128)(2,1)} %param.8) | copy-start | bytes 4718596
  0.0 8.7 %collective-permute-start = (bf16[1,16,2,1024]{3,2,1,0:T(2,128)(2,1)}, bf16[1,16,2,1024]{3,2,1,0:T(2,128)(2,1)S(1)}, u32[]{:S(2)}, u32[]{:S(2)}) collective-permute-start(bf16[1,16,2,1024]{3,2,1,0:T(2,128)(2,1)} %param.5), channel_id=1, source_target_pairs={{0,4},{4,8},{8,12},{12,16},{16,20},{20,24},{24,28},{1,5},{5,9},{9,... | collective-permute-start | bytes 196616 | tf_op jit(solution)/shard_map/ppermute | solution.py:22
  5.0 6.4 %collective-permute-start.1 = (bf16[1,16,2,1024]{3,2,1,0:T(2,128)(2,1)}, bf16[1,16,2,1024]{3,2,1,0:T(2,128)(2,1)S(1)}, u32[]{:S(2)}, u32[]{:S(2)}) collective-permute-start(bf16[1,16,2,1024]{3,2,1,0:T(2,128)(2,1)} %param.5), channel_id=1, source_target_pairs={{4,0},{8,4},{12,8},{16,12},{20,16},{24,20},{28,24},{5,1},{9,5},{13... | collective-permute-start | bytes 196616 | tf_op jit(solution)/shard_map/ppermute | solution.py:23
  11.4 1.8 %collective-permute-start.2 = (bf16[3,16,2,1024]{3,2,1,0:T(2,128)(2,1)S(1)}, bf16[3,16,2,1024]{3,2,1,0:T(2,128)(2,1)S(1)}, u32[]{:S(2)}, u32[]{:S(2)}) collective-permute-start(bf16[3,16,2,1024]{3,2,1,0:T(2,128)(2,1)S(1)} %constant_dynamic-update-slice_fusion), channel_id=1, source_target_pairs={{0,1},{1,0},{2,3},{3,2},{4,5},{5,4},{6,7},{7,6},{8,9},{9,8},{10,11... | collective-permute-start | bytes 589832 | tf_op jit(solution)/shard_map/ppermute | solution.py:64
  11.5 7.3 %collective-permute-start.3 = (bf16[3,16,2,1024]{3,2,1,0:T(2,128)(2,1)S(1)}, bf16[3,16,2,1024]{3,2,1,0:T(2,128)(2,1)S(1)}, u32[]{:S(2)}, u32[]{:S(2)}) collective-permute-start(bf16[3,16,2,1024]{3,2,1,0:T(2,128)(2,1)S(1)} %constant_dynamic-update-slice_fusion), channel_id=1, source_target_pairs={{0,2},{1,3},{2,0},{3,1},{4,6},{5,7},{6,4},{7,5},{8,10},{9,11},{10,... | collective-permute-start | bytes 589832 | tf_op jit(solution)/shard_map/ppermute | solution.py:68
  13.2 7.2 %copy-start.2 = (f32[1024]{0:T(1024)S(1)}, f32[1024]{0:T(1024)}, u32[]{:S(2)}) copy-start(f32[1024]{0:T(1024)} %param.7) | copy-start | bytes 12292
  18.8 1.4 %collective-permute-start.4 = (bf16[3,16,2,1024]{3,2,1,0:T(2,128)(2,1)S(1)}, bf16[3,16,2,1024]{3,2,1,0:T(2,128)(2,1)S(1)}, u32[]{:S(2)}, u32[]{:S(2)}) collective-permute-start(bf16[3,16,2,1024]{3,2,1,0:T(2,128)(2,1)S(1)} %collective-permute-done.3), channel_id=1, source_target_pairs={{0,1},{1,0},{2,3},{3,2},{4,5},{5,4},{6,7},{7,6},{8,9},{9,8},{10,11... | collective-permute-start | bytes 589832 | tf_op jit(solution)/shard_map/ppermute | solution.py:70
  24.0 9.7 %collective-permute-start.5 = (bf16[128,4,2,64]{0,3,1,2:T(8,128)(2,1)S(1)}, bf16[128,4,2,64]{0,3,1,2:T(8,128)(2,1)S(1)}, u32[]{:S(2)}, u32[]{:S(2)}) collective-permute-start(bf16[128,4,2,64]{0,3,1,2:T(8,128)(2,1)S(1)} %get-tuple-element.56), channel_id=1, source_target_pairs={{0,16},{4,20},{8,24},{12,28},{16,0},{20,4},{24,8},{28,12},{1,17},{... | collective-permute-start | bytes 393224 | tf_op jit(solution)/shard_map/ppermute | solution.py:43
  27.0 9.1 %collective-permute-start.6 = (bf16[128,4,2,64]{0,3,1,2:T(8,128)(2,1)S(1)}, bf16[128,4,2,64]{0,3,1,2:T(8,128)(2,1)}, u32[]{:S(2)}, u32[]{:S(2)}) collective-permute-start(bf16[128,4,2,64]{0,3,1,2:T(8,128)(2,1)S(1)} %get-tuple-element.56), channel_id=1, source_target_pairs={{0,4},{4,8},{8,12},{12,0},{16,20},{20,24},{24,28},{28,16},{1,5},{5... | collective-permute-start | bytes 393224 | tf_op jit(solution)/shard_map/ppermute | solution.py:47
  29.1 12.6 %collective-permute-start.8 = (bf16[128,4,2,64]{0,3,1,2:T(8,128)(2,1)S(1)}, bf16[128,4,2,64]{0,3,1,2:T(8,128)(2,1)}, u32[]{:S(2)}, u32[]{:S(2)}) collective-permute-start(bf16[128,4,2,64]{0,3,1,2:T(8,128)(2,1)S(1)} %get-tuple-element.56), channel_id=1, source_target_pairs={{0,8},{4,12},{8,0},{12,4},{16,24},{20,28},{24,16},{28,20},{1,9},{5... | collective-permute-start | bytes 393224 | tf_op jit(solution)/shard_map/ppermute | solution.py:47
  29.2 13.5 %collective-permute-start.10 = (bf16[128,4,2,64]{0,3,1,2:T(8,128)(2,1)S(1)}, bf16[128,4,2,64]{0,3,1,2:T(8,128)(2,1)S(1)}, u32[]{:S(2)}, u32[]{:S(2)}) collective-permute-start(bf16[128,4,2,64]{0,3,1,2:T(8,128)(2,1)S(1)} %get-tuple-element.56), channel_id=1, source_target_pairs={{0,12},{4,0},{8,4},{12,8},{16,28},{20,16},{24,20},{28,24},{1,13},{... | collective-permute-start | bytes 393224 | tf_op jit(solution)/shard_map/ppermute | solution.py:47
  33.7 7.9 %collective-permute-start.7 = (bf16[128,4,2,64]{0,3,1,2:T(8,128)(2,1)S(1)}, bf16[128,4,2,64]{0,3,1,2:T(8,128)(2,1)S(1)}, u32[]{:S(2)}, u32[]{:S(2)}) collective-permute-start(bf16[128,4,2,64]{0,3,1,2:T(8,128)(2,1)S(1)} %collective-permute-done.5), channel_id=1, source_target_pairs={{0,4},{4,8},{8,12},{12,0},{16,20},{20,24},{24,28},{28,16},{1,5},{5... | collective-permute-start | bytes 393224 | tf_op jit(solution)/shard_map/ppermute | solution.py:48
  35.9 6.8 %collective-permute-start.9 = (bf16[128,4,2,64]{0,3,1,2:T(8,128)(2,1)S(1)}, bf16[128,4,2,64]{0,3,1,2:T(8,128)(2,1)S(1)}, u32[]{:S(2)}, u32[]{:S(2)}) collective-permute-start(bf16[128,4,2,64]{0,3,1,2:T(8,128)(2,1)S(1)} %collective-permute-done.5), channel_id=1, source_target_pairs={{0,8},{4,12},{8,0},{12,4},{16,24},{20,28},{24,16},{28,20},{1,9},{5... | collective-permute-start | bytes 393224 | tf_op jit(solution)/shard_map/ppermute | solution.py:48
  36.1 6.9 %collective-permute-start.11 = (bf16[128,4,2,64]{0,3,1,2:T(8,128)(2,1)S(1)}, bf16[128,4,2,64]{0,3,1,2:T(8,128)(2,1)S(1)}, u32[]{:S(2)}, u32[]{:S(2)}) collective-permute-start(bf16[128,4,2,64]{0,3,1,2:T(8,128)(2,1)S(1)} %collective-permute-done.5), channel_id=1, source_target_pairs={{0,12},{4,0},{8,4},{12,8},{16,28},{20,16},{24,20},{28,24},{1,13},{... | collective-permute-start | bytes 393224 | tf_op jit(solution)/shard_map/ppermute | solution.py:48
  43.4 1.1 %copy-start.1 = (bf16[256,1024]{1,0:T(8,128)(2,1)S(1)}, bf16[256,1024]{1,0:T(8,128)(2,1)}, u32[]{:S(2)}) copy-start(bf16[256,1024]{1,0:T(8,128)(2,1)} %param.9) | copy-start | bytes 1572868
  44.7 4.3 %collective-permute-start.13 = (bf16[32,1024]{1,0:T(8,128)(2,1)S(1)}, bf16[32,1024]{1,0:T(8,128)(2,1)S(1)}, u32[]{:S(2)}, u32[]{:S(2)}) collective-permute-start(bf16[32,1024]{1,0:T(8,128)(2,1)S(1)} %get-tuple-element.47), channel_id=1, source_target_pairs={{0,2},{1,3},{2,0},{3,1},{4,6},{5,7},{6,4},{7,5},{8,10},{9,11},{10,... | collective-permute-start | bytes 196616 | tf_op jit(solution)/shard_map/ppermute | solution.py:203
  46.2 4.2 %collective-permute-start.14 = (bf16[32,1024]{1,0:T(8,128)(2,1)S(1)}, bf16[32,1024]{1,0:T(8,128)(2,1)S(1)}, u32[]{:S(2)}, u32[]{:S(2)}) collective-permute-start(bf16[32,1024]{1,0:T(8,128)(2,1)S(1)} %get-tuple-element.48), channel_id=1, source_target_pairs={{0,3},{1,2},{2,1},{3,0},{4,7},{5,6},{6,5},{7,4},{8,11},{9,10},{10,... | collective-permute-start | bytes 196616 | tf_op jit(solution)/shard_map/ppermute | solution.py:204
  47.7 2.8 %collective-permute-start.12 = (f32[32,1024]{1,0:T(8,128)S(1)}, f32[32,1024]{1,0:T(8,128)S(1)}, u32[]{:S(2)}, u32[]{:S(2)}) collective-permute-start(f32[32,1024]{1,0:T(8,128)S(1)} %get-tuple-element.43), channel_id=1, source_target_pairs={{0,1},{1,0},{2,3},{3,2},{4,5},{5,4},{6,7},{7,6},{8,9},{9,8},{10,11... | collective-permute-start | bytes 393224 | tf_op jit(solution)/shard_map/ppermute | solution.py:215

commit v18 on v16

--- a/solution.py
+++ b/solution.py
@@ -140,6 +140,7 @@
     )
     slab_tok = slab_rows.shape[0]
     projected = times_transposed(slab_rows, qkv_weight).astype(jnp.bfloat16)
+    projected = with_layout_constraint(projected, Layout(major_to_minor=(1, 0)))
     split_heads = projected.reshape(slab_tok, heads_here, 3, HS)
     queries = split_heads[:, :, 0]
     key_value = relayed(split_heads[:, :, 1:], "blk")

time: 51.8 us -> 51.6 us (level)
    unnamed x15 -> x17, local copies, waits for them, and re-layouts: 3.21 us -> 3.43 us
where the time goes in v18:
time: 51.6 us; the launch traced here: 51.1 us
  starting transfers between devices  21.1 us (41%)
  waiting for transfers between devices  15.8 us (31%)
  local copies, waits for them, and re-layouts  7.53 us (15%)
  other arithmetic  3.75 us (7%)
  matrix products  2.43 us (5%)
    ppermute x1, waiting for transfers between devices, gathered_by_chip(): far = lax.ppermute(piece, axis, chip_shift(size, shift))  5.55 us
    ppermute x1, starting transfers between devices, padded_2(): before = lax.ppermute(last, axis, up)  5 us
    ppermute x3, starting transfers between devices, relayed(): parts.append(lax.ppermute(piece, axis, pairs))  4.5 us
    ppermute x3, waiting for transfers between devices, relayed(): parts.append(lax.ppermute(crossed, axis, pairs))  3.47 us
    ppermute x3, starting transfers between devices, relayed(): parts.append(lax.ppermute(crossed, axis, pairs))  3.46 us
    unnamed x17, local copies, waits for them, and re-layouts  3.43 us
    ppermute x1, starting transfers between devices, relayed(): crossed = lax.ppermute(piece, axis, mirror)  2.98 us
    convert_element_type x1, other arithmetic, on_device(): positioned = summed.astype(jnp.bfloat16)  2.34 us
  transfers between devices with their start and end apart: 15, of which 9 were waited for; matrix products, arithmetic and copies ran while one was open for 15% of the time, Pallas kernels for 0%

profile of v18, /device:TPU:0, one launch (start us, length us, event | category | flops | bytes accessed | tf_op | source)
XLA Modules:
  0.0 51.1 jit_solution(14248030045804804168)
XLA Ops:
  0.0 5.0 %collective-permute-start = (bf16[1,16,2,1024]{3,2,1,0:T(2,128)(2,1)}, bf16[1,16,2,1024]{3,2,1,0:T(2,128)(2,1)S(1)}, u32[]{:S(2)}, u32[]{:S(2)}) collective-permute-start(bf16[1,16,2,1024]{3,2,1,0:T(2,128)(2,1)} %param.5), channel_id=1, source_target_pairs={{0,4},{4,8},{8,12},{12,16},{16,20},{20,24},{24,28},{1,5},{5,9},{9,... | collective-permute-start | bytes 196616 | tf_op jit(solution)/shard_map/ppermute | solution.py:22
  5.0 1.3 %collective-permute-start.1 = (bf16[1,16,2,1024]{3,2,1,0:T(2,128)(2,1)}, bf16[1,16,2,1024]{3,2,1,0:T(2,128)(2,1)S(1)}, u32[]{:S(2)}, u32[]{:S(2)}) collective-permute-start(bf16[1,16,2,1024]{3,2,1,0:T(2,128)(2,1)} %param.5), channel_id=1, source_target_pairs={{4,0},{8,4},{12,8},{16,12},{20,16},{24,20},{28,24},{5,1},{9,5},{13... | collective-permute-start | bytes 196616 | tf_op jit(solution)/shard_map/ppermute | solution.py:23
  6.3 1.3 %fusion.44 = (f32[1,1024]{1,0:T(1,128)S(1)}, f32[1,1024]{1,0:T(1,128)S(1)}, f32[1,1024]{1,0:T(1,128)S(1)}, f32[1,1024]{1,0:T(1,128)S(1)}, f32[1,1024]{1,0:T(1,12...) fusion(f32[27,1024]{1,0:T(8,128)} %param.6), kind=kLoop, calls=%fused_computation.111 | loop fusion | bytes 155648 | tf_op jit(solution)/shard_map/slice | solution.py:126
  7.6 1.0 %fusion.45 = (f32[1,1024]{1,0:T(1,128)S(1)}, f32[1,1024]{1,0:T(1,128)S(1)}, f32[1,1024]{1,0:T(1,128)S(1)}, f32[1,1024]{1,0:T(1,128)S(1)}, f32[1,1024]{1,0:T(1,12...) fusion(f32[27,1024]{1,0:T(8,128)} %param.6), kind=kLoop, calls=%fused_computation.112 | loop fusion | bytes 65536 | tf_op jit(solution)/shard_map/slice | solution.py:126
  8.7 0.0 collective-permute-done
  8.8 0.9 %constant_dynamic-update-slice_fusion.1 = bf16[3,16,2,1024]{3,2,1,0:T(2,128)(2,1)S(1)} fusion(bf16[3,16,2,1024]{3,2,1,0:T(2,128)(2,1)S(1)} %constant_dynamic-update-slice_fusion.2, bf16[1,16,2,1024]{3,2,1,0:T(2,128)(2,1)} %param.5), kind=kLoop, calls=%fused_computation.90 | loop fusion | bytes 131072
  9.7 1.7 %collective-permute-done.1 = bf16[1,16,2,1024]{3,2,1,0:T(2,128)(2,1)S(1)} collective-permute-done((bf16[1,16,2,1024]{3,2,1,0:T(2,128)(2,1)}, bf16[1,16,2,1024]{3,2,1,0:T(2,128)(2,1)S(1)}, u32[]{:S(2)}, u32[]{:S(2)}) %collective-permute-start.1) | collective-permute-done | bytes 65568 | tf_op jit(solution)/shard_map/ppermute | solution.py:23
  11.4 0.1 constant_dynamic-update-slice_fusion
  11.4 0.1 collective-permute-start.2
  11.5 1.6 %collective-permute-start.3 = (bf16[3,16,2,1024]{3,2,1,0:T(2,128)(2,1)S(1)}, bf16[3,16,2,1024]{3,2,1,0:T(2,128)(2,1)S(1)}, u32[]{:S(2)}, u32[]{:S(2)}) collective-permute-start(bf16[3,16,2,1024]{3,2,1,0:T(2,128)(2,1)S(1)} %constant_dynamic-update-slice_fusion), channel_id=1, source_target_pairs={{0,2},{1,3},{2,0},{3,1},{4,6},{5,7},{6,4},{7,5},{8,10},{9,11},{10,... | collective-permute-start | bytes 589832 | tf_op jit(solution)/shard_map/ppermute | solution.py:68
  13.1 0.1 broadcast_in_dim.27
  13.2 0.0 copy-start.2
  13.2 0.0 collective-permute-done.2
  13.3 5.5 %collective-permute-done.3 = bf16[3,16,2,1024]{3,2,1,0:T(2,128)(2,1)S(1)} collective-permute-done((bf16[3,16,2,1024]{3,2,1,0:T(2,128)(2,1)S(1)}, bf16[3,16,2,1024]{3,2,1,0:T(2,128)(2,1)S(1)}, u32[]{:S(2)}, u32[]{:S(2)}) %collective-permute-start.3) | collective-permute-done | bytes 196640 | tf_op jit(solution)/shard_map/ppermute | solution.py:68
  18.8 0.0 collective-permute-start.4
  18.9 1.4 %collective-permute-done.4 = bf16[3,16,2,1024]{3,2,1,0:T(2,128)(2,1)S(1)} collective-permute-done((bf16[3,16,2,1024]{3,2,1,0:T(2,128)(2,1)S(1)}, bf16[3,16,2,1024]{3,2,1,0:T(2,128)(2,1)S(1)}, u32[]{:S(2)}, u32[]{:S(2)}) %collective-permute-start.4) | collective-permute-done | bytes 196640 | tf_op jit(solution)/shard_map/ppermute | solution.py:70
  20.3 0.1 fusion.42
  20.4 2.3 %add_convert_fusion = bf16[1,16,8,1024]{3,1,2,0:T(8,128)(2,1)S(1)} fusion(bf16[1,16,8,1024]{3,1,2,0:T(8,128)(2,1)S(1)} %bitcast.119, bf16[1,16,8,1024]{3,1,2,0:T(8,128)(2,1)S(1)} %bitcast.118, bf16[1,16,8,1024]{3,1,2,0:T(8,128)(2,1)S(1)} %bitcast.117, bf16[3,16,8,1024]{3,1,2,0:T(8,128)(2,1)S(1)} %bitcast.114, f32[1024]{0:T(1024)S(1)} %bitcast.153, ...), kind=kLoop, calls=%fused_computation.77 | loop fusion | flops 10878976 | bytes 1949696 | tf_op jit(solution)/shard_map/convert_element_type | solution.py:133
  22.8 0.3 copy.29
  23.0 0.1 reshape.250
  23.2 0.6 %convolution_convert_fusion = bf16[128,768]{0,1:T(8,128)(2,1)S(1)} fusion(bf16[128,1024]{1,0:T(8,128)(2,1)S(1)} %reshape.250, bf16[768,1024]{1,0:T(8,128)(2,1)S(1)} %copy-done), kind=kOutput, calls=%fused_computation.26 | convolution fusion | flops 201424896 | bytes 2031616 | tf_op jit(solution)/shard_map/dot_general | solution.py:104
  23.8 3.0 %collective-permute-start.5 = (bf16[128,4,2,64]{0,3,1,2:T(8,128)(2,1)S(1)}, bf16[128,4,2,64]{0,3,1,2:T(8,128)(2,1)S(1)}, u32[]{:S(2)}, u32[]{:S(2)}) collective-permute-start(bf16[128,4,2,64]{0,3,1,2:T(8,128)(2,1)S(1)} %get-tuple-element.56), channel_id=1, source_target_pairs={{0,16},{4,20},{8,24},{12,28},{16,0},{20,4},{24,8},{28,12},{1,17},{... | collective-permute-start | bytes 393224 | tf_op jit(solution)/shard_map/ppermute | solution.py:43
  26.8 2.1 %collective-permute-start.6 = (bf16[128,4,2,64]{0,3,1,2:T(8,128)(2,1)S(1)}, bf16[128,4,2,64]{0,3,1,2:T(8,128)(2,1)}, u32[]{:S(2)}, u32[]{:S(2)}) collective-permute-start(bf16[128,4,2,64]{0,3,1,2:T(8,128)(2,1)S(1)} %get-tuple-element.56), channel_id=1, source_target_pairs={{0,4},{4,8},{8,12},{12,0},{16,20},{20,24},{24,28},{28,16},{1,5},{5... | collective-permute-start | bytes 393224 | tf_op jit(solution)/shard_map/ppermute | solution.py:47
  28.8 0.1 collective-permute-start.8
  29.0 2.3 %collective-permute-start.10 = (bf16[128,4,2,64]{0,3,1,2:T(8,128)(2,1)S(1)}, bf16[128,4,2,64]{0,3,1,2:T(8,128)(2,1)S(1)}, u32[]{:S(2)}, u32[]{:S(2)}) collective-permute-start(bf16[128,4,2,64]{0,3,1,2:T(8,128)(2,1)S(1)} %get-tuple-element.56), channel_id=1, source_target_pairs={{0,12},{4,0},{8,4},{12,8},{16,28},{20,16},{24,20},{28,24},{1,13},{... | collective-permute-start | bytes 393224 | tf_op jit(solution)/shard_map/ppermute | solution.py:47
  31.3 0.1 reshape_squeeze.2
  31.4 0.3 constant_dynamic-slice_fusion.2
  31.7 0.1 copy.20
  31.8 0.1 copy.19
  31.9 1.6 %collective-permute-done.5 = bf16[128,4,2,64]{0,3,1,2:T(8,128)(2,1)S(1)} collective-permute-done((bf16[128,4,2,64]{0,3,1,2:T(8,128)(2,1)S(1)}, bf16[128,4,2,64]{0,3,1,2:T(8,128)(2,1)S(1)}, u32[]{:S(2)}, u32[]{:S(2)}) %collective-permute-start.5) | collective-permute-done | bytes 131104 | tf_op jit(solution)/shard_map/ppermute | solution.py:43
  33.5 2.1 %collective-permute-start.7 = (bf16[128,4,2,64]{0,3,1,2:T(8,128)(2,1)S(1)}, bf16[128,4,2,64]{0,3,1,2:T(8,128)(2,1)S(1)}, u32[]{:S(2)}, u32[]{:S(2)}) collective-permute-start(bf16[128,4,2,64]{0,3,1,2:T(8,128)(2,1)S(1)} %collective-permute-done.5), channel_id=1, source_target_pairs={{0,4},{4,8},{8,12},{12,0},{16,20},{20,24},{24,28},{28,16},{1,5},{5... | collective-permute-start | bytes 393224 | tf_op jit(solution)/shard_map/ppermute | solution.py:48
  35.6 0.0 collective-permute-start.9
  35.7 0.2 collective-permute-done.6
  35.8 1.3 %collective-permute-start.11 = (bf16[128,4,2,64]{0,3,1,2:T(8,128)(2,1)S(1)}, bf16[128,4,2,64]{0,3,1,2:T(8,128)(2,1)S(1)}, u32[]{:S(2)}, u32[]{:S(2)}) collective-permute-start(bf16[128,4,2,64]{0,3,1,2:T(8,128)(2,1)S(1)} %collective-permute-done.5), channel_id=1, source_target_pairs={{0,12},{4,0},{8,4},{12,8},{16,28},{20,16},{24,20},{28,24},{1,13},{... | collective-permute-start | bytes 393224 | tf_op jit(solution)/shard_map/ppermute | solution.py:48
  37.2 0.9 %constant_dynamic-update-slice_fusion.8 = bf16[1024,4,2,64]{0,3,1,2:T(8,128)(2,1)S(1)} fusion(bf16[1024,4,2,64]{0,3,1,2:T(8,128)(2,1)S(1)} %constant_dynamic-update-slice_fusion.9, bf16[128,4,2,64]{0,3,1,2:T(8,128)(2,1)} %collective-permute-done.6), kind=kLoop, calls=%fused_computation.97 | loop fusion | bytes 262144
  38.1 3.3 %collective-permute-done.7 = bf16[128,4,2,64]{0,3,1,2:T(8,128)(2,1)S(1)} collective-permute-done((bf16[128,4,2,64]{0,3,1,2:T(8,128)(2,1)S(1)}, bf16[128,4,2,64]{0,3,1,2:T(8,128)(2,1)S(1)}, u32[]{:S(2)}, u32[]{:S(2)}) %collective-permute-start.7) | collective-permute-done | bytes 131104 | tf_op jit(solution)/shard_map/ppermute | solution.py:48
  41.4 0.0 collective-permute-done.8
  41.5 0.9 %constant_dynamic-update-slice_fusion.6 = bf16[1024,4,2,64]{0,3,1,2:T(8,128)(2,1)S(1)} fusion(bf16[1024,4,2,64]{0,3,1,2:T(8,128)(2,1)S(1)} %constant_dynamic-update-slice_fusion.7, bf16[128,4,2,64]{0,3,1,2:T(8,128)(2,1)} %collective-permute-done.8), kind=kLoop, calls=%fused_computation.95 | loop fusion | bytes 262144
  42.4 0.0 collective-permute-done.9
  42.5 0.0 collective-permute-done.10
  42.5 0.2 collective-permute-done.11
  42.8 0.4 fusion.46
  43.1 0.0 copy-start.1
  43.1 0.3 fusion.6
  43.5 0.4 fusion.5
  43.8 0.1 copy.17
  43.9 0.1 reshape.252
  44.0 0.2 copy-done.1
  44.2 0.2 convolution_convert_fusion.1
  44.4 1.6 %collective-permute-start.13 = (bf16[32,1024]{1,0:T(8,128)(2,1)S(1)}, bf16[32,1024]{1,0:T(8,128)(2,1)S(1)}, u32[]{:S(2)}, u32[]{:S(2)}) collective-permute-start(bf16[32,1024]{1,0:T(8,128)(2,1)S(1)} %get-tuple-element.47), channel_id=1, source_target_pairs={{0,2},{1,3},{2,0},{3,1},{4,6},{5,7},{6,4},{7,5},{8,10},{9,11},{10,... | collective-permute-start | bytes 196616 | tf_op jit(solution)/shard_map/ppermute | solution.py:204
  46.0 0.4 fusion.47
  46.4 0.3 fusion.8
  46.7 0.4 fusion.4
  47.1 0.1 copy.18
  47.1 0.1 dot_general.39
  47.2 0.2 fusion.37
  47.5 0.7 %collective-permute-start.12 = (f32[32,1024]{1,0:T(8,128)S(1)}, f32[32,1024]{1,0:T(8,128)S(1)}, u32[]{:S(2)}, u32[]{:S(2)}) collective-permute-start(f32[32,1024]{1,0:T(8,128)S(1)} %get-tuple-element.43), channel_id=1, source_target_pairs={{0,1},{1,0},{2,3},{3,2},{4,5},{5,4},{6,7},{7,6},{8,9},{9,8},{10,11... | collective-permute-start | bytes 393224 | tf_op jit(solution)/shard_map/ppermute | solution.py:216
  48.2 0.1 reshape.254
  48.3 0.5 collective-permute-done.13
  48.8 1.4 %collective-permute-done.14 = bf16[32,1024]{1,0:T(8,128)(2,1)S(1)} collective-permute-done((bf16[32,1024]{1,0:T(8,128)(2,1)S(1)}, bf16[32,1024]{1,0:T(8,128)(2,1)S(1)}, u32[]{:S(2)}, u32[]{:S(2)}) %collective-permute-start.14) | collective-permute-done | bytes 65568 | tf_op jit(solution)/shard_map/ppermute | solution.py:205
  50.2 0.1 add.269
  50.3 0.0 collective-permute-done.12
  50.3 0.1 reshape.255
  50.4 0.7 %add_convert_fusion.1 = bf16[1,16,2,1024]{3,2,1,0:T(2,128)(2,1)} fusion(f32[1,16,2,1024]{3,2,1,0:T(2,128)S(1)} %add.269, f32[1,16,2,1024]{3,2,1,0:T(2,128)S(1)} %reshape.254, f32[1,16,2,1024]{3,2,1,0:T(2,128)S(1)} %reshape.255), kind=kLoop, calls=%fused_computation.83 | loop fusion | flops 98304 | bytes 458752 | tf_op jit(solution)/shard_map/convert_element_type | solution.py:219
  (23 shorter events, 0.6 us)
Async XLA Ops:
  0.0 23.1 %copy-start = (bf16[768,1024]{1,0:T(8,128)(2,1)S(1)}, bf16[768,1024]{1,0:T(8,128)(2,1)}, u32[]{:S(2)}) copy-start(bf16[768,1024]{1,0:T(8,128)(2,1)} %param.8) | copy-start | bytes 4718596
  0.0 8.7 %collective-permute-start = (bf16[1,16,2,1024]{3,2,1,0:T(2,128)(2,1)}, bf16[1,16,2,1024]{3,2,1,0:T(2,128)(2,1)S(1)}, u32[]{:S(2)}, u32[]{:S(2)}) collective-permute-start(bf16[1,16,2,1024]{3,2,1,0:T(2,128)(2,1)} %param.5), channel_id=1, source_target_pairs={{0,4},{4,8},{8,12},{12,16},{16,20},{20,24},{24,28},{1,5},{5,9},{9,... | collective-permute-start | bytes 196616 | tf_op jit(solution)/shard_map/ppermute | solution.py:22
  5.0 6.4 %collective-permute-start.1 = (bf16[1,16,2,1024]{3,2,1,0:T(2,128)(2,1)}, bf16[1,16,2,1024]{3,2,1,0:T(2,128)(2,1)S(1)}, u32[]{:S(2)}, u32[]{:S(2)}) collective-permute-start(bf16[1,16,2,1024]{3,2,1,0:T(2,128)(2,1)} %param.5), channel_id=1, source_target_pairs={{4,0},{8,4},{12,8},{16,12},{20,16},{24,20},{28,24},{5,1},{9,5},{13... | collective-permute-start | bytes 196616 | tf_op jit(solution)/shard_map/ppermute | solution.py:23
  11.4 1.8 %collective-permute-start.2 = (bf16[3,16,2,1024]{3,2,1,0:T(2,128)(2,1)S(1)}, bf16[3,16,2,1024]{3,2,1,0:T(2,128)(2,1)S(1)}, u32[]{:S(2)}, u32[]{:S(2)}) collective-permute-start(bf16[3,16,2,1024]{3,2,1,0:T(2,128)(2,1)S(1)} %constant_dynamic-update-slice_fusion), channel_id=1, source_target_pairs={{0,1},{1,0},{2,3},{3,2},{4,5},{5,4},{6,7},{7,6},{8,9},{9,8},{10,11... | collective-permute-start | bytes 589832 | tf_op jit(solution)/shard_map/ppermute | solution.py:64
  11.5 7.3 %collective-permute-start.3 = (bf16[3,16,2,1024]{3,2,1,0:T(2,128)(2,1)S(1)}, bf16[3,16,2,1024]{3,2,1,0:T(2,128)(2,1)S(1)}, u32[]{:S(2)}, u32[]{:S(2)}) collective-permute-start(bf16[3,16,2,1024]{3,2,1,0:T(2,128)(2,1)S(1)} %constant_dynamic-update-slice_fusion), channel_id=1, source_target_pairs={{0,2},{1,3},{2,0},{3,1},{4,6},{5,7},{6,4},{7,5},{8,10},{9,11},{10,... | collective-permute-start | bytes 589832 | tf_op jit(solution)/shard_map/ppermute | solution.py:68
  13.2 7.2 %copy-start.2 = (f32[1024]{0:T(1024)S(1)}, f32[1024]{0:T(1024)}, u32[]{:S(2)}) copy-start(f32[1024]{0:T(1024)} %param.7) | copy-start | bytes 12292
  18.8 1.4 %collective-permute-start.4 = (bf16[3,16,2,1024]{3,2,1,0:T(2,128)(2,1)S(1)}, bf16[3,16,2,1024]{3,2,1,0:T(2,128)(2,1)S(1)}, u32[]{:S(2)}, u32[]{:S(2)}) collective-permute-start(bf16[3,16,2,1024]{3,2,1,0:T(2,128)(2,1)S(1)} %collective-permute-done.3), channel_id=1, source_target_pairs={{0,1},{1,0},{2,3},{3,2},{4,5},{5,4},{6,7},{7,6},{8,9},{9,8},{10,11... | collective-permute-start | bytes 589832 | tf_op jit(solution)/shard_map/ppermute | solution.py:70
  23.8 9.7 %collective-permute-start.5 = (bf16[128,4,2,64]{0,3,1,2:T(8,128)(2,1)S(1)}, bf16[128,4,2,64]{0,3,1,2:T(8,128)(2,1)S(1)}, u32[]{:S(2)}, u32[]{:S(2)}) collective-permute-start(bf16[128,4,2,64]{0,3,1,2:T(8,128)(2,1)S(1)} %get-tuple-element.56), channel_id=1, source_target_pairs={{0,16},{4,20},{8,24},{12,28},{16,0},{20,4},{24,8},{28,12},{1,17},{... | collective-permute-start | bytes 393224 | tf_op jit(solution)/shard_map/ppermute | solution.py:43
  26.8 9.1 %collective-permute-start.6 = (bf16[128,4,2,64]{0,3,1,2:T(8,128)(2,1)S(1)}, bf16[128,4,2,64]{0,3,1,2:T(8,128)(2,1)}, u32[]{:S(2)}, u32[]{:S(2)}) collective-permute-start(bf16[128,4,2,64]{0,3,1,2:T(8,128)(2,1)S(1)} %get-tuple-element.56), channel_id=1, source_target_pairs={{0,4},{4,8},{8,12},{12,0},{16,20},{20,24},{24,28},{28,16},{1,5},{5... | collective-permute-start | bytes 393224 | tf_op jit(solution)/shard_map/ppermute | solution.py:47
  28.8 12.6 %collective-permute-start.8 = (bf16[128,4,2,64]{0,3,1,2:T(8,128)(2,1)S(1)}, bf16[128,4,2,64]{0,3,1,2:T(8,128)(2,1)}, u32[]{:S(2)}, u32[]{:S(2)}) collective-permute-start(bf16[128,4,2,64]{0,3,1,2:T(8,128)(2,1)S(1)} %get-tuple-element.56), channel_id=1, source_target_pairs={{0,8},{4,12},{8,0},{12,4},{16,24},{20,28},{24,16},{28,20},{1,9},{5... | collective-permute-start | bytes 393224 | tf_op jit(solution)/shard_map/ppermute | solution.py:47
  29.0 13.5 %collective-permute-start.10 = (bf16[128,4,2,64]{0,3,1,2:T(8,128)(2,1)S(1)}, bf16[128,4,2,64]{0,3,1,2:T(8,128)(2,1)S(1)}, u32[]{:S(2)}, u32[]{:S(2)}) collective-permute-start(bf16[128,4,2,64]{0,3,1,2:T(8,128)(2,1)S(1)} %get-tuple-element.56), channel_id=1, source_target_pairs={{0,12},{4,0},{8,4},{12,8},{16,28},{20,16},{24,20},{28,24},{1,13},{... | collective-permute-start | bytes 393224 | tf_op jit(solution)/shard_map/ppermute | solution.py:47
  33.5 7.9 %collective-permute-start.7 = (bf16[128,4,2,64]{0,3,1,2:T(8,128)(2,1)S(1)}, bf16[128,4,2,64]{0,3,1,2:T(8,128)(2,1)S(1)}, u32[]{:S(2)}, u32[]{:S(2)}) collective-permute-start(bf16[128,4,2,64]{0,3,1,2:T(8,128)(2,1)S(1)} %collective-permute-done.5), channel_id=1, source_target_pairs={{0,4},{4,8},{8,12},{12,0},{16,20},{20,24},{24,28},{28,16},{1,5},{5... | collective-permute-start | bytes 393224 | tf_op jit(solution)/shard_map/ppermute | solution.py:48
  35.6 6.8 %collective-permute-start.9 = (bf16[128,4,2,64]{0,3,1,2:T(8,128)(2,1)S(1)}, bf16[128,4,2,64]{0,3,1,2:T(8,128)(2,1)S(1)}, u32[]{:S(2)}, u32[]{:S(2)}) collective-permute-start(bf16[128,4,2,64]{0,3,1,2:T(8,128)(2,1)S(1)} %collective-permute-done.5), channel_id=1, source_target_pairs={{0,8},{4,12},{8,0},{12,4},{16,24},{20,28},{24,16},{28,20},{1,9},{5... | collective-permute-start | bytes 393224 | tf_op jit(solution)/shard_map/ppermute | solution.py:48
  35.8 6.9 %collective-permute-start.11 = (bf16[128,4,2,64]{0,3,1,2:T(8,128)(2,1)S(1)}, bf16[128,4,2,64]{0,3,1,2:T(8,128)(2,1)S(1)}, u32[]{:S(2)}, u32[]{:S(2)}) collective-permute-start(bf16[128,4,2,64]{0,3,1,2:T(8,128)(2,1)S(1)} %collective-permute-done.5), channel_id=1, source_target_pairs={{0,12},{4,0},{8,4},{12,8},{16,28},{20,16},{24,20},{28,24},{1,13},{... | collective-permute-start | bytes 393224 | tf_op jit(solution)/shard_map/ppermute | solution.py:48
  43.1 1.1 %copy-start.1 = (bf16[256,1024]{1,0:T(8,128)(2,1)S(1)}, bf16[256,1024]{1,0:T(8,128)(2,1)}, u32[]{:S(2)}) copy-start(bf16[256,1024]{1,0:T(8,128)(2,1)} %param.9) | copy-start | bytes 1572868
  44.4 4.3 %collective-permute-start.13 = (bf16[32,1024]{1,0:T(8,128)(2,1)S(1)}, bf16[32,1024]{1,0:T(8,128)(2,1)S(1)}, u32[]{:S(2)}, u32[]{:S(2)}) collective-permute-start(bf16[32,1024]{1,0:T(8,128)(2,1)S(1)} %get-tuple-element.47), channel_id=1, source_target_pairs={{0,2},{1,3},{2,0},{3,1},{4,6},{5,7},{6,4},{7,5},{8,10},{9,11},{10,... | collective-permute-start | bytes 196616 | tf_op jit(solution)/shard_map/ppermute | solution.py:204
  46.0 4.2 %collective-permute-start.14 = (bf16[32,1024]{1,0:T(8,128)(2,1)S(1)}, bf16[32,1024]{1,0:T(8,128)(2,1)S(1)}, u32[]{:S(2)}, u32[]{:S(2)}) collective-permute-start(bf16[32,1024]{1,0:T(8,128)(2,1)S(1)} %get-tuple-element.48), channel_id=1, source_target_pairs={{0,3},{1,2},{2,1},{3,0},{4,7},{5,6},{6,5},{7,4},{8,11},{9,10},{10,... | collective-permute-start | bytes 196616 | tf_op jit(solution)/shard_map/ppermute | solution.py:205
  47.5 2.8 %collective-permute-start.12 = (f32[32,1024]{1,0:T(8,128)S(1)}, f32[32,1024]{1,0:T(8,128)S(1)}, u32[]{:S(2)}, u32[]{:S(2)}) collective-permute-start(f32[32,1024]{1,0:T(8,128)S(1)} %get-tuple-element.43), channel_id=1, source_target_pairs={{0,1},{1,0},{2,3},{3,2},{4,5},{5,4},{6,7},{7,6},{8,9},{9,8},{10,11... | collective-permute-start | bytes 393224 | tf_op jit(solution)/shard_map/ppermute | solution.py:216

commit v19 on v17

--- a/solution.py
+++ b/solution.py
@@ -195,6 +195,9 @@
         far_partial = far_partial.astype(jnp.bfloat16).reshape(2, local_tok, features)
         same_core = lax.dynamic_index_in_dim(far_partial, core, 0, keepdims=False)
         other_core = lax.dynamic_index_in_dim(far_partial, 1 - core, 0, keepdims=False)
+        out_layout = Layout(major_to_minor=tuple(range(tokens.ndim)))
+        same_core = with_layout_constraint(same_core.reshape(tokens.shape), out_layout)
+        other_core = with_layout_constraint(other_core.reshape(tokens.shape), out_layout)
         far_sent = (same_core, other_core)
         to_other_core = [
             (i, ((i // 2 + shift) % chips) * 2 + 1 - i % 2) for i in range(groups)

time: 51.8 us -> 53.2 us (1.027)
  waiting for transfers between devices: 15.8 us -> 17.5 us
    ppermute x1, waiting for transfers between devices: 0.49 us -> 2.48 us  [on_device(): lax.ppermute(same_core, 'uly', chip_shift(groups, shift))]
    ppermute x1, starting transfers between devices: 0.7 us -> 0.07 us  [on_device(): lax.ppermute(for_partner, 'uly', [(i, i ^ 1) for i in range(groups)])]
  transfers between devices with their start and end apart: 15 -> 15, of which waited for: 9 -> 9; matrix products, arithmetic and copies ran while one was open for 15% -> 12% of each run, Pallas kernels for 0% -> 0%
where the time goes in v19:
time: 53.2 us; the launch traced here: 52.7 us
  starting transfers between devices  20.8 us (39%)
  waiting for transfers between devices  17.5 us (33%)
  local copies, waits for them, and re-layouts  7.69 us (14%)
  other arithmetic  3.75 us (7%)
  matrix products  2.5 us (5%)
    ppermute x1, waiting for transfers between devices, gathered_by_chip(): far = lax.ppermute(piece, axis, chip_shift(size, shift))  5.55 us
    ppermute x1, starting transfers between devices, padded_2(): before = lax.ppermute(last, axis, up)  5 us
    ppermute x3, starting transfers between devices, relayed(): parts.append(lax.ppermute(piece, axis, pairs))  4.5 us
    ppermute x3, waiting for transfers between devices, relayed(): parts.append(lax.ppermute(crossed, axis, pairs))  3.47 us
    ppermute x3, starting transfers between devices, relayed(): parts.append(lax.ppermute(crossed, axis, pairs))  3.46 us
    unnamed x15, local copies, waits for them, and re-layouts  3.21 us
    ppermute x1, starting transfers between devices, relayed(): crossed = lax.ppermute(piece, axis, mirror)  2.99 us
    ppermute x1, waiting for transfers between devices, on_device(): lax.ppermute(same_core, 'uly', chip_shift(groups, shift))  2.48 us
  transfers between devices with their start and end apart: 15, of which 9 were waited for; matrix products, arithmetic and copies ran while one was open for 12% of the time, Pallas kernels for 0%

profile of v19, /device:TPU:0, one launch (start us, length us, event | category | flops | bytes accessed | tf_op | source)
XLA Modules:
  0.0 52.7 jit_solution(801585325579586604)
XLA Ops:
  0.0 5.0 %collective-permute-start = (bf16[1,16,2,1024]{3,2,1,0:T(2,128)(2,1)}, bf16[1,16,2,1024]{3,2,1,0:T(2,128)(2,1)S(1)}, u32[]{:S(2)}, u32[]{:S(2)}) collective-permute-start(bf16[1,16,2,1024]{3,2,1,0:T(2,128)(2,1)} %param.5), channel_id=1, source_target_pairs={{0,4},{4,8},{8,12},{12,16},{16,20},{20,24},{24,28},{1,5},{5,9},{9,... | collective-permute-start | bytes 196616 | tf_op jit(solution)/shard_map/ppermute | solution.py:22
  5.0 1.3 %collective-permute-start.1 = (bf16[1,16,2,1024]{3,2,1,0:T(2,128)(2,1)}, bf16[1,16,2,1024]{3,2,1,0:T(2,128)(2,1)S(1)}, u32[]{:S(2)}, u32[]{:S(2)}) collective-permute-start(bf16[1,16,2,1024]{3,2,1,0:T(2,128)(2,1)} %param.5), channel_id=1, source_target_pairs={{4,0},{8,4},{12,8},{16,12},{20,16},{24,20},{28,24},{5,1},{9,5},{13... | collective-permute-start | bytes 196616 | tf_op jit(solution)/shard_map/ppermute | solution.py:23
  6.3 1.3 %fusion.44 = (f32[1,1024]{1,0:T(1,128)S(1)}, f32[1,1024]{1,0:T(1,128)S(1)}, f32[1,1024]{1,0:T(1,128)S(1)}, f32[1,1024]{1,0:T(1,128)S(1)}, f32[1,1024]{1,0:T(1,12...) fusion(f32[27,1024]{1,0:T(8,128)} %param.6), kind=kLoop, calls=%fused_computation.110 | loop fusion | bytes 155648 | tf_op jit(solution)/shard_map/slice | solution.py:126
  7.6 1.0 %fusion.45 = (f32[1,1024]{1,0:T(1,128)S(1)}, f32[1,1024]{1,0:T(1,128)S(1)}, f32[1,1024]{1,0:T(1,128)S(1)}, f32[1,1024]{1,0:T(1,128)S(1)}, f32[1,1024]{1,0:T(1,12...) fusion(f32[27,1024]{1,0:T(8,128)} %param.6), kind=kLoop, calls=%fused_computation.111 | loop fusion | bytes 65536 | tf_op jit(solution)/shard_map/slice | solution.py:126
  8.7 0.0 collective-permute-done
  8.8 0.9 %constant_dynamic-update-slice_fusion.1 = bf16[3,16,2,1024]{3,2,1,0:T(2,128)(2,1)S(1)} fusion(bf16[3,16,2,1024]{3,2,1,0:T(2,128)(2,1)S(1)} %constant_dynamic-update-slice_fusion.2, bf16[1,16,2,1024]{3,2,1,0:T(2,128)(2,1)} %param.5), kind=kLoop, calls=%fused_computation.87 | loop fusion | bytes 131072
  9.7 1.7 %collective-permute-done.1 = bf16[1,16,2,1024]{3,2,1,0:T(2,128)(2,1)S(1)} collective-permute-done((bf16[1,16,2,1024]{3,2,1,0:T(2,128)(2,1)}, bf16[1,16,2,1024]{3,2,1,0:T(2,128)(2,1)S(1)}, u32[]{:S(2)}, u32[]{:S(2)}) %collective-permute-start.1) | collective-permute-done | bytes 65568 | tf_op jit(solution)/shard_map/ppermute | solution.py:23
  11.4 0.1 constant_dynamic-update-slice_fusion
  11.4 0.1 collective-permute-start.2
  11.5 1.6 %collective-permute-start.3 = (bf16[3,16,2,1024]{3,2,1,0:T(2,128)(2,1)S(1)}, bf16[3,16,2,1024]{3,2,1,0:T(2,128)(2,1)S(1)}, u32[]{:S(2)}, u32[]{:S(2)}) collective-permute-start(bf16[3,16,2,1024]{3,2,1,0:T(2,128)(2,1)S(1)} %constant_dynamic-update-slice_fusion), channel_id=1, source_target_pairs={{0,2},{1,3},{2,0},{3,1},{4,6},{5,7},{6,4},{7,5},{8,10},{9,11},{10,... | collective-permute-start | bytes 589832 | tf_op jit(solution)/shard_map/ppermute | solution.py:68
  13.1 0.1 broadcast_in_dim.27
  13.2 0.0 copy-start.2
  13.2 0.0 collective-permute-done.2
  13.3 5.5 %collective-permute-done.3 = bf16[3,16,2,1024]{3,2,1,0:T(2,128)(2,1)S(1)} collective-permute-done((bf16[3,16,2,1024]{3,2,1,0:T(2,128)(2,1)S(1)}, bf16[3,16,2,1024]{3,2,1,0:T(2,128)(2,1)S(1)}, u32[]{:S(2)}, u32[]{:S(2)}) %collective-permute-start.3) | collective-permute-done | bytes 196640 | tf_op jit(solution)/shard_map/ppermute | solution.py:68
  18.8 0.0 collective-permute-start.4
  18.9 1.4 %collective-permute-done.4 = bf16[3,16,2,1024]{3,2,1,0:T(2,128)(2,1)S(1)} collective-permute-done((bf16[3,16,2,1024]{3,2,1,0:T(2,128)(2,1)S(1)}, bf16[3,16,2,1024]{3,2,1,0:T(2,128)(2,1)S(1)}, u32[]{:S(2)}, u32[]{:S(2)}) %collective-permute-start.4) | collective-permute-done | bytes 196640 | tf_op jit(solution)/shard_map/ppermute | solution.py:70
  20.3 0.1 fusion.42
  20.4 2.3 %add_convert_fusion = bf16[1,16,8,1024]{3,1,2,0:T(8,128)(2,1)S(1)} fusion(bf16[1,16,8,1024]{3,1,2,0:T(8,128)(2,1)S(1)} %bitcast.115, bf16[1,16,8,1024]{3,1,2,0:T(8,128)(2,1)S(1)} %bitcast.114, bf16[1,16,8,1024]{3,1,2,0:T(8,128)(2,1)S(1)} %bitcast.113, bf16[3,16,8,1024]{3,1,2,0:T(8,128)(2,1)S(1)} %bitcast.110, f32[1024]{0:T(1024)S(1)} %bitcast.149, ...), kind=kLoop, calls=%fused_computation.77 | loop fusion | flops 10878976 | bytes 1949696 | tf_op jit(solution)/shard_map/convert_element_type | solution.py:133
  22.8 0.3 copy.38
  23.0 0.1 reshape.227
  23.2 0.7 %convolution_convert_fusion = bf16[128,768]{1,0:T(8,128)(2,1)S(1)} fusion(bf16[128,1024]{1,0:T(8,128)(2,1)S(1)} %reshape.227, bf16[768,1024]{1,0:T(8,128)(2,1)S(1)} %copy-done), kind=kOutput, calls=%fused_computation.26 | convolution fusion | flops 201424896 | bytes 2031616 | tf_op jit(solution)/shard_map/dot_general | solution.py:104
  23.8 0.2 copy.24
  24.0 3.0 %collective-permute-start.5 = (bf16[128,4,2,64]{0,3,1,2:T(8,128)(2,1)S(1)}, bf16[128,4,2,64]{0,3,1,2:T(8,128)(2,1)S(1)}, u32[]{:S(2)}, u32[]{:S(2)}) collective-permute-start(bf16[128,4,2,64]{0,3,1,2:T(8,128)(2,1)S(1)} %get-tuple-element.56), channel_id=1, source_target_pairs={{0,16},{4,20},{8,24},{12,28},{16,0},{20,4},{24,8},{28,12},{1,17},{... | collective-permute-start | bytes 393224 | tf_op jit(solution)/shard_map/ppermute | solution.py:43
  27.0 2.1 %collective-permute-start.6 = (bf16[128,4,2,64]{0,3,1,2:T(8,128)(2,1)S(1)}, bf16[128,4,2,64]{0,3,1,2:T(8,128)(2,1)}, u32[]{:S(2)}, u32[]{:S(2)}) collective-permute-start(bf16[128,4,2,64]{0,3,1,2:T(8,128)(2,1)S(1)} %get-tuple-element.56), channel_id=1, source_target_pairs={{0,4},{4,8},{8,12},{12,0},{16,20},{20,24},{24,28},{28,16},{1,5},{5... | collective-permute-start | bytes 393224 | tf_op jit(solution)/shard_map/ppermute | solution.py:47
  29.1 0.1 collective-permute-start.8
  29.2 2.3 %collective-permute-start.10 = (bf16[128,4,2,64]{0,3,1,2:T(8,128)(2,1)S(1)}, bf16[128,4,2,64]{0,3,1,2:T(8,128)(2,1)S(1)}, u32[]{:S(2)}, u32[]{:S(2)}) collective-permute-start(bf16[128,4,2,64]{0,3,1,2:T(8,128)(2,1)S(1)} %get-tuple-element.56), channel_id=1, source_target_pairs={{0,12},{4,0},{8,4},{12,8},{16,28},{20,16},{24,20},{28,24},{1,13},{... | collective-permute-start | bytes 393224 | tf_op jit(solution)/shard_map/ppermute | solution.py:47
  31.5 0.1 reshape_squeeze.2
  31.6 0.3 constant_dynamic-slice_fusion.4
  31.9 0.1 copy.26
  32.0 0.1 copy.25
  32.2 1.6 %collective-permute-done.5 = bf16[128,4,2,64]{0,3,1,2:T(8,128)(2,1)S(1)} collective-permute-done((bf16[128,4,2,64]{0,3,1,2:T(8,128)(2,1)S(1)}, bf16[128,4,2,64]{0,3,1,2:T(8,128)(2,1)S(1)}, u32[]{:S(2)}, u32[]{:S(2)}) %collective-permute-start.5) | collective-permute-done | bytes 131104 | tf_op jit(solution)/shard_map/ppermute | solution.py:43
  33.7 2.1 %collective-permute-start.7 = (bf16[128,4,2,64]{0,3,1,2:T(8,128)(2,1)S(1)}, bf16[128,4,2,64]{0,3,1,2:T(8,128)(2,1)S(1)}, u32[]{:S(2)}, u32[]{:S(2)}) collective-permute-start(bf16[128,4,2,64]{0,3,1,2:T(8,128)(2,1)S(1)} %collective-permute-done.5), channel_id=1, source_target_pairs={{0,4},{4,8},{8,12},{12,0},{16,20},{20,24},{24,28},{28,16},{1,5},{5... | collective-permute-start | bytes 393224 | tf_op jit(solution)/shard_map/ppermute | solution.py:48
  35.9 0.2 collective-permute-done.6
  36.1 1.3 %collective-permute-start.11 = (bf16[128,4,2,64]{0,3,1,2:T(8,128)(2,1)S(1)}, bf16[128,4,2,64]{0,3,1,2:T(8,128)(2,1)S(1)}, u32[]{:S(2)}, u32[]{:S(2)}) collective-permute-start(bf16[128,4,2,64]{0,3,1,2:T(8,128)(2,1)S(1)} %collective-permute-done.5), channel_id=1, source_target_pairs={{0,12},{4,0},{8,4},{12,8},{16,28},{20,16},{24,20},{28,24},{1,13},{... | collective-permute-start | bytes 393224 | tf_op jit(solution)/shard_map/ppermute | solution.py:48
  37.4 0.9 %constant_dynamic-update-slice_fusion.8 = bf16[1024,4,2,64]{0,3,1,2:T(8,128)(2,1)S(1)} fusion(bf16[1024,4,2,64]{0,3,1,2:T(8,128)(2,1)S(1)} %constant_dynamic-update-slice_fusion.9, bf16[128,4,2,64]{0,3,1,2:T(8,128)(2,1)} %collective-permute-done.6), kind=kLoop, calls=%fused_computation.94 | loop fusion | bytes 262144
  38.4 3.3 %collective-permute-done.7 = bf16[128,4,2,64]{0,3,1,2:T(8,128)(2,1)S(1)} collective-permute-done((bf16[128,4,2,64]{0,3,1,2:T(8,128)(2,1)S(1)}, bf16[128,4,2,64]{0,3,1,2:T(8,128)(2,1)S(1)}, u32[]{:S(2)}, u32[]{:S(2)}) %collective-permute-start.7) | collective-permute-done | bytes 131104 | tf_op jit(solution)/shard_map/ppermute | solution.py:48
  41.7 0.0 collective-permute-done.8
  41.7 0.9 %constant_dynamic-update-slice_fusion.6 = bf16[1024,4,2,64]{0,3,1,2:T(8,128)(2,1)S(1)} fusion(bf16[1024,4,2,64]{0,3,1,2:T(8,128)(2,1)S(1)} %constant_dynamic-update-slice_fusion.7, bf16[128,4,2,64]{0,3,1,2:T(8,128)(2,1)} %collective-permute-done.8), kind=kLoop, calls=%fused_computation.92 | loop fusion | bytes 262144
  42.7 0.0 collective-permute-done.9
  42.7 0.0 collective-permute-done.10
  42.8 0.2 collective-permute-done.11
  43.0 0.4 fusion.46
  43.4 0.0 copy-start.1
  43.4 0.3 fusion.6
  43.7 0.4 fusion.5
  44.1 0.1 copy.28
  44.1 0.1 reshape.229
  44.2 0.2 copy-done.1
  44.4 0.2 convolution_convert_fusion.1
  44.7 0.4 fusion.47
  45.1 0.3 fusion.8
  45.5 0.4 fusion.4
  45.8 0.1 copy.29
  45.9 0.1 dot_general.39
  46.0 0.2 fusion.37
  46.2 0.1 collective-permute-start.12
  46.3 1.6 %collective-permute-start.13 = (bf16[1,16,2,1024]{3,2,1,0:T(2,128)(2,1)S(1)}, bf16[1,16,2,1024]{3,2,1,0:T(2,128)(2,1)S(1)}, u32[]{:S(2)}, u32[]{:S(2)}) collective-permute-start(bf16[1,16,2,1024]{3,2,1,0:T(2,128)(2,1)S(1)} %reshape.231), channel_id=1, source_target_pairs={{0,2},{1,3},{2,0},{3,1},{4,6},{5,7},{6,4},{7,5},{8,10},{9,11},{10,... | collective-permute-start | bytes 196616 | tf_op jit(solution)/shard_map/ppermute | solution.py:206
  47.9 0.3 collective-permute-start.14
  48.2 0.1 reshape.233
  48.2 0.0 collective-permute-done.12
  48.3 0.1 reshape.234
  48.3 2.5 %collective-permute-done.13 = bf16[1,16,2,1024]{3,2,1,0:T(2,128)(2,1)S(1)} collective-permute-done((bf16[1,16,2,1024]{3,2,1,0:T(2,128)(2,1)S(1)}, bf16[1,16,2,1024]{3,2,1,0:T(2,128)(2,1)S(1)}, u32[]{:S(2)}, u32[]{:S(2)}) %collective-permute-start.13) | collective-permute-done | bytes 65568 | tf_op jit(solution)/shard_map/ppermute | solution.py:206
  50.8 1.1 %collective-permute-done.14 = bf16[1,16,2,1024]{3,2,1,0:T(2,128)(2,1)S(1)} collective-permute-done((bf16[1,16,2,1024]{3,2,1,0:T(2,128)(2,1)S(1)}, bf16[1,16,2,1024]{3,2,1,0:T(2,128)(2,1)S(1)}, u32[]{:S(2)}, u32[]{:S(2)}) %collective-permute-start.14) | collective-permute-done | bytes 65568 | tf_op jit(solution)/shard_map/ppermute | solution.py:207
  51.9 0.7 %add_convert_fusion.1 = bf16[1,16,2,1024]{3,2,1,0:T(2,128)(2,1)} fusion(bf16[1,16,2,1024]{3,2,1,0:T(2,128)(2,1)S(1)} %collective-permute-done.14, bf16[1,16,2,1024]{3,2,1,0:T(2,128)(2,1)S(1)} %collective-permute-done.13, f32[1,16,2,1024]{3,2,1,0:T(2,128)S(1)} %reshape.233, f32[1,16,2,1024]{3,2,1,0:T(2,128)S(1)} %reshape.234), kind=kLoop, calls=%fused_computation.83 | loop fusion | flops 196608 | bytes 458752 | tf_op jit(solution)/shard_map/convert_element_type | solution.py:222
  (24 shorter events, 0.6 us)
Async XLA Ops:
  0.0 23.1 %copy-start = (bf16[768,1024]{1,0:T(8,128)(2,1)S(1)}, bf16[768,1024]{1,0:T(8,128)(2,1)}, u32[]{:S(2)}) copy-start(bf16[768,1024]{1,0:T(8,128)(2,1)} %param.8) | copy-start | bytes 4718596
  0.0 8.7 %collective-permute-start = (bf16[1,16,2,1024]{3,2,1,0:T(2,128)(2,1)}, bf16[1,16,2,1024]{3,2,1,0:T(2,128)(2,1)S(1)}, u32[]{:S(2)}, u32[]{:S(2)}) collective-permute-start(bf16[1,16,2,1024]{3,2,1,0:T(2,128)(2,1)} %param.5), channel_id=1, source_target_pairs={{0,4},{4,8},{8,12},{12,16},{16,20},{20,24},{24,28},{1,5},{5,9},{9,... | collective-permute-start | bytes 196616 | tf_op jit(solution)/shard_map/ppermute | solution.py:22
  5.0 6.4 %collective-permute-start.1 = (bf16[1,16,2,1024]{3,2,1,0:T(2,128)(2,1)}, bf16[1,16,2,1024]{3,2,1,0:T(2,128)(2,1)S(1)}, u32[]{:S(2)}, u32[]{:S(2)}) collective-permute-start(bf16[1,16,2,1024]{3,2,1,0:T(2,128)(2,1)} %param.5), channel_id=1, source_target_pairs={{4,0},{8,4},{12,8},{16,12},{20,16},{24,20},{28,24},{5,1},{9,5},{13... | collective-permute-start | bytes 196616 | tf_op jit(solution)/shard_map/ppermute | solution.py:23
  11.4 1.8 %collective-permute-start.2 = (bf16[3,16,2,1024]{3,2,1,0:T(2,128)(2,1)S(1)}, bf16[3,16,2,1024]{3,2,1,0:T(2,128)(2,1)S(1)}, u32[]{:S(2)}, u32[]{:S(2)}) collective-permute-start(bf16[3,16,2,1024]{3,2,1,0:T(2,128)(2,1)S(1)} %constant_dynamic-update-slice_fusion), channel_id=1, source_target_pairs={{0,1},{1,0},{2,3},{3,2},{4,5},{5,4},{6,7},{7,6},{8,9},{9,8},{10,11... | collective-permute-start | bytes 589832 | tf_op jit(solution)/shard_map/ppermute | solution.py:64
  11.5 7.3 %collective-permute-start.3 = (bf16[3,16,2,1024]{3,2,1,0:T(2,128)(2,1)S(1)}, bf16[3,16,2,1024]{3,2,1,0:T(2,128)(2,1)S(1)}, u32[]{:S(2)}, u32[]{:S(2)}) collective-permute-start(bf16[3,16,2,1024]{3,2,1,0:T(2,128)(2,1)S(1)} %constant_dynamic-update-slice_fusion), channel_id=1, source_target_pairs={{0,2},{1,3},{2,0},{3,1},{4,6},{5,7},{6,4},{7,5},{8,10},{9,11},{10,... | collective-permute-start | bytes 589832 | tf_op jit(solution)/shard_map/ppermute | solution.py:68
  13.2 7.2 %copy-start.2 = (f32[1024]{0:T(1024)S(1)}, f32[1024]{0:T(1024)}, u32[]{:S(2)}) copy-start(f32[1024]{0:T(1024)} %param.7) | copy-start | bytes 12292
  18.8 1.4 %collective-permute-start.4 = (bf16[3,16,2,1024]{3,2,1,0:T(2,128)(2,1)S(1)}, bf16[3,16,2,1024]{3,2,1,0:T(2,128)(2,1)S(1)}, u32[]{:S(2)}, u32[]{:S(2)}) collective-permute-start(bf16[3,16,2,1024]{3,2,1,0:T(2,128)(2,1)S(1)} %collective-permute-done.3), channel_id=1, source_target_pairs={{0,1},{1,0},{2,3},{3,2},{4,5},{5,4},{6,7},{7,6},{8,9},{9,8},{10,11... | collective-permute-start | bytes 589832 | tf_op jit(solution)/shard_map/ppermute | solution.py:70
  24.0 9.7 %collective-permute-start.5 = (bf16[128,4,2,64]{0,3,1,2:T(8,128)(2,1)S(1)}, bf16[128,4,2,64]{0,3,1,2:T(8,128)(2,1)S(1)}, u32[]{:S(2)}, u32[]{:S(2)}) collective-permute-start(bf16[128,4,2,64]{0,3,1,2:T(8,128)(2,1)S(1)} %get-tuple-element.56), channel_id=1, source_target_pairs={{0,16},{4,20},{8,24},{12,28},{16,0},{20,4},{24,8},{28,12},{1,17},{... | collective-permute-start | bytes 393224 | tf_op jit(solution)/shard_map/ppermute | solution.py:43
  27.0 9.1 %collective-permute-start.6 = (bf16[128,4,2,64]{0,3,1,2:T(8,128)(2,1)S(1)}, bf16[128,4,2,64]{0,3,1,2:T(8,128)(2,1)}, u32[]{:S(2)}, u32[]{:S(2)}) collective-permute-start(bf16[128,4,2,64]{0,3,1,2:T(8,128)(2,1)S(1)} %get-tuple-element.56), channel_id=1, source_target_pairs={{0,4},{4,8},{8,12},{12,0},{16,20},{20,24},{24,28},{28,16},{1,5},{5... | collective-permute-start | bytes 393224 | tf_op jit(solution)/shard_map/ppermute | solution.py:47
  29.1 12.6 %collective-permute-start.8 = (bf16[128,4,2,64]{0,3,1,2:T(8,128)(2,1)S(1)}, bf16[128,4,2,64]{0,3,1,2:T(8,128)(2,1)}, u32[]{:S(2)}, u32[]{:S(2)}) collective-permute-start(bf16[128,4,2,64]{0,3,1,2:T(8,128)(2,1)S(1)} %get-tuple-element.56), channel_id=1, source_target_pairs={{0,8},{4,12},{8,0},{12,4},{16,24},{20,28},{24,16},{28,20},{1,9},{5... | collective-permute-start | bytes 393224 | tf_op jit(solution)/shard_map/ppermute | solution.py:47
  29.2 13.5 %collective-permute-start.10 = (bf16[128,4,2,64]{0,3,1,2:T(8,128)(2,1)S(1)}, bf16[128,4,2,64]{0,3,1,2:T(8,128)(2,1)S(1)}, u32[]{:S(2)}, u32[]{:S(2)}) collective-permute-start(bf16[128,4,2,64]{0,3,1,2:T(8,128)(2,1)S(1)} %get-tuple-element.56), channel_id=1, source_target_pairs={{0,12},{4,0},{8,4},{12,8},{16,28},{20,16},{24,20},{28,24},{1,13},{... | collective-permute-start | bytes 393224 | tf_op jit(solution)/shard_map/ppermute | solution.py:47
  33.7 7.9 %collective-permute-start.7 = (bf16[128,4,2,64]{0,3,1,2:T(8,128)(2,1)S(1)}, bf16[128,4,2,64]{0,3,1,2:T(8,128)(2,1)S(1)}, u32[]{:S(2)}, u32[]{:S(2)}) collective-permute-start(bf16[128,4,2,64]{0,3,1,2:T(8,128)(2,1)S(1)} %collective-permute-done.5), channel_id=1, source_target_pairs={{0,4},{4,8},{8,12},{12,0},{16,20},{20,24},{24,28},{28,16},{1,5},{5... | collective-permute-start | bytes 393224 | tf_op jit(solution)/shard_map/ppermute | solution.py:48
  35.9 6.8 %collective-permute-start.9 = (bf16[128,4,2,64]{0,3,1,2:T(8,128)(2,1)S(1)}, bf16[128,4,2,64]{0,3,1,2:T(8,128)(2,1)S(1)}, u32[]{:S(2)}, u32[]{:S(2)}) collective-permute-start(bf16[128,4,2,64]{0,3,1,2:T(8,128)(2,1)S(1)} %collective-permute-done.5), channel_id=1, source_target_pairs={{0,8},{4,12},{8,0},{12,4},{16,24},{20,28},{24,16},{28,20},{1,9},{5... | collective-permute-start | bytes 393224 | tf_op jit(solution)/shard_map/ppermute | solution.py:48
  36.1 6.9 %collective-permute-start.11 = (bf16[128,4,2,64]{0,3,1,2:T(8,128)(2,1)S(1)}, bf16[128,4,2,64]{0,3,1,2:T(8,128)(2,1)S(1)}, u32[]{:S(2)}, u32[]{:S(2)}) collective-permute-start(bf16[128,4,2,64]{0,3,1,2:T(8,128)(2,1)S(1)} %collective-permute-done.5), channel_id=1, source_target_pairs={{0,12},{4,0},{8,4},{12,8},{16,28},{20,16},{24,20},{28,24},{1,13},{... | collective-permute-start | bytes 393224 | tf_op jit(solution)/shard_map/ppermute | solution.py:48
  43.4 1.1 %copy-start.1 = (bf16[256,1024]{1,0:T(8,128)(2,1)S(1)}, bf16[256,1024]{1,0:T(8,128)(2,1)}, u32[]{:S(2)}) copy-start(bf16[256,1024]{1,0:T(8,128)(2,1)} %param.9) | copy-start | bytes 1572868
  46.2 2.0 %collective-permute-start.12 = (f32[32,1024]{1,0:T(8,128)S(1)}, f32[32,1024]{1,0:T(8,128)S(1)}, u32[]{:S(2)}, u32[]{:S(2)}) collective-permute-start(f32[32,1024]{1,0:T(8,128)S(1)} %get-tuple-element.43), channel_id=1, source_target_pairs={{0,1},{1,0},{2,3},{3,2},{4,5},{5,4},{6,7},{7,6},{8,9},{9,8},{10,11... | collective-permute-start | bytes 393224 | tf_op jit(solution)/shard_map/ppermute | solution.py:218
  46.3 4.5 %collective-permute-start.13 = (bf16[1,16,2,1024]{3,2,1,0:T(2,128)(2,1)S(1)}, bf16[1,16,2,1024]{3,2,1,0:T(2,128)(2,1)S(1)}, u32[]{:S(2)}, u32[]{:S(2)}) collective-permute-start(bf16[1,16,2,1024]{3,2,1,0:T(2,128)(2,1)S(1)} %reshape.231), channel_id=1, source_target_pairs={{0,2},{1,3},{2,0},{3,1},{4,6},{5,7},{6,4},{7,5},{8,10},{9,11},{10,... | collective-permute-start | bytes 196616 | tf_op jit(solution)/shard_map/ppermute | solution.py:206
  47.9 4.0 %collective-permute-start.14 = (bf16[1,16,2,1024]{3,2,1,0:T(2,128)(2,1)S(1)}, bf16[1,16,2,1024]{3,2,1,0:T(2,128)(2,1)S(1)}, u32[]{:S(2)}, u32[]{:S(2)}) collective-permute-start(bf16[1,16,2,1024]{3,2,1,0:T(2,128)(2,1)S(1)} %reshape.232), channel_id=1, source_target_pairs={{0,3},{1,2},{2,1},{3,0},{4,7},{5,6},{6,5},{7,4},{8,11},{9,10},{10,... | collective-permute-start | bytes 196616 | tf_op jit(solution)/shard_map/ppermute | solution.py:207

commit v20 on v15

--- a/solution.py
+++ b/solution.py
@@ -3,18 +3,22 @@
 import jax
 import jax.numpy as jnp
 from jax import lax
+from jax.experimental.layout import Layout, with_layout_constraint
 from jax.sharding import PartitionSpec as P
 
 HS = 64
 
 
-def padded_2(shard, sides, width):
+def padded_2(shard, sides, width, keep=None):
     for axis, dim in sides:
         size, length = (lax.axis_size(axis), shard.shape[dim])
         up = [(i, (i + 1) % size) for i in range(size - 1)]
         down = [(j, i) for i, j in up]
         last = lax.slice_in_dim(shard, length - width, length, axis=dim)
         initial = lax.slice_in_dim(shard, 0, width, axis=dim)
+        if keep is not None:
+            last = with_layout_constraint(last, keep)
+            initial = with_layout_constraint(initial, keep)
         before = lax.ppermute(last, axis, up)
         after = lax.ppermute(initial, axis, down)
         shard = jnp.concatenate([before, shard, after], axis=dim)
@@ -105,7 +109,8 @@
 def on_device(tokens, conv_weight, conv_bias, qkv_weight, out_weight):
     z_count, x_count, y_count, features = tokens.shape
     groups = lax.axis_size("uly")
-    with_halo = padded_2(tokens, (("blk", 0),), 1)
+    arrival = Layout(major_to_minor=tuple(range(tokens.ndim)))
+    with_halo = padded_2(tokens, (("blk", 0),), 1, arrival if y_count == 2 else None)
     slab_in = gathered_by_chip(with_halo, "uly")
     slab_in = slab_in.transpose(1, 2, 0, 3, 4).reshape(
         z_count + 2, x_count, groups * y_count, features

time: 52.3 us -> 51.8 us (level)
  local copies, waits for them, and re-layouts: 8.44 us -> 7.69 us
    unnamed x16 -> x15, local copies, waits for them, and re-layouts: 4.1 us -> 3.2 us
where the time goes in v20:
time: 51.8 us; the launch traced here: 51.3 us
  starting transfers between devices  21.1 us (41%)
  waiting for transfers between devices  15.8 us (31%)
  local copies, waits for them, and re-layouts  7.69 us (15%)
  other arithmetic  3.71 us (7%)
  matrix products  2.52 us (5%)
    ppermute x1, waiting for transfers between devices, gathered_by_chip(): far = lax.ppermute(piece, axis, chip_shift(size, shift))  5.55 us
    ppermute x1, starting transfers between devices, padded_2(): before = lax.ppermute(last, axis, up)  5 us
    ppermute x3, starting transfers between devices, relayed(): parts.append(lax.ppermute(piece, axis, pairs))  4.5 us
    ppermute x3, waiting for transfers between devices, relayed(): parts.append(lax.ppermute(crossed, axis, pairs))  3.47 us
    ppermute x3, starting transfers between devices, relayed(): parts.append(lax.ppermute(crossed, axis, pairs))  3.46 us
    unnamed x15, local copies, waits for them, and re-layouts  3.2 us
    ppermute x1, starting transfers between devices, relayed(): crossed = lax.ppermute(piece, axis, mirror)  2.99 us
    convert_element_type x1, other arithmetic, on_device(): positioned = summed.astype(jnp.bfloat16)  2.34 us
  transfers between devices with their start and end apart: 15, of which 9 were waited for; matrix products, arithmetic and copies ran while one was open for 15% of the time, Pallas kernels for 0%

profile of v20, /device:TPU:0, one launch (start us, length us, event | category | flops | bytes accessed | tf_op | source)
XLA Modules:
  0.0 51.3 jit_solution(4858407095759615911)
XLA Ops:
  0.0 5.0 %collective-permute-start = (bf16[1,16,2,1024]{3,2,1,0:T(2,128)(2,1)}, bf16[1,16,2,1024]{3,2,1,0:T(2,128)(2,1)S(1)}, u32[]{:S(2)}, u32[]{:S(2)}) collective-permute-start(bf16[1,16,2,1024]{3,2,1,0:T(2,128)(2,1)} %param.5), channel_id=1, source_target_pairs={{0,4},{4,8},{8,12},{12,16},{16,20},{20,24},{24,28},{1,5},{5,9},{9,... | collective-permute-start | bytes 196616 | tf_op jit(solution)/shard_map/ppermute | solution.py:22
  5.0 1.3 %collective-permute-start.1 = (bf16[1,16,2,1024]{3,2,1,0:T(2,128)(2,1)}, bf16[1,16,2,1024]{3,2,1,0:T(2,128)(2,1)S(1)}, u32[]{:S(2)}, u32[]{:S(2)}) collective-permute-start(bf16[1,16,2,1024]{3,2,1,0:T(2,128)(2,1)} %param.5), channel_id=1, source_target_pairs={{4,0},{8,4},{12,8},{16,12},{20,16},{24,20},{28,24},{5,1},{9,5},{13... | collective-permute-start | bytes 196616 | tf_op jit(solution)/shard_map/ppermute | solution.py:23
  6.3 1.3 %fusion.42 = (f32[1,1024]{1,0:T(1,128)S(1)}, f32[1,1024]{1,0:T(1,128)S(1)}, f32[1,1024]{1,0:T(1,128)S(1)}, f32[1,1024]{1,0:T(1,128)S(1)}, f32[1,1024]{1,0:T(1,12...) fusion(f32[27,1024]{1,0:T(8,128)} %param.6), kind=kLoop, calls=%fused_computation.103 | loop fusion | bytes 155648 | tf_op jit(solution)/shard_map/slice | solution.py:126
  7.6 1.0 %fusion.43 = (f32[1,1024]{1,0:T(1,128)S(1)}, f32[1,1024]{1,0:T(1,128)S(1)}, f32[1,1024]{1,0:T(1,128)S(1)}, f32[1,1024]{1,0:T(1,128)S(1)}, f32[1,1024]{1,0:T(1,12...) fusion(f32[27,1024]{1,0:T(8,128)} %param.6), kind=kLoop, calls=%fused_computation.104 | loop fusion | bytes 65536 | tf_op jit(solution)/shard_map/slice | solution.py:126
  8.8 0.9 %constant_dynamic-update-slice_fusion.1 = bf16[3,16,2,1024]{3,2,1,0:T(2,128)(2,1)S(1)} fusion(bf16[3,16,2,1024]{3,2,1,0:T(2,128)(2,1)S(1)} %constant_dynamic-update-slice_fusion.2, bf16[1,16,2,1024]{3,2,1,0:T(2,128)(2,1)} %param.5), kind=kLoop, calls=%fused_computation.88 | loop fusion | bytes 131072
  9.7 1.7 %collective-permute-done.1 = bf16[1,16,2,1024]{3,2,1,0:T(2,128)(2,1)S(1)} collective-permute-done((bf16[1,16,2,1024]{3,2,1,0:T(2,128)(2,1)}, bf16[1,16,2,1024]{3,2,1,0:T(2,128)(2,1)S(1)}, u32[]{:S(2)}, u32[]{:S(2)}) %collective-permute-start.1) | collective-permute-done | bytes 65568 | tf_op jit(solution)/shard_map/ppermute | solution.py:23
  11.4 0.1 constant_dynamic-update-slice_fusion
  11.4 0.1 collective-permute-start.2
  11.5 1.6 %collective-permute-start.3 = (bf16[3,16,2,1024]{3,2,1,0:T(2,128)(2,1)S(1)}, bf16[3,16,2,1024]{3,2,1,0:T(2,128)(2,1)S(1)}, u32[]{:S(2)}, u32[]{:S(2)}) collective-permute-start(bf16[3,16,2,1024]{3,2,1,0:T(2,128)(2,1)S(1)} %constant_dynamic-update-slice_fusion), channel_id=1, source_target_pairs={{0,2},{1,3},{2,0},{3,1},{4,6},{5,7},{6,4},{7,5},{8,10},{9,11},{10,... | collective-permute-start | bytes 589832 | tf_op jit(solution)/shard_map/ppermute | solution.py:68
  13.1 0.1 broadcast_in_dim.21
  13.2 0.0 copy-start.2
  13.2 0.0 collective-permute-done.2
  13.3 5.5 %collective-permute-done.3 = bf16[3,16,2,1024]{3,2,1,0:T(2,128)(2,1)S(1)} collective-permute-done((bf16[3,16,2,1024]{3,2,1,0:T(2,128)(2,1)S(1)}, bf16[3,16,2,1024]{3,2,1,0:T(2,128)(2,1)S(1)}, u32[]{:S(2)}, u32[]{:S(2)}) %collective-permute-start.3) | collective-permute-done | bytes 196640 | tf_op jit(solution)/shard_map/ppermute | solution.py:68
  18.8 0.0 collective-permute-start.4
  18.9 1.4 %collective-permute-done.4 = bf16[3,16,2,1024]{3,2,1,0:T(2,128)(2,1)S(1)} collective-permute-done((bf16[3,16,2,1024]{3,2,1,0:T(2,128)(2,1)S(1)}, bf16[3,16,2,1024]{3,2,1,0:T(2,128)(2,1)S(1)}, u32[]{:S(2)}, u32[]{:S(2)}) %collective-permute-start.4) | collective-permute-done | bytes 196640 | tf_op jit(solution)/shard_map/ppermute | solution.py:70
  20.3 0.1 fusion.40
  20.4 2.3 %add_convert_fusion = bf16[1,16,8,1024]{3,1,2,0:T(8,128)(2,1)S(1)} fusion(bf16[1,16,8,1024]{3,1,2,0:T(8,128)(2,1)S(1)} %bitcast.105, bf16[1,16,8,1024]{3,1,2,0:T(8,128)(2,1)S(1)} %bitcast.104, bf16[1,16,8,1024]{3,1,2,0:T(8,128)(2,1)S(1)} %bitcast.103, bf16[3,16,8,1024]{3,1,2,0:T(8,128)(2,1)S(1)} %bitcast.100, f32[1024]{0:T(1024)S(1)} %bitcast.139, ...), kind=kLoop, calls=%fused_computation.75 | loop fusion | flops 10878976 | bytes 1949696 | tf_op jit(solution)/shard_map/convert_element_type | solution.py:133
  22.8 0.3 copy.38
  23.0 0.1 reshape.226
  23.2 0.7 %convolution_convert_fusion = bf16[128,768]{1,0:T(8,128)(2,1)S(1)} fusion(bf16[128,1024]{1,0:T(8,128)(2,1)S(1)} %reshape.226, bf16[768,1024]{1,0:T(8,128)(2,1)S(1)} %copy-done), kind=kOutput, calls=%fused_computation.26 | convolution fusion | flops 201424896 | bytes 2031616 | tf_op jit(solution)/shard_map/dot_general | solution.py:104
  23.8 0.2 copy.24
  24.0 3.0 %collective-permute-start.5 = (bf16[128,4,2,64]{0,3,1,2:T(8,128)(2,1)S(1)}, bf16[128,4,2,64]{0,3,1,2:T(8,128)(2,1)S(1)}, u32[]{:S(2)}, u32[]{:S(2)}) collective-permute-start(bf16[128,4,2,64]{0,3,1,2:T(8,128)(2,1)S(1)} %get-tuple-element.16), channel_id=1, source_target_pairs={{0,16},{4,20},{8,24},{12,28},{16,0},{20,4},{24,8},{28,12},{1,17},{... | collective-permute-start | bytes 393224 | tf_op jit(solution)/shard_map/ppermute | solution.py:43
  27.0 2.1 %collective-permute-start.6 = (bf16[128,4,2,64]{0,3,1,2:T(8,128)(2,1)S(1)}, bf16[128,4,2,64]{0,3,1,2:T(8,128)(2,1)}, u32[]{:S(2)}, u32[]{:S(2)}) collective-permute-start(bf16[128,4,2,64]{0,3,1,2:T(8,128)(2,1)S(1)} %get-tuple-element.16), channel_id=1, source_target_pairs={{0,4},{4,8},{8,12},{12,0},{16,20},{20,24},{24,28},{28,16},{1,5},{5... | collective-permute-start | bytes 393224 | tf_op jit(solution)/shard_map/ppermute | solution.py:47
  29.1 0.1 collective-permute-start.8
  29.2 2.3 %collective-permute-start.10 = (bf16[128,4,2,64]{0,3,1,2:T(8,128)(2,1)S(1)}, bf16[128,4,2,64]{0,3,1,2:T(8,128)(2,1)S(1)}, u32[]{:S(2)}, u32[]{:S(2)}) collective-permute-start(bf16[128,4,2,64]{0,3,1,2:T(8,128)(2,1)S(1)} %get-tuple-element.16), channel_id=1, source_target_pairs={{0,12},{4,0},{8,4},{12,8},{16,28},{20,16},{24,20},{28,24},{1,13},{... | collective-permute-start | bytes 393224 | tf_op jit(solution)/shard_map/ppermute | solution.py:47
  31.5 0.1 reshape_squeeze.3
  31.6 0.3 constant_dynamic-slice_fusion.2
  31.9 0.1 copy.26
  32.0 0.1 copy.25
  32.2 1.6 %collective-permute-done.5 = bf16[128,4,2,64]{0,3,1,2:T(8,128)(2,1)S(1)} collective-permute-done((bf16[128,4,2,64]{0,3,1,2:T(8,128)(2,1)S(1)}, bf16[128,4,2,64]{0,3,1,2:T(8,128)(2,1)S(1)}, u32[]{:S(2)}, u32[]{:S(2)}) %collective-permute-start.5) | collective-permute-done | bytes 131104 | tf_op jit(solution)/shard_map/ppermute | solution.py:43
  33.7 2.1 %collective-permute-start.7 = (bf16[128,4,2,64]{0,3,1,2:T(8,128)(2,1)S(1)}, bf16[128,4,2,64]{0,3,1,2:T(8,128)(2,1)S(1)}, u32[]{:S(2)}, u32[]{:S(2)}) collective-permute-start(bf16[128,4,2,64]{0,3,1,2:T(8,128)(2,1)S(1)} %collective-permute-done.5), channel_id=1, source_target_pairs={{0,4},{4,8},{8,12},{12,0},{16,20},{20,24},{24,28},{28,16},{1,5},{5... | collective-permute-start | bytes 393224 | tf_op jit(solution)/shard_map/ppermute | solution.py:48
  35.9 0.2 collective-permute-done.6
  36.1 1.3 %collective-permute-start.11 = (bf16[128,4,2,64]{0,3,1,2:T(8,128)(2,1)S(1)}, bf16[128,4,2,64]{0,3,1,2:T(8,128)(2,1)S(1)}, u32[]{:S(2)}, u32[]{:S(2)}) collective-permute-start(bf16[128,4,2,64]{0,3,1,2:T(8,128)(2,1)S(1)} %collective-permute-done.5), channel_id=1, source_target_pairs={{0,12},{4,0},{8,4},{12,8},{16,28},{20,16},{24,20},{28,24},{1,13},{... | collective-permute-start | bytes 393224 | tf_op jit(solution)/shard_map/ppermute | solution.py:48
  37.4 0.9 %constant_dynamic-update-slice_fusion.8 = bf16[1024,4,2,64]{0,3,1,2:T(8,128)(2,1)S(1)} fusion(bf16[1024,4,2,64]{0,3,1,2:T(8,128)(2,1)S(1)} %constant_dynamic-update-slice_fusion.9, bf16[128,4,2,64]{0,3,1,2:T(8,128)(2,1)} %collective-permute-done.6), kind=kLoop, calls=%fused_computation.95 | loop fusion | bytes 262144
  38.4 3.3 %collective-permute-done.7 = bf16[128,4,2,64]{0,3,1,2:T(8,128)(2,1)S(1)} collective-permute-done((bf16[128,4,2,64]{0,3,1,2:T(8,128)(2,1)S(1)}, bf16[128,4,2,64]{0,3,1,2:T(8,128)(2,1)S(1)}, u32[]{:S(2)}, u32[]{:S(2)}) %collective-permute-start.7) | collective-permute-done | bytes 131104 | tf_op jit(solution)/shard_map/ppermute | solution.py:48
  41.7 0.0 collective-permute-done.8
  41.7 0.9 %constant_dynamic-update-slice_fusion.6 = bf16[1024,4,2,64]{0,3,1,2:T(8,128)(2,1)S(1)} fusion(bf16[1024,4,2,64]{0,3,1,2:T(8,128)(2,1)S(1)} %constant_dynamic-update-slice_fusion.7, bf16[128,4,2,64]{0,3,1,2:T(8,128)(2,1)} %collective-permute-done.8), kind=kLoop, calls=%fused_computation.93 | loop fusion | bytes 262144
  42.7 0.0 collective-permute-done.9
  42.7 0.0 collective-permute-done.10
  42.8 0.2 collective-permute-done.11
  43.0 0.4 fusion.44
  43.4 0.0 copy-start.1
  43.4 0.3 fusion.4
  43.7 0.4 fusion.3
  44.1 0.1 copy.28
  44.1 0.1 reshape.228
  44.2 0.2 copy-done.1
  44.4 0.2 convolution_convert_fusion.1
  44.7 1.6 %collective-permute-start.13 = (bf16[32,1024]{1,0:T(8,128)(2,1)S(1)}, bf16[32,1024]{1,0:T(8,128)(2,1)S(1)}, u32[]{:S(2)}, u32[]{:S(2)}) collective-permute-start(bf16[32,1024]{1,0:T(8,128)(2,1)S(1)} %get-tuple-element.14), channel_id=1, source_target_pairs={{0,2},{1,3},{2,0},{3,1},{4,6},{5,7},{6,4},{7,5},{8,10},{9,11},{10,... | collective-permute-start | bytes 196616 | tf_op jit(solution)/shard_map/ppermute | solution.py:222
  46.2 0.0 collective-permute-start.14
  46.2 0.4 fusion.45
  46.6 0.3 fusion.6
  46.9 0.4 fusion.2
  47.3 0.1 copy.29
  47.3 0.1 dot_general.35
  47.4 0.2 fusion.35
  47.7 0.7 %collective-permute-start.12 = (f32[32,1024]{1,0:T(8,128)S(1)}, f32[32,1024]{1,0:T(8,128)S(1)}, u32[]{:S(2)}, u32[]{:S(2)}) collective-permute-start(f32[32,1024]{1,0:T(8,128)S(1)} %get-tuple-element.10), channel_id=1, source_target_pairs={{0,1},{1,0},{2,3},{3,2},{4,5},{5,4},{6,7},{7,6},{8,9},{9,8},{10,11... | collective-permute-start | bytes 393224 | tf_op jit(solution)/shard_map/ppermute | solution.py:234
  48.4 0.1 reshape.230
  48.5 0.5 %collective-permute-done.13 = bf16[32,1024]{1,0:T(8,128)(2,1)S(1)} collective-permute-done((bf16[32,1024]{1,0:T(8,128)(2,1)S(1)}, bf16[32,1024]{1,0:T(8,128)(2,1)S(1)}, u32[]{:S(2)}, u32[]{:S(2)}) %collective-permute-start.13) | collective-permute-done | bytes 65568 | tf_op jit(solution)/shard_map/ppermute | solution.py:222
  49.0 1.4 %collective-permute-done.14 = bf16[32,1024]{1,0:T(8,128)(2,1)S(1)} collective-permute-done((bf16[32,1024]{1,0:T(8,128)(2,1)S(1)}, bf16[32,1024]{1,0:T(8,128)(2,1)S(1)}, u32[]{:S(2)}, u32[]{:S(2)}) %collective-permute-start.14) | collective-permute-done | bytes 65568 | tf_op jit(solution)/shard_map/ppermute | solution.py:223
  50.4 0.1 add.233
  50.5 0.0 collective-permute-done.12
  50.5 0.1 reshape.231
  50.6 0.7 %add_convert_fusion.1 = bf16[1,16,2,1024]{3,2,1,0:T(2,128)(2,1)} fusion(f32[1,16,2,1024]{3,2,1,0:T(2,128)S(1)} %add.233, f32[1,16,2,1024]{3,2,1,0:T(2,128)S(1)} %reshape.230, f32[1,16,2,1024]{3,2,1,0:T(2,128)S(1)} %reshape.231), kind=kLoop, calls=%fused_computation.81 | loop fusion | flops 98304 | bytes 458752 | tf_op jit(solution)/shard_map/convert_element_type | solution.py:237
  (20 shorter events, 0.5 us)
Async XLA Ops:
  0.0 23.1 %copy-start = (bf16[768,1024]{1,0:T(8,128)(2,1)S(1)}, bf16[768,1024]{1,0:T(8,128)(2,1)}, u32[]{:S(2)}) copy-start(bf16[768,1024]{1,0:T(8,128)(2,1)} %param.8) | copy-start | bytes 4718596
  0.0 8.7 %collective-permute-start = (bf16[1,16,2,1024]{3,2,1,0:T(2,128)(2,1)}, bf16[1,16,2,1024]{3,2,1,0:T(2,128)(2,1)S(1)}, u32[]{:S(2)}, u32[]{:S(2)}) collective-permute-start(bf16[1,16,2,1024]{3,2,1,0:T(2,128)(2,1)} %param.5), channel_id=1, source_target_pairs={{0,4},{4,8},{8,12},{12,16},{16,20},{20,24},{24,28},{1,5},{5,9},{9,... | collective-permute-start | bytes 196616 | tf_op jit(solution)/shard_map/ppermute | solution.py:22
  5.0 6.4 %collective-permute-start.1 = (bf16[1,16,2,1024]{3,2,1,0:T(2,128)(2,1)}, bf16[1,16,2,1024]{3,2,1,0:T(2,128)(2,1)S(1)}, u32[]{:S(2)}, u32[]{:S(2)}) collective-permute-start(bf16[1,16,2,1024]{3,2,1,0:T(2,128)(2,1)} %param.5), channel_id=1, source_target_pairs={{4,0},{8,4},{12,8},{16,12},{20,16},{24,20},{28,24},{5,1},{9,5},{13... | collective-permute-start | bytes 196616 | tf_op jit(solution)/shard_map/ppermute | solution.py:23
  11.4 1.8 %collective-permute-start.2 = (bf16[3,16,2,1024]{3,2,1,0:T(2,128)(2,1)S(1)}, bf16[3,16,2,1024]{3,2,1,0:T(2,128)(2,1)S(1)}, u32[]{:S(2)}, u32[]{:S(2)}) collective-permute-start(bf16[3,16,2,1024]{3,2,1,0:T(2,128)(2,1)S(1)} %constant_dynamic-update-slice_fusion), channel_id=1, source_target_pairs={{0,1},{1,0},{2,3},{3,2},{4,5},{5,4},{6,7},{7,6},{8,9},{9,8},{10,11... | collective-permute-start | bytes 589832 | tf_op jit(solution)/shard_map/ppermute | solution.py:64
  11.5 7.3 %collective-permute-start.3 = (bf16[3,16,2,1024]{3,2,1,0:T(2,128)(2,1)S(1)}, bf16[3,16,2,1024]{3,2,1,0:T(2,128)(2,1)S(1)}, u32[]{:S(2)}, u32[]{:S(2)}) collective-permute-start(bf16[3,16,2,1024]{3,2,1,0:T(2,128)(2,1)S(1)} %constant_dynamic-update-slice_fusion), channel_id=1, source_target_pairs={{0,2},{1,3},{2,0},{3,1},{4,6},{5,7},{6,4},{7,5},{8,10},{9,11},{10,... | collective-permute-start | bytes 589832 | tf_op jit(solution)/shard_map/ppermute | solution.py:68
  13.2 7.2 %copy-start.2 = (f32[1024]{0:T(1024)S(1)}, f32[1024]{0:T(1024)}, u32[]{:S(2)}) copy-start(f32[1024]{0:T(1024)} %param.7) | copy-start | bytes 12292
  18.8 1.4 %collective-permute-start.4 = (bf16[3,16,2,1024]{3,2,1,0:T(2,128)(2,1)S(1)}, bf16[3,16,2,1024]{3,2,1,0:T(2,128)(2,1)S(1)}, u32[]{:S(2)}, u32[]{:S(2)}) collective-permute-start(bf16[3,16,2,1024]{3,2,1,0:T(2,128)(2,1)S(1)} %collective-permute-done.3), channel_id=1, source_target_pairs={{0,1},{1,0},{2,3},{3,2},{4,5},{5,4},{6,7},{7,6},{8,9},{9,8},{10,11... | collective-permute-start | bytes 589832 | tf_op jit(solution)/shard_map/ppermute | solution.py:70
  24.0 9.7 %collective-permute-start.5 = (bf16[128,4,2,64]{0,3,1,2:T(8,128)(2,1)S(1)}, bf16[128,4,2,64]{0,3,1,2:T(8,128)(2,1)S(1)}, u32[]{:S(2)}, u32[]{:S(2)}) collective-permute-start(bf16[128,4,2,64]{0,3,1,2:T(8,128)(2,1)S(1)} %get-tuple-element.16), channel_id=1, source_target_pairs={{0,16},{4,20},{8,24},{12,28},{16,0},{20,4},{24,8},{28,12},{1,17},{... | collective-permute-start | bytes 393224 | tf_op jit(solution)/shard_map/ppermute | solution.py:43
  27.0 9.1 %collective-permute-start.6 = (bf16[128,4,2,64]{0,3,1,2:T(8,128)(2,1)S(1)}, bf16[128,4,2,64]{0,3,1,2:T(8,128)(2,1)}, u32[]{:S(2)}, u32[]{:S(2)}) collective-permute-start(bf16[128,4,2,64]{0,3,1,2:T(8,128)(2,1)S(1)} %get-tuple-element.16), channel_id=1, source_target_pairs={{0,4},{4,8},{8,12},{12,0},{16,20},{20,24},{24,28},{28,16},{1,5},{5... | collective-permute-start | bytes 393224 | tf_op jit(solution)/shard_map/ppermute | solution.py:47
  29.1 12.6 %collective-permute-start.8 = (bf16[128,4,2,64]{0,3,1,2:T(8,128)(2,1)S(1)}, bf16[128,4,2,64]{0,3,1,2:T(8,128)(2,1)}, u32[]{:S(2)}, u32[]{:S(2)}) collective-permute-start(bf16[128,4,2,64]{0,3,1,2:T(8,128)(2,1)S(1)} %get-tuple-element.16), channel_id=1, source_target_pairs={{0,8},{4,12},{8,0},{12,4},{16,24},{20,28},{24,16},{28,20},{1,9},{5... | collective-permute-start | bytes 393224 | tf_op jit(solution)/shard_map/ppermute | solution.py:47
  29.2 13.5 %collective-permute-start.10 = (bf16[128,4,2,64]{0,3,1,2:T(8,128)(2,1)S(1)}, bf16[128,4,2,64]{0,3,1,2:T(8,128)(2,1)S(1)}, u32[]{:S(2)}, u32[]{:S(2)}) collective-permute-start(bf16[128,4,2,64]{0,3,1,2:T(8,128)(2,1)S(1)} %get-tuple-element.16), channel_id=1, source_target_pairs={{0,12},{4,0},{8,4},{12,8},{16,28},{20,16},{24,20},{28,24},{1,13},{... | collective-permute-start | bytes 393224 | tf_op jit(solution)/shard_map/ppermute | solution.py:47
  33.7 7.9 %collective-permute-start.7 = (bf16[128,4,2,64]{0,3,1,2:T(8,128)(2,1)S(1)}, bf16[128,4,2,64]{0,3,1,2:T(8,128)(2,1)S(1)}, u32[]{:S(2)}, u32[]{:S(2)}) collective-permute-start(bf16[128,4,2,64]{0,3,1,2:T(8,128)(2,1)S(1)} %collective-permute-done.5), channel_id=1, source_target_pairs={{0,4},{4,8},{8,12},{12,0},{16,20},{20,24},{24,28},{28,16},{1,5},{5... | collective-permute-start | bytes 393224 | tf_op jit(solution)/shard_map/ppermute | solution.py:48
  35.9 6.8 %collective-permute-start.9 = (bf16[128,4,2,64]{0,3,1,2:T(8,128)(2,1)S(1)}, bf16[128,4,2,64]{0,3,1,2:T(8,128)(2,1)S(1)}, u32[]{:S(2)}, u32[]{:S(2)}) collective-permute-start(bf16[128,4,2,64]{0,3,1,2:T(8,128)(2,1)S(1)} %collective-permute-done.5), channel_id=1, source_target_pairs={{0,8},{4,12},{8,0},{12,4},{16,24},{20,28},{24,16},{28,20},{1,9},{5... | collective-permute-start | bytes 393224 | tf_op jit(solution)/shard_map/ppermute | solution.py:48
  36.1 6.9 %collective-permute-start.11 = (bf16[128,4,2,64]{0,3,1,2:T(8,128)(2,1)S(1)}, bf16[128,4,2,64]{0,3,1,2:T(8,128)(2,1)S(1)}, u32[]{:S(2)}, u32[]{:S(2)}) collective-permute-start(bf16[128,4,2,64]{0,3,1,2:T(8,128)(2,1)S(1)} %collective-permute-done.5), channel_id=1, source_target_pairs={{0,12},{4,0},{8,4},{12,8},{16,28},{20,16},{24,20},{28,24},{1,13},{... | collective-permute-start | bytes 393224 | tf_op jit(solution)/shard_map/ppermute | solution.py:48
  43.4 1.0 %copy-start.1 = (bf16[256,1024]{1,0:T(8,128)(2,1)S(1)}, bf16[256,1024]{1,0:T(8,128)(2,1)}, u32[]{:S(2)}) copy-start(bf16[256,1024]{1,0:T(8,128)(2,1)} %param.9) | copy-start | bytes 1572868
  44.7 4.3 %collective-permute-start.13 = (bf16[32,1024]{1,0:T(8,128)(2,1)S(1)}, bf16[32,1024]{1,0:T(8,128)(2,1)S(1)}, u32[]{:S(2)}, u32[]{:S(2)}) collective-permute-start(bf16[32,1024]{1,0:T(8,128)(2,1)S(1)} %get-tuple-element.14), channel_id=1, source_target_pairs={{0,2},{1,3},{2,0},{3,1},{4,6},{5,7},{6,4},{7,5},{8,10},{9,11},{10,... | collective-permute-start | bytes 196616 | tf_op jit(solution)/shard_map/ppermute | solution.py:222
  46.2 4.2 %collective-permute-start.14 = (bf16[32,1024]{1,0:T(8,128)(2,1)S(1)}, bf16[32,1024]{1,0:T(8,128)(2,1)S(1)}, u32[]{:S(2)}, u32[]{:S(2)}) collective-permute-start(bf16[32,1024]{1,0:T(8,128)(2,1)S(1)} %get-tuple-element.15), channel_id=1, source_target_pairs={{0,3},{1,2},{2,1},{3,0},{4,7},{5,6},{6,5},{7,4},{8,11},{9,10},{10,... | collective-permute-start | bytes 196616 | tf_op jit(solution)/shard_map/ppermute | solution.py:223
  47.7 2.8 %collective-permute-start.12 = (f32[32,1024]{1,0:T(8,128)S(1)}, f32[32,1024]{1,0:T(8,128)S(1)}, u32[]{:S(2)}, u32[]{:S(2)}) collective-permute-start(f32[32,1024]{1,0:T(8,128)S(1)} %get-tuple-element.10), channel_id=1, source_target_pairs={{0,1},{1,0},{2,3},{3,2},{4,5},{5,4},{6,7},{7,6},{8,9},{9,8},{10,11... | collective-permute-start | bytes 393224 | tf_op jit(solution)/shard_map/ppermute | solution.py:234

commit v21 on v20

--- a/solution.py
+++ b/solution.py
@@ -140,6 +140,7 @@
     )
     slab_tok = slab_rows.shape[0]
     projected = times_transposed(slab_rows, qkv_weight).astype(jnp.bfloat16)
+    projected = with_layout_constraint(projected, Layout(major_to_minor=(1, 0)))
     split_heads = projected.reshape(slab_tok, heads_here, 3, HS)
     queries = split_heads[:, :, 0]
     key_value = relayed(split_heads[:, :, 1:], "blk")

time: 51.8 us -> 51.5 us (level)
    unnamed x15 -> x17, local copies, waits for them, and re-layouts: 3.2 us -> 3.43 us
where the time goes in v21:
time: 51.5 us; the launch traced here: 51.1 us
  starting transfers between devices  21.2 us (41%)
  waiting for transfers between devices  15.8 us (31%)
  local copies, waits for them, and re-layouts  7.53 us (15%)
  other arithmetic  3.71 us (7%)
  matrix products  2.44 us (5%)
    ppermute x1, waiting for transfers between devices, gathered_by_chip(): far = lax.ppermute(piece, axis, chip_shift(size, shift))  5.55 us
    ppermute x1, starting transfers between devices, padded_2(): before = lax.ppermute(last, axis, up)  5 us
    ppermute x3, starting transfers between devices, relayed(): parts.append(lax.ppermute(piece, axis, pairs))  4.5 us
    ppermute x3, waiting for transfers between devices, relayed(): parts.append(lax.ppermute(crossed, axis, pairs))  3.47 us
    ppermute x3, starting transfers between devices, relayed(): parts.append(lax.ppermute(crossed, axis, pairs))  3.46 us
    unnamed x17, local copies, waits for them, and re-layouts  3.43 us
    ppermute x1, starting transfers between devices, relayed(): crossed = lax.ppermute(piece, axis, mirror)  2.98 us
    convert_element_type x1, other arithmetic, on_device(): positioned = summed.astype(jnp.bfloat16)  2.34 us
  transfers between devices with their start and end apart: 15, of which 9 were waited for; matrix products, arithmetic and copies ran while one was open for 15% of the time, Pallas kernels for 0%

profile of v21, /device:TPU:0, one launch (start us, length us, event | category | flops | bytes accessed | tf_op | source)
XLA Modules:
  0.0 51.1 jit_solution(7465347964695892805)
XLA Ops:
  0.0 5.0 %collective-permute-start = (bf16[1,16,2,1024]{3,2,1,0:T(2,128)(2,1)}, bf16[1,16,2,1024]{3,2,1,0:T(2,128)(2,1)S(1)}, u32[]{:S(2)}, u32[]{:S(2)}) collective-permute-start(bf16[1,16,2,1024]{3,2,1,0:T(2,128)(2,1)} %param.5), channel_id=1, source_target_pairs={{0,4},{4,8},{8,12},{12,16},{16,20},{20,24},{24,28},{1,5},{5,9},{9,... | collective-permute-start | bytes 196616 | tf_op jit(solution)/shard_map/ppermute | solution.py:22
  5.0 1.3 %collective-permute-start.1 = (bf16[1,16,2,1024]{3,2,1,0:T(2,128)(2,1)}, bf16[1,16,2,1024]{3,2,1,0:T(2,128)(2,1)S(1)}, u32[]{:S(2)}, u32[]{:S(2)}) collective-permute-start(bf16[1,16,2,1024]{3,2,1,0:T(2,128)(2,1)} %param.5), channel_id=1, source_target_pairs={{4,0},{8,4},{12,8},{16,12},{20,16},{24,20},{28,24},{5,1},{9,5},{13... | collective-permute-start | bytes 196616 | tf_op jit(solution)/shard_map/ppermute | solution.py:23
  6.3 1.3 %fusion.42 = (f32[1,1024]{1,0:T(1,128)S(1)}, f32[1,1024]{1,0:T(1,128)S(1)}, f32[1,1024]{1,0:T(1,128)S(1)}, f32[1,1024]{1,0:T(1,128)S(1)}, f32[1,1024]{1,0:T(1,12...) fusion(f32[27,1024]{1,0:T(8,128)} %param.6), kind=kLoop, calls=%fused_computation.103 | loop fusion | bytes 155648 | tf_op jit(solution)/shard_map/slice | solution.py:126
  7.6 1.0 %fusion.43 = (f32[1,1024]{1,0:T(1,128)S(1)}, f32[1,1024]{1,0:T(1,128)S(1)}, f32[1,1024]{1,0:T(1,128)S(1)}, f32[1,1024]{1,0:T(1,128)S(1)}, f32[1,1024]{1,0:T(1,12...) fusion(f32[27,1024]{1,0:T(8,128)} %param.6), kind=kLoop, calls=%fused_computation.104 | loop fusion | bytes 65536 | tf_op jit(solution)/shard_map/slice | solution.py:126
  8.7 0.0 collective-permute-done
  8.8 0.9 %constant_dynamic-update-slice_fusion.1 = bf16[3,16,2,1024]{3,2,1,0:T(2,128)(2,1)S(1)} fusion(bf16[3,16,2,1024]{3,2,1,0:T(2,128)(2,1)S(1)} %constant_dynamic-update-slice_fusion.2, bf16[1,16,2,1024]{3,2,1,0:T(2,128)(2,1)} %param.5), kind=kLoop, calls=%fused_computation.88 | loop fusion | bytes 131072
  9.7 1.7 %collective-permute-done.1 = bf16[1,16,2,1024]{3,2,1,0:T(2,128)(2,1)S(1)} collective-permute-done((bf16[1,16,2,1024]{3,2,1,0:T(2,128)(2,1)}, bf16[1,16,2,1024]{3,2,1,0:T(2,128)(2,1)S(1)}, u32[]{:S(2)}, u32[]{:S(2)}) %collective-permute-start.1) | collective-permute-done | bytes 65568 | tf_op jit(solution)/shard_map/ppermute | solution.py:23
  11.4 0.1 constant_dynamic-update-slice_fusion
  11.4 0.1 collective-permute-start.2
  11.5 1.6 %collective-permute-start.3 = (bf16[3,16,2,1024]{3,2,1,0:T(2,128)(2,1)S(1)}, bf16[3,16,2,1024]{3,2,1,0:T(2,128)(2,1)S(1)}, u32[]{:S(2)}, u32[]{:S(2)}) collective-permute-start(bf16[3,16,2,1024]{3,2,1,0:T(2,128)(2,1)S(1)} %constant_dynamic-update-slice_fusion), channel_id=1, source_target_pairs={{0,2},{1,3},{2,0},{3,1},{4,6},{5,7},{6,4},{7,5},{8,10},{9,11},{10,... | collective-permute-start | bytes 589832 | tf_op jit(solution)/shard_map/ppermute | solution.py:68
  13.1 0.1 broadcast_in_dim.21
  13.2 0.0 copy-start.2
  13.2 0.0 collective-permute-done.2
  13.3 5.5 %collective-permute-done.3 = bf16[3,16,2,1024]{3,2,1,0:T(2,128)(2,1)S(1)} collective-permute-done((bf16[3,16,2,1024]{3,2,1,0:T(2,128)(2,1)S(1)}, bf16[3,16,2,1024]{3,2,1,0:T(2,128)(2,1)S(1)}, u32[]{:S(2)}, u32[]{:S(2)}) %collective-permute-start.3) | collective-permute-done | bytes 196640 | tf_op jit(solution)/shard_map/ppermute | solution.py:68
  18.8 0.0 collective-permute-start.4
  18.9 1.4 %collective-permute-done.4 = bf16[3,16,2,1024]{3,2,1,0:T(2,128)(2,1)S(1)} collective-permute-done((bf16[3,16,2,1024]{3,2,1,0:T(2,128)(2,1)S(1)}, bf16[3,16,2,1024]{3,2,1,0:T(2,128)(2,1)S(1)}, u32[]{:S(2)}, u32[]{:S(2)}) %collective-permute-start.4) | collective-permute-done | bytes 196640 | tf_op jit(solution)/shard_map/ppermute | solution.py:70
  20.3 0.1 fusion.40
  20.4 2.3 %add_convert_fusion = bf16[1,16,8,1024]{3,1,2,0:T(8,128)(2,1)S(1)} fusion(bf16[1,16,8,1024]{3,1,2,0:T(8,128)(2,1)S(1)} %bitcast.105, bf16[1,16,8,1024]{3,1,2,0:T(8,128)(2,1)S(1)} %bitcast.104, bf16[1,16,8,1024]{3,1,2,0:T(8,128)(2,1)S(1)} %bitcast.103, bf16[3,16,8,1024]{3,1,2,0:T(8,128)(2,1)S(1)} %bitcast.100, f32[1024]{0:T(1024)S(1)} %bitcast.139, ...), kind=kLoop, calls=%fused_computation.75 | loop fusion | flops 10878976 | bytes 1949696 | tf_op jit(solution)/shard_map/convert_element_type | solution.py:133
  22.8 0.3 copy.29
  23.0 0.1 reshape.226
  23.2 0.6 %convolution_convert_fusion = bf16[128,768]{0,1:T(8,128)(2,1)S(1)} fusion(bf16[128,1024]{1,0:T(8,128)(2,1)S(1)} %reshape.226, bf16[768,1024]{1,0:T(8,128)(2,1)S(1)} %copy-done), kind=kOutput, calls=%fused_computation.26 | convolution fusion | flops 201424896 | bytes 2031616 | tf_op jit(solution)/shard_map/dot_general | solution.py:104
  23.8 3.0 %collective-permute-start.5 = (bf16[128,4,2,64]{0,3,1,2:T(8,128)(2,1)S(1)}, bf16[128,4,2,64]{0,3,1,2:T(8,128)(2,1)S(1)}, u32[]{:S(2)}, u32[]{:S(2)}) collective-permute-start(bf16[128,4,2,64]{0,3,1,2:T(8,128)(2,1)S(1)} %get-tuple-element.16), channel_id=1, source_target_pairs={{0,16},{4,20},{8,24},{12,28},{16,0},{20,4},{24,8},{28,12},{1,17},{... | collective-permute-start | bytes 393224 | tf_op jit(solution)/shard_map/ppermute | solution.py:43
  26.8 2.1 %collective-permute-start.6 = (bf16[128,4,2,64]{0,3,1,2:T(8,128)(2,1)S(1)}, bf16[128,4,2,64]{0,3,1,2:T(8,128)(2,1)}, u32[]{:S(2)}, u32[]{:S(2)}) collective-permute-start(bf16[128,4,2,64]{0,3,1,2:T(8,128)(2,1)S(1)} %get-tuple-element.16), channel_id=1, source_target_pairs={{0,4},{4,8},{8,12},{12,0},{16,20},{20,24},{24,28},{28,16},{1,5},{5... | collective-permute-start | bytes 393224 | tf_op jit(solution)/shard_map/ppermute | solution.py:47
  28.8 0.1 collective-permute-start.8
  29.0 2.3 %collective-permute-start.10 = (bf16[128,4,2,64]{0,3,1,2:T(8,128)(2,1)S(1)}, bf16[128,4,2,64]{0,3,1,2:T(8,128)(2,1)S(1)}, u32[]{:S(2)}, u32[]{:S(2)}) collective-permute-start(bf16[128,4,2,64]{0,3,1,2:T(8,128)(2,1)S(1)} %get-tuple-element.16), channel_id=1, source_target_pairs={{0,12},{4,0},{8,4},{12,8},{16,28},{20,16},{24,20},{28,24},{1,13},{... | collective-permute-start | bytes 393224 | tf_op jit(solution)/shard_map/ppermute | solution.py:47
  31.3 0.1 reshape_squeeze.3
  31.4 0.3 constant_dynamic-slice_fusion.2
  31.7 0.1 copy.20
  31.8 0.1 copy.19
  31.9 1.6 %collective-permute-done.5 = bf16[128,4,2,64]{0,3,1,2:T(8,128)(2,1)S(1)} collective-permute-done((bf16[128,4,2,64]{0,3,1,2:T(8,128)(2,1)S(1)}, bf16[128,4,2,64]{0,3,1,2:T(8,128)(2,1)S(1)}, u32[]{:S(2)}, u32[]{:S(2)}) %collective-permute-start.5) | collective-permute-done | bytes 131104 | tf_op jit(solution)/shard_map/ppermute | solution.py:43
  33.5 2.1 %collective-permute-start.7 = (bf16[128,4,2,64]{0,3,1,2:T(8,128)(2,1)S(1)}, bf16[128,4,2,64]{0,3,1,2:T(8,128)(2,1)S(1)}, u32[]{:S(2)}, u32[]{:S(2)}) collective-permute-start(bf16[128,4,2,64]{0,3,1,2:T(8,128)(2,1)S(1)} %collective-permute-done.5), channel_id=1, source_target_pairs={{0,4},{4,8},{8,12},{12,0},{16,20},{20,24},{24,28},{28,16},{1,5},{5... | collective-permute-start | bytes 393224 | tf_op jit(solution)/shard_map/ppermute | solution.py:48
  35.6 0.0 collective-permute-start.9
  35.7 0.2 collective-permute-done.6
  35.8 1.3 %collective-permute-start.11 = (bf16[128,4,2,64]{0,3,1,2:T(8,128)(2,1)S(1)}, bf16[128,4,2,64]{0,3,1,2:T(8,128)(2,1)S(1)}, u32[]{:S(2)}, u32[]{:S(2)}) collective-permute-start(bf16[128,4,2,64]{0,3,1,2:T(8,128)(2,1)S(1)} %collective-permute-done.5), channel_id=1, source_target_pairs={{0,12},{4,0},{8,4},{12,8},{16,28},{20,16},{24,20},{28,24},{1,13},{... | collective-permute-start | bytes 393224 | tf_op jit(solution)/shard_map/ppermute | solution.py:48
  37.2 0.9 %constant_dynamic-update-slice_fusion.8 = bf16[1024,4,2,64]{0,3,1,2:T(8,128)(2,1)S(1)} fusion(bf16[1024,4,2,64]{0,3,1,2:T(8,128)(2,1)S(1)} %constant_dynamic-update-slice_fusion.9, bf16[128,4,2,64]{0,3,1,2:T(8,128)(2,1)} %collective-permute-done.6), kind=kLoop, calls=%fused_computation.95 | loop fusion | bytes 262144
  38.1 3.3 %collective-permute-done.7 = bf16[128,4,2,64]{0,3,1,2:T(8,128)(2,1)S(1)} collective-permute-done((bf16[128,4,2,64]{0,3,1,2:T(8,128)(2,1)S(1)}, bf16[128,4,2,64]{0,3,1,2:T(8,128)(2,1)S(1)}, u32[]{:S(2)}, u32[]{:S(2)}) %collective-permute-start.7) | collective-permute-done | bytes 131104 | tf_op jit(solution)/shard_map/ppermute | solution.py:48
  41.4 0.0 collective-permute-done.8
  41.5 0.9 %constant_dynamic-update-slice_fusion.6 = bf16[1024,4,2,64]{0,3,1,2:T(8,128)(2,1)S(1)} fusion(bf16[1024,4,2,64]{0,3,1,2:T(8,128)(2,1)S(1)} %constant_dynamic-update-slice_fusion.7, bf16[128,4,2,64]{0,3,1,2:T(8,128)(2,1)} %collective-permute-done.8), kind=kLoop, calls=%fused_computation.93 | loop fusion | bytes 262144
  42.4 0.0 collective-permute-done.9
  42.5 0.0 collective-permute-done.10
  42.5 0.2 collective-permute-done.11
  42.8 0.4 fusion.44
  43.1 0.0 copy-start.1
  43.1 0.3 fusion.4
  43.4 0.4 fusion.3
  43.8 0.1 copy.17
  43.9 0.1 reshape.228
  44.0 0.2 copy-done.1
  44.2 0.2 convolution_convert_fusion.1
  44.4 1.6 %collective-permute-start.13 = (bf16[32,1024]{1,0:T(8,128)(2,1)S(1)}, bf16[32,1024]{1,0:T(8,128)(2,1)S(1)}, u32[]{:S(2)}, u32[]{:S(2)}) collective-permute-start(bf16[32,1024]{1,0:T(8,128)(2,1)S(1)} %get-tuple-element.14), channel_id=1, source_target_pairs={{0,2},{1,3},{2,0},{3,1},{4,6},{5,7},{6,4},{7,5},{8,10},{9,11},{10,... | collective-permute-start | bytes 196616 | tf_op jit(solution)/shard_map/ppermute | solution.py:223
  46.0 0.0 collective-permute-start.14
  46.0 0.4 fusion.45
  46.3 0.3 fusion.6
  46.7 0.4 fusion.2
  47.0 0.1 copy.18
  47.1 0.1 dot_general.35
  47.2 0.2 fusion.35
  47.4 0.7 %collective-permute-start.12 = (f32[32,1024]{1,0:T(8,128)S(1)}, f32[32,1024]{1,0:T(8,128)S(1)}, u32[]{:S(2)}, u32[]{:S(2)}) collective-permute-start(f32[32,1024]{1,0:T(8,128)S(1)} %get-tuple-element.10), channel_id=1, source_target_pairs={{0,1},{1,0},{2,3},{3,2},{4,5},{5,4},{6,7},{7,6},{8,9},{9,8},{10,11... | collective-permute-start | bytes 393224 | tf_op jit(solution)/shard_map/ppermute | solution.py:235
  48.2 0.1 reshape.230
  48.2 0.5 %collective-permute-done.13 = bf16[32,1024]{1,0:T(8,128)(2,1)S(1)} collective-permute-done((bf16[32,1024]{1,0:T(8,128)(2,1)S(1)}, bf16[32,1024]{1,0:T(8,128)(2,1)S(1)}, u32[]{:S(2)}, u32[]{:S(2)}) %collective-permute-start.13) | collective-permute-done | bytes 65568 | tf_op jit(solution)/shard_map/ppermute | solution.py:223
  48.7 1.4 %collective-permute-done.14 = bf16[32,1024]{1,0:T(8,128)(2,1)S(1)} collective-permute-done((bf16[32,1024]{1,0:T(8,128)(2,1)S(1)}, bf16[32,1024]{1,0:T(8,128)(2,1)S(1)}, u32[]{:S(2)}, u32[]{:S(2)}) %collective-permute-start.14) | collective-permute-done | bytes 65568 | tf_op jit(solution)/shard_map/ppermute | solution.py:224
  50.2 0.1 add.233
  50.3 0.1 reshape.231
  50.3 0.7 %add_convert_fusion.1 = bf16[1,16,2,1024]{3,2,1,0:T(2,128)(2,1)} fusion(f32[1,16,2,1024]{3,2,1,0:T(2,128)S(1)} %add.233, f32[1,16,2,1024]{3,2,1,0:T(2,128)S(1)} %reshape.230, f32[1,16,2,1024]{3,2,1,0:T(2,128)S(1)} %reshape.231), kind=kLoop, calls=%fused_computation.81 | loop fusion | flops 98304 | bytes 458752 | tf_op jit(solution)/shard_map/convert_element_type | solution.py:238
  (19 shorter events, 0.5 us)
Async XLA Ops:
  0.0 23.1 %copy-start = (bf16[768,1024]{1,0:T(8,128)(2,1)S(1)}, bf16[768,1024]{1,0:T(8,128)(2,1)}, u32[]{:S(2)}) copy-start(bf16[768,1024]{1,0:T(8,128)(2,1)} %param.8) | copy-start | bytes 4718596
  0.0 8.7 %collective-permute-start = (bf16[1,16,2,1024]{3,2,1,0:T(2,128)(2,1)}, bf16[1,16,2,1024]{3,2,1,0:T(2,128)(2,1)S(1)}, u32[]{:S(2)}, u32[]{:S(2)}) collective-permute-start(bf16[1,16,2,1024]{3,2,1,0:T(2,128)(2,1)} %param.5), channel_id=1, source_target_pairs={{0,4},{4,8},{8,12},{12,16},{16,20},{20,24},{24,28},{1,5},{5,9},{9,... | collective-permute-start | bytes 196616 | tf_op jit(solution)/shard_map/ppermute | solution.py:22
  5.0 6.4 %collective-permute-start.1 = (bf16[1,16,2,1024]{3,2,1,0:T(2,128)(2,1)}, bf16[1,16,2,1024]{3,2,1,0:T(2,128)(2,1)S(1)}, u32[]{:S(2)}, u32[]{:S(2)}) collective-permute-start(bf16[1,16,2,1024]{3,2,1,0:T(2,128)(2,1)} %param.5), channel_id=1, source_target_pairs={{4,0},{8,4},{12,8},{16,12},{20,16},{24,20},{28,24},{5,1},{9,5},{13... | collective-permute-start | bytes 196616 | tf_op jit(solution)/shard_map/ppermute | solution.py:23
  11.4 1.8 %collective-permute-start.2 = (bf16[3,16,2,1024]{3,2,1,0:T(2,128)(2,1)S(1)}, bf16[3,16,2,1024]{3,2,1,0:T(2,128)(2,1)S(1)}, u32[]{:S(2)}, u32[]{:S(2)}) collective-permute-start(bf16[3,16,2,1024]{3,2,1,0:T(2,128)(2,1)S(1)} %constant_dynamic-update-slice_fusion), channel_id=1, source_target_pairs={{0,1},{1,0},{2,3},{3,2},{4,5},{5,4},{6,7},{7,6},{8,9},{9,8},{10,11... | collective-permute-start | bytes 589832 | tf_op jit(solution)/shard_map/ppermute | solution.py:64
  11.5 7.3 %collective-permute-start.3 = (bf16[3,16,2,1024]{3,2,1,0:T(2,128)(2,1)S(1)}, bf16[3,16,2,1024]{3,2,1,0:T(2,128)(2,1)S(1)}, u32[]{:S(2)}, u32[]{:S(2)}) collective-permute-start(bf16[3,16,2,1024]{3,2,1,0:T(2,128)(2,1)S(1)} %constant_dynamic-update-slice_fusion), channel_id=1, source_target_pairs={{0,2},{1,3},{2,0},{3,1},{4,6},{5,7},{6,4},{7,5},{8,10},{9,11},{10,... | collective-permute-start | bytes 589832 | tf_op jit(solution)/shard_map/ppermute | solution.py:68
  13.2 7.2 %copy-start.2 = (f32[1024]{0:T(1024)S(1)}, f32[1024]{0:T(1024)}, u32[]{:S(2)}) copy-start(f32[1024]{0:T(1024)} %param.7) | copy-start | bytes 12292
  18.8 1.4 %collective-permute-start.4 = (bf16[3,16,2,1024]{3,2,1,0:T(2,128)(2,1)S(1)}, bf16[3,16,2,1024]{3,2,1,0:T(2,128)(2,1)S(1)}, u32[]{:S(2)}, u32[]{:S(2)}) collective-permute-start(bf16[3,16,2,1024]{3,2,1,0:T(2,128)(2,1)S(1)} %collective-permute-done.3), channel_id=1, source_target_pairs={{0,1},{1,0},{2,3},{3,2},{4,5},{5,4},{6,7},{7,6},{8,9},{9,8},{10,11... | collective-permute-start | bytes 589832 | tf_op jit(solution)/shard_map/ppermute | solution.py:70
  23.8 9.7 %collective-permute-start.5 = (bf16[128,4,2,64]{0,3,1,2:T(8,128)(2,1)S(1)}, bf16[128,4,2,64]{0,3,1,2:T(8,128)(2,1)S(1)}, u32[]{:S(2)}, u32[]{:S(2)}) collective-permute-start(bf16[128,4,2,64]{0,3,1,2:T(8,128)(2,1)S(1)} %get-tuple-element.16), channel_id=1, source_target_pairs={{0,16},{4,20},{8,24},{12,28},{16,0},{20,4},{24,8},{28,12},{1,17},{... | collective-permute-start | bytes 393224 | tf_op jit(solution)/shard_map/ppermute | solution.py:43
  26.8 9.1 %collective-permute-start.6 = (bf16[128,4,2,64]{0,3,1,2:T(8,128)(2,1)S(1)}, bf16[128,4,2,64]{0,3,1,2:T(8,128)(2,1)}, u32[]{:S(2)}, u32[]{:S(2)}) collective-permute-start(bf16[128,4,2,64]{0,3,1,2:T(8,128)(2,1)S(1)} %get-tuple-element.16), channel_id=1, source_target_pairs={{0,4},{4,8},{8,12},{12,0},{16,20},{20,24},{24,28},{28,16},{1,5},{5... | collective-permute-start | bytes 393224 | tf_op jit(solution)/shard_map/ppermute | solution.py:47
  28.8 12.6 %collective-permute-start.8 = (bf16[128,4,2,64]{0,3,1,2:T(8,128)(2,1)S(1)}, bf16[128,4,2,64]{0,3,1,2:T(8,128)(2,1)}, u32[]{:S(2)}, u32[]{:S(2)}) collective-permute-start(bf16[128,4,2,64]{0,3,1,2:T(8,128)(2,1)S(1)} %get-tuple-element.16), channel_id=1, source_target_pairs={{0,8},{4,12},{8,0},{12,4},{16,24},{20,28},{24,16},{28,20},{1,9},{5... | collective-permute-start | bytes 393224 | tf_op jit(solution)/shard_map/ppermute | solution.py:47
  29.0 13.5 %collective-permute-start.10 = (bf16[128,4,2,64]{0,3,1,2:T(8,128)(2,1)S(1)}, bf16[128,4,2,64]{0,3,1,2:T(8,128)(2,1)S(1)}, u32[]{:S(2)}, u32[]{:S(2)}) collective-permute-start(bf16[128,4,2,64]{0,3,1,2:T(8,128)(2,1)S(1)} %get-tuple-element.16), channel_id=1, source_target_pairs={{0,12},{4,0},{8,4},{12,8},{16,28},{20,16},{24,20},{28,24},{1,13},{... | collective-permute-start | bytes 393224 | tf_op jit(solution)/shard_map/ppermute | solution.py:47
  33.5 7.9 %collective-permute-start.7 = (bf16[128,4,2,64]{0,3,1,2:T(8,128)(2,1)S(1)}, bf16[128,4,2,64]{0,3,1,2:T(8,128)(2,1)S(1)}, u32[]{:S(2)}, u32[]{:S(2)}) collective-permute-start(bf16[128,4,2,64]{0,3,1,2:T(8,128)(2,1)S(1)} %collective-permute-done.5), channel_id=1, source_target_pairs={{0,4},{4,8},{8,12},{12,0},{16,20},{20,24},{24,28},{28,16},{1,5},{5... | collective-permute-start | bytes 393224 | tf_op jit(solution)/shard_map/ppermute | solution.py:48
  35.6 6.8 %collective-permute-start.9 = (bf16[128,4,2,64]{0,3,1,2:T(8,128)(2,1)S(1)}, bf16[128,4,2,64]{0,3,1,2:T(8,128)(2,1)S(1)}, u32[]{:S(2)}, u32[]{:S(2)}) collective-permute-start(bf16[128,4,2,64]{0,3,1,2:T(8,128)(2,1)S(1)} %collective-permute-done.5), channel_id=1, source_target_pairs={{0,8},{4,12},{8,0},{12,4},{16,24},{20,28},{24,16},{28,20},{1,9},{5... | collective-permute-start | bytes 393224 | tf_op jit(solution)/shard_map/ppermute | solution.py:48
  35.8 6.9 %collective-permute-start.11 = (bf16[128,4,2,64]{0,3,1,2:T(8,128)(2,1)S(1)}, bf16[128,4,2,64]{0,3,1,2:T(8,128)(2,1)S(1)}, u32[]{:S(2)}, u32[]{:S(2)}) collective-permute-start(bf16[128,4,2,64]{0,3,1,2:T(8,128)(2,1)S(1)} %collective-permute-done.5), channel_id=1, source_target_pairs={{0,12},{4,0},{8,4},{12,8},{16,28},{20,16},{24,20},{28,24},{1,13},{... | collective-permute-start | bytes 393224 | tf_op jit(solution)/shard_map/ppermute | solution.py:48
  43.1 1.0 %copy-start.1 = (bf16[256,1024]{1,0:T(8,128)(2,1)S(1)}, bf16[256,1024]{1,0:T(8,128)(2,1)}, u32[]{:S(2)}) copy-start(bf16[256,1024]{1,0:T(8,128)(2,1)} %param.9) | copy-start | bytes 1572868
  44.4 4.3 %collective-permute-start.13 = (bf16[32,1024]{1,0:T(8,128)(2,1)S(1)}, bf16[32,1024]{1,0:T(8,128)(2,1)S(1)}, u32[]{:S(2)}, u32[]{:S(2)}) collective-permute-start(bf16[32,1024]{1,0:T(8,128)(2,1)S(1)} %get-tuple-element.14), channel_id=1, source_target_pairs={{0,2},{1,3},{2,0},{3,1},{4,6},{5,7},{6,4},{7,5},{8,10},{9,11},{10,... | collective-permute-start | bytes 196616 | tf_op jit(solution)/shard_map/ppermute | solution.py:223
  46.0 4.2 %collective-permute-start.14 = (bf16[32,1024]{1,0:T(8,128)(2,1)S(1)}, bf16[32,1024]{1,0:T(8,128)(2,1)S(1)}, u32[]{:S(2)}, u32[]{:S(2)}) collective-permute-start(bf16[32,1024]{1,0:T(8,128)(2,1)S(1)} %get-tuple-element.15), channel_id=1, source_target_pairs={{0,3},{1,2},{2,1},{3,0},{4,7},{5,6},{6,5},{7,4},{8,11},{9,10},{10,... | collective-permute-start | bytes 196616 | tf_op jit(solution)/shard_map/ppermute | solution.py:224
  47.4 2.8 %collective-permute-start.12 = (f32[32,1024]{1,0:T(8,128)S(1)}, f32[32,1024]{1,0:T(8,128)S(1)}, u32[]{:S(2)}, u32[]{:S(2)}) collective-permute-start(f32[32,1024]{1,0:T(8,128)S(1)} %get-tuple-element.10), channel_id=1, source_target_pairs={{0,1},{1,0},{2,3},{3,2},{4,5},{5,4},{6,7},{7,6},{8,9},{9,8},{10,11... | collective-permute-start | bytes 393224 | tf_op jit(solution)/shard_map/ppermute | solution.py:235
